TPU v7x, 32 devices: a whole 2x2x4 slice. The times are simulated.
32 devices in a mesh: groups: 2 (over y), video: 4 (over z), tensor: 4 (over x, core).
Axes of the slice: x: 2, y: 2, z: 4, core: 2. Of those that a mesh axis runs over, the one named last changes fastest.
Arguments:
- frames: bfloat16 [24, 256, 6144], P(('groups', 'video')), parts along dimension 0, may hold values from -610 to 610
- frame_video: int32 [24], P(('groups', 'video')), parts along dimension 0, may hold values from 0 to 3, never falling along the last dimension, each value on 1 to 6 neighbouring positions
- qkv_weight: bfloat16 [6144, 3, 3072], P('video', None, 'tensor'), may hold values from -0.078125 to 0.078125
- conn_weight: bfloat16 [3072, 3, 4096], P('tensor', None, 'video'), may hold values from -6 to 6
Outputs:
- summary: bfloat16 [384, 4096], P(('groups', 'video'), 'tensor'), parts along dimension 0
There are 2 independent parts, one for each index of `groups`. A program takes and returns all parts, laid end to end along the dimension named above; an argument that names none is the same for every part. Nothing has to cross between parts.
All inputs are finite; a program needn't handle non-finite values.
Results may differ from a plain program's by a relative error of at most 0.009.
Values may be sent and summed in bfloat16 or wider, within the bound.
No kernel may reach another device: no remote copies, remote signals or barrier semaphores. Data moves between devices by JAX's collectives and lax.ppermute only.
A program may use at most 192 MiB of HBM per device.

v0:
```python
import math

import jax
import jax.numpy as jnp
from jax import lax
from jax.sharding import PartitionSpec as P

HD = 128
PATCH = 256
POOL = 16


def rms_norm(values):
    return values * lax.rsqrt(jnp.mean(values * values, axis=-1, keepdims=True) + 1e-06)


def per_device(frames, frame_video, qkv_weight, conn_weight):
    scale = 1.0 / math.sqrt(HD)
    blocks = math.isqrt(POOL)
    inner = math.isqrt(PATCH) // blocks
    nframes = frames.shape[0]
    patch_rows = nframes * PATCH
    wide = frames.astype(jnp.float32)
    center = wide - jnp.mean(wide, axis=-1, keepdims=True)
    normed = center * lax.rsqrt(jnp.mean(center * center, axis=-1, keepdims=True) + 1e-06)
    normed = normed.astype(jnp.bfloat16).reshape(patch_rows, frames.shape[2])
    local_cols = qkv_weight.shape[1] * qkv_weight.shape[2]
    piece = lax.all_gather(qkv_weight, "video", axis=0, tiled=True)
    proj = jnp.dot(
        normed, piece.reshape(piece.shape[0], local_cols), preferred_element_type=jnp.float32
    )
    heads_local = qkv_weight.shape[2] // HD
    proj = proj.reshape(nframes, PATCH, 3, heads_local, HD)
    query = rms_norm(proj[:, :, 0]).astype(jnp.bfloat16)
    keys = rms_norm(proj[:, :, 1]).astype(jnp.bfloat16)
    values = proj[:, :, 2].astype(jnp.bfloat16)
    scores = jnp.einsum("fphd,fkhd->fhpk", query, keys, preferred_element_type=jnp.float32) * scale
    probs = jnp.exp(scores)
    probs = (probs / jnp.sum(probs, axis=-1, keepdims=True)).astype(jnp.bfloat16)
    attended = jnp.einsum("fhpk,fkhd->fphd", probs, values, preferred_element_type=jnp.float32)
    grid = attended.reshape(nframes, blocks, inner, blocks, inner, heads_local, HD)
    pooled = (
        jnp.mean(grid, axis=(2, 4)).reshape(nframes * POOL, heads_local * HD).astype(jnp.bfloat16)
    )
    rows = nframes * POOL
    partial_proj = jnp.einsum(
        "rc,ckt->rkt",
        pooled,
        lax.all_gather(conn_weight, "video", axis=2, tiled=True),
        preferred_element_type=jnp.float32,
    )
    clip_proj = lax.psum_scatter(
        partial_proj.astype(jnp.bfloat16), "tensor", scatter_dimension=2, tiled=True
    ).astype(jnp.float32)
    t_heads = clip_proj.shape[2] // HD
    tquery = rms_norm(clip_proj[:, 0].reshape(rows, t_heads, HD)).astype(jnp.bfloat16)
    tkey = rms_norm(clip_proj[:, 1].reshape(rows, t_heads, HD)).astype(jnp.bfloat16)
    tvalue = clip_proj[:, 2].astype(jnp.bfloat16)
    tkey_flat = tkey.reshape(rows, t_heads * HD)
    seg_rows = jnp.repeat(frame_video, POOL)
    query_frame = lax.axis_index("video") * nframes + jnp.arange(rows, dtype=jnp.int32) // POOL
    key_part = lax.all_gather(tkey_flat, "video", axis=0, tiled=True)
    value_part = lax.all_gather(tvalue, "video", axis=0, tiled=True)
    seg_part = lax.all_gather(seg_rows, "video", axis=0, tiled=True)
    count = key_part.shape[0]
    key_frame = jnp.arange(count, dtype=jnp.int32) // POOL
    allowed = (seg_part[None, :] == seg_rows[:, None]) & (
        key_frame[None, :] <= query_frame[:, None]
    )
    logits = (
        jnp.einsum(
            "rhd,khd->hrk",
            tquery,
            key_part.reshape(count, t_heads, HD),
            preferred_element_type=jnp.float32,
        )
        * scale
    )
    weights = jnp.where(allowed[None], jnp.exp(logits), jnp.float32(0.0))
    numer = jnp.einsum(
        "hrk,khd->rhd",
        weights.astype(jnp.bfloat16),
        value_part.reshape(count, t_heads, HD),
        preferred_element_type=jnp.float32,
    )
    denom = jnp.sum(weights, axis=-1)
    numer, denom = (numer, denom)
    summary = numer / jnp.transpose(denom)[:, :, None]
    return summary.reshape(rows, t_heads * HD).astype(jnp.bfloat16)


def solution(mesh):
    return jax.shard_map(
        per_device,
        mesh=mesh,
        in_specs=(
            P(("groups", "video"), None, None),
            P(("groups", "video")),
            P("video", None, "tensor"),
            P("tensor", None, "video"),
        ),
        out_specs=P(("groups", "video"), "tensor"),
        check_vma=False,
    )
```

profile of v0, /device:TPU:10, one launch (start us, length us, event | category | flops | bytes accessed | tf_op | source)
XLA Modules:
  0.0 892.0 jit_solution(1376324522640257826)
XLA Ops:
  6.5 10.3 %copy.32 = bf16[1536,3,768]{0,2,1:T(8,128)(2,1)} copy(bf16[1536,3,768]{2,0,1:T(8,128)(2,1)} %param.6) | data formatting | bytes 14155776 | tf_op args[2]
  16.9 0.7 all-gather.6.cloned.1.call-update
  17.7 5.2 convert_reduce_fusion
  22.9 1.2 copy-done
  24.0 2.6 fusion.2
  26.6 464.9 %all-gather.4.cloned.1.call-done = bf16[6144,3,768]{0,2,1:T(8,128)(2,1)} async-done(((bf16[1536,3,768]{0,2,1:T(8,128)(2,1)}), bf16[6144,3,768]{0,2,1:T(8,128)(2,1)}) %all-gather.4.cloned.1.call-update) | async-done | bytes 28311568 | tf_op jit(solution)/shard_map/all_gather | solution.py:28
  491.5 29.8 %fusion.5 = f32[3,256,3,6,128]{1,4,3,2,0:T(8,128)S(1)} fusion(bf16[3,6,128,6144,1]{3,2,1,0,4:T(8,128)(2,1)} %bitcast.92, bf16[3,256,6144]{2,1,0:T(8,128)(2,1)} %param.4, f32[3,256]{1,0:T(4,128)S(1)} %add_rsqrt_fusion.4, f32[3,256]{1,0:T(4,128)S(1)} %broadcast_multiply_fusion), kind=kOutput, calls=%fused_computation.7 | convolution fusion | flops 21762146304 | bytes 44832768 | tf_op jit(solution)/shard_map/dot_general | solution.py:29
  521.3 0.5 multiply_reduce_fusion.1
  521.9 1.2 fusion.9
  523.0 2.4 fusion.11
  525.4 2.0 copy.36
  527.5 1.0 reduce_sum.86
  528.5 0.1 reshape.178
  528.7 285.9 %all-gather.6.cloned.1.call-done = bf16[768,3,4096]{2,0,1:T(8,128)(2,1)} async-done(((bf16[768,3,1024]{2,0,1:T(8,128)(2,1)}), bf16[768,3,4096]{2,0,1:T(8,128)(2,1)}) %all-gather.6.cloned.1.call-update) | async-done | bytes 18874384 | tf_op jit(solution)/shard_map/all_gather | solution.py:49
  814.6 10.8 %convolution_convert_fusion = bf16[48,3,4096]{2,0,1:T(8,128)(2,1)} fusion(bf16[48,768,1]{1,0,2:T(8,128)(2,1)S(1)} %reshape.178, bf16[768,3,4096]{2,0,1:T(8,128)(2,1)} %all-gather.6.cloned.1.call-done), kind=kOutput, calls=%fused_computation.10 | convolution fusion | flops 906559488 | bytes 20127744 | tf_op jit(solution)/shard_map/rc,ckt->rkt/dot_general | solution.py:46
  825.5 0.1 reshape.171
  825.5 0.6 dynamic-slice
  826.8 0.2 dynamic-update-slice
  827.0 8.2 all-reduce
  835.3 16.0 %reduce-scatter.2.cloned.1.call-done = bf16[48,3,1024]{2,0,1:T(8,128)(2,1)} async-done(((bf16[48,3,4096]{2,0,1:T(8,128)(2,1)}), bf16[48,3,1024]{2,0,1:T(8,128)(2,1)}) %reduce-scatter.2.cloned.1.call-update) | async-done | bytes 294928 | tf_op jit(solution)/shard_map/reduce_scatter | solution.py:52
  851.3 0.9 slice.31
  852.2 15.2 %all-gather = bf16[192,1,1024]{2,0,1:T(8,128)(2,1)S(1)} all-gather(bf16[48,1,1024]{2,0,1:T(8,128)(2,1)S(1)} %slice.31), channel_id=2, replica_groups=mesh['groups'=2,'video'=4,'tensor'=4] {'video'}, dimensions={0}, use_global_device_ids=true | all-gather | bytes 491520 | tf_op jit(solution)/shard_map/all_gather | solution.py:63
  867.4 1.0 convert_element_type.61
  868.6 0.1 multiply_reduce_fusion.2
  868.8 0.1 copy.39
  868.8 0.1 multiply_convert_fusion.4
  869.0 0.1 reduce_sum.88
  869.3 0.1 mul.101
  869.5 14.7 %all_gather.19 = bf16[192,1024]{1,0:T(8,128)(2,1)S(1)} all-gather(bf16[48,1024]{1,0:T(8,128)(2,1)S(1)} %fusion.25), channel_id=1, replica_groups=mesh['groups'=2,'video'=4,'tensor'=4] {'video'}, dimensions={0}, use_global_device_ids=true | all-gather | bytes 491520 | tf_op jit(solution)/shard_map/all_gather | solution.py:62
  884.1 0.4 fusion.30
  884.6 0.3 fusion.21
  884.9 0.7 copy.70
  (30 shorter events, 0.8 us)
Async XLA Ops:
  6.5 485.0 %all-gather.4.cloned.1.call-start = ((), (), s32[]{:S(2)}) async-start(), calls=%async_computation.1 | async-start | bytes 35389440 | tf_op jit(solution)/shard_map/all_gather | solution.py:28
  16.9 797.7 %all-gather.6.cloned.1.call-start = ((), (), s32[]{:S(2)}) async-start(), calls=%async_computation.2 | async-start | bytes 23592960 | tf_op jit(solution)/shard_map/all_gather | solution.py:49
  17.6 833.7 %reduce-scatter.2.cloned.1.call-start = ((), (), s32[]{:S(2)}) async-start(), calls=%async_computation.3 | async-start | bytes 1474560 | tf_op jit(solution)/shard_map/reduce_scatter | solution.py:52
  17.7 6.4 copy-start
  528.6 296.7 %copy-start.1 = (s32[3]{0:T(128)S(1)}, s32[3]{0:T(128)}, u32[]{:S(2)}) copy-start(s32[3]{0:T(128)} %param.5) | copy-start | bytes 40
  528.6 296.9 %copy-start.2 = (u32[32]{0:T(128)S(1)}, u32[32]{0:T(128)}, u32[]{:S(2)}) copy-start(u32[32]{0:T(128)} %constant.63) | copy-start | bytes 388
Sparse Core Ops, SparseCore 0:
  17.0 474.4 all-gather.3
  493.1 321.4 all-gather.5
  825.5 25.7 reduce-scatter.1
where the time goes:
time: 895 us; the launch traced here: 892 us
  waiting for transfers between devices  768 us (86%)
  matrix products  44.8 us (5%)
  blocking collectives  38 us (4%)
  local copies, waits for them, and re-layouts  16.8 us (2%)
  between operations  14 us (2%)
  other arithmetic  10.9 us (1%)
    all_gather x1, waiting for transfers between devices, per_device(): piece = lax.all_gather(qkv_weight, 'video', axis=0, tiled=True)  465 us
    all_gather x1, waiting for transfers between devices, per_device(): lax.all_gather(conn_weight, 'video', axis=2, tiled=True)  286 us
    dot_general x1, matrix products, per_device(): jnp.dot(normed, piece.reshape(piece.shape[0], local_cols), preferred_elem...  29.8 us
  transfers between devices with their start and end apart: 3, of which 3 were waited for; matrix products, arithmetic and copies ran while one was open for 5% of the time, Pallas kernels for 0%

commit v1 on v0

v1 whole, which is shorter than its diff:
```python
import math

import jax
import jax.numpy as jnp
from jax import lax
from jax.sharding import PartitionSpec as P

HD = 128
PATCH = 256
POOL = 16


def rms_norm(values):
    return values * lax.rsqrt(jnp.mean(values * values, axis=-1, keepdims=True) + 1e-06)


def per_device(frames, frame_video, qkv_weight, conn_weight):
    scale = 1.0 / math.sqrt(HD)
    blocks = math.isqrt(POOL)
    inner = math.isqrt(PATCH) // blocks
    nframes = frames.shape[0]
    patch_rows = nframes * PATCH
    n_video = lax.axis_size("video")
    n_groups = lax.axis_size("groups")
    wide = frames.astype(jnp.float32)
    center = wide - jnp.mean(wide, axis=-1, keepdims=True)
    normed = center * lax.rsqrt(jnp.mean(center * center, axis=-1, keepdims=True) + 1e-06)
    normed = normed.astype(jnp.bfloat16).reshape(patch_rows, frames.shape[2])
    local_cols = qkv_weight.shape[1] * qkv_weight.shape[2]
    share = qkv_weight.shape[0] // n_groups
    mine = lax.dynamic_slice_in_dim(qkv_weight, lax.axis_index("groups") * share, share, axis=0)
    piece = lax.all_gather(mine, ("video", "groups"), axis=0, tiled=True)
    proj = jnp.dot(
        normed, piece.reshape(piece.shape[0], local_cols), preferred_element_type=jnp.float32
    )
    heads_local = qkv_weight.shape[2] // HD
    proj = proj.reshape(nframes, PATCH, 3, heads_local, HD)
    query = rms_norm(proj[:, :, 0]).astype(jnp.bfloat16)
    keys = rms_norm(proj[:, :, 1]).astype(jnp.bfloat16)
    values = proj[:, :, 2].astype(jnp.bfloat16)
    scores = jnp.einsum("fphd,fkhd->fhpk", query, keys, preferred_element_type=jnp.float32) * scale
    probs = jnp.exp(scores)
    probs = (probs / jnp.sum(probs, axis=-1, keepdims=True)).astype(jnp.bfloat16)
    attended = jnp.einsum("fhpk,fkhd->fphd", probs, values, preferred_element_type=jnp.float32)
    grid = attended.reshape(nframes, blocks, inner, blocks, inner, heads_local, HD)
    pooled = (
        jnp.mean(grid, axis=(2, 4)).reshape(nframes * POOL, heads_local * HD).astype(jnp.bfloat16)
    )
    pooled_all = lax.all_gather(pooled, "video", axis=0, tiled=True)
    rows = pooled_all.shape[0]
    partial_proj = jnp.einsum(
        "rc,ckt->rkt", pooled_all, conn_weight, preferred_element_type=jnp.float32
    )
    clip_rows = lax.psum_scatter(
        partial_proj.astype(jnp.bfloat16), "tensor", scatter_dimension=0, tiled=True
    )
    clip_rows = lax.all_gather(clip_rows, "video", axis=2, tiled=True)
    clip_proj = lax.all_to_all(clip_rows, "tensor", 2, 0, tiled=True).astype(jnp.float32)
    t_heads = clip_proj.shape[2] // HD
    out_rows = rows // n_video
    first = lax.axis_index("video") * out_rows
    own = lax.dynamic_slice_in_dim(clip_proj[:, 0], first, out_rows, axis=0)
    tquery = rms_norm(own.reshape(out_rows, t_heads, HD)).astype(jnp.bfloat16)
    tkey = rms_norm(clip_proj[:, 1].reshape(rows, t_heads, HD)).astype(jnp.bfloat16)
    tvalue = clip_proj[:, 2].reshape(rows, t_heads, HD).astype(jnp.bfloat16)
    video_all = lax.all_gather(frame_video, "video", axis=0, tiled=True)
    seg_rows = jnp.repeat(video_all, POOL)
    row_frame = jnp.arange(rows, dtype=jnp.int32) // POOL
    own_seg = lax.dynamic_slice_in_dim(seg_rows, first, out_rows)
    own_frame = lax.dynamic_slice_in_dim(row_frame, first, out_rows)
    allowed = (seg_rows[None, :] == own_seg[:, None]) & (row_frame[None, :] <= own_frame[:, None])
    logits = jnp.einsum("rhd,khd->hrk", tquery, tkey, preferred_element_type=jnp.float32) * scale
    weights = jnp.where(allowed[None], jnp.exp(logits), jnp.float32(0.0))
    numer = jnp.einsum(
        "hrk,khd->rhd", weights.astype(jnp.bfloat16), tvalue, preferred_element_type=jnp.float32
    )
    denom = jnp.sum(weights, axis=-1)
    summary = numer / jnp.transpose(denom)[:, :, None]
    return summary.reshape(out_rows, t_heads * HD).astype(jnp.bfloat16)


def solution(mesh):
    return jax.shard_map(
        per_device,
        mesh=mesh,
        in_specs=(
            P(("groups", "video"), None, None),
            P(("groups", "video")),
            P("video", None, "tensor"),
            P("tensor", None, "video"),
        ),
        out_specs=P(("groups", "video"), "tensor"),
        check_vma=False,
    )
```

time: 895 us -> 724 us (0.81)
  waiting for transfers between devices: 768 us -> 592 us
  local copies, waits for them, and re-layouts: 16.8 us -> 35.3 us
  blocking collectives: 38 us -> 21.5 us
    all_gather x2, waiting for transfers between devices: 751 us -> 562 us  [the longest x1 529 us: per_device(): piece = lax.all_gather(mine, ('video', 'groups'), axis=0, tiled=True)]
    all_gather x2 -> x1, blocking collectives: 29.9 us -> 14.6 us  [per_device(): pooled_all = lax.all_gather(pooled, 'video', axis=0, tiled=True)]
    reduce_scatter x1, waiting for transfers between devices: 16 us -> 25 us  [per_device(): lax.psum_scatter(partial_proj.astype(jnp.bfloat16), 'tensor', scatter_dim...]
    unnamed x13 -> x16, local copies, waits for them, and re-layouts: 12.5 us -> 18.1 us
  transfers between devices with their start and end apart: 3 -> 4, of which waited for: 3 -> 4; matrix products, arithmetic and copies ran while one was open for 5% -> 2% of each run, Pallas kernels for 0% -> 0%
where the time goes in v1:
time: 724 us; the launch traced here: 720 us
  waiting for transfers between devices  592 us (82%)
  matrix products  38.6 us (5%)
  local copies, waits for them, and re-layouts  35.3 us (5%)
  blocking collectives  21.5 us (3%)
  other arithmetic  14.4 us (2%)
  between operations  14 us (2%)
    all_gather x1, waiting for transfers between devices, per_device(): piece = lax.all_gather(mine, ('video', 'groups'), axis=0, tiled=True)  529 us
    all_gather x1, waiting for transfers between devices, per_device(): clip_rows = lax.all_gather(clip_rows, 'video', axis=2, tiled=True)  32.5 us
    dot_general x1, matrix products, per_device(): jnp.dot(normed, piece.reshape(piece.shape[0], local_cols), preferred_elem...  29.8 us
    reduce_scatter x1, waiting for transfers between devices, per_device(): lax.psum_scatter(partial_proj.astype(jnp.bfloat16), 'tensor', scatter_dim...  25 us
    unnamed x16, local copies, waits for them, and re-layouts  18.1 us
    all_gather x1, blocking collectives, per_device(): pooled_all = lax.all_gather(pooled, 'video', axis=0, tiled=True)  14.6 us
  transfers between devices with their start and end apart: 4, of which 4 were waited for; matrix products, arithmetic and copies ran while one was open for 2% of the time, Pallas kernels for 0%

profile of v1, /device:TPU:10, one launch (start us, length us, event | category | flops | bytes accessed | tf_op | source)
XLA Modules:
  0.0 719.8 jit_solution(10306326276578816863)
XLA Ops:
  6.5 2.2 constant_dynamic-slice_fusion
  8.8 3.7 copy.80
  12.6 5.0 convert_reduce_fusion
  17.6 6.6 fusion.2
  24.2 529.0 %all-gather.3.cloned.1.call-done = bf16[6144,3,768]{0,2,1:T(8,128)(2,1)} async-done(((bf16[768,3,768]{0,2,1:T(8,128)(2,1)}), bf16[6144,3,768]{0,2,1:T(8,128)(2,1)}) %all-gather.3.cloned.1.call-update) | async-done | bytes 28311568 | tf_op jit(solution)/shard_map/all_gather | solution.py:32
  553.2 29.8 %fusion.5 = f32[3,256,3,6,128]{1,4,3,2,0:T(8,128)S(1)} fusion(bf16[3,6,128,6144,1]{3,2,1,0,4:T(8,128)(2,1)} %bitcast.96, bf16[3,256,6144]{2,1,0:T(8,128)(2,1)} %param.4, f32[3,256]{1,0:T(4,128)S(1)} %add_rsqrt_fusion.4, f32[3,256]{1,0:T(4,128)S(1)} %broadcast_multiply_fusion), kind=kOutput, calls=%fused_computation.7 | convolution fusion | flops 21762146304 | bytes 44832768 | tf_op jit(solution)/shard_map/dot_general | solution.py:33
  583.0 0.5 multiply_reduce_fusion.1
  583.6 1.2 fusion.9
  584.7 2.4 fusion.11
  587.1 2.0 copy.61
  589.2 1.0 reduce_sum.86
  590.2 14.6 %all_gather.13 = bf16[192,768]{1,0:T(8,128)(2,1)S(1)} all-gather(bf16[48,768]{1,0:T(8,128)(2,1)S(1)} %bitcast.95), channel_id=1, replica_groups=mesh['groups'=2,'video'=4,'tensor'=4] {'video'}, dimensions={0}, use_global_device_ids=true | all-gather | bytes 368640 | tf_op jit(solution)/shard_map/all_gather | solution.py:49
  604.8 4.5 convolution_convert_fusion
  609.4 25.0 %reduce-scatter.2.cloned.1.call-done = bf16[48,3,1024]{2,0,1:T(8,128)(2,1)} async-done(((bf16[192,3,1024]{2,0,1:T(8,128)(2,1)}), bf16[48,3,1024]{2,0,1:T(8,128)(2,1)}) %reduce-scatter.2.cloned.1.call-update) | async-done | bytes 294928 | tf_op jit(solution)/shard_map/reduce_scatter | solution.py:54
  634.3 32.5 %all-gather.5.cloned.1.call-done = bf16[48,3,4096]{2,0,1:T(8,128)(2,1)} async-done(((bf16[48,3,1024]{2,0,1:T(8,128)(2,1)}), bf16[48,3,4096]{2,0,1:T(8,128)(2,1)}) %all-gather.5.cloned.1.call-update) | async-done | bytes 1179664 | tf_op jit(solution)/shard_map/all_gather | solution.py:57
  666.9 6.2 copy.63
  673.1 6.9 reshape.157
  680.0 4.1 all-to-all-start
  684.0 0.6 dynamic-slice.1
  685.3 0.2 dynamic-update-slice
  685.5 7.0 all-reduce
  692.9 5.3 all-to-all-done
  698.2 6.3 reshape.158
  704.5 5.4 copy.65
  709.9 0.4 bitcast_convert_fusion
  710.8 0.1 multiply_convert_fusion.5
  710.9 0.1 copy.84
  711.1 0.3 multiply_reduce_fusion.2
  711.5 0.3 multiply_convert_fusion.4
  711.9 0.5 fusion.29
  712.4 0.3 fusion.21
  712.6 0.7 copy.98
  (35 shorter events, 1.4 us)
Async XLA Ops:
  6.5 546.7 %all-gather.3.cloned.1.call-start = ((), (), s32[]{:S(2)}) async-start(), calls=%async_computation.2 | async-start | bytes 31850496 | tf_op jit(solution)/shard_map/all_gather | solution.py:32
  12.5 621.8 %reduce-scatter.2.cloned.1.call-start = ((), (), s32[]{:S(2)}) async-start(), calls=%async_computation.3 | async-start | bytes 1474560 | tf_op jit(solution)/shard_map/reduce_scatter | solution.py:54
  609.3 57.6 %all-gather.5.cloned.1.call-start = ((), (), s32[]{:S(2)}) async-start(), calls=%async_computation.4 | async-start | bytes 1474560 | tf_op jit(solution)/shard_map/all_gather | solution.py:57
  673.1 11.0 %copy-start.1 = (u32[32]{0:T(128)S(1)}, u32[32]{0:T(128)}, u32[]{:S(2)}) copy-start(u32[32]{0:T(128)} %constant.70) | copy-start | bytes 388
  673.1 12.2 %copy-start = (s32[3]{0:T(128)S(1)}, s32[3]{0:T(128)}, u32[]{:S(2)}) copy-start(s32[3]{0:T(128)} %param.5) | copy-start | bytes 40
  680.0 18.3 %all-to-all-start = ((bf16[4,2,73728]{2,1,0:T(2,128)(2,1)}), bf16[4,2,73728]{2,1,0:T(2,128)(2,1)S(1)}, u32[]{:S(2)}, u32[]{:S(2)}) async-start(bf16[4,2,73728]{2,1,0:T(2,128)(2,1)} %reshape.157), calls=%async_computation.1 | async-start | bytes 2359296 | tf_op jit(solution)/shard_map/all_to_all | solution.py:58
Sparse Core Ops, SparseCore 0:
  12.7 540.5 all-gather.2
  609.4 24.8 reduce-scatter.1
  636.0 30.8 all-gather.4

commit v2 on v1

--- a/solution.py
+++ b/solution.py
@@ -14,6 +14,47 @@
     return values * lax.rsqrt(jnp.mean(values * values, axis=-1, keepdims=True) + 1e-06)
 
 
+SPLIT = 1
+
+
+def project(normed, qkv_weight, n_video, n_groups):
+    assert n_groups == 2
+    v = lax.axis_index("video")
+    g = lax.axis_index("groups")
+    local_rows, parts, cols = qkv_weight.shape
+    half = local_rows // 2
+    srows = half // SPLIT
+    n = normed.shape[0]
+    blocks = normed.reshape(n, n_video, 2, SPLIT, srows)
+    outs = []
+    for j in range(parts):
+        acc = None
+        for s in range(SPLIT):
+            mine = lax.dynamic_slice_in_dim(qkv_weight[:, j], g * half + s * srows, srows, axis=0)
+            other = lax.dynamic_slice_in_dim(qkv_weight[:, j], (1 - g) * half + s * srows, srows, axis=0)
+            gathered = lax.all_gather(mine, "video", axis=0, tiled=False)
+            twice = jnp.concatenate([gathered, gathered], axis=0)
+            onward = lax.dynamic_slice_in_dim(twice, v + 1, n_video - 1, axis=0)
+            received = lax.ppermute(onward, "groups", [(0, 1), (1, 0)])
+            cut = blocks[:, :, :, s]
+            own_half = lax.dynamic_index_in_dim(cut, g, axis=2, keepdims=False)
+            other_half = lax.dynamic_index_in_dim(cut, 1 - g, axis=2, keepdims=False)
+            own_piece = lax.dynamic_index_in_dim(other_half, v, axis=1, keepdims=False)
+            rolled = lax.dynamic_slice_in_dim(
+                jnp.concatenate([other_half, other_half], axis=1), v + 1, n_video - 1, axis=1
+            )
+            part = jnp.dot(own_piece, other, preferred_element_type=jnp.float32)
+            part = part + jnp.einsum(
+                "nvd,vdc->nc", own_half, gathered, preferred_element_type=jnp.float32
+            )
+            part = part + jnp.einsum(
+                "nvd,vdc->nc", rolled, received, preferred_element_type=jnp.float32
+            )
+            acc = part if acc is None else acc + part
+        outs.append(acc)
+    return jnp.stack(outs, axis=1)
+
+
 def per_device(frames, frame_video, qkv_weight, conn_weight):
     scale = 1.0 / math.sqrt(HD)
     blocks = math.isqrt(POOL)
@@ -26,15 +67,8 @@
     center = wide - jnp.mean(wide, axis=-1, keepdims=True)
     normed = center * lax.rsqrt(jnp.mean(center * center, axis=-1, keepdims=True) + 1e-06)
     normed = normed.astype(jnp.bfloat16).reshape(patch_rows, frames.shape[2])
-    local_cols = qkv_weight.shape[1] * qkv_weight.shape[2]
-    share = qkv_weight.shape[0] // n_groups
-    mine = lax.dynamic_slice_in_dim(qkv_weight, lax.axis_index("groups") * share, share, axis=0)
-    piece = lax.all_gather(mine, ("video", "groups"), axis=0, tiled=True)
-    proj = jnp.dot(
-        normed, piece.reshape(piece.shape[0], local_cols), preferred_element_type=jnp.float32
-    )
     heads_local = qkv_weight.shape[2] // HD
-    proj = proj.reshape(nframes, PATCH, 3, heads_local, HD)
+    proj = project(normed, qkv_weight, n_video, n_groups).reshape(nframes, PATCH, 3, heads_local, HD)
     query = rms_norm(proj[:, :, 0]).astype(jnp.bfloat16)
     keys = rms_norm(proj[:, :, 1]).astype(jnp.bfloat16)
     values = proj[:, :, 2].astype(jnp.bfloat16)

time: 724 us -> 551 us (0.76)
  the two profiles are of different devices: /device:TPU:10 before, /device:TPU:0 now
where the time goes in v2:
time: 551 us; the launch traced here: 541 us
  waiting for transfers between devices  271 us (49%)
  local copies, waits for them, and re-layouts  104 us (19%)
  other arithmetic  62.5 us (11%)
  matrix products  59.4 us (11%)
  blocking collectives  22 us (4%)
  between operations  14.6 us (3%)
  starting transfers between devices  8.24 us (1%)
    all_gather x3, waiting for transfers between devices, project(): gathered = lax.all_gather(mine, 'video', axis=0, tiled=False)  176 us
    ppermute x3, waiting for transfers between devices, project(): received = lax.ppermute(onward, 'groups', [(0, 1), (1, 0)])  32.2 us
    all_gather x1, waiting for transfers between devices, per_device(): clip_rows = lax.all_gather(clip_rows, 'video', axis=2, tiled=True)  32 us
    dynamic_slice x2, local copies, waits for them, and re-layouts, project(): other_half = lax.dynamic_index_in_dim(cut, 1 - g, axis=2, keepdims=False)  26.1 us
    concatenate x3, other arithmetic, project(): twice = jnp.concatenate([gathered, gathered], axis=0)  25.4 us
    reduce_scatter x1, waiting for transfers between devices, per_device(): lax.psum_scatter(partial_proj.astype(jnp.bfloat16), 'tensor', scatter_dim...  24 us
    dot_general x3, matrix products, project(): jnp.einsum('nvd,vdc->nc', own_half, gathered, preferred_element_type=jnp....  21.6 us
    dot_general x3, matrix products, project(): jnp.einsum('nvd,vdc->nc', rolled, received, preferred_element_type=jnp.fl...  21.6 us
  transfers between devices with their start and end apart: 9, of which 7 were waited for; matrix products, arithmetic and copies ran while one was open for 28% of the time, Pallas kernels for 0%

profile of v2, /device:TPU:0, one launch (start us, length us, event | category | flops | bytes accessed | tf_op | source)
XLA Modules:
  0.0 541.5 jit_solution(10868952410632623928)
XLA Ops:
  6.5 5.7 %fusion.54 = (bf16[1536,1,768]{2,0,1:T(8,128)(2,1)}, bf16[1536,1,768]{2,0,1:T(8,128)(2,1)S(1)}, bf16[1536,1,768]{2,0,1:T(8,128)(2,1)}) fusion(bf16[1536,3,768]{2,0,1:T(8,128)(2,1)} %param.6), kind=kLoop, calls=%fused_computation.108 | loop fusion | bytes 14155776 | tf_op jit(solution)/shard_map/slice | solution.py:34
  18.4 5.2 convert_reduce_fusion
  27.7 12.4 %fusion.3 = bf16[3,256,6144]{2,1,0:T(8,128)(2,1)} fusion(bf16[3,256,6144]{2,1,0:T(8,128)(2,1)} %param.4, f32[3,256]{1,0:T(4,128)S(1)} %add_rsqrt_fusion.4, f32[3,256]{1,0:T(4,128)S(1)} %broadcast_multiply_fusion), kind=kLoop, calls=%fused_computation.5 | loop fusion | flops 18874368 | bytes 18880512 | tf_op jit(solution)/shard_map/convert_element_type | solution.py:69
  40.0 15.3 %squeeze_reshape_reshape.2 = bf16[768,4,2,768]{3,2,1,0:T(2,128)(2,1)} reshape(bf16[3,256,6144]{2,1,0:T(8,128)(2,1)} %fusion.3) | data formatting | bytes 18874368 | tf_op jit(solution)/shard_map/squeeze;reshape;reshape | solution.py:39
  55.3 22.4 %constant_dynamic-slice_fusion.2 = (bf16[768,4,1,768]{3,2,1,0:T(2,128)(2,1)S(1)}, bf16[768,4,1,768]{3,2,1,0:T(2,128)(2,1)}) fusion(bf16[768,4,2,768]{3,2,1,0:T(2,128)(2,1)} %squeeze_reshape_reshape.2, s32[]{:T(128)S(6)} %select_n.61, s32[]{:T(128)S(6)} %select_n.64), kind=kLoop, calls=%fused_computation.88 | loop fusion | bytes 18874376 | tf_op jit(solution)/shard_map/jit(dynamic_index_in_dim)/dynamic_slice | solution.py:41
  81.5 4.3 constant_dynamic-slice_fusion.5
  93.3 13.7 %all-gather.10.cloned.1.call-done = bf16[3072,1,768]{2,0,1:T(8,128)(2,1)} async-done(((bf16[768,1,768]{2,0,1:T(8,128)(2,1)}), bf16[3072,1,768]{2,0,1:T(8,128)(2,1)}) %all-gather.10.cloned.1.call-update) | async-done | bytes 4718608 | tf_op jit(solution)/shard_map/all_gather | solution.py:35
  107.0 5.1 fusion.13
  117.2 79.2 %all-gather.12.cloned.1.call-done = bf16[3072,1,768]{2,0,1:T(8,128)(2,1)} async-done(((bf16[768,1,768]{2,0,1:T(8,128)(2,1)}), bf16[3072,1,768]{2,0,1:T(8,128)(2,1)}) %all-gather.12.cloned.1.call-update) | async-done | bytes 4718608 | tf_op jit(solution)/shard_map/all_gather | solution.py:35
  196.4 5.0 fusion.12
  202.9 83.0 %all-gather.14.cloned.1.call-done = bf16[3072,1,768]{2,0,1:T(8,128)(2,1)} async-done(((bf16[768,1,768]{2,0,1:T(8,128)(2,1)}), bf16[3072,1,768]{2,0,1:T(8,128)(2,1)}) %all-gather.14.cloned.1.call-update) | async-done | bytes 4718608 | tf_op jit(solution)/shard_map/all_gather | solution.py:35
  285.9 15.4 %fusion.11 = bf16[3,768,768]{2,1,0:T(8,128)(2,1)} fusion(s32[]{:T(128)S(6)} %select_n.66, bf16[4,768,768]{2,1,0:T(8,128)(2,1)} %bitcast.125), kind=kLoop, calls=%fused_computation.24 | loop fusion | flops 1769472 | bytes 8257540 | tf_op jit(solution)/shard_map/concatenate | solution.py:36
  302.8 10.3 %fusion.8 = f32[768,768,1]{1,0,2:T(8,128)S(1)} fusion(bf16[4,768,768]{2,1,0:T(8,128)(2,1)} %bitcast.120, bf16[768,4,1,768]{3,2,1,0:T(2,128)(2,1)} %get-tuple-element.6), kind=kOutput, calls=%fused_computation.18 | convolution fusion | flops 3623878656 | bytes 11796480 | tf_op jit(solution)/shard_map/nvd,vdc->nc/dot_general | solution.py:47
  313.2 5.6 %fusion.6 = f32[768,768,1]{1,0,2:T(8,128)} fusion(bf16[4,768,768]{2,1,0:T(8,128)(2,1)S(1)} %bitcast.124, bf16[768,4,1,768]{3,2,1,0:T(2,128)(2,1)S(1)} %bitcast.116), kind=kOutput, calls=%fused_computation.16 | convolution fusion | flops 3623878656 | bytes 11796480 | tf_op jit(solution)/shard_map/nvd,vdc->nc/dot_general | solution.py:47
  318.8 5.7 %fusion.4 = f32[768,768,1]{1,0,2:T(8,128)} fusion(bf16[4,768,768]{2,1,0:T(8,128)(2,1)S(1)} %bitcast.128, bf16[768,4,1,768]{3,2,1,0:T(2,128)(2,1)S(1)} %bitcast.116), kind=kOutput, calls=%fused_computation.14 | convolution fusion | flops 3623878656 | bytes 11796480 | tf_op jit(solution)/shard_map/nvd,vdc->nc/dot_general | solution.py:47
  324.5 6.0 %fusion.15 = bf16[768,768]{1,0:T(8,128)(2,1)} fusion(f32[768,768]{1,0:T(8,128)S(1)} %copy-done.7, f32[768,768,1]{1,0,2:T(8,128)S(1)} %fusion.8, bf16[768,3,768]{2,0,1:T(8,128)(2,1)S(1)} %fusion.14, bf16[3,768,768]{2,1,0:T(8,128)(2,1)} %collective-permute-done), kind=kOutput, calls=%fused_computation.37 | convolution fusion | flops 2719678464 | bytes 12976128 | tf_op jit(solution)/shard_map/nvd,vdc->nc/dot_general | solution.py:50
  330.5 3.8 convert_element_type.64
  334.3 6.9 %bitcast_add_fusion.2 = f32[768,768]{1,0:T(8,128)} fusion(f32[768,768]{1,0:T(8,128)} %fusion.22, f32[768,768,1]{1,0,2:T(8,128)} %fusion.6, bf16[768,3,768]{2,0,1:T(8,128)(2,1)S(1)} %fusion.14, bf16[3,768,768]{2,1,0:T(8,128)(2,1)} %collective-permute-done.1), kind=kOutput, calls=%fused_computation.34 | convolution fusion | flops 2719088640 | bytes 14155776 | tf_op jit(solution)/shard_map/nvd,vdc->nc/dot_general | solution.py:50
  347.8 32.2 %collective-permute-done.2 = bf16[3,768,768]{2,1,0:T(8,128)(2,1)} collective-permute-done((bf16[3,768,768]{2,1,0:T(8,128)(2,1)}, bf16[3,768,768]{2,1,0:T(8,128)(2,1)}, u32[]{:S(2)}, u32[]{:S(2)}) %collective-permute-start.2) | collective-permute-done | bytes 3538976 | tf_op jit(solution)/shard_map/ppermute | solution.py:38
  380.0 8.8 %bitcast_add_fusion = f32[768,768]{1,0:T(8,128)} fusion(f32[768,768]{1,0:T(8,128)} %fusion.20, f32[768,768,1]{1,0,2:T(8,128)} %fusion.4, bf16[768,3,768]{2,0,1:T(8,128)(2,1)} %copy-done.3, bf16[3,768,768]{2,1,0:T(8,128)(2,1)} %collective-permute-done.2), kind=kOutput, calls=%fused_computation.32 | convolution fusion | flops 2719088640 | bytes 14155776 | tf_op jit(solution)/shard_map/nvd,vdc->nc/dot_general | solution.py:50
  388.7 3.8 squeeze.35
  400.8 3.8 multiply_convert_fusion
  411.6 14.6 %all_gather.33 = bf16[192,768]{1,0:T(8,128)(2,1)S(1)} all-gather(bf16[48,768]{1,0:T(8,128)(2,1)S(1)} %bitcast.132), channel_id=1, replica_groups=mesh['groups'=2,'video'=4,'tensor'=4] {'video'}, dimensions={0}, use_global_device_ids=true | all-gather | bytes 368640 | tf_op jit(solution)/shard_map/all_gather | solution.py:83
  426.1 4.5 convolution_convert_fusion
  430.7 24.0 %reduce-scatter.2.cloned.1.call-done = bf16[48,3,1024]{2,0,1:T(8,128)(2,1)} async-done(((bf16[192,3,1024]{2,0,1:T(8,128)(2,1)}), bf16[48,3,1024]{2,0,1:T(8,128)(2,1)}) %reduce-scatter.2.cloned.1.call-update) | async-done | bytes 294928 | tf_op jit(solution)/shard_map/reduce_scatter | solution.py:88
  454.8 32.0 %all-gather.8.cloned.1.call-done = bf16[48,3,4096]{2,0,1:T(8,128)(2,1)} async-done(((bf16[48,3,1024]{2,0,1:T(8,128)(2,1)}), bf16[48,3,4096]{2,0,1:T(8,128)(2,1)}) %all-gather.8.cloned.1.call-update) | async-done | bytes 1179664 | tf_op jit(solution)/shard_map/all_gather | solution.py:91
  486.7 6.2 %copy.92 = bf16[48,3,4096]{0,1,2:T(4,128)(2,1)} copy(bf16[48,3,4096]{2,0,1:T(8,128)(2,1)} %all-gather.8.cloned.1.call-done) | data formatting | bytes 2359296 | tf_op jit(solution)/shard_map/all_gather | solution.py:91
  492.9 6.9 %reshape.176 = bf16[4,2,73728]{2,1,0:T(2,128)(2,1)} reshape(bf16[4096,3,48]{2,1,0:T(4,128)(2,1)} %bitcast.112) | data formatting | bytes 2359296
  504.9 7.4 %all-reduce = s32[12]{0:T(128)S(1)} all-reduce(s32[12]{0:T(128)S(1)} %dynamic-update-slice), channel_id=1, replica_groups=mesh['groups'=2,'video'=4,'tensor'=4] {'video'}, use_global_device_ids=true, to_apply=%add | all-reduce | flops 12 | bytes 96
  512.7 6.5 %all-to-all-done = bf16[4,2,73728]{2,1,0:T(2,128)(2,1)S(1)} async-done(((bf16[4,2,73728]{2,1,0:T(2,128)(2,1)}), bf16[4,2,73728]{2,1,0:T(2,128)(2,1)S(1)}, u32[]{:S(2)}, u32[]{:S(2)}) %all-to-all-start) | async-done | bytes 1179680 | tf_op jit(solution)/shard_map/all_to_all | solution.py:92
  519.2 6.6 %reshape.177 = bf16[4096,3,48]{2,1,0:T(4,128)(2,1)} reshape(bf16[4,2,73728]{2,1,0:T(2,128)(2,1)S(1)} %all-to-all-done) | data formatting | bytes 2359296
  525.7 5.4 copy.94
  (105 shorter events, 59.6 us)
Async XLA Ops:
  6.5 100.4 %all-gather.10.cloned.1.call-start = ((), (), s32[]{:S(2)}) async-start(), calls=%async_computation.4 | async-start | bytes 5898240 | tf_op jit(solution)/shard_map/all_gather | solution.py:35
  14.7 181.7 %all-gather.12.cloned.1.call-start = ((), (), s32[]{:S(2)}) async-start(), calls=%async_computation.5 | async-start | bytes 5898240 | tf_op jit(solution)/shard_map/all_gather | solution.py:35
  17.1 268.8 %all-gather.14.cloned.1.call-start = ((), (), s32[]{:S(2)}) async-start(), calls=%async_computation.6 | async-start | bytes 5898240 | tf_op jit(solution)/shard_map/all_gather | solution.py:35
  18.3 436.4 %reduce-scatter.2.cloned.1.call-start = ((), (), s32[]{:S(2)}) async-start(), calls=%async_computation.2 | async-start | bytes 1474560 | tf_op jit(solution)/shard_map/reduce_scatter | solution.py:88
  18.4 6.7 %copy-start = (bf16[3,256,6144]{2,1,0:T(8,128)(2,1)S(1)}, bf16[3,256,6144]{2,1,0:T(8,128)(2,1)}, u32[]{:S(2)}) copy-start(bf16[3,256,6144]{2,1,0:T(8,128)(2,1)} %param.4) | copy-start | bytes 28311556
  81.5 4.3 copy-start.2
  85.7 2.5 copy-start.1
  112.0 212.5 %collective-permute-start = (bf16[3,768,768]{2,1,0:T(8,128)(2,1)}, bf16[3,768,768]{2,1,0:T(8,128)(2,1)}, u32[]{:S(2)}, u32[]{:S(2)}) collective-permute-start(bf16[3,768,768]{2,1,0:T(8,128)(2,1)} %fusion.13), channel_id=1, source_target_pairs={{0,16},{16,0},{1,17},{17,1},{2,18},{18,2},{3,19},{19,3},{4,20},{20... | collective-permute-start | bytes 10616840 | tf_op jit(solution)/shard_map/ppermute | solution.py:38
  117.2 217.0 %copy-start.3 = (bf16[768,3,768]{2,0,1:T(8,128)(2,1)}, bf16[768,3,768]{2,0,1:T(8,128)(2,1)S(1)}, u32[]{:S(2)}) copy-start(bf16[768,3,768]{2,0,1:T(8,128)(2,1)S(1)} %fusion.14) | copy-start | bytes 10616836
  201.4 132.8 %collective-permute-start.1 = (bf16[3,768,768]{2,1,0:T(8,128)(2,1)}, bf16[3,768,768]{2,1,0:T(8,128)(2,1)}, u32[]{:S(2)}, u32[]{:S(2)}) collective-permute-start(bf16[3,768,768]{2,1,0:T(8,128)(2,1)} %fusion.12), channel_id=1, source_target_pairs={{0,16},{16,0},{1,17},{17,1},{2,18},{18,2},{3,19},{19,3},{4,20},{20... | collective-permute-start | bytes 10616840 | tf_op jit(solution)/shard_map/ppermute | solution.py:38
  285.9 27.2 %slice-start = ((s8[9437184]{0:T(1024)(128)(4,1)}), s8[1048576]{0:T(1024)(128)(4,1)S(1)}, s32[]{:S(2)}) async-start(s8[9437184]{0:T(1024)(128)(4,1)} %bitcast.115), calls=%async_computation.7 | async-start | bytes 2097152
  285.9 27.3 %slice-start.3 = ((s8[4718592]{0:T(1024)(128)(4,1)}), s8[4194304]{0:T(1024)(128)(4,1)S(1)}, s32[]{:S(2)}) async-start(s8[4718592]{0:T(1024)(128)(4,1)} %bitcast.122), calls=%async_computation.10 | async-start | bytes 8388608
  301.3 78.7 %collective-permute-start.2 = (bf16[3,768,768]{2,1,0:T(8,128)(2,1)}, bf16[3,768,768]{2,1,0:T(8,128)(2,1)}, u32[]{:S(2)}, u32[]{:S(2)}) collective-permute-start(bf16[3,768,768]{2,1,0:T(8,128)(2,1)} %fusion.11), channel_id=1, source_target_pairs={{0,16},{16,0},{1,17},{17,1},{2,18},{18,2},{3,19},{19,3},{4,20},{20... | collective-permute-start | bytes 10616840 | tf_op jit(solution)/shard_map/ppermute | solution.py:38
  302.8 10.4 %slice-start.1 = ((s8[9437184]{0:T(1024)(128)(4,1)}), s8[4194304]{0:T(1024)(128)(4,1)S(1)}, s32[]{:S(2)}) async-start(s8[9437184]{0:T(1024)(128)(4,1)} %bitcast.115), calls=%async_computation.8 | async-start | bytes 8388608
  302.8 10.4 %slice-start.2 = ((s8[9437184]{0:T(1024)(128)(4,1)}), s8[4194304]{0:T(1024)(128)(4,1)S(1)}, s32[]{:S(2)}) async-start(s8[9437184]{0:T(1024)(128)(4,1)} %bitcast.115), calls=%async_computation.9 | async-start | bytes 8388608
  302.8 10.4 %slice-start.4 = ((s8[4718592]{0:T(1024)(128)(4,1)}), s8[524288]{0:T(1024)(128)(4,1)S(1)}, s32[]{:S(2)}) async-start(s8[4718592]{0:T(1024)(128)(4,1)} %bitcast.122), calls=%async_computation.11 | async-start | bytes 1048576
  302.8 16.0 %slice-start.5 = ((s8[4718592]{0:T(1024)(128)(4,1)}), s8[4194304]{0:T(1024)(128)(4,1)S(1)}, s32[]{:S(2)}) async-start(s8[4718592]{0:T(1024)(128)(4,1)} %bitcast.126), calls=%async_computation.12 | async-start | bytes 8388608
  313.2 5.6 %slice-start.6 = ((s8[4718592]{0:T(1024)(128)(4,1)}), s8[524288]{0:T(1024)(128)(4,1)S(1)}, s32[]{:S(2)}) async-start(s8[4718592]{0:T(1024)(128)(4,1)} %bitcast.126), calls=%async_computation.13 | async-start | bytes 1048576
  318.8 5.7 %copy-start.7 = (f32[768,768]{1,0:T(8,128)S(1)}, f32[768,768]{1,0:T(8,128)}, u32[]{:S(2)}) copy-start(f32[768,768]{1,0:T(8,128)} %fusion.24) | copy-start | bytes 7077892
  404.6 1.4 copy-start.4
  430.7 56.0 %all-gather.8.cloned.1.call-start = ((), (), s32[]{:S(2)}) async-start(), calls=%async_computation.3 | async-start | bytes 1474560 | tf_op jit(solution)/shard_map/all_gather | solution.py:91
  492.9 10.4 %copy-start.6 = (u32[32]{0:T(128)S(1)}, u32[32]{0:T(128)}, u32[]{:S(2)}) copy-start(u32[32]{0:T(128)} %constant.125) | copy-start | bytes 388
  492.9 11.7 %copy-start.5 = (s32[3]{0:T(128)S(1)}, s32[3]{0:T(128)}, u32[]{:S(2)}) copy-start(s32[3]{0:T(128)} %param.5) | copy-start | bytes 40
  499.8 19.4 %all-to-all-start = ((bf16[4,2,73728]{2,1,0:T(2,128)(2,1)}), bf16[4,2,73728]{2,1,0:T(2,128)(2,1)S(1)}, u32[]{:S(2)}, u32[]{:S(2)}) async-start(bf16[4,2,73728]{2,1,0:T(2,128)(2,1)} %reshape.176), calls=%async_computation.1 | async-start | bytes 2359296 | tf_op jit(solution)/shard_map/all_to_all | solution.py:92
Sparse Core Ops, SparseCore 0:
  14.8 92.0 all-gather.9
  108.5 87.8 all-gather.11
  198.0 87.8 all-gather.13
  430.8 23.8 reduce-scatter.1
  456.2 30.4 all-gather.7

commit v3 on v2

--- a/solution.py
+++ b/solution.py
@@ -14,7 +14,7 @@
     return values * lax.rsqrt(jnp.mean(values * values, axis=-1, keepdims=True) + 1e-06)
 
 
-SPLIT = 1
+SPLIT = 2
 
 
 def project(normed, qkv_weight, n_video, n_groups):
@@ -67,6 +67,8 @@
     center = wide - jnp.mean(wide, axis=-1, keepdims=True)
     normed = center * lax.rsqrt(jnp.mean(center * center, axis=-1, keepdims=True) + 1e-06)
     normed = normed.astype(jnp.bfloat16).reshape(patch_rows, frames.shape[2])
+    video_all = lax.all_gather(frame_video, "video", axis=0, tiled=True)
+    video_all, normed = lax.optimization_barrier((video_all, normed))
     heads_local = qkv_weight.shape[2] // HD
     proj = project(normed, qkv_weight, n_video, n_groups).reshape(nframes, PATCH, 3, heads_local, HD)
     query = rms_norm(proj[:, :, 0]).astype(jnp.bfloat16)
@@ -85,11 +87,17 @@
     partial_proj = jnp.einsum(
         "rc,ckt->rkt", pooled_all, conn_weight, preferred_element_type=jnp.float32
     )
-    clip_rows = lax.psum_scatter(
-        partial_proj.astype(jnp.bfloat16), "tensor", scatter_dimension=0, tiled=True
-    )
-    clip_rows = lax.all_gather(clip_rows, "video", axis=2, tiled=True)
-    clip_proj = lax.all_to_all(clip_rows, "tensor", 2, 0, tiled=True).astype(jnp.float32)
+    n_tensor = lax.axis_size("tensor")
+    if n_video == n_tensor:
+        summed = lax.psum(partial_proj.astype(jnp.bfloat16), "tensor")
+        swap = [(a * n_tensor + b, b * n_tensor + a) for a in range(n_video) for b in range(n_tensor)]
+        clip_proj = lax.ppermute(summed, ("video", "tensor"), swap).astype(jnp.float32)
+    else:
+        clip_rows = lax.psum_scatter(
+            partial_proj.astype(jnp.bfloat16), "tensor", scatter_dimension=0, tiled=True
+        )
+        clip_rows = lax.all_gather(clip_rows, "video", axis=2, tiled=True)
+        clip_proj = lax.all_to_all(clip_rows, "tensor", 2, 0, tiled=True).astype(jnp.float32)
     t_heads = clip_proj.shape[2] // HD
     out_rows = rows // n_video
     first = lax.axis_index("video") * out_rows
@@ -97,7 +105,6 @@
     tquery = rms_norm(own.reshape(out_rows, t_heads, HD)).astype(jnp.bfloat16)
     tkey = rms_norm(clip_proj[:, 1].reshape(rows, t_heads, HD)).astype(jnp.bfloat16)
     tvalue = clip_proj[:, 2].reshape(rows, t_heads, HD).astype(jnp.bfloat16)
-    video_all = lax.all_gather(frame_video, "video", axis=0, tiled=True)
     seg_rows = jnp.repeat(video_all, POOL)
     row_frame = jnp.arange(rows, dtype=jnp.int32) // POOL
     own_seg = lax.dynamic_slice_in_dim(seg_rows, first, out_rows)

time: 551 us -> 562 us (1.020)
  the two profiles are of different devices: /device:TPU:0 before, /device:TPU:10 now
where the time goes in v3:
time: 562 us; the launch traced here: 551 us
  waiting for transfers between devices  293 us (52%)
  matrix products  94.4 us (17%)
  local copies, waits for them, and re-layouts  61.9 us (11%)
  other arithmetic  52 us (9%)
  blocking collectives  23.5 us (4%)
  between operations  15.1 us (3%)
  starting transfers between devices  10.7 us (2%)
    all_gather x6, waiting for transfers between devices, project(): gathered = lax.all_gather(mine, 'video', axis=0, tiled=False)  161 us
    ppermute x1, waiting for transfers between devices, per_device(): lax.ppermute(summed, ('video', 'tensor'), swap).astype(jnp.float32)  52.3 us
    ppermute x6, waiting for transfers between devices, project(): received = lax.ppermute(onward, 'groups', [(0, 1), (1, 0)])  40.7 us
    dot_general x6, matrix products, project(): jnp.einsum('nvd,vdc->nc', own_half, gathered, preferred_element_type=jnp....  38.9 us
    psum x1, waiting for transfers between devices, per_device(): summed = lax.psum(partial_proj.astype(jnp.bfloat16), 'tensor')  37.7 us
    dot_general x6, matrix products, project(): jnp.einsum('nvd,vdc->nc', rolled, received, preferred_element_type=jnp.fl...  27.5 us
    dot_general x6, matrix products, project(): part = jnp.dot(own_piece, other, preferred_element_type=jnp.float32)  19.4 us
    concatenate x6, other arithmetic, project(): twice = jnp.concatenate([gathered, gathered], axis=0)  15.7 us
  transfers between devices with their start and end apart: 14, of which 9 were waited for; matrix products, arithmetic and copies ran while one was open for 31% of the time, Pallas kernels for 0%

profile of v3, /device:TPU:10, one launch (start us, length us, event | category | flops | bytes accessed | tf_op | source)
XLA Modules:
  0.0 551.1 jit_solution(7432853954058970552)
XLA Ops:
  6.5 5.7 %fusion.95 = (bf16[1536,1,768]{2,0,1:T(8,128)(2,1)}, bf16[1536,1,768]{2,0,1:T(8,128)(2,1)S(1)}, bf16[1536,1,768]{2,0,1:T(8,128)(2,1)}) fusion(bf16[1536,3,768]{2,0,1:T(8,128)(2,1)} %param.6), kind=kLoop, calls=%fused_computation.163 | loop fusion | bytes 14155776 | tf_op jit(solution)/shard_map/slice | solution.py:34
  21.0 5.5 convert_reduce_fusion
  30.6 12.3 %fusion.3 = bf16[3,256,6144]{2,1,0:T(8,128)(2,1)} fusion(bf16[3,256,6144]{2,1,0:T(8,128)(2,1)} %param.4, f32[3,256]{1,0:T(4,128)S(1)} %add_rsqrt_fusion.4, f32[3,256]{1,0:T(4,128)S(1)} %broadcast_multiply_fusion), kind=kLoop, calls=%fused_computation.5 | loop fusion | flops 18874368 | bytes 18880512 | tf_op jit(solution)/shard_map/convert_element_type | solution.py:69
  44.4 8.9 %all-reduce = s32[12]{0:T(128)S(1)} all-reduce(s32[12]{0:T(128)S(1)} %dynamic-update-slice), channel_id=1, replica_groups=mesh['groups'=2,'video'=4,'tensor'=4] {'video'}, use_global_device_ids=true, to_apply=%add | all-reduce | flops 12 | bytes 96 | tf_op jit(solution)/shard_map/optimization_barrier | solution.py:71
  53.3 12.6 %copy.74 = bf16[768,6144]{0,1:T(8,128)(2,1)} copy(bf16[768,6144]{1,0:T(8,128)(2,1)} %bitcast.179) | data formatting | bytes 18874368 | tf_op jit(solution)/shard_map/optimization_barrier | solution.py:71
  65.9 8.4 %fusion.94 = (bf16[768,4,2,1,384]{0,4,3,2,1:T(8,128)(2,1)}, bf16[768,4,2,1,384]{0,4,3,2,1:T(8,128)(2,1)}) fusion(bf16[768,4,2,2,384]{0,4,3,2,1:T(8,128)(2,1)} %bitcast.180), kind=kLoop, calls=%fused_computation.162 | loop fusion | bytes 18874368 | tf_op jit(solution)/shard_map/slice | solution.py:39
  74.4 3.7 fusion.54
  83.8 3.5 fusion.59
  93.6 4.3 copy.78
  121.5 46.1 %all-gather.17.cloned.1.call-done = bf16[1536,1,768]{2,0,1:T(8,128)(2,1)} async-done(((bf16[384,1,768]{2,0,1:T(8,128)(2,1)}), bf16[1536,1,768]{2,0,1:T(8,128)(2,1)}) %all-gather.17.cloned.1.call-update) | async-done | bytes 2359312 | tf_op jit(solution)/shard_map/all_gather | solution.py:35
  167.6 3.4 fusion.31
  171.0 5.7 %fusion.15 = f32[768,768,1]{1,0,2:T(8,128)} fusion(bf16[4,384,768]{2,1,0:T(8,128)(2,1)S(1)} %bitcast.182, bf16[768,4,2,1,384]{0,4,3,2,1:T(8,128)(2,1)} %get-tuple-element.9, s32[]{:T(128)S(6)} %select_n.89), kind=kOutput, calls=%fused_computation.39 | convolution fusion | flops 1811939328 | bytes 7077892 | tf_op jit(solution)/shard_map/nvd,vdc->nc/dot_general | solution.py:47
  176.8 3.5 fusion.9
  180.3 3.5 fusion.13
  183.8 34.6 %all-gather.19.cloned.1.call-done = bf16[1536,1,768]{2,0,1:T(8,128)(2,1)} async-done(((bf16[384,1,768]{2,0,1:T(8,128)(2,1)}), bf16[1536,1,768]{2,0,1:T(8,128)(2,1)}) %all-gather.19.cloned.1.call-update) | async-done | bytes 2359312 | tf_op jit(solution)/shard_map/all_gather | solution.py:35
  218.3 14.4 %fusion.7 = f32[768,768,1]{1,0,2:T(8,128)} fusion(bf16[4,384,768]{2,1,0:T(8,128)(2,1)} %bitcast.189, bf16[768,4,2,1,384]{0,4,3,2,1:T(8,128)(2,1)} %get-tuple-element.10, s32[]{:T(128)S(6)} %select_n.89), kind=kOutput, calls=%fused_computation.31 | convolution fusion | flops 1811939328 | bytes 7077892 | tf_op jit(solution)/shard_map/nvd,vdc->nc/dot_general | solution.py:47
  236.7 32.4 %all-gather.21.cloned.1.call-done = bf16[1536,1,768]{2,0,1:T(8,128)(2,1)} async-done(((bf16[384,1,768]{2,0,1:T(8,128)(2,1)}), bf16[1536,1,768]{2,0,1:T(8,128)(2,1)}) %all-gather.21.cloned.1.call-update) | async-done | bytes 2359312 | tf_op jit(solution)/shard_map/all_gather | solution.py:35
  269.1 5.8 %fusion.11 = f32[768,768,1]{1,0,2:T(8,128)} fusion(bf16[4,384,768]{2,1,0:T(8,128)(2,1)} %bitcast.185, bf16[768,4,2,1,384]{0,4,3,2,1:T(8,128)(2,1)} %get-tuple-element.9, s32[]{:T(128)S(6)} %select_n.89), kind=kOutput, calls=%fused_computation.35 | convolution fusion | flops 1811939328 | bytes 7077892 | tf_op jit(solution)/shard_map/nvd,vdc->nc/dot_general | solution.py:47
  274.9 44.9 %all-gather.23.cloned.1.call-done = bf16[1536,1,768]{2,0,1:T(8,128)(2,1)} async-done(((bf16[384,1,768]{2,0,1:T(8,128)(2,1)}), bf16[1536,1,768]{2,0,1:T(8,128)(2,1)}) %all-gather.23.cloned.1.call-update) | async-done | bytes 2359312 | tf_op jit(solution)/shard_map/all_gather | solution.py:35
  319.8 6.0 %fusion.5 = f32[768,768,1]{1,0,2:T(8,128)} fusion(bf16[4,384,768]{2,1,0:T(8,128)(2,1)} %bitcast.191, bf16[768,4,2,1,384]{0,4,3,2,1:T(8,128)(2,1)} %get-tuple-element.10, s32[]{:T(128)S(6)} %select_n.89), kind=kOutput, calls=%fused_computation.29 | convolution fusion | flops 1811939328 | bytes 7077892 | tf_op jit(solution)/shard_map/nvd,vdc->nc/dot_general | solution.py:47
  334.9 3.5 fusion.20
  338.4 4.6 fusion.98
  345.5 8.3 %fusion.18 = f32[768,768]{1,0:T(8,128)} fusion(f32[768,768]{1,0:T(8,128)} %fusion.50, f32[768,768,1]{1,0,2:T(8,128)} %fusion.7, f32[768,768,1]{1,0,2:T(8,128)} %fusion.98, f32[768,768]{1,0:T(8,128)} %fusion.52, f32[768,768,1]{1,0,2:T(8,128)} %fusion.13, bf16[768,3,384]{2,0,1:T(8,128)(2,1)S(1)} %fusion.33, bf16[3,384,768]{2,1,0:T(8,128)(2,1)} %collective-permute-done.3), kind=kOutput, calls=%fused_computation.47 | convolution fusion | flops 1361903616 | bytes 17694720 | tf_op jit(solution)/shard_map/nvd,vdc->nc/dot_general | solution.py:50
  353.7 3.8 squeeze.64
  360.7 3.5 multiply_convert_fusion.1
  364.1 7.3 %collective-permute-done.4 = bf16[3,384,768]{2,1,0:T(8,128)(2,1)} collective-permute-done((bf16[3,384,768]{2,1,0:T(8,128)(2,1)}, bf16[3,384,768]{2,1,0:T(8,128)(2,1)}, u32[]{:S(2)}, u32[]{:S(2)}) %collective-permute-start.4) | collective-permute-done | bytes 1769504 | tf_op jit(solution)/shard_map/ppermute | solution.py:38
  374.6 33.3 %collective-permute-done.5 = bf16[3,384,768]{2,1,0:T(8,128)(2,1)} collective-permute-done((bf16[3,384,768]{2,1,0:T(8,128)(2,1)}, bf16[3,384,768]{2,1,0:T(8,128)(2,1)}, u32[]{:S(2)}, u32[]{:S(2)}) %collective-permute-start.5) | collective-permute-done | bytes 1769504 | tf_op jit(solution)/shard_map/ppermute | solution.py:38
  408.0 4.8 fusion.17
  427.5 14.6 %all_gather.55 = bf16[192,768]{1,0:T(8,128)(2,1)S(1)} all-gather(bf16[48,768]{1,0:T(8,128)(2,1)S(1)} %bitcast.200), channel_id=1, replica_groups=mesh['groups'=2,'video'=4,'tensor'=4] {'video'}, dimensions={0}, use_global_device_ids=true | all-gather | bytes 368640 | tf_op jit(solution)/shard_map/all_gather | solution.py:85
  442.1 4.5 convolution_convert_fusion
  446.7 37.7 %all-reduce.3.cloned.1.call-done = bf16[192,3,1024]{2,0,1:T(8,128)(2,1)} async-done(((bf16[192,3,1024]{2,0,1:T(8,128)(2,1)}), bf16[192,3,1024]{2,0,1:T(8,128)(2,1)}) %all-reduce.3.cloned.1.call-update) | async-done | bytes 1179664 | tf_op jit(solution)/shard_map/psum | solution.py:92
  488.2 52.3 %collective-permute-done.6 = bf16[192,3,1024]{2,0,1:T(8,128)(2,1)S(1)} collective-permute-done((bf16[192,3,1024]{2,0,1:T(8,128)(2,1)}, bf16[192,3,1024]{2,0,1:T(8,128)(2,1)S(1)}, u32[]{:S(2)}, u32[]{:S(2)}) %collective-permute-start.6) | collective-permute-done | bytes 1179680 | tf_op jit(solution)/shard_map/ppermute | solution.py:94
  (158 shorter events, 92.7 us)
Async XLA Ops:
  6.5 102.3 %all-gather.13.cloned.1.call-start = ((), (), s32[]{:S(2)}) async-start(), calls=%async_computation.1 | async-start | bytes 2949120 | tf_op jit(solution)/shard_map/all_gather | solution.py:35
  12.2 7.0 %copy-start.9 = (bf16[1536,1,768]{2,0,1:T(8,128)(2,1)}, bf16[1536,1,768]{2,0,1:T(8,128)(2,1)S(1)}, u32[]{:S(2)}) copy-start(bf16[1536,1,768]{2,0,1:T(8,128)(2,1)S(1)} %get-tuple-element.12) | copy-start | bytes 7077892
  15.5 101.2 %all-gather.15.cloned.1.call-start = ((), (), s32[]{:S(2)}) async-start(), calls=%async_computation.2 | async-start | bytes 2949120 | tf_op jit(solution)/shard_map/all_gather | solution.py:35
  16.2 151.4 %all-gather.17.cloned.1.call-start = ((), (), s32[]{:S(2)}) async-start(), calls=%async_computation.3 | async-start | bytes 2949120 | tf_op jit(solution)/shard_map/all_gather | solution.py:35
  18.6 199.7 %all-gather.19.cloned.1.call-start = ((), (), s32[]{:S(2)}) async-start(), calls=%async_computation.4 | async-start | bytes 2949120 | tf_op jit(solution)/shard_map/all_gather | solution.py:35
  19.2 249.9 %all-gather.21.cloned.1.call-start = ((), (), s32[]{:S(2)}) async-start(), calls=%async_computation.5 | async-start | bytes 2949120 | tf_op jit(solution)/shard_map/all_gather | solution.py:35
  20.4 299.5 %all-gather.23.cloned.1.call-start = ((), (), s32[]{:S(2)}) async-start(), calls=%async_computation.6 | async-start | bytes 2949120 | tf_op jit(solution)/shard_map/all_gather | solution.py:35
  21.0 463.4 %all-reduce.3.cloned.1.call-start = ((), (), s32[]{:S(2)}) async-start(), calls=%async_computation | async-start | bytes 2359296 | tf_op jit(solution)/shard_map/psum | solution.py:92
  21.0 7.0 %copy-start = (bf16[3,256,6144]{2,1,0:T(8,128)(2,1)S(1)}, bf16[3,256,6144]{2,1,0:T(8,128)(2,1)}, u32[]{:S(2)}) copy-start(bf16[3,256,6144]{2,1,0:T(8,128)(2,1)} %param.4) | copy-start | bytes 28311556
  30.6 12.3 %copy-start.25 = (u32[32]{0:T(128)S(1)}, u32[32]{0:T(128)}, u32[]{:S(2)}) copy-start(u32[32]{0:T(128)} %constant.186) | copy-start | bytes 388
  30.6 13.5 %copy-start.24 = (s32[3]{0:T(128)S(1)}, s32[3]{0:T(128)}, u32[]{:S(2)}) copy-start(s32[3]{0:T(128)} %param.5) | copy-start | bytes 40
  65.9 12.2 %copy-start.11 = (bf16[1536,1,768]{2,0,1:T(8,128)(2,1)S(1)}, bf16[1536,1,768]{2,0,1:T(8,128)(2,1)}, u32[]{:S(2)}) copy-start(bf16[1536,1,768]{2,0,1:T(8,128)(2,1)} %get-tuple-element.13) | copy-start | bytes 7077892
  112.1 219.0 %collective-permute-start = (bf16[3,384,768]{2,1,0:T(8,128)(2,1)}, bf16[3,384,768]{2,1,0:T(8,128)(2,1)}, u32[]{:S(2)}, u32[]{:S(2)}) collective-permute-start(bf16[3,384,768]{2,1,0:T(8,128)(2,1)} %fusion.34), channel_id=1, source_target_pairs={{0,16},{16,0},{1,17},{17,1},{2,18},{18,2},{3,19},{19,3},{4,20},{20... | collective-permute-start | bytes 5308424 | tf_op jit(solution)/shard_map/ppermute | solution.py:38
  116.7 60.0 %slice-start = ((s8[4718592]{0:T(1024)(128)(4,1)}), s8[524288]{0:T(1024)(128)(4,1)S(1)}, s32[]{:S(2)}) async-start(s8[4718592]{0:T(1024)(128)(4,1)} %bitcast.175), calls=%async_computation.7 | async-start | bytes 1048576
  120.0 214.8 %collective-permute-start.1 = (bf16[3,384,768]{2,1,0:T(8,128)(2,1)}, bf16[3,384,768]{2,1,0:T(8,128)(2,1)}, u32[]{:S(2)}, u32[]{:S(2)}) collective-permute-start(bf16[3,384,768]{2,1,0:T(8,128)(2,1)} %fusion.32), channel_id=1, source_target_pairs={{0,16},{16,0},{1,17},{17,1},{2,18},{18,2},{3,19},{19,3},{4,20},{20... | collective-permute-start | bytes 5308424 | tf_op jit(solution)/shard_map/ppermute | solution.py:38
  167.6 9.1 %slice-start.1 = ((s8[4718592]{0:T(1024)(128)(4,1)}), s8[4194304]{0:T(1024)(128)(4,1)S(1)}, s32[]{:S(2)}) async-start(s8[4718592]{0:T(1024)(128)(4,1)} %bitcast.175), calls=%async_computation.8 | async-start | bytes 8388608
  167.6 9.1 %copy-start.13 = (bf16[1536,1,768]{2,0,1:T(8,128)(2,1)S(1)}, bf16[1536,1,768]{2,0,1:T(8,128)(2,1)}, u32[]{:S(2)}) copy-start(bf16[1536,1,768]{2,0,1:T(8,128)(2,1)} %all-gather.15.cloned.1.call-done) | copy-start | bytes 7077892
  167.6 12.7 %slice-start.2 = ((s8[4718592]{0:T(1024)(128)(4,1)}), s8[524288]{0:T(1024)(128)(4,1)S(1)}, s32[]{:S(2)}) async-start(s8[4718592]{0:T(1024)(128)(4,1)} %bitcast.177), calls=%async_computation.9 | async-start | bytes 1048576
  171.0 9.2 %slice-start.3 = ((s8[4718592]{0:T(1024)(128)(4,1)}), s8[4194304]{0:T(1024)(128)(4,1)S(1)}, s32[]{:S(2)}) async-start(s8[4718592]{0:T(1024)(128)(4,1)} %bitcast.177), calls=%async_computation.10 | async-start | bytes 8388608
  218.3 14.4 %copy-start.16 = (bf16[1536,1,768]{2,0,1:T(8,128)(2,1)S(1)}, bf16[1536,1,768]{2,0,1:T(8,128)(2,1)}, u32[]{:S(2)}) copy-start(bf16[1536,1,768]{2,0,1:T(8,128)(2,1)} %all-gather.19.cloned.1.call-done) | copy-start | bytes 7077892
  234.7 103.7 %collective-permute-start.2 = (bf16[3,384,768]{2,1,0:T(8,128)(2,1)}, bf16[3,384,768]{2,1,0:T(8,128)(2,1)}, u32[]{:S(2)}, u32[]{:S(2)}) collective-permute-start(bf16[3,384,768]{2,1,0:T(8,128)(2,1)} %fusion.31), channel_id=1, source_target_pairs={{0,16},{16,0},{1,17},{17,1},{2,18},{18,2},{3,19},{19,3},{4,20},{20... | collective-permute-start | bytes 5308424 | tf_op jit(solution)/shard_map/ppermute | solution.py:38
  236.2 109.3 %collective-permute-start.3 = (bf16[3,384,768]{2,1,0:T(8,128)(2,1)}, bf16[3,384,768]{2,1,0:T(8,128)(2,1)}, u32[]{:S(2)}, u32[]{:S(2)}) collective-permute-start(bf16[3,384,768]{2,1,0:T(8,128)(2,1)} %fusion.30), channel_id=1, source_target_pairs={{0,16},{16,0},{1,17},{17,1},{2,18},{18,2},{3,19},{19,3},{4,20},{20... | collective-permute-start | bytes 5308424 | tf_op jit(solution)/shard_map/ppermute | solution.py:38
  319.8 6.0 %copy-start.14 = (bf16[1536,1,768]{2,0,1:T(8,128)(2,1)S(1)}, bf16[1536,1,768]{2,0,1:T(8,128)(2,1)}, u32[]{:S(2)}) copy-start(bf16[1536,1,768]{2,0,1:T(8,128)(2,1)} %all-gather.21.cloned.1.call-done) | copy-start | bytes 7077892
  327.7 7.2 %copy-start.19 = (f32[768,768,1]{1,0,2:T(8,128)S(1)}, f32[768,768,1]{1,0,2:T(8,128)}, u32[]{:S(2)}) copy-start(f32[768,768,1]{1,0,2:T(8,128)} %fusion.9) | copy-start | bytes 7077892
  329.6 41.8 %collective-permute-start.4 = (bf16[3,384,768]{2,1,0:T(8,128)(2,1)}, bf16[3,384,768]{2,1,0:T(8,128)(2,1)}, u32[]{:S(2)}, u32[]{:S(2)}) collective-permute-start(bf16[3,384,768]{2,1,0:T(8,128)(2,1)} %fusion.29), channel_id=1, source_target_pairs={{0,16},{16,0},{1,17},{17,1},{2,18},{18,2},{3,19},{19,3},{4,20},{20... | collective-permute-start | bytes 5308424 | tf_op jit(solution)/shard_map/ppermute | solution.py:38
  331.1 76.9 %collective-permute-start.5 = (bf16[3,384,768]{2,1,0:T(8,128)(2,1)}, bf16[3,384,768]{2,1,0:T(8,128)(2,1)}, u32[]{:S(2)}, u32[]{:S(2)}) collective-permute-start(bf16[3,384,768]{2,1,0:T(8,128)(2,1)} %fusion.28), channel_id=1, source_target_pairs={{0,16},{16,0},{1,17},{17,1},{2,18},{18,2},{3,19},{19,3},{4,20},{20... | collective-permute-start | bytes 5308424 | tf_op jit(solution)/shard_map/ppermute | solution.py:38
  360.6 10.8 %copy-start.22 = (bf16[768,3,384]{2,0,1:T(8,128)(2,1)S(1)}, bf16[768,3,384]{2,0,1:T(8,128)(2,1)}, u32[]{:S(2)}) copy-start(bf16[768,3,384]{2,0,1:T(8,128)(2,1)} %fusion.35) | copy-start | bytes 5308420
  360.7 47.3 %copy-start.8 = (f32[768,768,1]{1,0,2:T(8,128)S(1)}, f32[768,768,1]{1,0,2:T(8,128)}, u32[]{:S(2)}) copy-start(f32[768,768,1]{1,0,2:T(8,128)} %fusion.5) | copy-start | bytes 7077892
  364.1 43.9 %copy-start.3 = (f32[768,768]{1,0:T(8,128)S(1)}, f32[768,768]{1,0:T(8,128)}, u32[]{:S(2)}) copy-start(f32[768,768]{1,0:T(8,128)} %fusion.46) | copy-start | bytes 7077892
  364.1 43.9 %copy-start.4 = (f32[768,768]{1,0:T(8,128)S(1)}, f32[768,768]{1,0:T(8,128)}, u32[]{:S(2)}) copy-start(f32[768,768]{1,0:T(8,128)} %fusion.48) | copy-start | bytes 7077892
  364.1 43.9 %copy-start.7 = (f32[768,768,1]{1,0,2:T(8,128)S(1)}, f32[768,768,1]{1,0,2:T(8,128)}, u32[]{:S(2)}) copy-start(f32[768,768,1]{1,0,2:T(8,128)} %fusion.11) | copy-start | bytes 7077892
  484.4 56.1 %collective-permute-start.6 = (bf16[192,3,1024]{2,0,1:T(8,128)(2,1)}, bf16[192,3,1024]{2,0,1:T(8,128)(2,1)S(1)}, u32[]{:S(2)}, u32[]{:S(2)}) collective-permute-start(bf16[192,3,1024]{2,0,1:T(8,128)(2,1)} %all-reduce.3.cloned.1.call-done), channel_id=1, source_target_pairs={{0,0},{1,4},{2,8},{3,12},{4,1},{5,5},{6,9},{7,13},{8,2},{9,6},{10,... | collective-permute-start | bytes 3538952 | tf_op jit(solution)/shard_map/ppermute | solution.py:94
  (12 other events, 40.7 us)
Sparse Core Ops, SparseCore 0:
  15.6 50.1 all-gather.12
  67.4 49.2 all-gather.14
  118.3 49.2 all-gather.16
  169.0 49.2 all-gather.18
  219.8 49.2 all-gather.20
  270.5 49.2 all-gather.22
  446.8 37.5 all-reduce.2

commit v4 on v1

v4 whole, which is shorter than its diff:
```python
import math

import jax
import jax.numpy as jnp
from jax import lax
from jax.sharding import PartitionSpec as P

HD = 128
PATCH = 256
POOL = 16


def rms_norm(values):
    return values * lax.rsqrt(jnp.mean(values * values, axis=-1, keepdims=True) + 1e-06)


def head_chunks(heads):
    if heads >= 4 and heads % 2 == 0:
        return [1] + [2] * ((heads - 2) // 2) + [1]
    return [1] * heads


def moved_weights(chunk, n_video):
    v = lax.axis_index("video")
    g = lax.axis_index("groups")
    half = chunk.shape[0] // 2
    mine = lax.dynamic_slice_in_dim(chunk, g * half, half, axis=0)
    other = lax.dynamic_slice_in_dim(chunk, (1 - g) * half, half, axis=0)
    gathered = lax.all_gather(mine, "video", axis=0, tiled=False)
    twice = jnp.concatenate([gathered, gathered], axis=0)
    onward = lax.dynamic_slice_in_dim(twice, v + 1, n_video - 1, axis=0)
    received = lax.ppermute(onward, "groups", [(0, 1), (1, 0)])
    return other, gathered, received


def attend(proj, nframes, heads, scale, blocks, inner):
    proj = proj.reshape(nframes, PATCH, 3, heads, HD)
    query = rms_norm(proj[:, :, 0]).astype(jnp.bfloat16)
    keys = rms_norm(proj[:, :, 1]).astype(jnp.bfloat16)
    values = proj[:, :, 2].astype(jnp.bfloat16)
    scores = jnp.einsum("fphd,fkhd->fhpk", query, keys, preferred_element_type=jnp.float32) * scale
    probs = jnp.exp(scores)
    probs = (probs / jnp.sum(probs, axis=-1, keepdims=True)).astype(jnp.bfloat16)
    attended = jnp.einsum("fhpk,fkhd->fphd", probs, values, preferred_element_type=jnp.float32)
    grid = attended.reshape(nframes, blocks, inner, blocks, inner, heads, HD)
    return jnp.mean(grid, axis=(2, 4)).reshape(nframes * POOL, heads * HD).astype(jnp.bfloat16)


def per_device(frames, frame_video, qkv_weight, conn_weight):
    scale = 1.0 / math.sqrt(HD)
    blocks = math.isqrt(POOL)
    inner = math.isqrt(PATCH) // blocks
    nframes = frames.shape[0]
    patch_rows = nframes * PATCH
    n_video = lax.axis_size("video")
    assert lax.axis_size("groups") == 2
    v = lax.axis_index("video")
    g = lax.axis_index("groups")
    wide = frames.astype(jnp.float32)
    center = wide - jnp.mean(wide, axis=-1, keepdims=True)
    normed = center * lax.rsqrt(jnp.mean(center * center, axis=-1, keepdims=True) + 1e-06)
    normed = normed.astype(jnp.bfloat16).reshape(patch_rows, frames.shape[2])
    half = qkv_weight.shape[0] // 2
    cut = normed.reshape(patch_rows, n_video, 2, half)
    own_half = lax.dynamic_index_in_dim(cut, g, axis=2, keepdims=False)
    other_half = lax.dynamic_index_in_dim(cut, 1 - g, axis=2, keepdims=False)
    own_piece = lax.dynamic_index_in_dim(other_half, v, axis=1, keepdims=False)
    rolled = lax.dynamic_slice_in_dim(
        jnp.concatenate([other_half, other_half], axis=1), v + 1, n_video - 1, axis=1
    )
    heads_local = qkv_weight.shape[2] // HD
    pooled_parts = []
    first = 0
    for size in head_chunks(heads_local):
        chunk = qkv_weight[:, :, first * HD:(first + size) * HD]
        first += size
        width = 3 * size * HD
        other, gathered, received = moved_weights(chunk, n_video)
        proj = jnp.dot(own_piece, other.reshape(half, width), preferred_element_type=jnp.float32)
        proj = proj + jnp.einsum(
            "nvd,vdc->nc", own_half, gathered.reshape(n_video, half, width),
            preferred_element_type=jnp.float32,
        )
        proj = proj + jnp.einsum(
            "nvd,vdc->nc", rolled, received.reshape(n_video - 1, half, width),
            preferred_element_type=jnp.float32,
        )
        pooled_parts.append(attend(proj, nframes, size, scale, blocks, inner))
    pooled = jnp.concatenate(pooled_parts, axis=1)
    pooled_all = lax.all_gather(pooled, "video", axis=0, tiled=True)
    rows = pooled_all.shape[0]
    partial_proj = jnp.einsum(
        "rc,ckt->rkt", pooled_all, conn_weight, preferred_element_type=jnp.float32
    )
    clip_rows = lax.psum_scatter(
        partial_proj.astype(jnp.bfloat16), "tensor", scatter_dimension=0, tiled=True
    )
    clip_rows = lax.all_gather(clip_rows, "video", axis=2, tiled=True)
    clip_proj = lax.all_to_all(clip_rows, "tensor", 2, 0, tiled=True).astype(jnp.float32)
    t_heads = clip_proj.shape[2] // HD
    out_rows = rows // n_video
    start = v * out_rows
    own = lax.dynamic_slice_in_dim(clip_proj[:, 0], start, out_rows, axis=0)
    tquery = rms_norm(own.reshape(out_rows, t_heads, HD)).astype(jnp.bfloat16)
    tkey = rms_norm(clip_proj[:, 1].reshape(rows, t_heads, HD)).astype(jnp.bfloat16)
    tvalue = clip_proj[:, 2].reshape(rows, t_heads, HD).astype(jnp.bfloat16)
    video_all = lax.all_gather(frame_video, "video", axis=0, tiled=True)
    seg_rows = jnp.repeat(video_all, POOL)
    row_frame = jnp.arange(rows, dtype=jnp.int32) // POOL
    own_seg = lax.dynamic_slice_in_dim(seg_rows, start, out_rows)
    own_frame = lax.dynamic_slice_in_dim(row_frame, start, out_rows)
    allowed = (seg_rows[None, :] == own_seg[:, None]) & (row_frame[None, :] <= own_frame[:, None])
    logits = jnp.einsum("rhd,khd->hrk", tquery, tkey, preferred_element_type=jnp.float32) * scale
    weights = jnp.where(allowed[None], jnp.exp(logits), jnp.float32(0.0))
    numer = jnp.einsum(
        "hrk,khd->rhd", weights.astype(jnp.bfloat16), tvalue, preferred_element_type=jnp.float32
    )
    denom = jnp.sum(weights, axis=-1)
    summary = numer / jnp.transpose(denom)[:, :, None]
    return summary.reshape(out_rows, t_heads * HD).astype(jnp.bfloat16)


def solution(mesh):
    return jax.shard_map(
        per_device,
        mesh=mesh,
        in_specs=(
            P(("groups", "video"), None, None),
            P(("groups", "video")),
            P("video", None, "tensor"),
            P("tensor", None, "video"),
        ),
        out_specs=P(("groups", "video"), "tensor"),
        check_vma=False,
    )
```

time: 724 us -> 544 us (0.75)
  the two profiles are of different devices: /device:TPU:10 before, /device:TPU:0 now
where the time goes in v4:
time: 544 us; the launch traced here: 534 us
  waiting for transfers between devices  205 us (38%)
  local copies, waits for them, and re-layouts  163 us (30%)
  matrix products  68.1 us (13%)
  other arithmetic  50.6 us (9%)
  blocking collectives  22 us (4%)
  between operations  15.1 us (3%)
  starting transfers between devices  9.94 us (2%)
    ppermute x4, waiting for transfers between devices, moved_weights(): received = lax.ppermute(onward, 'groups', [(0, 1), (1, 0)])  75.7 us
    all_gather x4, waiting for transfers between devices, moved_weights(): gathered = lax.all_gather(mine, 'video', axis=0, tiled=False)  67.1 us
    all_gather x1, waiting for transfers between devices, per_device(): clip_rows = lax.all_gather(clip_rows, 'video', axis=2, tiled=True)  32 us
    unnamed x77, local copies, waits for them, and re-layouts  31.8 us
    dynamic_slice x2, local copies, waits for them, and re-layouts, per_device(): other_half = lax.dynamic_index_in_dim(cut, 1 - g, axis=2, keepdims=False)  29.8 us
    reshape x4, local copies, waits for them, and re-layouts, per_device(): gathered.reshape(n_video, half, width)  27.1 us
    reduce_scatter x1, waiting for transfers between devices, per_device(): lax.psum_scatter(partial_proj.astype(jnp.bfloat16), 'tensor', scatter_dim...  24 us
    dot_general x4, matrix products, per_device(): jnp.einsum('nvd,vdc->nc', rolled, received.reshape(n_video - 1, half, wid...  23.7 us
  transfers between devices with their start and end apart: 11, of which 7 were waited for; matrix products, arithmetic and copies ran while one was open for 41% of the time, Pallas kernels for 0%

profile of v4, /device:TPU:0, one launch (start us, length us, event | category | flops | bytes accessed | tf_op | source)
XLA Modules:
  0.0 534.2 jit_solution(71458435880263329)
XLA Ops:
  20.0 5.4 %convert_reduce_fusion = f32[3,256]{1,0:T(4,128)S(1)} fusion(bf16[3,256,6144]{2,1,0:T(8,128)(2,1)} %param.4), kind=kLoop, calls=%fused_computation.1 | loop fusion | flops 9436416 | bytes 9440256 | tf_op jit(solution)/shard_map/reduce_sum | solution.py:60
  25.4 6.3 %fusion.2 = f32[3,256]{1,0:T(4,128)S(1)} fusion(bf16[3,256,6144]{2,1,0:T(8,128)(2,1)} %param.4, f32[3,256]{1,0:T(4,128)S(1)} %broadcast_multiply_fusion), kind=kLoop, calls=%fused_computation.4 | loop fusion | flops 18873600 | bytes 9443328 | tf_op jit(solution)/shard_map/reduce_sum | solution.py:61
  31.7 12.3 %fusion.3 = bf16[3,256,6144]{2,1,0:T(8,128)(2,1)} fusion(bf16[3,256,6144]{2,1,0:T(8,128)(2,1)} %param.4, f32[3,256]{1,0:T(4,128)S(1)} %add_rsqrt_fusion.10, f32[3,256]{1,0:T(4,128)S(1)} %broadcast_multiply_fusion), kind=kLoop, calls=%fused_computation.5 | loop fusion | flops 18874368 | bytes 18880512 | tf_op jit(solution)/shard_map/convert_element_type | solution.py:62
  44.0 15.6 %reshape_reshape.3 = bf16[768,4,2,768]{3,2,1,0:T(2,128)(2,1)} reshape(bf16[3,256,6144]{2,1,0:T(8,128)(2,1)} %fusion.3) | data formatting | bytes 18874368 | tf_op jit(solution)/shard_map/reshape;reshape | solution.py:64
  59.6 22.4 %constant_dynamic-slice_fusion.6 = (bf16[768,4,1,768]{3,2,1,0:T(2,128)(2,1)}, bf16[768,4,1,768]{3,2,1,0:T(2,128)(2,1)}) fusion(bf16[768,4,2,768]{3,2,1,0:T(2,128)(2,1)} %reshape_reshape.3, s32[]{:T(128)S(6)} %select_n.56, s32[]{:T(128)S(6)} %select_n.59), kind=kLoop, calls=%fused_computation.150 | loop fusion | bytes 18874376 | tf_op jit(solution)/shard_map/jit(dynamic_index_in_dim)/dynamic_slice | solution.py:66
  82.0 7.5 %copy.261 = bf16[768,4,1,768]{3,0,1,2:T(8,128)(2,1)} copy(bf16[768,4,1,768]{3,2,1,0:T(2,128)(2,1)} %get-tuple-element.10) | data formatting | bytes 9437184 | tf_op jit(solution)/shard_map/jit(dynamic_index_in_dim)/dynamic_slice | solution.py:65
  94.9 7.4 %copy.408 = bf16[768,4,1,768]{3,0,1,2:T(8,128)(2,1)} copy(bf16[768,4,1,768]{3,2,1,0:T(2,128)(2,1)} %get-tuple-element.9) | data formatting | bytes 9437184 | tf_op jit(solution)/shard_map/jit(dynamic_index_in_dim)/dynamic_slice | solution.py:66
  107.0 5.1 fusion.16
  130.8 4.5 reshape.420
  135.4 5.3 fusion.21
  141.6 4.6 fusion.26
  148.0 15.5 %collective-permute-done = bf16[3,768,3,128]{1,3,2,0:T(8,128)(2,1)} collective-permute-done((bf16[3,768,3,128]{1,3,2,0:T(8,128)(2,1)}, bf16[3,768,3,128]{1,3,2,0:T(8,128)(2,1)}, u32[]{:S(2)}, u32[]{:S(2)}) %collective-permute-start) | collective-permute-done | bytes 1769504 | tf_op jit(solution)/shard_map/ppermute | solution.py:32
  163.6 4.6 fusion.31
  171.9 28.8 %collective-permute-done.3 = bf16[3,768,3,128]{1,3,2,0:T(8,128)(2,1)} collective-permute-done((bf16[3,768,3,128]{1,3,2,0:T(8,128)(2,1)}, bf16[3,768,3,128]{1,3,2,0:T(8,128)(2,1)}, u32[]{:S(2)}, u32[]{:S(2)}) %collective-permute-start.3) | collective-permute-done | bytes 1769504 | tf_op jit(solution)/shard_map/ppermute | solution.py:32
  200.7 5.6 %fusion.32 = f32[768,384]{1,0:T(8,128)} fusion(f32[768,384]{1,0:T(8,128)S(1)} %copy-done.16, bf16[768,3,768]{2,0,1:T(8,128)(2,1)} %fusion.16, bf16[3,768,384]{1,2,0:T(8,128)(2,1)} %bitcast.33), kind=kOutput, calls=%fused_computation.54 | convolution fusion | flops 1359249408 | bytes 7667712 | tf_op jit(solution)/shard_map/nvd,vdc->nc/dot_general | solution.py:84
  226.9 67.1 %all-gather.16.cloned.1.call-done = bf16[3072,3,256]{0,2,1:T(8,128)(2,1)} async-done(((bf16[768,3,256]{0,2,1:T(8,128)(2,1)}), bf16[3072,3,256]{0,2,1:T(8,128)(2,1)}) %all-gather.16.cloned.1.call-update) | async-done | bytes 4718608 | tf_op jit(solution)/shard_map/all_gather | solution.py:29
  302.4 9.8 %reshape.410 = bf16[4,768,768]{1,0,2:T(4,128)(2,1)} reshape(bf16[3072,3,256]{0,2,1:T(8,128)(2,1)} %all-gather.14.cloned.1.call-done) | data formatting | bytes 9437184 | tf_op jit(solution)/shard_map/reshape | solution.py:81
  312.2 9.8 %reshape.415 = bf16[4,768,768]{1,0,2:T(4,128)(2,1)} reshape(bf16[3072,3,256]{0,2,1:T(8,128)(2,1)} %all-gather.16.cloned.1.call-done) | data formatting | bytes 9437184 | tf_op jit(solution)/shard_map/reshape | solution.py:81
  322.0 7.3 %fusion.8 = f32[768,768,1]{1,0,2:T(8,128)S(1)} fusion(bf16[768,4,1,768]{3,0,1,2:T(8,128)(2,1)} %copy.261, bf16[4,768,768]{1,0,2:T(4,128)(2,1)} %reshape.410), kind=kOutput, calls=%fused_computation.22 | convolution fusion | flops 3623878656 | bytes 11796480 | tf_op jit(solution)/shard_map/nvd,vdc->nc/dot_general | solution.py:80
  329.4 5.3 fusion.6
  334.6 6.4 %bitcast_add_fusion.2 = f32[768,768]{1,0:T(8,128)} fusion(f32[768,768]{1,0:T(8,128)S(1)} %copy-done.23, f32[768,768,1]{1,0,2:T(8,128)S(1)} %fusion.8, bf16[768,3,768]{2,0,1:T(8,128)(2,1)S(1)} %copy-done.8, bf16[3,768,768]{1,2,0:T(8,128)(2,1)} %bitcast.15), kind=kOutput, calls=%fused_computation.36 | convolution fusion | flops 2719088640 | bytes 14155776 | tf_op jit(solution)/shard_map/nvd,vdc->nc/dot_general | solution.py:84
  347.1 31.4 %collective-permute-done.2 = bf16[3,768,3,256]{1,3,2,0:T(8,128)(2,1)} collective-permute-done((bf16[3,768,3,256]{1,3,2,0:T(8,128)(2,1)}, bf16[3,768,3,256]{1,3,2,0:T(8,128)(2,1)}, u32[]{:S(2)}, u32[]{:S(2)}) %collective-permute-start.2) | collective-permute-done | bytes 3538976 | tf_op jit(solution)/shard_map/ppermute | solution.py:32
  378.5 7.0 %bitcast_add_fusion = f32[768,768]{1,0:T(8,128)} fusion(f32[768,768]{1,0:T(8,128)} %fusion.38, f32[768,768,1]{1,0,2:T(8,128)} %fusion.6, bf16[768,3,768]{2,0,1:T(8,128)(2,1)S(1)} %copy-done.9, bf16[3,768,768]{1,2,0:T(8,128)(2,1)} %bitcast.24), kind=kOutput, calls=%fused_computation.34 | convolution fusion | flops 2719088640 | bytes 14155776 | tf_op jit(solution)/shard_map/nvd,vdc->nc/dot_general | solution.py:84
  404.2 14.6 %all_gather.41 = bf16[192,768]{1,0:T(8,128)(2,1)S(1)} all-gather(bf16[48,768]{1,0:T(8,128)(2,1)S(1)} %pad_maximum_fusion), channel_id=1, replica_groups=mesh['groups'=2,'video'=4,'tensor'=4] {'video'}, dimensions={0}, use_global_device_ids=true | all-gather | bytes 368640 | tf_op jit(solution)/shard_map/all_gather | solution.py:90
  423.3 24.0 %reduce-scatter.2.cloned.1.call-done = bf16[48,3,1024]{2,0,1:T(8,128)(2,1)} async-done(((bf16[192,3,1024]{2,0,1:T(8,128)(2,1)}), bf16[48,3,1024]{2,0,1:T(8,128)(2,1)}) %reduce-scatter.2.cloned.1.call-update) | async-done | bytes 294928 | tf_op jit(solution)/shard_map/reduce_scatter | solution.py:95
  447.4 32.0 %all-gather.10.cloned.1.call-done = bf16[48,3,4096]{2,0,1:T(8,128)(2,1)} async-done(((bf16[48,3,1024]{2,0,1:T(8,128)(2,1)}), bf16[48,3,4096]{2,0,1:T(8,128)(2,1)}) %all-gather.10.cloned.1.call-update) | async-done | bytes 1179664 | tf_op jit(solution)/shard_map/all_gather | solution.py:98
  479.3 6.2 %copy.300 = bf16[48,3,4096]{0,1,2:T(4,128)(2,1)} copy(bf16[48,3,4096]{2,0,1:T(8,128)(2,1)} %all-gather.10.cloned.1.call-done) | data formatting | bytes 2359296 | tf_op jit(solution)/shard_map/all_gather | solution.py:98
  485.5 6.9 %reshape.447 = bf16[4,2,73728]{2,1,0:T(2,128)(2,1)} reshape(bf16[4096,3,48]{2,1,0:T(4,128)(2,1)} %bitcast.219) | data formatting | bytes 2359296
  497.6 7.4 %all-reduce = s32[12]{0:T(128)S(1)} all-reduce(s32[12]{0:T(128)S(1)} %dynamic-update-slice), channel_id=1, replica_groups=mesh['groups'=2,'video'=4,'tensor'=4] {'video'}, use_global_device_ids=true, to_apply=%add | all-reduce | flops 12 | bytes 96
  505.4 6.5 %all-to-all-done = bf16[4,2,73728]{2,1,0:T(2,128)(2,1)S(1)} async-done(((bf16[4,2,73728]{2,1,0:T(2,128)(2,1)}), bf16[4,2,73728]{2,1,0:T(2,128)(2,1)S(1)}, u32[]{:S(2)}, u32[]{:S(2)}) %all-to-all-start) | async-done | bytes 1179680 | tf_op jit(solution)/shard_map/all_to_all | solution.py:99
  511.9 6.5 %reshape.448 = bf16[4096,3,48]{2,1,0:T(4,128)(2,1)} reshape(bf16[4,2,73728]{2,1,0:T(2,128)(2,1)S(1)} %all-to-all-done) | data formatting | bytes 2359296
  518.4 5.4 %copy.302 = bf16[4,48,3,1024]{3,1,0,2:T(8,128)(2,1)S(1)} copy(bf16[4,48,3,1024]{1,2,3,0:T(4,128)(2,1)} %bitcast.220) | data formatting | bytes 2359296 | tf_op jit(solution)/shard_map/convert_element_type | solution.py:99
  (186 shorter events, 114.6 us)
Async XLA Ops:
  6.5 110.8 %all-gather.12.cloned.1.call-start = ((), (), s32[]{:S(2)}) async-start(), calls=%async_computation.4 | async-start | bytes 2949120 | tf_op jit(solution)/shard_map/all_gather | solution.py:29
  10.6 113.2 %all-gather.18.cloned.1.call-start = ((), (), s32[]{:S(2)}) async-start(), calls=%async_computation.7 | async-start | bytes 2949120 | tf_op jit(solution)/shard_map/all_gather | solution.py:29
  11.8 203.7 %all-gather.14.cloned.1.call-start = ((), (), s32[]{:S(2)}) async-start(), calls=%async_computation.5 | async-start | bytes 5898240 | tf_op jit(solution)/shard_map/all_gather | solution.py:29
  18.3 275.7 %all-gather.16.cloned.1.call-start = ((), (), s32[]{:S(2)}) async-start(), calls=%async_computation.6 | async-start | bytes 5898240 | tf_op jit(solution)/shard_map/all_gather | solution.py:29
  19.9 427.4 %reduce-scatter.2.cloned.1.call-start = ((), (), s32[]{:S(2)}) async-start(), calls=%async_computation.2 | async-start | bytes 1474560 | tf_op jit(solution)/shard_map/reduce_scatter | solution.py:95
  82.0 7.5 %copy-start.11 = (bf16[768,3,128]{2,0,1:T(8,128)(2,1)S(1)}, bf16[768,3,128]{2,0,1:T(8,128)(2,1)}, u32[]{:S(2)}) copy-start(bf16[768,3,128]{2,0,1:T(8,128)(2,1)} %get-tuple-element.36) | copy-start | bytes 1769476
  107.0 5.1 copy-start.14
  112.1 2.6 copy-start.15
  121.1 42.5 %collective-permute-start = (bf16[3,768,3,128]{1,3,2,0:T(8,128)(2,1)}, bf16[3,768,3,128]{1,3,2,0:T(8,128)(2,1)}, u32[]{:S(2)}, u32[]{:S(2)}) collective-permute-start(bf16[3,768,3,128]{1,3,2,0:T(8,128)(2,1)} %fusion.20), channel_id=1, source_target_pairs={{0,16},{16,0},{1,17},{17,1},{2,18},{18,2},{3,19},{19,3},{4,20},{20... | collective-permute-start | bytes 5308424 | tf_op jit(solution)/shard_map/ppermute | solution.py:32
  127.7 73.0 %collective-permute-start.3 = (bf16[3,768,3,128]{1,3,2,0:T(8,128)(2,1)}, bf16[3,768,3,128]{1,3,2,0:T(8,128)(2,1)}, u32[]{:S(2)}, u32[]{:S(2)}) collective-permute-start(bf16[3,768,3,128]{1,3,2,0:T(8,128)(2,1)} %fusion.19), channel_id=1, source_target_pairs={{0,16},{16,0},{1,17},{17,1},{2,18},{18,2},{3,19},{19,3},{4,20},{20... | collective-permute-start | bytes 5308424 | tf_op jit(solution)/shard_map/ppermute | solution.py:32
  135.4 5.4 %copy-start.12 = (bf16[768,3,128]{0,2,1:T(8,128)(2,1)S(1)}, bf16[768,3,128]{0,2,1:T(8,128)(2,1)}, u32[]{:S(2)}) copy-start(bf16[768,3,128]{0,2,1:T(8,128)(2,1)} %copy.323) | copy-start | bytes 1769476
  141.6 4.6 copy-start.13
  146.2 17.4 %copy-start.7 = (bf16[768,3,768]{2,0,1:T(8,128)(2,1)S(1)}, bf16[768,3,768]{2,0,1:T(8,128)(2,1)}, u32[]{:S(2)}) copy-start(bf16[768,3,768]{2,0,1:T(8,128)(2,1)} %fusion.16) | copy-start | bytes 10616836
  168.2 32.5 %copy-start.16 = (f32[768,384]{1,0:T(8,128)S(1)}, f32[768,384]{1,0:T(8,128)}, u32[]{:S(2)}) copy-start(f32[768,384]{1,0:T(8,128)} %convolution_add_fusion) | copy-start | bytes 3538948
  218.2 4.8 copy-start.18
  221.3 113.3 %collective-permute-start.1 = (bf16[3,768,3,256]{1,3,2,0:T(8,128)(2,1)}, bf16[3,768,3,256]{1,3,2,0:T(8,128)(2,1)}, u32[]{:S(2)}, u32[]{:S(2)}) collective-permute-start(bf16[3,768,3,256]{1,3,2,0:T(8,128)(2,1)} %fusion.15), channel_id=1, source_target_pairs={{0,16},{16,0},{1,17},{17,1},{2,18},{18,2},{3,19},{19,3},{4,20},{20... | collective-permute-start | bytes 10616840 | tf_op jit(solution)/shard_map/ppermute | solution.py:32
  299.8 78.7 %collective-permute-start.2 = (bf16[3,768,3,256]{1,3,2,0:T(8,128)(2,1)}, bf16[3,768,3,256]{1,3,2,0:T(8,128)(2,1)}, u32[]{:S(2)}, u32[]{:S(2)}) collective-permute-start(bf16[3,768,3,256]{1,3,2,0:T(8,128)(2,1)} %fusion.14), channel_id=1, source_target_pairs={{0,16},{16,0},{1,17},{17,1},{2,18},{18,2},{3,19},{19,3},{4,20},{20... | collective-permute-start | bytes 10616840 | tf_op jit(solution)/shard_map/ppermute | solution.py:32
  312.2 17.1 %slice-start = ((s8[4718592]{0:T(1024)(128)(4,1)}), s8[524288]{0:T(1024)(128)(4,1)S(1)}, s32[]{:S(2)}) async-start(s8[4718592]{0:T(1024)(128)(4,1)} %bitcast.227), calls=%async_computation.8 | async-start | bytes 1048576
  322.0 7.3 %slice-start.1 = ((s8[4718592]{0:T(1024)(128)(4,1)}), s8[4194304]{0:T(1024)(128)(4,1)S(1)}, s32[]{:S(2)}) async-start(s8[4718592]{0:T(1024)(128)(4,1)} %bitcast.227), calls=%async_computation.9 | async-start | bytes 8388608
  322.0 7.3 %copy-start.6 = (bf16[4,768,768]{1,0,2:T(4,128)(2,1)S(1)}, bf16[4,768,768]{1,0,2:T(4,128)(2,1)}, u32[]{:S(2)}) copy-start(bf16[4,768,768]{1,0,2:T(4,128)(2,1)} %reshape.415) | copy-start | bytes 14155780
  329.3 5.3 copy-start.8
  329.3 5.3 copy-start.23
  344.4 34.1 %copy-start.9 = (bf16[768,3,768]{2,0,1:T(8,128)(2,1)S(1)}, bf16[768,3,768]{2,0,1:T(8,128)(2,1)}, u32[]{:S(2)}) copy-start(bf16[768,3,768]{2,0,1:T(8,128)(2,1)} %fusion.16) | copy-start | bytes 10616836
  388.3 2.1 copy-start.4
  390.0 2.6 copy-start.3
  390.0 2.6 copy-start.5
  396.8 2.1 copy-start.1
  400.9 2.1 copy-start.17
  423.3 56.1 %all-gather.10.cloned.1.call-start = ((), (), s32[]{:S(2)}) async-start(), calls=%async_computation.3 | async-start | bytes 1474560 | tf_op jit(solution)/shard_map/all_gather | solution.py:98
  492.4 3.7 copy-start.22
  492.4 4.9 copy-start.21
  492.4 19.5 %all-to-all-start = ((bf16[4,2,73728]{2,1,0:T(2,128)(2,1)}), bf16[4,2,73728]{2,1,0:T(2,128)(2,1)S(1)}, u32[]{:S(2)}, u32[]{:S(2)}) async-start(bf16[4,2,73728]{2,1,0:T(2,128)(2,1)} %reshape.447), calls=%async_computation.1 | async-start | bytes 2359296 | tf_op jit(solution)/shard_map/all_to_all | solution.py:99
  (5 other events, 7.3 us)
Sparse Core Ops, SparseCore 0:
  10.7 53.1 all-gather.11
  65.5 49.2 all-gather.17
  116.4 88.2 all-gather.13
  206.1 87.8 all-gather.15
  423.4 23.9 reduce-scatter.1
  448.9 30.4 all-gather.9

commit v5 on v4

--- a/solution.py
+++ b/solution.py
@@ -29,8 +29,11 @@
     gathered = lax.all_gather(mine, "video", axis=0, tiled=False)
     twice = jnp.concatenate([gathered, gathered], axis=0)
     onward = lax.dynamic_slice_in_dim(twice, v + 1, n_video - 1, axis=0)
-    received = lax.ppermute(onward, "groups", [(0, 1), (1, 0)])
-    return other, gathered, received
+    return other, gathered, onward
+
+
+def forward(onward):
+    return lax.ppermute(onward, "groups", [(0, 1), (1, 0)])
 
 
 def attend(proj, nframes, heads, scale, blocks, inner):
@@ -56,6 +59,10 @@
     assert lax.axis_size("groups") == 2
     v = lax.axis_index("video")
     g = lax.axis_index("groups")
+    heads_local = qkv_weight.shape[2] // HD
+    sizes = head_chunks(heads_local)
+    first_moved = moved_weights(qkv_weight[:, :, :sizes[0] * HD], n_video)
+    onward0, frames = lax.optimization_barrier((first_moved[2], frames))
     wide = frames.astype(jnp.float32)
     center = wide - jnp.mean(wide, axis=-1, keepdims=True)
     normed = center * lax.rsqrt(jnp.mean(center * center, axis=-1, keepdims=True) + 1e-06)
@@ -68,14 +75,20 @@
     rolled = lax.dynamic_slice_in_dim(
         jnp.concatenate([other_half, other_half], axis=1), v + 1, n_video - 1, axis=1
     )
-    heads_local = qkv_weight.shape[2] // HD
+    video_all = lax.all_gather(frame_video, "video", axis=0, tiled=True)
     pooled_parts = []
     first = 0
-    for size in head_chunks(heads_local):
+    for index, size in enumerate(sizes):
         chunk = qkv_weight[:, :, first * HD:(first + size) * HD]
         first += size
         width = 3 * size * HD
-        other, gathered, received = moved_weights(chunk, n_video)
+        if index == 0:
+            other, gathered = first_moved[0], first_moved[1]
+            received = forward(onward0)
+            video_all, received = lax.optimization_barrier((video_all, received))
+        else:
+            other, gathered, onward = moved_weights(chunk, n_video)
+            received = forward(onward)
         proj = jnp.dot(own_piece, other.reshape(half, width), preferred_element_type=jnp.float32)
         proj = proj + jnp.einsum(
             "nvd,vdc->nc", own_half, gathered.reshape(n_video, half, width),
@@ -95,8 +108,13 @@
     clip_rows = lax.psum_scatter(
         partial_proj.astype(jnp.bfloat16), "tensor", scatter_dimension=0, tiled=True
     )
-    clip_rows = lax.all_gather(clip_rows, "video", axis=2, tiled=True)
-    clip_proj = lax.all_to_all(clip_rows, "tensor", 2, 0, tiled=True).astype(jnp.float32)
+    n_tensor = lax.axis_size("tensor")
+    clip_rows = lax.all_gather(clip_rows, "video", axis=0, tiled=False)
+    sub = n_video // n_tensor
+    clip_rows = clip_rows.reshape((n_tensor, sub) + clip_rows.shape[1:])
+    clip_proj = lax.all_to_all(clip_rows, "tensor", 0, 0, tiled=False)
+    clip_proj = jnp.transpose(clip_proj, (0, 2, 3, 1, 4))
+    clip_proj = clip_proj.reshape(rows, 3, -1).astype(jnp.float32)
     t_heads = clip_proj.shape[2] // HD
     out_rows = rows // n_video
     start = v * out_rows
@@ -104,7 +122,6 @@
     tquery = rms_norm(own.reshape(out_rows, t_heads, HD)).astype(jnp.bfloat16)
     tkey = rms_norm(clip_proj[:, 1].reshape(rows, t_heads, HD)).astype(jnp.bfloat16)
     tvalue = clip_proj[:, 2].reshape(rows, t_heads, HD).astype(jnp.bfloat16)
-    video_all = lax.all_gather(frame_video, "video", axis=0, tiled=True)
     seg_rows = jnp.repeat(video_all, POOL)
     row_frame = jnp.arange(rows, dtype=jnp.int32) // POOL
     own_seg = lax.dynamic_slice_in_dim(seg_rows, start, out_rows)

time: 544 us -> 521 us (0.958)
  the two profiles are of different devices: /device:TPU:0 before, /device:TPU:10 now
where the time goes in v5:
time: 521 us; the launch traced here: 513 us
  waiting for transfers between devices  223 us (43%)
  local copies, waits for them, and re-layouts  134 us (26%)
  matrix products  64.8 us (12%)
  other arithmetic  42.7 us (8%)
  blocking collectives  24.1 us (5%)
  between operations  15.2 us (3%)
  starting transfers between devices  9.27 us (2%)
    all_gather x4, waiting for transfers between devices, moved_weights(): gathered = lax.all_gather(mine, 'video', axis=0, tiled=False)  83.8 us
    ppermute x4, waiting for transfers between devices, forward(): return lax.ppermute(onward, 'groups', [(0, 1), (1, 0)])  67 us
    all_gather x1, waiting for transfers between devices, per_device(): clip_rows = lax.all_gather(clip_rows, 'video', axis=0, tiled=False)  32.4 us
    reshape x4, local copies, waits for them, and re-layouts, per_device(): gathered.reshape(n_video, half, width)  27.7 us
    reduce_scatter x1, waiting for transfers between devices, per_device(): lax.psum_scatter(partial_proj.astype(jnp.bfloat16), 'tensor', scatter_dim...  26 us
    dynamic_slice x2, local copies, waits for them, and re-layouts, per_device(): other_half = lax.dynamic_index_in_dim(cut, 1 - g, axis=2, keepdims=False)  25.2 us
    dot_general x4, matrix products, per_device(): jnp.einsum('nvd,vdc->nc', rolled, received.reshape(n_video - 1, half, wid...  22.6 us
    unnamed x90, local copies, waits for them, and re-layouts  19.3 us
  transfers between devices with their start and end apart: 11, of which 8 were waited for; matrix products, arithmetic and copies ran while one was open for 39% of the time, Pallas kernels for 0%

profile of v5, /device:TPU:10, one launch (start us, length us, event | category | flops | bytes accessed | tf_op | source)
XLA Modules:
  0.0 512.9 jit_solution(1826026921156449068)
XLA Ops:
  22.9 9.2 %all-reduce = s32[12]{0:T(128)S(1)} all-reduce(s32[12]{0:T(128)S(1)} %dynamic-update-slice), channel_id=1, replica_groups=mesh['groups'=2,'video'=4,'tensor'=4] {'video'}, use_global_device_ids=true, to_apply=%add | all-reduce | flops 12 | bytes 96 | tf_op jit(solution)/shard_map/optimization_barrier | solution.py:88
  37.5 23.5 %all-gather.11.cloned.1.call-done = bf16[3072,3,128]{0,2,1:T(8,128)(2,1)} async-done(((bf16[768,3,128]{0,2,1:T(8,128)(2,1)}), bf16[3072,3,128]{0,2,1:T(8,128)(2,1)}) %all-gather.11.cloned.1.call-update) | async-done | bytes 2359312 | tf_op jit(solution)/shard_map/all_gather | solution.py:29
  64.8 5.2 %convert_reduce_fusion = f32[3,256]{1,0:T(4,128)S(1)} fusion(bf16[3,256,6144]{2,1,0:T(8,128)(2,1)} %param.4), kind=kLoop, calls=%fused_computation.1 | loop fusion | flops 9436416 | bytes 9440256 | tf_op jit(solution)/shard_map/reduce_sum | solution.py:67
  72.6 12.3 %fusion.3 = bf16[3,256,6144]{2,1,0:T(8,128)(2,1)} fusion(bf16[3,256,6144]{2,1,0:T(8,128)(2,1)} %param.4, f32[3,256]{1,0:T(4,128)S(1)} %add_rsqrt_fusion.10, f32[3,256]{1,0:T(4,128)S(1)} %broadcast_multiply_fusion), kind=kLoop, calls=%fused_computation.5 | loop fusion | flops 18874368 | bytes 18880512 | tf_op jit(solution)/shard_map/convert_element_type | solution.py:69
  84.9 15.3 %reshape_reshape.3 = bf16[768,4,2,768]{3,2,1,0:T(2,128)(2,1)} reshape(bf16[3,256,6144]{2,1,0:T(8,128)(2,1)} %fusion.3) | data formatting | bytes 18874368 | tf_op jit(solution)/shard_map/reshape;reshape | solution.py:71
  100.1 21.6 %constant_dynamic-slice_fusion.6 = (bf16[768,4,1,768]{3,2,1,0:T(2,128)(2,1)S(1)}, bf16[768,4,1,768]{3,2,1,0:T(2,128)(2,1)S(1)}) fusion(bf16[768,4,2,768]{3,2,1,0:T(2,128)(2,1)} %reshape_reshape.3, s32[]{:T(128)S(6)} %select_n.58, s32[]{:T(128)S(6)} %select_n.61), kind=kLoop, calls=%fused_computation.150 | loop fusion | bytes 18874376 | tf_op jit(solution)/shard_map/jit(dynamic_index_in_dim)/dynamic_slice | solution.py:73
  121.7 3.7 copy.400
  126.9 3.8 copy.258
  130.7 4.1 constant_dynamic-slice_fusion.9
  142.3 4.9 reshape.421
  147.3 4.0 fusion.40
  162.8 4.5 collective-permute-done
  167.2 3.5 convolution_bitcast_fusion.1
  176.3 27.5 %collective-permute-done.3 = bf16[3,768,3,128]{1,3,2,0:T(8,128)(2,1)} collective-permute-done((bf16[3,768,3,128]{1,3,2,0:T(8,128)(2,1)}, bf16[3,768,3,128]{1,3,2,0:T(8,128)(2,1)}, u32[]{:S(2)}, u32[]{:S(2)}) %collective-permute-start.3) | collective-permute-done | bytes 1769504 | tf_op jit(solution)/shard_map/ppermute | solution.py:36
  203.8 5.6 %fusion.32 = f32[768,384]{1,0:T(8,128)} fusion(f32[768,384]{1,0:T(8,128)S(1)} %copy-done.16, bf16[768,3,768]{2,0,1:T(8,128)(2,1)} %copy-done.7, bf16[3,768,384]{1,2,0:T(8,128)(2,1)} %bitcast.34), kind=kOutput, calls=%fused_computation.54 | convolution fusion | flops 1359249408 | bytes 7667712 | tf_op jit(solution)/shard_map/nvd,vdc->nc/dot_general | solution.py:97
  211.7 3.3 multiply_reduce_fusion.8
  215.5 3.3 multiply_reduce_fusion.6
  229.8 60.3 %all-gather.15.cloned.1.call-done = bf16[3072,3,256]{0,2,1:T(8,128)(2,1)} async-done(((bf16[768,3,256]{0,2,1:T(8,128)(2,1)}), bf16[3072,3,256]{0,2,1:T(8,128)(2,1)}) %all-gather.15.cloned.1.call-update) | async-done | bytes 4718608 | tf_op jit(solution)/shard_map/all_gather | solution.py:29
  298.5 10.0 %reshape.411 = bf16[4,768,768]{1,0,2:T(4,128)(2,1)} reshape(bf16[3072,3,256]{0,2,1:T(8,128)(2,1)} %all-gather.13.cloned.1.call-done) | data formatting | bytes 9437184 | tf_op jit(solution)/shard_map/reshape | solution.py:94
  308.5 9.8 %reshape.416 = bf16[4,768,768]{1,0,2:T(4,128)(2,1)} reshape(bf16[3072,3,256]{0,2,1:T(8,128)(2,1)} %all-gather.15.cloned.1.call-done) | data formatting | bytes 9437184 | tf_op jit(solution)/shard_map/reshape | solution.py:94
  318.3 7.3 %fusion.8 = f32[768,768,1]{1,0,2:T(8,128)S(1)} fusion(bf16[768,4,1,768]{3,0,1,2:T(8,128)(2,1)} %copy.258, bf16[4,768,768]{1,0,2:T(4,128)(2,1)} %reshape.411), kind=kOutput, calls=%fused_computation.22 | convolution fusion | flops 3623878656 | bytes 11796480 | tf_op jit(solution)/shard_map/nvd,vdc->nc/dot_general | solution.py:93
  325.6 5.3 %fusion.6 = f32[768,768,1]{1,0,2:T(8,128)} fusion(bf16[768,4,1,768]{3,0,1,2:T(8,128)(2,1)S(1)} %bitcast.226, bf16[4,768,768]{1,0,2:T(4,128)(2,1)S(1)} %copy-done.6), kind=kOutput, calls=%fused_computation.20 | convolution fusion | flops 3623878656 | bytes 11796480 | tf_op jit(solution)/shard_map/nvd,vdc->nc/dot_general | solution.py:93
  330.9 6.4 %bitcast_add_fusion.2 = f32[768,768]{1,0:T(8,128)} fusion(f32[768,768]{1,0:T(8,128)S(1)} %copy-done.23, f32[768,768,1]{1,0,2:T(8,128)S(1)} %fusion.8, bf16[768,3,768]{2,0,1:T(8,128)(2,1)S(1)} %copy-done.8, bf16[3,768,768]{1,2,0:T(8,128)(2,1)} %bitcast.16), kind=kOutput, calls=%fused_computation.36 | convolution fusion | flops 2719088640 | bytes 14155776 | tf_op jit(solution)/shard_map/nvd,vdc->nc/dot_general | solution.py:97
  342.9 35.0 %collective-permute-done.2 = bf16[3,768,3,256]{1,3,2,0:T(8,128)(2,1)} collective-permute-done((bf16[3,768,3,256]{1,3,2,0:T(8,128)(2,1)}, bf16[3,768,3,256]{1,3,2,0:T(8,128)(2,1)}, u32[]{:S(2)}, u32[]{:S(2)}) %collective-permute-start.2) | collective-permute-done | bytes 3538976 | tf_op jit(solution)/shard_map/ppermute | solution.py:36
  377.9 6.9 %bitcast_add_fusion = f32[768,768]{1,0:T(8,128)} fusion(f32[768,768]{1,0:T(8,128)} %fusion.38, f32[768,768,1]{1,0,2:T(8,128)} %fusion.6, bf16[768,3,768]{2,0,1:T(8,128)(2,1)S(1)} %copy-done.9, bf16[3,768,768]{1,2,0:T(8,128)(2,1)} %bitcast.25), kind=kOutput, calls=%fused_computation.34 | convolution fusion | flops 2719088640 | bytes 14155776 | tf_op jit(solution)/shard_map/nvd,vdc->nc/dot_general | solution.py:97
  384.9 3.1 reshape.418
  403.9 14.9 %all_gather.45 = bf16[192,768]{1,0:T(8,128)(2,1)S(1)} all-gather(bf16[48,768]{1,0:T(8,128)(2,1)S(1)} %pad_maximum_fusion), channel_id=1, replica_groups=mesh['groups'=2,'video'=4,'tensor'=4] {'video'}, dimensions={0}, use_global_device_ids=true | all-gather | bytes 368640 | tf_op jit(solution)/shard_map/all_gather | solution.py:103
  418.7 4.5 convolution_convert_fusion
  423.3 26.0 %reduce-scatter.2.cloned.1.call-done = bf16[48,3,1024]{2,0,1:T(8,128)(2,1)} async-done(((bf16[192,3,1024]{2,0,1:T(8,128)(2,1)}), bf16[48,3,1024]{2,0,1:T(8,128)(2,1)}) %reduce-scatter.2.cloned.1.call-update) | async-done | bytes 294928 | tf_op jit(solution)/shard_map/reduce_scatter | solution.py:108
  449.4 32.4 %all-gather.19.cloned.1.call-done = bf16[192,3,1024]{2,0,1:T(8,128)(2,1)} async-done(((bf16[48,3,1024]{2,0,1:T(8,128)(2,1)}), bf16[192,3,1024]{2,0,1:T(8,128)(2,1)}) %all-gather.19.cloned.1.call-update) | async-done | bytes 1179664 | tf_op jit(solution)/shard_map/all_gather | solution.py:112
  484.1 4.1 all-to-all-start
  488.5 13.8 %all-to-all-done = bf16[4,1,48,3,1024]{4,2,3,1,0:T(8,128)(2,1)S(1)} async-done(((bf16[4,1,48,3,1024]{4,2,3,1,0:T(8,128)(2,1)}), bf16[4,1,48,3,1024]{4,2,3,1,0:T(8,128)(2,1)S(1)}, u32[]{:S(2)}, u32[]{:S(2)}) %all-to-all-start) | async-done | bytes 1179680 | tf_op jit(solution)/shard_map/all_to_all | solution.py:115
  (202 shorter events, 102.8 us)
Async XLA Ops:
  6.5 54.4 %all-gather.11.cloned.1.call-start = ((), (), s32[]{:S(2)}) async-start(), calls=%async_computation.3 | async-start | bytes 2949120 | tf_op jit(solution)/shard_map/all_gather | solution.py:29
  10.7 124.4 %all-gather.17.cloned.1.call-start = ((), (), s32[]{:S(2)}) async-start(), calls=%async_computation.6 | async-start | bytes 2949120 | tf_op jit(solution)/shard_map/all_gather | solution.py:29
  11.8 207.0 %all-gather.13.cloned.1.call-start = ((), (), s32[]{:S(2)}) async-start(), calls=%async_computation.4 | async-start | bytes 5898240 | tf_op jit(solution)/shard_map/all_gather | solution.py:29
  18.7 2.7 copy-start.22
  18.7 4.0 copy-start.21
  18.7 13.4 %copy-start.11 = (bf16[768,3,128]{2,0,1:T(8,128)(2,1)S(1)}, bf16[768,3,128]{2,0,1:T(8,128)(2,1)}, u32[]{:S(2)}) copy-start(bf16[768,3,128]{2,0,1:T(8,128)(2,1)} %get-tuple-element.42) | copy-start | bytes 1769476
  18.7 271.3 %all-gather.15.cloned.1.call-start = ((), (), s32[]{:S(2)}) async-start(), calls=%async_computation.5 | async-start | bytes 5898240 | tf_op jit(solution)/shard_map/all_gather | solution.py:29
  21.4 428.0 %reduce-scatter.2.cloned.1.call-start = ((), (), s32[]{:S(2)}) async-start(), calls=%async_computation.2 | async-start | bytes 1474560 | tf_op jit(solution)/shard_map/reduce_scatter | solution.py:108
  34.8 35.2 %slice-start = ((s8[9437184]{0:T(1024)(128)(4,1)}), s8[1048576]{0:T(1024)(128)(4,1)S(1)}, s32[]{:S(2)}) async-start(s8[9437184]{0:T(1024)(128)(4,1)} %bitcast.206), calls=%async_computation.8 | async-start | bytes 2097152
  60.9 9.1 %slice-start.1 = ((s8[9437184]{0:T(1024)(128)(4,1)}), s8[4194304]{0:T(1024)(128)(4,1)S(1)}, s32[]{:S(2)}) async-start(s8[9437184]{0:T(1024)(128)(4,1)} %bitcast.206), calls=%async_computation.9 | async-start | bytes 8388608
  64.8 5.2 %slice-start.2 = ((s8[9437184]{0:T(1024)(128)(4,1)}), s8[4194304]{0:T(1024)(128)(4,1)S(1)}, s32[]{:S(2)}) async-start(s8[9437184]{0:T(1024)(128)(4,1)} %bitcast.206), calls=%async_computation.10 | async-start | bytes 8388608
  125.4 41.8 %collective-permute-start = (bf16[3,768,3,128]{1,3,2,0:T(8,128)(2,1)}, bf16[3,768,3,128]{1,3,2,0:T(8,128)(2,1)}, u32[]{:S(2)}, u32[]{:S(2)}) collective-permute-start(bf16[3,768,3,128]{1,3,2,0:T(8,128)(2,1)} %fusion.20), channel_id=1, source_target_pairs={{0,16},{16,0},{1,17},{17,1},{2,18},{18,2},{3,19},{19,3},{4,20},{20... | collective-permute-start | bytes 5308424 | tf_op jit(solution)/shard_map/ppermute | solution.py:36
  138.8 64.9 %collective-permute-start.3 = (bf16[3,768,3,128]{1,3,2,0:T(8,128)(2,1)}, bf16[3,768,3,128]{1,3,2,0:T(8,128)(2,1)}, u32[]{:S(2)}, u32[]{:S(2)}) collective-permute-start(bf16[3,768,3,128]{1,3,2,0:T(8,128)(2,1)} %fusion.19), channel_id=1, source_target_pairs={{0,16},{16,0},{1,17},{17,1},{2,18},{18,2},{3,19},{19,3},{4,20},{20... | collective-permute-start | bytes 5308424 | tf_op jit(solution)/shard_map/ppermute | solution.py:36
  147.3 4.0 copy-start.15
  147.3 8.3 %slice-start.5 = ((s8[4718592]{0:T(1024)(128)(4,1)}), s8[4194304]{0:T(1024)(128)(4,1)S(1)}, s32[]{:S(2)}) async-start(s8[4718592]{0:T(1024)(128)(4,1)} %bitcast.223), calls=%async_computation.13 | async-start | bytes 8388608
  151.3 3.0 slice-start.4
  151.3 4.3 slice-start.6
  155.6 11.6 %copy-start.7 = (bf16[768,3,768]{2,0,1:T(8,128)(2,1)}, bf16[768,3,768]{2,0,1:T(8,128)(2,1)S(1)}, u32[]{:S(2)}) copy-start(bf16[768,3,768]{2,0,1:T(8,128)(2,1)S(1)} %fusion.16) | copy-start | bytes 10616836
  155.6 2.6 copy-start.14
  167.2 3.6 copy-start.13
  172.7 31.1 %copy-start.16 = (f32[768,384]{1,0:T(8,128)S(1)}, f32[768,384]{1,0:T(8,128)}, u32[]{:S(2)}) copy-start(f32[768,384]{1,0:T(8,128)} %convolution_add_fusion) | copy-start | bytes 3538948
  221.6 4.6 copy-start.18
  224.7 106.2 %collective-permute-start.1 = (bf16[3,768,3,256]{1,3,2,0:T(8,128)(2,1)}, bf16[3,768,3,256]{1,3,2,0:T(8,128)(2,1)}, u32[]{:S(2)}, u32[]{:S(2)}) collective-permute-start(bf16[3,768,3,256]{1,3,2,0:T(8,128)(2,1)} %fusion.15), channel_id=1, source_target_pairs={{0,16},{16,0},{1,17},{17,1},{2,18},{18,2},{3,19},{19,3},{4,20},{20... | collective-permute-start | bytes 10616840 | tf_op jit(solution)/shard_map/ppermute | solution.py:36
  295.8 82.1 %collective-permute-start.2 = (bf16[3,768,3,256]{1,3,2,0:T(8,128)(2,1)}, bf16[3,768,3,256]{1,3,2,0:T(8,128)(2,1)}, u32[]{:S(2)}, u32[]{:S(2)}) collective-permute-start(bf16[3,768,3,256]{1,3,2,0:T(8,128)(2,1)} %fusion.14), channel_id=1, source_target_pairs={{0,16},{16,0},{1,17},{17,1},{2,18},{18,2},{3,19},{19,3},{4,20},{20... | collective-permute-start | bytes 10616840 | tf_op jit(solution)/shard_map/ppermute | solution.py:36
  308.5 17.1 %slice-start.7 = ((s8[4718592]{0:T(1024)(128)(4,1)}), s8[524288]{0:T(1024)(128)(4,1)S(1)}, s32[]{:S(2)}) async-start(s8[4718592]{0:T(1024)(128)(4,1)} %bitcast.225), calls=%async_computation.15 | async-start | bytes 1048576
  318.3 7.3 %slice-start.8 = ((s8[4718592]{0:T(1024)(128)(4,1)}), s8[4194304]{0:T(1024)(128)(4,1)S(1)}, s32[]{:S(2)}) async-start(s8[4718592]{0:T(1024)(128)(4,1)} %bitcast.225), calls=%async_computation.16 | async-start | bytes 8388608
  318.3 7.3 %copy-start.6 = (bf16[4,768,768]{1,0,2:T(4,128)(2,1)S(1)}, bf16[4,768,768]{1,0,2:T(4,128)(2,1)}, u32[]{:S(2)}) copy-start(bf16[4,768,768]{1,0,2:T(4,128)(2,1)} %reshape.416) | copy-start | bytes 14155780
  325.6 5.3 %copy-start.8 = (bf16[768,3,768]{2,0,1:T(8,128)(2,1)S(1)}, bf16[768,3,768]{2,0,1:T(8,128)(2,1)}, u32[]{:S(2)}) copy-start(bf16[768,3,768]{2,0,1:T(8,128)(2,1)} %copy-done.7) | copy-start | bytes 10616836
  325.6 5.3 %copy-start.23 = (f32[768,768]{1,0:T(8,128)S(1)}, f32[768,768]{1,0:T(8,128)}, u32[]{:S(2)}) copy-start(f32[768,768]{1,0:T(8,128)} %fusion.40) | copy-start | bytes 7077892
  340.2 37.7 %copy-start.9 = (bf16[768,3,768]{2,0,1:T(8,128)(2,1)S(1)}, bf16[768,3,768]{2,0,1:T(8,128)(2,1)}, u32[]{:S(2)}) copy-start(bf16[768,3,768]{2,0,1:T(8,128)(2,1)} %copy-done.7) | copy-start | bytes 10616836
  423.3 58.4 %all-gather.19.cloned.1.call-start = ((), (), s32[]{:S(2)}) async-start(), calls=%async_computation.7 | async-start | bytes 1474560 | tf_op jit(solution)/shard_map/all_gather | solution.py:112
  484.1 18.3 %all-to-all-start = ((bf16[4,1,48,3,1024]{4,2,3,1,0:T(8,128)(2,1)}), bf16[4,1,48,3,1024]{4,2,3,1,0:T(8,128)(2,1)S(1)}, u32[]{:S(2)}, u32[]{:S(2)}) async-start(bf16[4,1,48,3,1024]{4,2,3,1,0:T(8,128)(2,1)} %copy.295), calls=%async_computation.1 | async-start | bytes 2359296 | tf_op jit(solution)/shard_map/all_to_all | solution.py:115
  (12 other events, 23.2 us)
Sparse Core Ops, SparseCore 0:
  10.8 50.1 all-gather.10
  62.5 49.3 all-gather.16
  113.4 87.2 all-gather.12
  202.2 87.8 all-gather.14
  423.4 25.8 reduce-scatter.1
  450.8 30.8 all-gather.18

commit v6 on v5

--- a/solution.py
+++ b/solution.py
@@ -20,16 +20,18 @@
     return [1] * heads
 
 
-def moved_weights(chunk, n_video):
+def moved_weights(chunk, n_video, after=None):
     v = lax.axis_index("video")
     g = lax.axis_index("groups")
     half = chunk.shape[0] // 2
     mine = lax.dynamic_slice_in_dim(chunk, g * half, half, axis=0)
+    if after is not None:
+        mine, after = lax.optimization_barrier((mine, after))
     other = lax.dynamic_slice_in_dim(chunk, (1 - g) * half, half, axis=0)
     gathered = lax.all_gather(mine, "video", axis=0, tiled=False)
     twice = jnp.concatenate([gathered, gathered], axis=0)
     onward = lax.dynamic_slice_in_dim(twice, v + 1, n_video - 1, axis=0)
-    return other, gathered, onward
+    return [other, gathered, onward], after
 
 
 def forward(onward):
@@ -61,8 +63,21 @@
     g = lax.axis_index("groups")
     heads_local = qkv_weight.shape[2] // HD
     sizes = head_chunks(heads_local)
-    first_moved = moved_weights(qkv_weight[:, :, :sizes[0] * HD], n_video)
-    onward0, frames = lax.optimization_barrier((first_moved[2], frames))
+    moved = []
+    first = 0
+    for size in sizes:
+        chunk = qkv_weight[:, :, first * HD:(first + size) * HD]
+        first += size
+        if len(moved) == len(sizes) - 1 and len(sizes) > 2:
+            whole_rows, moved[-1][1] = lax.optimization_barrier((chunk, moved[-1][1]))
+            step = [lax.all_gather(whole_rows, "video", axis=0, tiled=True), None, None]
+        elif moved:
+            step, moved[-1][1] = moved_weights(chunk, n_video, after=moved[-1][1])
+        else:
+            step, _ = moved_weights(chunk, n_video)
+            step.append(forward(step[2]))
+            step[3], frames = lax.optimization_barrier((step[3], frames))
+        moved.append(step)
     wide = frames.astype(jnp.float32)
     center = wide - jnp.mean(wide, axis=-1, keepdims=True)
     normed = center * lax.rsqrt(jnp.mean(center * center, axis=-1, keepdims=True) + 1e-06)
@@ -77,17 +92,18 @@
     )
     video_all = lax.all_gather(frame_video, "video", axis=0, tiled=True)
     pooled_parts = []
-    first = 0
     for index, size in enumerate(sizes):
-        chunk = qkv_weight[:, :, first * HD:(first + size) * HD]
-        first += size
         width = 3 * size * HD
+        if moved[index][1] is None:
+            full = moved[index][0].reshape(n_video * 2 * half, width)
+            proj = jnp.dot(normed, full, preferred_element_type=jnp.float32)
+            pooled_parts.append(attend(proj, nframes, size, scale, blocks, inner))
+            continue
+        other, gathered, onward = moved[index][:3]
         if index == 0:
-            other, gathered = first_moved[0], first_moved[1]
-            received = forward(onward0)
+            received = moved[index][3]
             video_all, received = lax.optimization_barrier((video_all, received))
         else:
-            other, gathered, onward = moved_weights(chunk, n_video)
             received = forward(onward)
         proj = jnp.dot(own_piece, other.reshape(half, width), preferred_element_type=jnp.float32)
         proj = proj + jnp.einsum(
@@ -109,12 +125,25 @@
         partial_proj.astype(jnp.bfloat16), "tensor", scatter_dimension=0, tiled=True
     )
     n_tensor = lax.axis_size("tensor")
-    clip_rows = lax.all_gather(clip_rows, "video", axis=0, tiled=False)
-    sub = n_video // n_tensor
-    clip_rows = clip_rows.reshape((n_tensor, sub) + clip_rows.shape[1:])
-    clip_proj = lax.all_to_all(clip_rows, "tensor", 0, 0, tiled=False)
-    clip_proj = jnp.transpose(clip_proj, (0, 2, 3, 1, 4))
-    clip_proj = clip_proj.reshape(rows, 3, -1).astype(jnp.float32)
+    if n_video == n_tensor:
+        t = lax.axis_index("tensor")
+        pieces = [None] * n_tensor
+        for k in range(n_tensor):
+            pairs = [(a * n_tensor + b, ((b + k) % n_tensor) * n_tensor + a)
+                     for a in range(n_video) for b in range(n_tensor)]
+            got = lax.ppermute(clip_rows, ("video", "tensor"), pairs)
+            pieces[k] = got
+        source = [(v - k) % n_tensor for k in range(n_tensor)]
+        stacked = jnp.stack(pieces, axis=0)
+        order = jnp.argsort(jnp.stack(source))
+        clip_proj = jnp.take(stacked, order, axis=0).reshape(rows, 3, -1).astype(jnp.float32)
+    else:
+        clip_rows = lax.all_gather(clip_rows, "video", axis=0, tiled=False)
+        sub = n_video // n_tensor
+        clip_rows = clip_rows.reshape((n_tensor, sub) + clip_rows.shape[1:])
+        clip_proj = lax.all_to_all(clip_rows, "tensor", 0, 0, tiled=False)
+        clip_proj = jnp.transpose(clip_proj, (0, 2, 3, 1, 4))
+        clip_proj = clip_proj.reshape(rows, 3, -1).astype(jnp.float32)
     t_heads = clip_proj.shape[2] // HD
     out_rows = rows // n_video
     start = v * out_rows

time: 521 us -> 513 us (0.985)
  local copies, waits for them, and re-layouts: 134 us -> 105 us
  waiting for transfers between devices: 223 us -> 239 us
    ppermute x4 -> x3, waiting for transfers between devices: 67 us -> 108 us  [forward(): return lax.ppermute(onward, 'groups', [(0, 1), (1, 0)])]
    all_gather x1, waiting for transfers between devices: 32.4 us -> 0.02 us  [per_device(): step = [lax.all_gather(whole_rows, 'video', axis=0, tiled=True), None, None]]
    reshape x5 -> x0, local copies, waits for them, and re-layouts: 30.1 us -> none  [the longest x4 27.7 us: per_device(): gathered.reshape(n_video, half, width)]
    ppermute x0 -> x4, waiting for transfers between devices: none -> 26.4 us  [per_device(): got = lax.ppermute(clip_rows, ('video', 'tensor'), pairs)]
    all_gather x4 -> x6, local copies, waits for them, and re-layouts: 9.49 us -> 26.3 us  [moved_weights(): gathered = lax.all_gather(mine, 'video', axis=0, tiled=False)]
    all_to_all x1 -> x0, waiting for transfers between devices: 13.8 us -> none  [per_device(): clip_proj = lax.all_to_all(clip_rows, 'tensor', 0, 0, tiled=False)]
    dot_general x0 -> x1, matrix products: none -> 11 us  [per_device(): proj = jnp.dot(normed, full, preferred_element_type=jnp.float32)]
    unnamed x90 -> x64, local copies, waits for them, and re-layouts: 19.3 us -> 9.5 us
  transfers between devices with their start and end apart: 11 -> 12, of which waited for: 8 -> 11; matrix products, arithmetic and copies ran while one was open for 39% -> 35% of each run, Pallas kernels for 0% -> 0%
where the time goes in v6:
time: 513 us; the launch traced here: 504 us
  waiting for transfers between devices  239 us (47%)
  local copies, waits for them, and re-layouts  105 us (20%)
  matrix products  70 us (14%)
  other arithmetic  40.8 us (8%)
  blocking collectives  22.3 us (4%)
  between operations  15.2 us (3%)
  starting transfers between devices  11.8 us (2%)
    ppermute x3, waiting for transfers between devices, forward(): return lax.ppermute(onward, 'groups', [(0, 1), (1, 0)])  108 us
    all_gather x3, waiting for transfers between devices, moved_weights(): gathered = lax.all_gather(mine, 'video', axis=0, tiled=False)  79.5 us
    ppermute x4, waiting for transfers between devices, per_device(): got = lax.ppermute(clip_rows, ('video', 'tensor'), pairs)  26.4 us
    all_gather x6, local copies, waits for them, and re-layouts, moved_weights(): gathered = lax.all_gather(mine, 'video', axis=0, tiled=False)  26.3 us
    reduce_scatter x1, waiting for transfers between devices, per_device(): lax.psum_scatter(partial_proj.astype(jnp.bfloat16), 'tensor', scatter_dim...  24.7 us
    dynamic_slice x2, local copies, waits for them, and re-layouts, per_device(): other_half = lax.dynamic_index_in_dim(cut, 1 - g, axis=2, keepdims=False)  24.1 us
    dot_general x3, matrix products, per_device(): jnp.einsum('nvd,vdc->nc', own_half, gathered.reshape(n_video, half, width...  23.8 us
    dot_general x3, matrix products, per_device(): jnp.einsum('nvd,vdc->nc', rolled, received.reshape(n_video - 1, half, wid...  17.2 us
  transfers between devices with their start and end apart: 12, of which 11 were waited for; matrix products, arithmetic and copies ran while one was open for 35% of the time, Pallas kernels for 0%

profile of v6, /device:TPU:10, one launch (start us, length us, event | category | flops | bytes accessed | tf_op | source)
XLA Modules:
  0.0 504.1 jit_solution(12204212703205041370)
XLA Ops:
  6.5 2.9 fusion.85
  17.5 44.1 %all-gather.10.cloned.1.call-done = bf16[3072,3,128]{0,2,1:T(8,128)(2,1)} async-done(((bf16[768,3,128]{0,2,1:T(8,128)(2,1)}), bf16[3072,3,128]{0,2,1:T(8,128)(2,1)}) %all-gather.10.cloned.1.call-update) | async-done | bytes 2359312 | tf_op jit(solution)/shard_map/all_gather | solution.py:31
  61.6 5.7 %reshape.436 = bf16[4,768,3,128]{1,0,3,2:T(4,128)(2,1)} reshape(bf16[3072,3,128]{0,2,1:T(8,128)(2,1)} %all-gather.10.cloned.1.call-done) | data formatting | bytes 4718592 | tf_op jit(solution)/shard_map/all_gather | solution.py:31
  72.5 7.8 %all-reduce = s32[12]{0:T(128)S(1)} all-reduce(s32[12]{0:T(128)S(1)} %dynamic-update-slice), channel_id=1, replica_groups=mesh['groups'=2,'video'=4,'tensor'=4] {'video'}, use_global_device_ids=true, to_apply=%add | all-reduce | flops 12 | bytes 96 | tf_op jit(solution)/shard_map/optimization_barrier | solution.py:105
  88.5 21.5 %collective-permute-done = bf16[3,768,3,128]{1,3,2,0:T(8,128)(2,1)} collective-permute-done((bf16[3,768,3,128]{1,3,2,0:T(8,128)(2,1)}, bf16[3,768,3,128]{1,3,2,0:T(8,128)(2,1)}, u32[]{:S(2)}, u32[]{:S(2)}) %collective-permute-start) | collective-permute-done | bytes 1769504 | tf_op jit(solution)/shard_map/ppermute | solution.py:38
  110.0 5.1 %convert_reduce_fusion = f32[3,256]{1,0:T(4,128)S(1)} fusion(bf16[3,256,6144]{2,1,0:T(8,128)(2,1)} %param.4), kind=kLoop, calls=%fused_computation.2 | loop fusion | flops 9436416 | bytes 9440256 | tf_op jit(solution)/shard_map/reduce_sum | solution.py:82
  115.1 6.3 %fusion.2 = f32[3,256]{1,0:T(4,128)S(1)} fusion(bf16[3,256,6144]{2,1,0:T(8,128)(2,1)} %param.4, f32[3,256]{1,0:T(4,128)S(1)} %broadcast_multiply_fusion), kind=kLoop, calls=%fused_computation.5 | loop fusion | flops 18873600 | bytes 9443328 | tf_op jit(solution)/shard_map/reduce_sum | solution.py:83
  121.4 33.4 %all-gather.12.cloned.1.call-done = bf16[3072,3,256]{0,2,1:T(8,128)(2,1)} async-done(((bf16[768,3,256]{0,2,1:T(8,128)(2,1)}), bf16[3072,3,256]{0,2,1:T(8,128)(2,1)}) %all-gather.12.cloned.1.call-update) | async-done | bytes 4718608 | tf_op jit(solution)/shard_map/all_gather | solution.py:31
  154.9 9.7 %reshape.437 = bf16[4,768,3,256]{1,0,3,2:T(4,128)(2,1)} reshape(bf16[3072,3,256]{0,2,1:T(8,128)(2,1)} %all-gather.12.cloned.1.call-done) | data formatting | bytes 9437184 | tf_op jit(solution)/shard_map/all_gather | solution.py:31
  164.9 12.4 %fusion.3 = bf16[3,256,6144]{2,1,0:T(8,128)(2,1)} fusion(bf16[3,256,6144]{2,1,0:T(8,128)(2,1)} %param.4, f32[3,256]{1,0:T(4,128)S(1)} %add_rsqrt_fusion.10, f32[3,256]{1,0:T(4,128)S(1)} %broadcast_multiply_fusion), kind=kLoop, calls=%fused_computation.6 | loop fusion | flops 18874368 | bytes 18880512 | tf_op jit(solution)/shard_map/convert_element_type | solution.py:84
  177.3 15.3 %reshape_reshape.3 = bf16[768,4,2,768]{3,2,1,0:T(2,128)(2,1)} reshape(bf16[3,256,6144]{2,1,0:T(8,128)(2,1)} %fusion.3) | data formatting | bytes 18874368 | tf_op jit(solution)/shard_map/reshape;reshape | solution.py:86
  192.5 22.6 %constant_dynamic-slice_fusion.3 = (bf16[768,4,1,768]{3,2,1,0:T(2,128)(2,1)S(1)}, bf16[768,4,1,768]{3,2,1,0:T(2,128)(2,1)}) fusion(bf16[768,4,2,768]{3,2,1,0:T(2,128)(2,1)} %reshape_reshape.3, s32[]{:T(128)S(6)} %select_n.89, s32[]{:T(128)S(6)} %select_n.92), kind=kLoop, calls=%fused_computation.144 | loop fusion | bytes 18874376 | tf_op jit(solution)/shard_map/jit(dynamic_index_in_dim)/dynamic_slice | solution.py:88
  218.0 5.4 %constant_dynamic-slice_fusion.7 = bf16[768,1,1,768]{3,2,1,0:T(2,128)(2,1)S(1)} fusion(bf16[768,4,2,768]{3,2,1,0:T(2,128)(2,1)} %reshape_reshape.3, s32[]{:T(128)S(6)} %select_n.88, s32[]{:T(128)S(6)} %select_n.90), kind=kLoop, calls=%fused_computation.148 | loop fusion | bytes 2359304 | tf_op jit(solution)/shard_map/jit(dynamic_index_in_dim)/dynamic_slice | solution.py:89
  223.5 4.4 convolution_bitcast_fusion
  231.0 3.2 fusion.16
  238.5 3.3 multiply_reduce_fusion.8
  244.0 4.0 fusion.37
  252.5 9.7 %reshape.438 = bf16[4,768,3,256]{1,0,3,2:T(4,128)(2,1)} reshape(bf16[3072,3,256]{0,2,1:T(8,128)(2,1)} %all-gather.14.cloned.1.call-done) | data formatting | bytes 9437184 | tf_op jit(solution)/shard_map/all_gather | solution.py:31
  262.3 10.6 %fusion.9 = f32[768,768,1]{1,0,2:T(8,128)S(1)} fusion(bf16[4,768,768]{1,0,2:T(4,128)(2,1)} %bitcast.237, bf16[768,4,1,768]{3,2,1,0:T(2,128)(2,1)} %get-tuple-element.34), kind=kOutput, calls=%fused_computation.22 | convolution fusion | flops 3623878656 | bytes 11796480 | tf_op jit(solution)/shard_map/nvd,vdc->nc/dot_general | solution.py:109
  273.4 3.1 fusion.15
  278.0 35.9 %collective-permute-done.1 = bf16[3,768,3,256]{1,3,2,0:T(8,128)(2,1)} collective-permute-done((bf16[3,768,3,256]{1,3,2,0:T(8,128)(2,1)}, bf16[3,768,3,256]{1,3,2,0:T(8,128)(2,1)}, u32[]{:S(2)}, u32[]{:S(2)}) %collective-permute-start.1) | collective-permute-done | bytes 3538976 | tf_op jit(solution)/shard_map/ppermute | solution.py:38
  313.9 6.4 %bitcast_add_fusion.2 = f32[768,768]{1,0:T(8,128)} fusion(f32[768,768]{1,0:T(8,128)S(1)} %copy-done.15, f32[768,768,1]{1,0,2:T(8,128)S(1)} %fusion.9, bf16[768,3,768]{2,0,1:T(8,128)(2,1)S(1)} %copy-done.7, bf16[3,768,768]{1,2,0:T(8,128)(2,1)} %bitcast.22), kind=kOutput, calls=%fused_computation.35 | convolution fusion | flops 2719088640 | bytes 14155776 | tf_op jit(solution)/shard_map/nvd,vdc->nc/dot_general | solution.py:113
  327.2 10.6 %fusion.7 = f32[768,768,1]{1,0,2:T(8,128)S(1)} fusion(bf16[4,768,768]{1,0,2:T(4,128)(2,1)} %bitcast.238, bf16[768,4,1,768]{3,2,1,0:T(2,128)(2,1)} %get-tuple-element.34), kind=kOutput, calls=%fused_computation.20 | convolution fusion | flops 3623878656 | bytes 11796480 | tf_op jit(solution)/shard_map/nvd,vdc->nc/dot_general | solution.py:109
  337.8 50.9 %collective-permute-done.2 = bf16[3,768,3,256]{1,3,2,0:T(8,128)(2,1)} collective-permute-done((bf16[3,768,3,256]{1,3,2,0:T(8,128)(2,1)}, bf16[3,768,3,256]{1,3,2,0:T(8,128)(2,1)}, u32[]{:S(2)}, u32[]{:S(2)}) %collective-permute-start.2) | collective-permute-done | bytes 3538976 | tf_op jit(solution)/shard_map/ppermute | solution.py:38
  388.7 6.5 %bitcast_add_fusion = f32[768,768]{1,0:T(8,128)} fusion(f32[768,768]{1,0:T(8,128)S(1)} %copy-done.14, f32[768,768,1]{1,0,2:T(8,128)S(1)} %fusion.7, bf16[768,3,768]{2,0,1:T(8,128)(2,1)S(1)} %copy-done.8, bf16[3,768,768]{1,2,0:T(8,128)(2,1)} %bitcast.32), kind=kOutput, calls=%fused_computation.33 | convolution fusion | flops 2719088640 | bytes 14155776 | tf_op jit(solution)/shard_map/nvd,vdc->nc/dot_general | solution.py:113
  402.0 11.0 %fusion.20 = f32[3,256,3,1,128]{1,4,2,0,3:T(8,128)S(1)} fusion(bf16[6144,3,128]{0,2,1:T(8,128)(2,1)} %all-gather.8.cloned.1.call-done, bf16[3,256,6144]{2,1,0:T(8,128)(2,1)} %fusion.3), kind=kOutput, calls=%fused_computation.44 | convolution fusion | flops 3623878656 | bytes 15335424 | tf_op jit(solution)/shard_map/dot_general | solution.py:99
  414.1 14.5 %all_gather.35 = bf16[192,768]{1,0:T(8,128)(2,1)S(1)} all-gather(bf16[48,768]{1,0:T(8,128)(2,1)S(1)} %pad_maximum_fusion.1), channel_id=1, replica_groups=mesh['groups'=2,'video'=4,'tensor'=4] {'video'}, dimensions={0}, use_global_device_ids=true | all-gather | bytes 368640 | tf_op jit(solution)/shard_map/all_gather | solution.py:119
  428.6 4.5 convolution_convert_fusion
  434.3 24.7 %reduce-scatter.2.cloned.1.call-done = bf16[48,3,1024]{2,0,1:T(8,128)(2,1)} async-done(((bf16[192,3,1024]{2,0,1:T(8,128)(2,1)}), bf16[48,3,1024]{2,0,1:T(8,128)(2,1)}) %reduce-scatter.2.cloned.1.call-update) | async-done | bytes 294928 | tf_op jit(solution)/shard_map/reduce_scatter | solution.py:124
  459.0 3.7 collective-permute-start.3
  466.4 17.1 %collective-permute-done.3 = bf16[48,3,1024]{2,0,1:T(8,128)(2,1)S(1)} collective-permute-done((bf16[48,3,1024]{2,0,1:T(8,128)(2,1)}, bf16[48,3,1024]{2,0,1:T(8,128)(2,1)S(1)}, u32[]{:S(2)}, u32[]{:S(2)}) %collective-permute-start.3) | collective-permute-done | bytes 294944 | tf_op jit(solution)/shard_map/ppermute | solution.py:134
  483.4 6.8 %collective-permute-done.4 = bf16[48,3,1024]{2,0,1:T(8,128)(2,1)S(1)} collective-permute-done((bf16[48,3,1024]{2,0,1:T(8,128)(2,1)}, bf16[48,3,1024]{2,0,1:T(8,128)(2,1)S(1)}, u32[]{:S(2)}, u32[]{:S(2)}) %collective-permute-start.4) | collective-permute-done | bytes 294944 | tf_op jit(solution)/shard_map/ppermute | solution.py:134
  (180 shorter events, 65.8 us)
Async XLA Ops:
  6.5 55.1 %all-gather.10.cloned.1.call-start = ((), (), s32[]{:S(2)}) async-start(), calls=%async_computation.3 | async-start | bytes 2949120 | tf_op jit(solution)/shard_map/all_gather | solution.py:31
  11.4 143.4 %all-gather.12.cloned.1.call-start = ((), (), s32[]{:S(2)}) async-start(), calls=%async_computation.4 | async-start | bytes 5898240 | tf_op jit(solution)/shard_map/all_gather | solution.py:31
  61.6 5.8 %copy-start = (bf16[3072,3,128]{0,2,1:T(8,128)(2,1)S(1)}, bf16[3072,3,128]{0,2,1:T(8,128)(2,1)}, u32[]{:S(2)}) copy-start(bf16[3072,3,128]{0,2,1:T(8,128)(2,1)} %all-gather.10.cloned.1.call-done) | copy-start | bytes 7077892
  67.3 185.2 %all-gather.14.cloned.1.call-start = ((), (), s32[]{:S(2)}) async-start(), calls=%async_computation.5 | async-start | bytes 5898240 | tf_op jit(solution)/shard_map/all_gather | solution.py:31
  67.6 3.4 copy-start.13
  67.6 4.6 copy-start.12
  67.6 14.7 %copy-start.4 = (bf16[768,3,256]{2,0,1:T(8,128)(2,1)S(1)}, bf16[768,3,256]{2,0,1:T(8,128)(2,1)}, u32[]{:S(2)}) copy-start(bf16[768,3,256]{2,0,1:T(8,128)(2,1)} %get-tuple-element.46) | copy-start | bytes 3538948
  69.5 14.4 %copy-start.3 = (bf16[768,3,256]{2,0,1:T(8,128)(2,1)S(1)}, bf16[768,3,256]{2,0,1:T(8,128)(2,1)}, u32[]{:S(2)}) copy-start(bf16[768,3,256]{2,0,1:T(8,128)(2,1)} %get-tuple-element.54) | copy-start | bytes 3538948
  69.5 40.4 %collective-permute-start = (bf16[3,768,3,128]{1,3,2,0:T(8,128)(2,1)}, bf16[3,768,3,128]{1,3,2,0:T(8,128)(2,1)}, u32[]{:S(2)}, u32[]{:S(2)}) collective-permute-start(bf16[3,768,3,128]{1,3,2,0:T(8,128)(2,1)} %fusion.19), channel_id=1, source_target_pairs={{0,16},{16,0},{1,17},{17,1},{2,18},{18,2},{3,19},{19,3},{4,20},{20... | collective-permute-start | bytes 5308424 | tf_op jit(solution)/shard_map/ppermute | solution.py:38
  164.6 237.4 %all-gather.8.cloned.1.call-start = ((), (), s32[]{:S(2)}) async-start(), calls=%async_computation.1 | async-start | bytes 5898240 | tf_op jit(solution)/shard_map/all_gather | solution.py:73
  215.1 12.7 %slice-start.4 = ((s8[9437184]{0:T(1024)(128)(4,1)}), s8[1048576]{0:T(1024)(128)(4,1)S(1)}, s32[]{:S(2)}) async-start(s8[9437184]{0:T(1024)(128)(4,1)} %bitcast.234), calls=%async_computation.10 | async-start | bytes 2097152
  215.1 12.7 %slice-start.5 = ((s8[9437184]{0:T(1024)(128)(4,1)}), s8[4194304]{0:T(1024)(128)(4,1)S(1)}, s32[]{:S(2)}) async-start(s8[9437184]{0:T(1024)(128)(4,1)} %bitcast.234), calls=%async_computation.11 | async-start | bytes 8388608
  218.0 5.5 %copy-start.6 = (bf16[768,3,768]{2,0,1:T(8,128)(2,1)}, bf16[768,3,768]{2,0,1:T(8,128)(2,1)S(1)}, u32[]{:S(2)}) copy-start(bf16[768,3,768]{2,0,1:T(8,128)(2,1)S(1)} %fusion.17) | copy-start | bytes 10616836
  218.0 9.9 %slice-start.6 = ((s8[9437184]{0:T(1024)(128)(4,1)}), s8[4194304]{0:T(1024)(128)(4,1)S(1)}, s32[]{:S(2)}) async-start(s8[9437184]{0:T(1024)(128)(4,1)} %bitcast.234), calls=%async_computation.12 | async-start | bytes 8388608
  223.4 12.2 %copy-start.1 = (bf16[768,1,1,768]{3,2,1,0:T(2,128)(2,1)}, bf16[768,1,1,768]{3,2,1,0:T(2,128)(2,1)S(1)}, u32[]{:S(2)}) copy-start(bf16[768,1,1,768]{3,2,1,0:T(2,128)(2,1)S(1)} %constant_dynamic-slice_fusion.7) | copy-start | bytes 3538948
  223.4 4.4 copy-start.9
  223.5 7.1 %slice-start = ((s8[4718592]{0:T(1024)(128)(4,1)}), s8[4194304]{0:T(1024)(128)(4,1)S(1)}, s32[]{:S(2)}) async-start(s8[4718592]{0:T(1024)(128)(4,1)} %bitcast.224), calls=%async_computation.6 | async-start | bytes 8388608
  231.0 4.6 copy-start.10
  234.2 79.7 %collective-permute-start.1 = (bf16[3,768,3,256]{1,3,2,0:T(8,128)(2,1)}, bf16[3,768,3,256]{1,3,2,0:T(8,128)(2,1)}, u32[]{:S(2)}, u32[]{:S(2)}) collective-permute-start(bf16[3,768,3,256]{1,3,2,0:T(8,128)(2,1)} %fusion.16), channel_id=1, source_target_pairs={{0,16},{16,0},{1,17},{17,1},{2,18},{18,2},{3,19},{19,3},{4,20},{20... | collective-permute-start | bytes 10616840 | tf_op jit(solution)/shard_map/ppermute | solution.py:38
  244.0 4.0 copy-start.11
  262.2 10.7 %slice-start.2 = ((s8[4718592]{0:T(1024)(128)(4,1)}), s8[524288]{0:T(1024)(128)(4,1)S(1)}, s32[]{:S(2)}) async-start(s8[4718592]{0:T(1024)(128)(4,1)} %bitcast.227), calls=%async_computation.8 | async-start | bytes 1048576
  262.3 196.8 %reduce-scatter.2.cloned.1.call-start = ((), (), s32[]{:S(2)}) async-start(), calls=%async_computation.2 | async-start | bytes 1474560 | tf_op jit(solution)/shard_map/reduce_scatter | solution.py:124
  262.3 10.6 %slice-start.3 = ((s8[4718592]{0:T(1024)(128)(4,1)}), s8[4194304]{0:T(1024)(128)(4,1)S(1)}, s32[]{:S(2)}) async-start(s8[4718592]{0:T(1024)(128)(4,1)} %bitcast.227), calls=%async_computation.9 | async-start | bytes 8388608
  273.4 40.5 %copy-start.7 = (bf16[768,3,768]{2,0,1:T(8,128)(2,1)S(1)}, bf16[768,3,768]{2,0,1:T(8,128)(2,1)}, u32[]{:S(2)}) copy-start(bf16[768,3,768]{2,0,1:T(8,128)(2,1)} %copy-done.6) | copy-start | bytes 10616836
  273.4 40.5 %copy-start.15 = (f32[768,768]{1,0:T(8,128)S(1)}, f32[768,768]{1,0:T(8,128)}, u32[]{:S(2)}) copy-start(f32[768,768]{1,0:T(8,128)} %fusion.37) | copy-start | bytes 7077892
  276.5 112.2 %collective-permute-start.2 = (bf16[3,768,3,256]{1,3,2,0:T(8,128)(2,1)}, bf16[3,768,3,256]{1,3,2,0:T(8,128)(2,1)}, u32[]{:S(2)}, u32[]{:S(2)}) collective-permute-start(bf16[3,768,3,256]{1,3,2,0:T(8,128)(2,1)} %fusion.15), channel_id=1, source_target_pairs={{0,16},{16,0},{1,17},{17,1},{2,18},{18,2},{3,19},{19,3},{4,20},{20... | collective-permute-start | bytes 10616840 | tf_op jit(solution)/shard_map/ppermute | solution.py:38
  327.1 61.6 %copy-start.8 = (bf16[768,3,768]{2,0,1:T(8,128)(2,1)S(1)}, bf16[768,3,768]{2,0,1:T(8,128)(2,1)}, u32[]{:S(2)}) copy-start(bf16[768,3,768]{2,0,1:T(8,128)(2,1)} %copy-done.6) | copy-start | bytes 10616836
  327.1 61.6 %copy-start.14 = (f32[768,768]{1,0:T(8,128)S(1)}, f32[768,768]{1,0:T(8,128)}, u32[]{:S(2)}) copy-start(f32[768,768]{1,0:T(8,128)} %fusion.35) | copy-start | bytes 7077892
  459.0 24.4 %collective-permute-start.3 = (bf16[48,3,1024]{2,0,1:T(8,128)(2,1)}, bf16[48,3,1024]{2,0,1:T(8,128)(2,1)S(1)}, u32[]{:S(2)}, u32[]{:S(2)}) collective-permute-start(bf16[48,3,1024]{2,0,1:T(8,128)(2,1)} %reduce-scatter.2.cloned.1.call-done), channel_id=1, source_target_pairs={{0,0},{1,4},{2,8},{3,12},{4,1},{5,5},{6,9},{7,13},{8,2},{9,6},{10,... | collective-permute-start | bytes 884744 | tf_op jit(solution)/shard_map/ppermute | solution.py:134
  462.8 27.5 %collective-permute-start.4 = (bf16[48,3,1024]{2,0,1:T(8,128)(2,1)}, bf16[48,3,1024]{2,0,1:T(8,128)(2,1)S(1)}, u32[]{:S(2)}, u32[]{:S(2)}) collective-permute-start(bf16[48,3,1024]{2,0,1:T(8,128)(2,1)} %reduce-scatter.2.cloned.1.call-done), channel_id=1, source_target_pairs={{0,4},{1,8},{2,12},{3,0},{4,5},{5,9},{6,13},{7,1},{8,6},{9,10},{10... | collective-permute-start | bytes 884744 | tf_op jit(solution)/shard_map/ppermute | solution.py:134
  464.0 27.3 %collective-permute-start.5 = (bf16[48,3,1024]{2,0,1:T(8,128)(2,1)}, bf16[48,3,1024]{2,0,1:T(8,128)(2,1)S(1)}, u32[]{:S(2)}, u32[]{:S(2)}) collective-permute-start(bf16[48,3,1024]{2,0,1:T(8,128)(2,1)} %reduce-scatter.2.cloned.1.call-done), channel_id=1, source_target_pairs={{0,8},{1,12},{2,0},{3,4},{4,9},{5,13},{6,1},{7,5},{8,10},{9,14},{1... | collective-permute-start | bytes 884744 | tf_op jit(solution)/shard_map/ppermute | solution.py:134
  464.9 27.9 %collective-permute-start.6 = (bf16[48,3,1024]{2,0,1:T(8,128)(2,1)}, bf16[48,3,1024]{2,0,1:T(8,128)(2,1)S(1)}, u32[]{:S(2)}, u32[]{:S(2)}) collective-permute-start(bf16[48,3,1024]{2,0,1:T(8,128)(2,1)} %reduce-scatter.2.cloned.1.call-done), channel_id=1, source_target_pairs={{0,12},{1,0},{2,4},{3,8},{4,13},{5,1},{6,5},{7,9},{8,14},{9,2},{10... | collective-permute-start | bytes 884744 | tf_op jit(solution)/shard_map/ppermute | solution.py:134
  (3 other events, 6.0 us)
Sparse Core Ops, SparseCore 0:
  11.5 50.0 all-gather.9
  67.4 87.3 all-gather.11
  164.7 87.7 all-gather.13
  262.4 87.8 all-gather.7
  433.3 25.6 reduce-scatter.1

commit v7 on v6

--- a/solution.py
+++ b/solution.py
@@ -29,8 +29,10 @@
         mine, after = lax.optimization_barrier((mine, after))
     other = lax.dynamic_slice_in_dim(chunk, (1 - g) * half, half, axis=0)
     gathered = lax.all_gather(mine, "video", axis=0, tiled=False)
-    twice = jnp.concatenate([gathered, gathered], axis=0)
-    onward = lax.dynamic_slice_in_dim(twice, v + 1, n_video - 1, axis=0)
+    onward = jnp.stack(
+        [lax.dynamic_index_in_dim(gathered, (v + 1 + i) % n_video, axis=0, keepdims=False)
+         for i in range(n_video - 1)]
+    )
     return [other, gathered, onward], after
 
 
@@ -76,20 +78,20 @@
         else:
             step, _ = moved_weights(chunk, n_video)
             step.append(forward(step[2]))
-            step[3], frames = lax.optimization_barrier((step[3], frames))
         moved.append(step)
     wide = frames.astype(jnp.float32)
     center = wide - jnp.mean(wide, axis=-1, keepdims=True)
     normed = center * lax.rsqrt(jnp.mean(center * center, axis=-1, keepdims=True) + 1e-06)
     normed = normed.astype(jnp.bfloat16).reshape(patch_rows, frames.shape[2])
-    half = qkv_weight.shape[0] // 2
-    cut = normed.reshape(patch_rows, n_video, 2, half)
-    own_half = lax.dynamic_index_in_dim(cut, g, axis=2, keepdims=False)
-    other_half = lax.dynamic_index_in_dim(cut, 1 - g, axis=2, keepdims=False)
-    own_piece = lax.dynamic_index_in_dim(other_half, v, axis=1, keepdims=False)
-    rolled = lax.dynamic_slice_in_dim(
-        jnp.concatenate([other_half, other_half], axis=1), v + 1, n_video - 1, axis=1
-    )
+    local_rows = qkv_weight.shape[0]
+    half = local_rows // 2
+
+    def columns(shard, which):
+        return lax.dynamic_slice_in_dim(normed, shard * local_rows + which * half, half, axis=1)
+
+    own_half = jnp.stack([columns(u, g) for u in range(n_video)], axis=1)
+    own_piece = columns(v, 1 - g)
+    rolled = jnp.stack([columns((v + 1 + i) % n_video, 1 - g) for i in range(n_video - 1)], axis=1)
     video_all = lax.all_gather(frame_video, "video", axis=0, tiled=True)
     pooled_parts = []
     for index, size in enumerate(sizes):

time: 513 us -> 505 us (0.984); the launches traced: 504 us -> 501 us
    ppermute x3, waiting for transfers between devices: 108 us -> 79.5 us  [forward(): return lax.ppermute(onward, 'groups', [(0, 1), (1, 0)])]
    all_gather x3, waiting for transfers between devices: 79.5 us -> 108 us  [moved_weights(): gathered = lax.all_gather(mine, 'video', axis=0, tiled=False)]
    another operation x1, local copies, waits for them, and re-layouts: 15.3 us -> 1.01 us  [per_device(): jnp.stack([columns((v + 1 + i) % n_video, 1 - g) for i in range(n_video -...]
    concatenate x4 -> x0, other arithmetic: 9.39 us -> none  [the longest x3 8.12 us: moved_weights(): twice = jnp.concatenate([gathered, gathered], axis=0)]
    unnamed x64 -> x83, local copies, waits for them, and re-layouts: 9.5 us -> 16.5 us
    another operation x0 -> x3, other arithmetic: none -> 5.7 us  [moved_weights(): jnp.stack([lax.dynamic_index_in_dim(gathered, (v + 1 + i) % n_video, axis...]
    all_gather x6 -> x3, local copies, waits for them, and re-layouts: 26.3 us -> 24.2 us  [moved_weights(): gathered = lax.all_gather(mine, 'video', axis=0, tiled=False)]
  transfers between devices with their start and end apart: 12 -> 12, of which waited for: 11 -> 9; matrix products, arithmetic and copies ran while one was open for 35% -> 36% of each run, Pallas kernels for 0% -> 0%
where the time goes in v7:
time: 505 us; the launch traced here: 501 us
  waiting for transfers between devices  239 us (47%)
  local copies, waits for them, and re-layouts  104 us (21%)
  matrix products  70.2 us (14%)
  other arithmetic  37.6 us (7%)
  blocking collectives  23.4 us (5%)
  between operations  15.1 us (3%)
  starting transfers between devices  11.9 us (2%)
    all_gather x3, waiting for transfers between devices, moved_weights(): gathered = lax.all_gather(mine, 'video', axis=0, tiled=False)  108 us
    ppermute x3, waiting for transfers between devices, forward(): return lax.ppermute(onward, 'groups', [(0, 1), (1, 0)])  79.5 us
    dynamic_slice x3, local copies, waits for them, and re-layouts, moved_weights(): lax.dynamic_index_in_dim(gathered, (v + 1 + i) % n_video, axis=0, keepdim...  34.4 us
    ppermute x4, waiting for transfers between devices, per_device(): got = lax.ppermute(clip_rows, ('video', 'tensor'), pairs)  26.4 us
    reduce_scatter x1, waiting for transfers between devices, per_device(): lax.psum_scatter(partial_proj.astype(jnp.bfloat16), 'tensor', scatter_dim...  24.8 us
    all_gather x3, local copies, waits for them, and re-layouts, moved_weights(): gathered = lax.all_gather(mine, 'video', axis=0, tiled=False)  24.2 us
    dot_general x3, matrix products, per_device(): jnp.einsum('nvd,vdc->nc', own_half, gathered.reshape(n_video, half, width...  19 us
    dot_general x3, matrix products, per_device(): jnp.einsum('nvd,vdc->nc', rolled, received.reshape(n_video - 1, half, wid...  17.3 us
  transfers between devices with their start and end apart: 12, of which 9 were waited for; matrix products, arithmetic and copies ran while one was open for 36% of the time, Pallas kernels for 0%

profile of v7, /device:TPU:10, one launch (start us, length us, event | category | flops | bytes accessed | tf_op | source)
XLA Modules:
  0.0 501.4 jit_solution(13204290403778979352)
XLA Ops:
  17.4 44.1 %all-gather.10.cloned.1.call-done = bf16[3072,3,128]{0,2,1:T(8,128)(2,1)} async-done(((bf16[768,3,128]{0,2,1:T(8,128)(2,1)}), bf16[3072,3,128]{0,2,1:T(8,128)(2,1)}) %all-gather.10.cloned.1.call-update) | async-done | bytes 2359312 | tf_op jit(solution)/shard_map/all_gather | solution.py:31
  61.6 4.5 reshape.437
  70.7 5.3 %convert_reduce_fusion = f32[3,256]{1,0:T(4,128)S(1)} fusion(bf16[3,256,6144]{2,1,0:T(8,128)(2,1)} %param.4), kind=kLoop, calls=%fused_computation.2 | loop fusion | flops 9436416 | bytes 9440256 | tf_op jit(solution)/shard_map/reduce_sum | solution.py:83
  76.0 6.6 %fusion.2 = f32[3,256]{1,0:T(4,128)S(1)} fusion(bf16[3,256,6144]{2,1,0:T(8,128)(2,1)} %param.4, f32[3,256]{1,0:T(4,128)S(1)} %broadcast_multiply_fusion), kind=kLoop, calls=%fused_computation.5 | loop fusion | flops 18873600 | bytes 9443328 | tf_op jit(solution)/shard_map/reduce_sum | solution.py:84
  82.6 3.8 constant_dynamic-slice_fusion.11
  89.6 64.0 %all-gather.12.cloned.1.call-done = bf16[3072,3,256]{0,2,1:T(8,128)(2,1)} async-done(((bf16[768,3,256]{0,2,1:T(8,128)(2,1)}), bf16[3072,3,256]{0,2,1:T(8,128)(2,1)}) %all-gather.12.cloned.1.call-update) | async-done | bytes 4718608 | tf_op jit(solution)/shard_map/all_gather | solution.py:31
  153.6 9.7 %reshape.438 = bf16[4,768,3,256]{1,0,3,2:T(4,128)(2,1)} reshape(bf16[3072,3,256]{0,2,1:T(8,128)(2,1)} %all-gather.12.cloned.1.call-done) | data formatting | bytes 9437184 | tf_op jit(solution)/shard_map/all_gather | solution.py:31
  163.6 12.4 %fusion.3 = bf16[3,256,6144]{2,1,0:T(8,128)(2,1)} fusion(bf16[3,256,6144]{2,1,0:T(8,128)(2,1)} %param.4, f32[3,256]{1,0:T(4,128)S(1)} %add_rsqrt_fusion.10, f32[3,256]{1,0:T(4,128)S(1)} %broadcast_multiply_fusion), kind=kLoop, calls=%fused_computation.6 | loop fusion | flops 18874368 | bytes 18880512 | tf_op jit(solution)/shard_map/convert_element_type | solution.py:85
  176.0 9.3 %all-reduce = s32[12]{0:T(128)S(1)} all-reduce(s32[12]{0:T(128)S(1)} %dynamic-update-slice), channel_id=1, replica_groups=mesh['groups'=2,'video'=4,'tensor'=4] {'video'}, use_global_device_ids=true, to_apply=%add | all-reduce | flops 12 | bytes 96 | tf_op jit(solution)/shard_map/optimization_barrier | solution.py:107
  194.1 4.4 fusion.31
  198.5 4.1 fusion.29
  203.7 3.6 fusion.18
  207.4 4.5 convolution_bitcast_fusion
  211.9 15.5 %constant_dynamic-slice_fusion.6 = (bf16[1,768,3,256]{1,0,3,2:T(2,128)(2,1)}, bf16[1,768,3,256]{1,0,3,2:T(2,128)(2,1)}, bf16[1,768,3,256]{1,0,3,2:T(2,128)(2,1)S(1)}) fusion(bf16[4,768,3,256]{1,0,3,2:T(4,128)(2,1)} %reshape.438, s32[]{:T(128)S(6)} %select_n.148, s32[]{:T(128)S(6)} %select_n.149, s32[]{:T(128)S(6)} %select_n.150), kind=kLoop, calls=%fused_computation.142 | loop fusion | bytes 7077900 | tf_op jit(solution)/shard_map/jit(dynamic_index_in_dim)/dynamic_slice | solution.py:33
  237.7 3.3 multiply_reduce_fusion.8
  244.9 8.3 %fusion.9 = f32[768,768,1]{1,0,2:T(8,128)} fusion(bf16[4,768,768]{1,0,2:T(4,128)(2,1)} %bitcast.208, bf16[768,1,768]{2,0,1:T(8,128)(2,1)S(1)} %copy-done.16, bf16[768,1,768]{2,0,1:T(8,128)(2,1)S(1)} %copy-done.19, bf16[768,1,768]{2,0,1:T(8,128)(2,1)} %copy-done.21, bf16[768,1,768]{2,0,1:T(8,128)(2,1)} %copy-done.22), kind=kOutput, calls=%fused_computation.13 | convolution fusion | flops 3630956544 | bytes 11796480 | tf_op jit(solution)/shard_map/nvd,vdc->nc/dot_general | solution.py:111
  253.3 9.9 %reshape.439 = bf16[4,768,3,256]{1,0,3,2:T(4,128)(2,1)} reshape(bf16[3072,3,256]{0,2,1:T(8,128)(2,1)} %all-gather.14.cloned.1.call-done) | data formatting | bytes 9437184 | tf_op jit(solution)/shard_map/all_gather | solution.py:31
  263.2 15.1 %constant_dynamic-slice_fusion.2 = (bf16[1,768,3,256]{1,0,3,2:T(2,128)(2,1)}, bf16[1,768,3,256]{1,0,3,2:T(2,128)(2,1)}, bf16[1,768,3,256]{1,0,3,2:T(2,128)(2,1)S(1)}) fusion(bf16[4,768,3,256]{1,0,3,2:T(4,128)(2,1)} %reshape.439, s32[]{:T(128)S(6)} %select_n.148, s32[]{:T(128)S(6)} %select_n.149, s32[]{:T(128)S(6)} %select_n.150), kind=kLoop, calls=%fused_computation.138 | loop fusion | bytes 7077900 | tf_op jit(solution)/shard_map/jit(dynamic_index_in_dim)/dynamic_slice | solution.py:33
  284.4 27.6 %collective-permute-done.1 = bf16[3,768,3,256]{1,3,2,0:T(8,128)(2,1)} collective-permute-done((bf16[3,768,3,256]{1,3,2,0:T(8,128)(2,1)}, bf16[3,768,3,256]{1,3,2,0:T(8,128)(2,1)}, u32[]{:S(2)}, u32[]{:S(2)}) %collective-permute-start.1) | collective-permute-done | bytes 3538976 | tf_op jit(solution)/shard_map/ppermute | solution.py:40
  312.0 6.4 %bitcast_add_fusion.2 = f32[768,768]{1,0:T(8,128)} fusion(f32[768,768]{1,0:T(8,128)S(1)} %copy-done.26, f32[768,768,1]{1,0,2:T(8,128)S(1)} %copy-done.27, bf16[3,768,768]{1,2,0:T(8,128)(2,1)} %bitcast.28, bf16[768,1,768]{2,0,1:T(8,128)(2,1)S(1)} %copy-done.10, bf16[768,1,768]{2,0,1:T(8,128)(2,1)S(1)} %copy-done.13, bf16[768,1,768]{2,0,1:T(8,128)(2,1)S(1)} %copy-done.7), kind=kOutput, calls=%fused_computation.20 | convolution fusion | flops 2722627584 | bytes 14155776 | tf_op jit(solution)/shard_map/nvd,vdc->nc/dot_general | solution.py:115
  318.5 2.9 reshape.418
  327.6 7.0 %fusion.7 = f32[768,768,1]{1,0,2:T(8,128)S(1)} fusion(bf16[4,768,768]{1,0,2:T(4,128)(2,1)} %bitcast.209, bf16[768,1,768]{2,0,1:T(8,128)(2,1)S(1)} %copy-done.17, bf16[768,1,768]{2,0,1:T(8,128)(2,1)S(1)} %copy-done.20, bf16[768,1,768]{2,0,1:T(8,128)(2,1)} %copy-done.21, bf16[768,1,768]{2,0,1:T(8,128)(2,1)} %copy-done.22), kind=kOutput, calls=%fused_computation.11 | convolution fusion | flops 3630956544 | bytes 11796480 | tf_op jit(solution)/shard_map/nvd,vdc->nc/dot_general | solution.py:111
  334.6 51.9 %collective-permute-done.2 = bf16[3,768,3,256]{1,3,2,0:T(8,128)(2,1)} collective-permute-done((bf16[3,768,3,256]{1,3,2,0:T(8,128)(2,1)}, bf16[3,768,3,256]{1,3,2,0:T(8,128)(2,1)}, u32[]{:S(2)}, u32[]{:S(2)}) %collective-permute-start.2) | collective-permute-done | bytes 3538976 | tf_op jit(solution)/shard_map/ppermute | solution.py:40
  386.5 6.4 %bitcast_add_fusion = f32[768,768]{1,0:T(8,128)} fusion(f32[768,768]{1,0:T(8,128)S(1)} %copy-done.25, f32[768,768,1]{1,0,2:T(8,128)S(1)} %fusion.7, bf16[3,768,768]{1,2,0:T(8,128)(2,1)} %bitcast.38, bf16[768,1,768]{2,0,1:T(8,128)(2,1)S(1)} %copy-done.11, bf16[768,1,768]{2,0,1:T(8,128)(2,1)S(1)} %copy-done.14, bf16[768,1,768]{2,0,1:T(8,128)(2,1)S(1)} %copy-done.8), kind=kOutput, calls=%fused_computation.18 | convolution fusion | flops 2722627584 | bytes 14155776 | tf_op jit(solution)/shard_map/nvd,vdc->nc/dot_general | solution.py:115
  392.9 2.9 reshape.423
  400.1 11.0 %fusion.13 = f32[3,256,3,1,128]{1,4,2,0,3:T(8,128)S(1)} fusion(bf16[6144,3,128]{0,2,1:T(8,128)(2,1)} %all-gather.8.cloned.1.call-done, bf16[3,256,6144]{2,1,0:T(8,128)(2,1)} %fusion.3), kind=kOutput, calls=%fused_computation.30 | convolution fusion | flops 3623878656 | bytes 15335424 | tf_op jit(solution)/shard_map/dot_general | solution.py:101
  412.1 14.0 %all_gather.35 = bf16[192,768]{1,0:T(8,128)(2,1)S(1)} all-gather(bf16[48,768]{1,0:T(8,128)(2,1)S(1)} %pad_maximum_fusion.6), channel_id=1, replica_groups=mesh['groups'=2,'video'=4,'tensor'=4] {'video'}, dimensions={0}, use_global_device_ids=true | all-gather | bytes 368640 | tf_op jit(solution)/shard_map/all_gather | solution.py:121
  426.1 4.5 convolution_convert_fusion
  431.8 24.8 %reduce-scatter.2.cloned.1.call-done = bf16[48,3,1024]{2,0,1:T(8,128)(2,1)} async-done(((bf16[192,3,1024]{2,0,1:T(8,128)(2,1)}), bf16[48,3,1024]{2,0,1:T(8,128)(2,1)}) %reduce-scatter.2.cloned.1.call-update) | async-done | bytes 294928 | tf_op jit(solution)/shard_map/reduce_scatter | solution.py:126
  456.5 3.7 collective-permute-start.3
  463.9 17.2 %collective-permute-done.3 = bf16[48,3,1024]{2,0,1:T(8,128)(2,1)S(1)} collective-permute-done((bf16[48,3,1024]{2,0,1:T(8,128)(2,1)}, bf16[48,3,1024]{2,0,1:T(8,128)(2,1)S(1)}, u32[]{:S(2)}, u32[]{:S(2)}) %collective-permute-start.3) | collective-permute-done | bytes 294944 | tf_op jit(solution)/shard_map/ppermute | solution.py:136
  481.0 6.7 %collective-permute-done.4 = bf16[48,3,1024]{2,0,1:T(8,128)(2,1)S(1)} collective-permute-done((bf16[48,3,1024]{2,0,1:T(8,128)(2,1)}, bf16[48,3,1024]{2,0,1:T(8,128)(2,1)S(1)}, u32[]{:S(2)}, u32[]{:S(2)}) %collective-permute-start.4) | collective-permute-done | bytes 294944 | tf_op jit(solution)/shard_map/ppermute | solution.py:136
  (192 shorter events, 70.6 us)
Async XLA Ops:
  6.5 55.0 %all-gather.10.cloned.1.call-start = ((), (), s32[]{:S(2)}) async-start(), calls=%async_computation.3 | async-start | bytes 2949120 | tf_op jit(solution)/shard_map/all_gather | solution.py:31
  11.4 142.2 %all-gather.12.cloned.1.call-start = ((), (), s32[]{:S(2)}) async-start(), calls=%async_computation.4 | async-start | bytes 5898240 | tf_op jit(solution)/shard_map/all_gather | solution.py:31
  66.1 4.3 copy-start.23
  66.2 187.1 %all-gather.14.cloned.1.call-start = ((), (), s32[]{:S(2)}) async-start(), calls=%async_computation.5 | async-start | bytes 5898240 | tf_op jit(solution)/shard_map/all_gather | solution.py:31
  88.1 119.2 %collective-permute-start = (bf16[3,768,3,128]{1,3,2,0:T(8,128)(2,1)}, bf16[3,768,3,128]{1,3,2,0:T(8,128)(2,1)}, u32[]{:S(2)}, u32[]{:S(2)}) collective-permute-start(bf16[3,768,3,128]{1,3,2,0:T(8,128)(2,1)} %pad_maximum_fusion.4), channel_id=1, source_target_pairs={{0,16},{16,0},{1,17},{17,1},{2,18},{18,2},{3,19},{19,3},{4,20},{20... | collective-permute-start | bytes 5308424 | tf_op jit(solution)/shard_map/ppermute | solution.py:40
  163.4 236.7 %all-gather.8.cloned.1.call-start = ((), (), s32[]{:S(2)}) async-start(), calls=%async_computation.1 | async-start | bytes 5898240 | tf_op jit(solution)/shard_map/all_gather | solution.py:75
  194.1 8.5 %copy-start = (bf16[3,256,6144]{2,1,0:T(8,128)(2,1)S(1)}, bf16[3,256,6144]{2,1,0:T(8,128)(2,1)}, u32[]{:S(2)}) copy-start(bf16[3,256,6144]{2,1,0:T(8,128)(2,1)} %fusion.3) | copy-start | bytes 28311556
  203.6 3.7 copy-start.15
  203.6 3.7 copy-start.18
  203.6 3.7 copy-start.21
  203.6 3.7 copy-start.22
  203.7 3.7 copy-start.6
  203.7 3.7 copy-start.9
  203.7 3.7 copy-start.12
  230.2 3.5 copy-start.3
  230.2 3.5 copy-start.4
  232.2 79.7 %collective-permute-start.1 = (bf16[3,768,3,256]{1,3,2,0:T(8,128)(2,1)}, bf16[3,768,3,256]{1,3,2,0:T(8,128)(2,1)}, u32[]{:S(2)}, u32[]{:S(2)}) collective-permute-start(bf16[3,768,3,256]{1,3,2,0:T(8,128)(2,1)} %pad_maximum_fusion.2), channel_id=1, source_target_pairs={{0,16},{16,0},{1,17},{17,1},{2,18},{18,2},{3,19},{19,3},{4,20},{20... | collective-permute-start | bytes 10616840 | tf_op jit(solution)/shard_map/ppermute | solution.py:40
  263.2 193.3 %reduce-scatter.2.cloned.1.call-start = ((), (), s32[]{:S(2)}) async-start(), calls=%async_computation.2 | async-start | bytes 1474560 | tf_op jit(solution)/shard_map/reduce_scatter | solution.py:126
  280.9 31.1 %copy-start.27 = (f32[768,768,1]{1,0,2:T(8,128)S(1)}, f32[768,768,1]{1,0,2:T(8,128)}, u32[]{:S(2)}) copy-start(f32[768,768,1]{1,0,2:T(8,128)} %fusion.9) | copy-start | bytes 7077892
  281.1 30.9 %copy-start.7 = (bf16[768,1,768]{2,0,1:T(8,128)(2,1)S(1)}, bf16[768,1,768]{2,0,1:T(8,128)(2,1)}, u32[]{:S(2)}) copy-start(bf16[768,1,768]{2,0,1:T(8,128)(2,1)} %copy-done.6) | copy-start | bytes 3538948
  281.1 30.9 %copy-start.10 = (bf16[768,1,768]{2,0,1:T(8,128)(2,1)S(1)}, bf16[768,1,768]{2,0,1:T(8,128)(2,1)}, u32[]{:S(2)}) copy-start(bf16[768,1,768]{2,0,1:T(8,128)(2,1)} %copy-done.9) | copy-start | bytes 3538948
  281.1 30.9 %copy-start.13 = (bf16[768,1,768]{2,0,1:T(8,128)(2,1)S(1)}, bf16[768,1,768]{2,0,1:T(8,128)(2,1)}, u32[]{:S(2)}) copy-start(bf16[768,1,768]{2,0,1:T(8,128)(2,1)} %copy-done.12) | copy-start | bytes 3538948
  281.1 30.9 %copy-start.26 = (f32[768,768]{1,0:T(8,128)S(1)}, f32[768,768]{1,0:T(8,128)}, u32[]{:S(2)}) copy-start(f32[768,768]{1,0:T(8,128)} %fusion.31) | copy-start | bytes 7077892
  283.3 103.2 %collective-permute-start.2 = (bf16[3,768,3,256]{1,3,2,0:T(8,128)(2,1)}, bf16[3,768,3,256]{1,3,2,0:T(8,128)(2,1)}, u32[]{:S(2)}, u32[]{:S(2)}) collective-permute-start(bf16[3,768,3,256]{1,3,2,0:T(8,128)(2,1)} %pad_maximum_fusion.3), channel_id=1, source_target_pairs={{0,16},{16,0},{1,17},{17,1},{2,18},{18,2},{3,19},{19,3},{4,20},{20... | collective-permute-start | bytes 10616840 | tf_op jit(solution)/shard_map/ppermute | solution.py:40
  327.5 59.0 %copy-start.8 = (bf16[768,1,768]{2,0,1:T(8,128)(2,1)S(1)}, bf16[768,1,768]{2,0,1:T(8,128)(2,1)}, u32[]{:S(2)}) copy-start(bf16[768,1,768]{2,0,1:T(8,128)(2,1)} %copy-done.6) | copy-start | bytes 3538948
  327.5 59.0 %copy-start.11 = (bf16[768,1,768]{2,0,1:T(8,128)(2,1)S(1)}, bf16[768,1,768]{2,0,1:T(8,128)(2,1)}, u32[]{:S(2)}) copy-start(bf16[768,1,768]{2,0,1:T(8,128)(2,1)} %copy-done.9) | copy-start | bytes 3538948
  327.5 59.0 %copy-start.14 = (bf16[768,1,768]{2,0,1:T(8,128)(2,1)S(1)}, bf16[768,1,768]{2,0,1:T(8,128)(2,1)}, u32[]{:S(2)}) copy-start(bf16[768,1,768]{2,0,1:T(8,128)(2,1)} %copy-done.12) | copy-start | bytes 3538948
  327.5 59.0 %copy-start.25 = (f32[768,768]{1,0:T(8,128)S(1)}, f32[768,768]{1,0:T(8,128)}, u32[]{:S(2)}) copy-start(f32[768,768]{1,0:T(8,128)} %fusion.29) | copy-start | bytes 7077892
  456.5 24.5 %collective-permute-start.3 = (bf16[48,3,1024]{2,0,1:T(8,128)(2,1)}, bf16[48,3,1024]{2,0,1:T(8,128)(2,1)S(1)}, u32[]{:S(2)}, u32[]{:S(2)}) collective-permute-start(bf16[48,3,1024]{2,0,1:T(8,128)(2,1)} %reduce-scatter.2.cloned.1.call-done), channel_id=1, source_target_pairs={{0,0},{1,4},{2,8},{3,12},{4,1},{5,5},{6,9},{7,13},{8,2},{9,6},{10,... | collective-permute-start | bytes 884744 | tf_op jit(solution)/shard_map/ppermute | solution.py:136
  460.3 27.5 %collective-permute-start.4 = (bf16[48,3,1024]{2,0,1:T(8,128)(2,1)}, bf16[48,3,1024]{2,0,1:T(8,128)(2,1)S(1)}, u32[]{:S(2)}, u32[]{:S(2)}) collective-permute-start(bf16[48,3,1024]{2,0,1:T(8,128)(2,1)} %reduce-scatter.2.cloned.1.call-done), channel_id=1, source_target_pairs={{0,4},{1,8},{2,12},{3,0},{4,5},{5,9},{6,13},{7,1},{8,6},{9,10},{10... | collective-permute-start | bytes 884744 | tf_op jit(solution)/shard_map/ppermute | solution.py:136
  461.5 27.4 %collective-permute-start.5 = (bf16[48,3,1024]{2,0,1:T(8,128)(2,1)}, bf16[48,3,1024]{2,0,1:T(8,128)(2,1)S(1)}, u32[]{:S(2)}, u32[]{:S(2)}) collective-permute-start(bf16[48,3,1024]{2,0,1:T(8,128)(2,1)} %reduce-scatter.2.cloned.1.call-done), channel_id=1, source_target_pairs={{0,8},{1,12},{2,0},{3,4},{4,9},{5,13},{6,1},{7,5},{8,10},{9,14},{1... | collective-permute-start | bytes 884744 | tf_op jit(solution)/shard_map/ppermute | solution.py:136
  462.3 28.0 %collective-permute-start.6 = (bf16[48,3,1024]{2,0,1:T(8,128)(2,1)}, bf16[48,3,1024]{2,0,1:T(8,128)(2,1)S(1)}, u32[]{:S(2)}, u32[]{:S(2)}) collective-permute-start(bf16[48,3,1024]{2,0,1:T(8,128)(2,1)} %reduce-scatter.2.cloned.1.call-done), channel_id=1, source_target_pairs={{0,12},{1,0},{2,4},{3,8},{4,13},{5,1},{6,5},{7,9},{8,14},{9,2},{10... | collective-permute-start | bytes 884744 | tf_op jit(solution)/shard_map/ppermute | solution.py:136
  (8 other events, 22.0 us)
Sparse Core Ops, SparseCore 0:
  11.5 50.0 all-gather.9
  66.3 87.3 all-gather.11
  163.5 87.9 all-gather.13
  263.3 87.1 all-gather.7
  430.7 25.7 reduce-scatter.1

commit v8 on v7

--- a/solution.py
+++ b/solution.py
@@ -67,17 +67,24 @@
     sizes = head_chunks(heads_local)
     moved = []
     first = 0
-    for size in sizes:
+    for index, size in enumerate(sizes):
         chunk = qkv_weight[:, :, first * HD:(first + size) * HD]
         first += size
-        if len(moved) == len(sizes) - 1 and len(sizes) > 2:
-            whole_rows, moved[-1][1] = lax.optimization_barrier((chunk, moved[-1][1]))
-            step = [lax.all_gather(whole_rows, "video", axis=0, tiled=True), None, None]
-        elif moved:
-            step, moved[-1][1] = moved_weights(chunk, n_video, after=moved[-1][1])
+        after = None
+        if index >= 1:
+            after = [moved[index - 1][1]]
+            if index >= 2 and moved[index - 2][3] is not None:
+                after.append(moved[index - 2][3])
+        if index == len(sizes) - 1 and len(sizes) > 2:
+            whole_rows, after = lax.optimization_barrier((chunk, after))
+            step = [lax.all_gather(whole_rows, "video", axis=0, tiled=True), None, None, None]
         else:
-            step, _ = moved_weights(chunk, n_video)
+            step, after = moved_weights(chunk, n_video, after=after)
             step.append(forward(step[2]))
+        if after is not None:
+            moved[index - 1][1] = after[0]
+            if len(after) > 1:
+                moved[index - 2][3] = after[1]
         moved.append(step)
     wide = frames.astype(jnp.float32)
     center = wide - jnp.mean(wide, axis=-1, keepdims=True)
@@ -101,12 +108,9 @@
             proj = jnp.dot(normed, full, preferred_element_type=jnp.float32)
             pooled_parts.append(attend(proj, nframes, size, scale, blocks, inner))
             continue
-        other, gathered, onward = moved[index][:3]
+        other, gathered, onward, received = moved[index]
         if index == 0:
-            received = moved[index][3]
             video_all, received = lax.optimization_barrier((video_all, received))
-        else:
-            received = forward(onward)
         proj = jnp.dot(own_piece, other.reshape(half, width), preferred_element_type=jnp.float32)
         proj = proj + jnp.einsum(
             "nvd,vdc->nc", own_half, gathered.reshape(n_video, half, width),

time: 505 us -> 506 us (level)
  other arithmetic: 37.6 us -> 29.6 us
  waiting for transfers between devices: 239 us -> 245 us
    all_gather x3, waiting for transfers between devices: 108 us -> 115 us  [moved_weights(): gathered = lax.all_gather(mine, 'video', axis=0, tiled=False)]
    unnamed x83 -> x89, local copies, waits for them, and re-layouts: 16.5 us -> 18.8 us
  transfers between devices with their start and end apart: 12 -> 12, of which waited for: 9 -> 10; matrix products, arithmetic and copies ran while one was open for 36% -> 34% of each run, Pallas kernels for 0% -> 0%
where the time goes in v8:
time: 506 us; the launch traced here: 502 us
  waiting for transfers between devices  245 us (48%)
  local copies, waits for them, and re-layouts  108 us (21%)
  matrix products  68.3 us (13%)
  other arithmetic  29.6 us (6%)
  blocking collectives  23 us (5%)
  between operations  15 us (3%)
  starting transfers between devices  12 us (2%)
    all_gather x3, waiting for transfers between devices, moved_weights(): gathered = lax.all_gather(mine, 'video', axis=0, tiled=False)  115 us
    ppermute x3, waiting for transfers between devices, forward(): return lax.ppermute(onward, 'groups', [(0, 1), (1, 0)])  79.5 us
    dynamic_slice x3, local copies, waits for them, and re-layouts, moved_weights(): lax.dynamic_index_in_dim(gathered, (v + 1 + i) % n_video, axis=0, keepdim...  33.7 us
    ppermute x4, waiting for transfers between devices, per_device(): got = lax.ppermute(clip_rows, ('video', 'tensor'), pairs)  26.5 us
    reduce_scatter x1, waiting for transfers between devices, per_device(): lax.psum_scatter(partial_proj.astype(jnp.bfloat16), 'tensor', scatter_dim...  24.8 us
    all_gather x3, local copies, waits for them, and re-layouts, moved_weights(): gathered = lax.all_gather(mine, 'video', axis=0, tiled=False)  24 us
    unnamed x89, local copies, waits for them, and re-layouts  18.8 us
    dot_general x3, matrix products, per_device(): jnp.einsum('nvd,vdc->nc', own_half, gathered.reshape(n_video, half, width...  18 us
  transfers between devices with their start and end apart: 12, of which 10 were waited for; matrix products, arithmetic and copies ran while one was open for 34% of the time, Pallas kernels for 0%

profile of v8, /device:TPU:10, one launch (start us, length us, event | category | flops | bytes accessed | tf_op | source)
XLA Modules:
  0.0 501.6 jit_solution(16537313577888512071)
XLA Ops:
  6.5 2.8 fusion.73
  17.6 44.0 %all-gather.10.cloned.1.call-done = bf16[3072,3,128]{0,2,1:T(8,128)(2,1)} async-done(((bf16[768,3,128]{0,2,1:T(8,128)(2,1)}), bf16[3072,3,128]{0,2,1:T(8,128)(2,1)}) %all-gather.10.cloned.1.call-update) | async-done | bytes 2359312 | tf_op jit(solution)/shard_map/all_gather | solution.py:31
  61.6 4.5 reshape.437
  67.7 8.1 %all-reduce = s32[12]{0:T(128)S(1)} all-reduce(s32[12]{0:T(128)S(1)} %dynamic-update-slice), channel_id=1, replica_groups=mesh['groups'=2,'video'=4,'tensor'=4] {'video'}, use_global_device_ids=true, to_apply=%add | all-reduce | flops 12 | bytes 96 | tf_op jit(solution)/shard_map/optimization_barrier | solution.py:113
  86.7 3.8 constant_dynamic-slice_fusion.10
  97.7 56.0 %all-gather.12.cloned.1.call-done = bf16[3072,3,256]{0,2,1:T(8,128)(2,1)} async-done(((bf16[768,3,256]{0,2,1:T(8,128)(2,1)}), bf16[3072,3,256]{0,2,1:T(8,128)(2,1)}) %all-gather.12.cloned.1.call-update) | async-done | bytes 4718608 | tf_op jit(solution)/shard_map/all_gather | solution.py:31
  153.7 9.7 %reshape.438 = bf16[4,768,3,256]{1,0,3,2:T(4,128)(2,1)} reshape(bf16[3072,3,256]{0,2,1:T(8,128)(2,1)} %all-gather.12.cloned.1.call-done) | data formatting | bytes 9437184 | tf_op jit(solution)/shard_map/all_gather | solution.py:31
  163.7 12.4 %fusion.3 = bf16[3,256,6144]{2,1,0:T(8,128)(2,1)} fusion(bf16[3,256,6144]{2,1,0:T(8,128)(2,1)} %param.4, f32[3,256]{1,0:T(4,128)S(1)} %add_rsqrt_fusion.10, f32[3,256]{1,0:T(4,128)S(1)} %broadcast_multiply_fusion), kind=kLoop, calls=%fused_computation.6 | loop fusion | flops 18874368 | bytes 18880512 | tf_op jit(solution)/shard_map/convert_element_type | solution.py:92
  176.1 4.3 fusion.31
  180.4 4.2 fusion.29
  184.6 3.3 dynamic-slice_bitcast_fusion.2
  187.9 14.9 %constant_dynamic-slice_fusion.6 = (bf16[1,768,3,256]{1,0,3,2:T(2,128)(2,1)}, bf16[1,768,3,256]{1,0,3,2:T(2,128)(2,1)}, bf16[1,768,3,256]{1,0,3,2:T(2,128)(2,1)}) fusion(bf16[4,768,3,256]{1,0,3,2:T(4,128)(2,1)} %reshape.438, s32[]{:T(128)S(6)} %select_n.148, s32[]{:T(128)S(6)} %select_n.149, s32[]{:T(128)S(6)} %select_n.150), kind=kLoop, calls=%fused_computation.142 | loop fusion | bytes 7077900 | tf_op jit(solution)/shard_map/jit(dynamic_index_in_dim)/dynamic_slice | solution.py:33
  213.4 3.6 convolution_bitcast_fusion
  221.4 3.3 multiply_reduce_fusion.8
  228.6 8.3 %fusion.9 = f32[768,768,1]{1,0,2:T(8,128)} fusion(bf16[4,768,768]{1,0,2:T(4,128)(2,1)} %bitcast.210, bf16[768,1,768]{2,0,1:T(8,128)(2,1)S(1)} %copy-done.16, bf16[768,1,768]{2,0,1:T(8,128)(2,1)S(1)} %copy-done.19, bf16[768,1,768]{2,0,1:T(8,128)(2,1)} %get-tuple-element.38, bf16[768,1,768]{2,0,1:T(8,128)(2,1)} %get-tuple-element.39), kind=kOutput, calls=%fused_computation.13 | convolution fusion | flops 3630956544 | bytes 11796480 | tf_op jit(solution)/shard_map/nvd,vdc->nc/dot_general | solution.py:115
  236.9 14.5 %all-gather.14.cloned.1.call-done = bf16[3072,3,256]{0,2,1:T(8,128)(2,1)} async-done(((bf16[768,3,256]{0,2,1:T(8,128)(2,1)}), bf16[3072,3,256]{0,2,1:T(8,128)(2,1)}) %all-gather.14.cloned.1.call-update) | async-done | bytes 4718608 | tf_op jit(solution)/shard_map/all_gather | solution.py:31
  251.4 9.7 %reshape.439 = bf16[4,768,3,256]{1,0,3,2:T(4,128)(2,1)} reshape(bf16[3072,3,256]{0,2,1:T(8,128)(2,1)} %all-gather.14.cloned.1.call-done) | data formatting | bytes 9437184 | tf_op jit(solution)/shard_map/all_gather | solution.py:31
  261.2 26.6 %collective-permute-done.1 = bf16[3,768,3,256]{1,3,2,0:T(8,128)(2,1)} collective-permute-done((bf16[3,768,3,256]{1,3,2,0:T(8,128)(2,1)}, bf16[3,768,3,256]{1,3,2,0:T(8,128)(2,1)}, u32[]{:S(2)}, u32[]{:S(2)}) %collective-permute-start.1) | collective-permute-done | bytes 3538976 | tf_op jit(solution)/shard_map/ppermute | solution.py:40
  288.0 15.0 %constant_dynamic-slice_fusion.2 = (bf16[1,768,3,256]{1,0,3,2:T(2,128)(2,1)}, bf16[1,768,3,256]{1,0,3,2:T(2,128)(2,1)}, bf16[1,768,3,256]{1,0,3,2:T(2,128)(2,1)S(1)}) fusion(bf16[4,768,3,256]{1,0,3,2:T(4,128)(2,1)} %reshape.439, s32[]{:T(128)S(6)} %select_n.148, s32[]{:T(128)S(6)} %select_n.149, s32[]{:T(128)S(6)} %select_n.150), kind=kLoop, calls=%fused_computation.138 | loop fusion | bytes 7077900 | tf_op jit(solution)/shard_map/jit(dynamic_index_in_dim)/dynamic_slice | solution.py:33
  310.4 6.4 %bitcast_add_fusion.2 = f32[768,768]{1,0:T(8,128)} fusion(f32[768,768]{1,0:T(8,128)S(1)} %copy-done.26, f32[768,768,1]{1,0,2:T(8,128)S(1)} %copy-done.27, bf16[3,768,768]{1,2,0:T(8,128)(2,1)} %bitcast.28, bf16[768,1,768]{2,0,1:T(8,128)(2,1)S(1)} %copy-done.10, bf16[768,1,768]{2,0,1:T(8,128)(2,1)S(1)} %copy-done.13, bf16[768,1,768]{2,0,1:T(8,128)(2,1)S(1)} %copy-done.7), kind=kOutput, calls=%fused_computation.20 | convolution fusion | flops 2722627584 | bytes 14155776 | tf_op jit(solution)/shard_map/nvd,vdc->nc/dot_general | solution.py:119
  316.8 2.9 reshape.418
  325.9 7.1 %fusion.7 = f32[768,768,1]{1,0,2:T(8,128)S(1)} fusion(bf16[4,768,768]{1,0,2:T(4,128)(2,1)} %bitcast.211, bf16[768,1,768]{2,0,1:T(8,128)(2,1)S(1)} %copy-done.17, bf16[768,1,768]{2,0,1:T(8,128)(2,1)S(1)} %copy-done.20, bf16[768,1,768]{2,0,1:T(8,128)(2,1)} %get-tuple-element.38, bf16[768,1,768]{2,0,1:T(8,128)(2,1)} %get-tuple-element.39), kind=kOutput, calls=%fused_computation.11 | convolution fusion | flops 3630956544 | bytes 11796480 | tf_op jit(solution)/shard_map/nvd,vdc->nc/dot_general | solution.py:115
  333.0 52.9 %collective-permute-done.2 = bf16[3,768,3,256]{1,3,2,0:T(8,128)(2,1)} collective-permute-done((bf16[3,768,3,256]{1,3,2,0:T(8,128)(2,1)}, bf16[3,768,3,256]{1,3,2,0:T(8,128)(2,1)}, u32[]{:S(2)}, u32[]{:S(2)}) %collective-permute-start.2) | collective-permute-done | bytes 3538976 | tf_op jit(solution)/shard_map/ppermute | solution.py:40
  385.9 6.4 %bitcast_add_fusion = f32[768,768]{1,0:T(8,128)} fusion(f32[768,768]{1,0:T(8,128)S(1)} %copy-done.25, f32[768,768,1]{1,0,2:T(8,128)S(1)} %fusion.7, bf16[3,768,768]{1,2,0:T(8,128)(2,1)} %bitcast.38, bf16[768,1,768]{2,0,1:T(8,128)(2,1)S(1)} %copy-done.11, bf16[768,1,768]{2,0,1:T(8,128)(2,1)S(1)} %copy-done.14, bf16[768,1,768]{2,0,1:T(8,128)(2,1)S(1)} %copy-done.8), kind=kOutput, calls=%fused_computation.18 | convolution fusion | flops 2722627584 | bytes 14155776 | tf_op jit(solution)/shard_map/nvd,vdc->nc/dot_general | solution.py:119
  392.3 2.9 reshape.423
  399.5 11.0 %fusion.13 = f32[3,256,3,1,128]{1,4,2,0,3:T(8,128)S(1)} fusion(bf16[6144,3,128]{0,2,1:T(8,128)(2,1)} %all-gather.8.cloned.1.call-done, bf16[3,256,6144]{2,1,0:T(8,128)(2,1)} %fusion.3), kind=kOutput, calls=%fused_computation.30 | convolution fusion | flops 3623878656 | bytes 15335424 | tf_op jit(solution)/shard_map/dot_general | solution.py:108
  411.5 14.8 %all_gather.35 = bf16[192,768]{1,0:T(8,128)(2,1)S(1)} all-gather(bf16[48,768]{1,0:T(8,128)(2,1)S(1)} %pad_maximum_fusion.6), channel_id=1, replica_groups=mesh['groups'=2,'video'=4,'tensor'=4] {'video'}, dimensions={0}, use_global_device_ids=true | all-gather | bytes 368640 | tf_op jit(solution)/shard_map/all_gather | solution.py:125
  426.3 4.5 convolution_convert_fusion
  432.0 24.8 %reduce-scatter.2.cloned.1.call-done = bf16[48,3,1024]{2,0,1:T(8,128)(2,1)} async-done(((bf16[192,3,1024]{2,0,1:T(8,128)(2,1)}), bf16[48,3,1024]{2,0,1:T(8,128)(2,1)}) %reduce-scatter.2.cloned.1.call-update) | async-done | bytes 294928 | tf_op jit(solution)/shard_map/reduce_scatter | solution.py:130
  456.8 3.7 collective-permute-start.3
  464.1 17.1 %collective-permute-done.3 = bf16[48,3,1024]{2,0,1:T(8,128)(2,1)S(1)} collective-permute-done((bf16[48,3,1024]{2,0,1:T(8,128)(2,1)}, bf16[48,3,1024]{2,0,1:T(8,128)(2,1)S(1)}, u32[]{:S(2)}, u32[]{:S(2)}) %collective-permute-start.3) | collective-permute-done | bytes 294944 | tf_op jit(solution)/shard_map/ppermute | solution.py:140
  481.2 6.8 %collective-permute-done.4 = bf16[48,3,1024]{2,0,1:T(8,128)(2,1)S(1)} collective-permute-done((bf16[48,3,1024]{2,0,1:T(8,128)(2,1)}, bf16[48,3,1024]{2,0,1:T(8,128)(2,1)S(1)}, u32[]{:S(2)}, u32[]{:S(2)}) %collective-permute-start.4) | collective-permute-done | bytes 294944 | tf_op jit(solution)/shard_map/ppermute | solution.py:140
  (199 shorter events, 75.9 us)
Async XLA Ops:
  6.5 55.1 %all-gather.10.cloned.1.call-start = ((), (), s32[]{:S(2)}) async-start(), calls=%async_computation.3 | async-start | bytes 2949120 | tf_op jit(solution)/shard_map/all_gather | solution.py:31
  11.4 142.3 %all-gather.12.cloned.1.call-start = ((), (), s32[]{:S(2)}) async-start(), calls=%async_computation.4 | async-start | bytes 5898240 | tf_op jit(solution)/shard_map/all_gather | solution.py:31
  17.6 48.7 %copy-start.24 = (u32[32]{0:T(128)S(1)}, u32[32]{0:T(128)}, u32[]{:S(2)}) copy-start(u32[32]{0:T(128)} %constant.194) | copy-start | bytes 388
  17.6 49.9 %copy-start.23 = (s32[3]{0:T(128)S(1)}, s32[3]{0:T(128)}, u32[]{:S(2)}) copy-start(s32[3]{0:T(128)} %param.5) | copy-start | bytes 40
  66.1 12.2 %copy-start.4 = (bf16[768,3,128]{2,0,1:T(8,128)(2,1)S(1)}, bf16[768,3,128]{2,0,1:T(8,128)(2,1)}, u32[]{:S(2)}) copy-start(bf16[768,3,128]{2,0,1:T(8,128)(2,1)} %get-tuple-element.63) | copy-start | bytes 1769476
  66.2 185.3 %all-gather.14.cloned.1.call-start = ((), (), s32[]{:S(2)}) async-start(), calls=%async_computation.5 | async-start | bytes 5898240 | tf_op jit(solution)/shard_map/all_gather | solution.py:31
  79.4 14.3 %slice-start = ((s8[9437184]{0:T(1024)(128)(4,1)}), s8[1048576]{0:T(1024)(128)(4,1)S(1)}, s32[]{:S(2)}) async-start(s8[9437184]{0:T(1024)(128)(4,1)} %bitcast.204), calls=%async_computation.6 | async-start | bytes 2097152
  86.7 7.0 %slice-start.1 = ((s8[9437184]{0:T(1024)(128)(4,1)}), s8[4194304]{0:T(1024)(128)(4,1)S(1)}, s32[]{:S(2)}) async-start(s8[9437184]{0:T(1024)(128)(4,1)} %bitcast.204), calls=%async_computation.7 | async-start | bytes 8388608
  92.2 71.2 %collective-permute-start = (bf16[3,768,3,128]{1,3,2,0:T(8,128)(2,1)}, bf16[3,768,3,128]{1,3,2,0:T(8,128)(2,1)}, u32[]{:S(2)}, u32[]{:S(2)}) collective-permute-start(bf16[3,768,3,128]{1,3,2,0:T(8,128)(2,1)} %pad_maximum_fusion.4), channel_id=1, source_target_pairs={{0,16},{16,0},{1,17},{17,1},{2,18},{18,2},{3,19},{19,3},{4,20},{20... | collective-permute-start | bytes 5308424 | tf_op jit(solution)/shard_map/ppermute | solution.py:40
  163.5 236.0 %all-gather.8.cloned.1.call-start = ((), (), s32[]{:S(2)}) async-start(), calls=%async_computation.1 | async-start | bytes 5898240 | tf_op jit(solution)/shard_map/all_gather | solution.py:80
  176.1 8.5 %copy-start = (bf16[3,256,6144]{2,1,0:T(8,128)(2,1)S(1)}, bf16[3,256,6144]{2,1,0:T(8,128)(2,1)}, u32[]{:S(2)}) copy-start(bf16[3,256,6144]{2,1,0:T(8,128)(2,1)} %fusion.3) | copy-start | bytes 28311556
  207.0 3.6 copy-start.15
  207.1 3.5 copy-start.18
  207.1 3.5 copy-start.21
  207.1 3.6 copy-start.22
  209.1 78.7 %collective-permute-start.1 = (bf16[3,768,3,256]{1,3,2,0:T(8,128)(2,1)}, bf16[3,768,3,256]{1,3,2,0:T(8,128)(2,1)}, u32[]{:S(2)}, u32[]{:S(2)}) collective-permute-start(bf16[3,768,3,256]{1,3,2,0:T(8,128)(2,1)} %pad_maximum_fusion.2), channel_id=1, source_target_pairs={{0,16},{16,0},{1,17},{17,1},{2,18},{18,2},{3,19},{19,3},{4,20},{20... | collective-permute-start | bytes 10616840 | tf_op jit(solution)/shard_map/ppermute | solution.py:40
  213.3 3.6 copy-start.5
  287.8 168.9 %reduce-scatter.2.cloned.1.call-start = ((), (), s32[]{:S(2)}) async-start(), calls=%async_computation.2 | async-start | bytes 1474560 | tf_op jit(solution)/shard_map/reduce_scatter | solution.py:130
  305.6 4.0 copy-start.27
  305.8 3.8 copy-start.7
  305.8 3.8 copy-start.10
  305.8 3.8 copy-start.13
  305.8 4.6 copy-start.26
  308.1 77.8 %collective-permute-start.2 = (bf16[3,768,3,256]{1,3,2,0:T(8,128)(2,1)}, bf16[3,768,3,256]{1,3,2,0:T(8,128)(2,1)}, u32[]{:S(2)}, u32[]{:S(2)}) collective-permute-start(bf16[3,768,3,256]{1,3,2,0:T(8,128)(2,1)} %pad_maximum_fusion.3), channel_id=1, source_target_pairs={{0,16},{16,0},{1,17},{17,1},{2,18},{18,2},{3,19},{19,3},{4,20},{20... | collective-permute-start | bytes 10616840 | tf_op jit(solution)/shard_map/ppermute | solution.py:40
  325.9 60.0 %copy-start.8 = (bf16[768,1,768]{2,0,1:T(8,128)(2,1)S(1)}, bf16[768,1,768]{2,0,1:T(8,128)(2,1)}, u32[]{:S(2)}) copy-start(bf16[768,1,768]{2,0,1:T(8,128)(2,1)} %get-tuple-element.33) | copy-start | bytes 3538948
  325.9 60.0 %copy-start.11 = (bf16[768,1,768]{2,0,1:T(8,128)(2,1)S(1)}, bf16[768,1,768]{2,0,1:T(8,128)(2,1)}, u32[]{:S(2)}) copy-start(bf16[768,1,768]{2,0,1:T(8,128)(2,1)} %get-tuple-element.34) | copy-start | bytes 3538948
  325.9 60.0 %copy-start.14 = (bf16[768,1,768]{2,0,1:T(8,128)(2,1)S(1)}, bf16[768,1,768]{2,0,1:T(8,128)(2,1)}, u32[]{:S(2)}) copy-start(bf16[768,1,768]{2,0,1:T(8,128)(2,1)} %get-tuple-element.35) | copy-start | bytes 3538948
  325.9 60.0 %copy-start.25 = (f32[768,768]{1,0:T(8,128)S(1)}, f32[768,768]{1,0:T(8,128)}, u32[]{:S(2)}) copy-start(f32[768,768]{1,0:T(8,128)} %fusion.29) | copy-start | bytes 7077892
  456.8 24.5 %collective-permute-start.3 = (bf16[48,3,1024]{2,0,1:T(8,128)(2,1)}, bf16[48,3,1024]{2,0,1:T(8,128)(2,1)S(1)}, u32[]{:S(2)}, u32[]{:S(2)}) collective-permute-start(bf16[48,3,1024]{2,0,1:T(8,128)(2,1)} %reduce-scatter.2.cloned.1.call-done), channel_id=1, source_target_pairs={{0,0},{1,4},{2,8},{3,12},{4,1},{5,5},{6,9},{7,13},{8,2},{9,6},{10,... | collective-permute-start | bytes 884744 | tf_op jit(solution)/shard_map/ppermute | solution.py:140
  460.5 27.5 %collective-permute-start.4 = (bf16[48,3,1024]{2,0,1:T(8,128)(2,1)}, bf16[48,3,1024]{2,0,1:T(8,128)(2,1)S(1)}, u32[]{:S(2)}, u32[]{:S(2)}) collective-permute-start(bf16[48,3,1024]{2,0,1:T(8,128)(2,1)} %reduce-scatter.2.cloned.1.call-done), channel_id=1, source_target_pairs={{0,4},{1,8},{2,12},{3,0},{4,5},{5,9},{6,13},{7,1},{8,6},{9,10},{10... | collective-permute-start | bytes 884744 | tf_op jit(solution)/shard_map/ppermute | solution.py:140
  461.7 27.3 %collective-permute-start.5 = (bf16[48,3,1024]{2,0,1:T(8,128)(2,1)}, bf16[48,3,1024]{2,0,1:T(8,128)(2,1)S(1)}, u32[]{:S(2)}, u32[]{:S(2)}) collective-permute-start(bf16[48,3,1024]{2,0,1:T(8,128)(2,1)} %reduce-scatter.2.cloned.1.call-done), channel_id=1, source_target_pairs={{0,8},{1,12},{2,0},{3,4},{4,9},{5,13},{6,1},{7,5},{8,10},{9,14},{1... | collective-permute-start | bytes 884744 | tf_op jit(solution)/shard_map/ppermute | solution.py:140
  462.6 28.0 %collective-permute-start.6 = (bf16[48,3,1024]{2,0,1:T(8,128)(2,1)}, bf16[48,3,1024]{2,0,1:T(8,128)(2,1)S(1)}, u32[]{:S(2)}, u32[]{:S(2)}) collective-permute-start(bf16[48,3,1024]{2,0,1:T(8,128)(2,1)} %reduce-scatter.2.cloned.1.call-done), channel_id=1, source_target_pairs={{0,12},{1,0},{2,4},{3,8},{4,13},{5,1},{6,5},{7,9},{8,14},{9,2},{10... | collective-permute-start | bytes 884744 | tf_op jit(solution)/shard_map/ppermute | solution.py:140
  (11 other events, 28.1 us)
Sparse Core Ops, SparseCore 0:
  11.6 50.0 all-gather.9
  66.3 87.3 all-gather.11
  163.6 87.8 all-gather.13
  287.9 87.9 all-gather.7
  431.0 25.7 reduce-scatter.1

commit v9 on v7

--- a/solution.py
+++ b/solution.py
@@ -16,7 +16,7 @@
 
 def head_chunks(heads):
     if heads >= 4 and heads % 2 == 0:
-        return [1] + [2] * ((heads - 2) // 2) + [1]
+        return [2] * ((heads - 2) // 2) + [1, 1]
     return [1] * heads
 
 

time: 505 us -> 514 us (1.018)
  waiting for transfers between devices: 239 us -> 245 us
    ppermute x3, waiting for transfers between devices: 79.5 us -> 104 us  [forward(): return lax.ppermute(onward, 'groups', [(0, 1), (1, 0)])]
    all_gather x3, waiting for transfers between devices: 108 us -> 88.7 us  [moved_weights(): gathered = lax.all_gather(mine, 'video', axis=0, tiled=False)]
  transfers between devices with their start and end apart: 12 -> 12, of which waited for: 9 -> 10; matrix products, arithmetic and copies ran while one was open for 36% -> 32% of each run, Pallas kernels for 0% -> 0%
where the time goes in v9:
time: 514 us; the launch traced here: 509 us
  waiting for transfers between devices  245 us (48%)
  local copies, waits for them, and re-layouts  108 us (21%)
  matrix products  71 us (14%)
  other arithmetic  35.7 us (7%)
  blocking collectives  23 us (4%)
  between operations  15.1 us (3%)
  starting transfers between devices  11.7 us (2%)
    ppermute x3, waiting for transfers between devices, forward(): return lax.ppermute(onward, 'groups', [(0, 1), (1, 0)])  104 us
    all_gather x3, waiting for transfers between devices, moved_weights(): gathered = lax.all_gather(mine, 'video', axis=0, tiled=False)  88.7 us
    dynamic_slice x3, local copies, waits for them, and re-layouts, moved_weights(): lax.dynamic_index_in_dim(gathered, (v + 1 + i) % n_video, axis=0, keepdim...  33.9 us
    ppermute x4, waiting for transfers between devices, per_device(): got = lax.ppermute(clip_rows, ('video', 'tensor'), pairs)  26.4 us
    reduce_scatter x1, waiting for transfers between devices, per_device(): lax.psum_scatter(partial_proj.astype(jnp.bfloat16), 'tensor', scatter_dim...  24.8 us
    all_gather x3, local copies, waits for them, and re-layouts, moved_weights(): gathered = lax.all_gather(mine, 'video', axis=0, tiled=False)  24.4 us
    dot_general x3, matrix products, per_device(): jnp.einsum('nvd,vdc->nc', own_half, gathered.reshape(n_video, half, width...  19.7 us
    unnamed x83, local copies, waits for them, and re-layouts  16.5 us
  transfers between devices with their start and end apart: 12, of which 10 were waited for; matrix products, arithmetic and copies ran while one was open for 32% of the time, Pallas kernels for 0%

profile of v9, /device:TPU:10, one launch (start us, length us, event | category | flops | bytes accessed | tf_op | source)
XLA Modules:
  0.0 509.4 jit_solution(2828748778705726383)
XLA Ops:
  6.5 4.1 fusion.73
  18.2 8.4 %all-reduce = s32[12]{0:T(128)S(1)} all-reduce(s32[12]{0:T(128)S(1)} %dynamic-update-slice), channel_id=1, replica_groups=mesh['groups'=2,'video'=4,'tensor'=4] {'video'}, use_global_device_ids=true, to_apply=%add | all-reduce | flops 12 | bytes 96 | tf_op jit(solution)/shard_map/optimization_barrier | solution.py:107
  29.7 75.2 %all-gather.10.cloned.1.call-done = bf16[3072,3,256]{0,2,1:T(8,128)(2,1)} async-done(((bf16[768,3,256]{0,2,1:T(8,128)(2,1)}), bf16[3072,3,256]{0,2,1:T(8,128)(2,1)}) %all-gather.10.cloned.1.call-update) | async-done | bytes 4718608 | tf_op jit(solution)/shard_map/all_gather | solution.py:31
  104.9 9.7 %reshape.437 = bf16[4,768,3,256]{1,0,3,2:T(4,128)(2,1)} reshape(bf16[3072,3,256]{0,2,1:T(8,128)(2,1)} %all-gather.10.cloned.1.call-done) | data formatting | bytes 9437184 | tf_op jit(solution)/shard_map/all_gather | solution.py:31
  124.0 5.6 %convert_reduce_fusion = f32[3,256]{1,0:T(4,128)S(1)} fusion(bf16[3,256,6144]{2,1,0:T(8,128)(2,1)} %param.4), kind=kLoop, calls=%fused_computation.2 | loop fusion | flops 9436416 | bytes 9440256 | tf_op jit(solution)/shard_map/reduce_sum | solution.py:83
  129.6 6.3 %fusion.2 = f32[3,256]{1,0:T(4,128)S(1)} fusion(bf16[3,256,6144]{2,1,0:T(8,128)(2,1)} %param.4, f32[3,256]{1,0:T(4,128)S(1)} %broadcast_multiply_fusion), kind=kLoop, calls=%fused_computation.5 | loop fusion | flops 18873600 | bytes 9443328 | tf_op jit(solution)/shard_map/reduce_sum | solution.py:84
  135.8 15.0 %constant_dynamic-slice_fusion.11 = (bf16[1,768,3,256]{1,0,3,2:T(2,128)(2,1)}, bf16[1,768,3,256]{1,0,3,2:T(2,128)(2,1)}, bf16[1,768,3,256]{1,0,3,2:T(2,128)(2,1)S(1)}) fusion(bf16[4,768,3,256]{1,0,3,2:T(4,128)(2,1)} %reshape.437, s32[]{:T(128)S(6)} %select_n.148, s32[]{:T(128)S(6)} %select_n.149, s32[]{:T(128)S(6)} %select_n.150), kind=kLoop, calls=%fused_computation.147 | loop fusion | bytes 7077900 | tf_op jit(solution)/shard_map/jit(dynamic_index_in_dim)/dynamic_slice | solution.py:33
  155.7 12.3 %fusion.3 = bf16[3,256,6144]{2,1,0:T(8,128)(2,1)} fusion(bf16[3,256,6144]{2,1,0:T(8,128)(2,1)} %param.4, f32[3,256]{1,0:T(4,128)S(1)} %add_rsqrt_fusion.10, f32[3,256]{1,0:T(4,128)S(1)} %broadcast_multiply_fusion), kind=kLoop, calls=%fused_computation.6 | loop fusion | flops 18874368 | bytes 18880512 | tf_op jit(solution)/shard_map/convert_element_type | solution.py:85
  167.9 4.3 fusion.32
  172.2 4.3 fusion.30
  179.3 7.8 %fusion.9 = f32[768,768,1]{1,0,2:T(8,128)} fusion(bf16[4,768,768]{1,0,2:T(4,128)(2,1)S(1)} %bitcast.212, bf16[768,1,768]{2,0,1:T(8,128)(2,1)S(1)} %get-tuple-element.32, bf16[768,1,768]{2,0,1:T(8,128)(2,1)S(1)} %get-tuple-element.33, bf16[768,1,768]{2,0,1:T(8,128)(2,1)} %get-tuple-element.34, bf16[768,1,768]{2,0,1:T(8,128)(2,1)} %get-tuple-element.35), kind=kOutput, calls=%fused_computation.13 | convolution fusion | flops 3630956544 | bytes 11796480 | tf_op jit(solution)/shard_map/nvd,vdc->nc/dot_general | solution.py:111
  187.0 45.6 %collective-permute-done = bf16[3,768,3,256]{1,3,2,0:T(8,128)(2,1)} collective-permute-done((bf16[3,768,3,256]{1,3,2,0:T(8,128)(2,1)S(1)}, bf16[3,768,3,256]{1,3,2,0:T(8,128)(2,1)}, u32[]{:S(2)}, u32[]{:S(2)}) %collective-permute-start) | collective-permute-done | bytes 3538976 | tf_op jit(solution)/shard_map/ppermute | solution.py:40
  232.7 10.1 %reshape.438 = bf16[4,768,3,256]{1,0,3,2:T(4,128)(2,1)} reshape(bf16[3072,3,256]{0,2,1:T(8,128)(2,1)} %all-gather.12.cloned.1.call-done) | data formatting | bytes 9437184 | tf_op jit(solution)/shard_map/all_gather | solution.py:31
  242.9 15.0 %constant_dynamic-slice_fusion.6 = (bf16[1,768,3,256]{1,0,3,2:T(2,128)(2,1)}, bf16[1,768,3,256]{1,0,3,2:T(2,128)(2,1)}, bf16[1,768,3,256]{1,0,3,2:T(2,128)(2,1)S(1)}) fusion(bf16[4,768,3,256]{1,0,3,2:T(4,128)(2,1)} %reshape.438, s32[]{:T(128)S(6)} %select_n.148, s32[]{:T(128)S(6)} %select_n.149, s32[]{:T(128)S(6)} %select_n.150), kind=kLoop, calls=%fused_computation.142 | loop fusion | bytes 7077900 | tf_op jit(solution)/shard_map/jit(dynamic_index_in_dim)/dynamic_slice | solution.py:33
  265.3 6.5 %bitcast_add_fusion.2 = f32[768,768]{1,0:T(8,128)} fusion(f32[768,768]{1,0:T(8,128)S(1)} %copy-done.24, f32[768,768,1]{1,0,2:T(8,128)S(1)} %copy-done.25, bf16[3,768,768]{1,2,0:T(8,128)(2,1)} %bitcast.16, bf16[768,1,768]{2,0,1:T(8,128)(2,1)S(1)} %copy-done.11, bf16[768,1,768]{2,0,1:T(8,128)(2,1)S(1)} %copy-done.14, bf16[768,1,768]{2,0,1:T(8,128)(2,1)S(1)} %copy-done.8), kind=kOutput, calls=%fused_computation.22 | convolution fusion | flops 2722627584 | bytes 14155776 | tf_op jit(solution)/shard_map/nvd,vdc->nc/dot_general | solution.py:115
  279.3 13.6 %all-gather.14.cloned.1.call-done = bf16[3072,3,128]{0,2,1:T(8,128)(2,1)} async-done(((bf16[768,3,128]{0,2,1:T(8,128)(2,1)}), bf16[3072,3,128]{0,2,1:T(8,128)(2,1)}) %all-gather.14.cloned.1.call-update) | async-done | bytes 2359312 | tf_op jit(solution)/shard_map/all_gather | solution.py:31
  292.9 4.5 reshape.439
  297.5 7.4 %fusion.7 = f32[768,768,1]{1,0,2:T(8,128)S(1)} fusion(bf16[4,768,768]{1,0,2:T(4,128)(2,1)} %bitcast.213, bf16[768,1,768]{2,0,1:T(8,128)(2,1)S(1)} %copy-done.18, bf16[768,1,768]{2,0,1:T(8,128)(2,1)} %copy-done.19, bf16[768,1,768]{2,0,1:T(8,128)(2,1)} %get-tuple-element.34, bf16[768,1,768]{2,0,1:T(8,128)(2,1)} %get-tuple-element.35), kind=kOutput, calls=%fused_computation.11 | convolution fusion | flops 3630956544 | bytes 11796480 | tf_op jit(solution)/shard_map/nvd,vdc->nc/dot_general | solution.py:111
  305.0 35.9 %collective-permute-done.1 = bf16[3,768,3,256]{1,3,2,0:T(8,128)(2,1)} collective-permute-done((bf16[3,768,3,256]{1,3,2,0:T(8,128)(2,1)}, bf16[3,768,3,256]{1,3,2,0:T(8,128)(2,1)}, u32[]{:S(2)}, u32[]{:S(2)}) %collective-permute-start.1) | collective-permute-done | bytes 3538976 | tf_op jit(solution)/shard_map/ppermute | solution.py:40
  340.9 6.5 %bitcast_add_fusion = f32[768,768]{1,0:T(8,128)} fusion(f32[768,768]{1,0:T(8,128)S(1)} %copy-done.23, f32[768,768,1]{1,0,2:T(8,128)S(1)} %fusion.7, bf16[3,768,768]{1,2,0:T(8,128)(2,1)} %bitcast.26, bf16[768,1,768]{2,0,1:T(8,128)(2,1)S(1)} %copy-done.12, bf16[768,1,768]{2,0,1:T(8,128)(2,1)S(1)} %copy-done.15, bf16[768,1,768]{2,0,1:T(8,128)(2,1)S(1)} %copy-done.9), kind=kOutput, calls=%fused_computation.20 | convolution fusion | flops 2722627584 | bytes 14155776 | tf_op jit(solution)/shard_map/nvd,vdc->nc/dot_general | solution.py:115
  347.3 4.0 reshape.418
  353.2 3.8 constant_dynamic-slice_fusion.2
  368.0 4.5 fusion.18
  374.8 22.9 %collective-permute-done.2 = bf16[3,768,3,128]{1,3,2,0:T(8,128)(2,1)} collective-permute-done((bf16[3,768,3,128]{1,3,2,0:T(8,128)(2,1)}, bf16[3,768,3,128]{1,3,2,0:T(8,128)(2,1)}, u32[]{:S(2)}, u32[]{:S(2)}) %collective-permute-start.2) | collective-permute-done | bytes 1769504 | tf_op jit(solution)/shard_map/ppermute | solution.py:40
  397.8 3.5 fusion.21
  407.2 11.0 %fusion.13 = f32[3,256,3,1,128]{1,4,2,0,3:T(8,128)S(1)} fusion(bf16[6144,3,128]{0,2,1:T(8,128)(2,1)} %all-gather.8.cloned.1.call-done, bf16[3,256,6144]{2,1,0:T(8,128)(2,1)} %fusion.3), kind=kOutput, calls=%fused_computation.30 | convolution fusion | flops 3623878656 | bytes 15335424 | tf_op jit(solution)/shard_map/dot_general | solution.py:101
  419.4 14.5 %all_gather.35 = bf16[192,768]{1,0:T(8,128)(2,1)S(1)} all-gather(bf16[48,768]{1,0:T(8,128)(2,1)S(1)} %pad_maximum_fusion.6), channel_id=1, replica_groups=mesh['groups'=2,'video'=4,'tensor'=4] {'video'}, dimensions={0}, use_global_device_ids=true | all-gather | bytes 368640 | tf_op jit(solution)/shard_map/all_gather | solution.py:121
  433.9 4.5 convolution_convert_fusion
  439.6 24.8 %reduce-scatter.2.cloned.1.call-done = bf16[48,3,1024]{2,0,1:T(8,128)(2,1)} async-done(((bf16[192,3,1024]{2,0,1:T(8,128)(2,1)}), bf16[48,3,1024]{2,0,1:T(8,128)(2,1)}) %reduce-scatter.2.cloned.1.call-update) | async-done | bytes 294928 | tf_op jit(solution)/shard_map/reduce_scatter | solution.py:126
  464.4 3.7 collective-permute-start.3
  471.7 17.1 %collective-permute-done.3 = bf16[48,3,1024]{2,0,1:T(8,128)(2,1)S(1)} collective-permute-done((bf16[48,3,1024]{2,0,1:T(8,128)(2,1)}, bf16[48,3,1024]{2,0,1:T(8,128)(2,1)S(1)}, u32[]{:S(2)}, u32[]{:S(2)}) %collective-permute-start.3) | collective-permute-done | bytes 294944 | tf_op jit(solution)/shard_map/ppermute | solution.py:136
  488.9 6.8 %collective-permute-done.4 = bf16[48,3,1024]{2,0,1:T(8,128)(2,1)S(1)} collective-permute-done((bf16[48,3,1024]{2,0,1:T(8,128)(2,1)}, bf16[48,3,1024]{2,0,1:T(8,128)(2,1)S(1)}, u32[]{:S(2)}, u32[]{:S(2)}) %collective-permute-start.4) | collective-permute-done | bytes 294944 | tf_op jit(solution)/shard_map/ppermute | solution.py:136
  (193 shorter events, 74.8 us)
Async XLA Ops:
  6.5 98.3 %all-gather.10.cloned.1.call-start = ((), (), s32[]{:S(2)}) async-start(), calls=%async_computation.3 | async-start | bytes 5898240 | tf_op jit(solution)/shard_map/all_gather | solution.py:31
  14.1 3.8 copy-start.21
  14.1 12.5 %copy-start.5 = (bf16[768,3,256]{2,0,1:T(8,128)(2,1)S(1)}, bf16[768,3,256]{2,0,1:T(8,128)(2,1)}, u32[]{:S(2)}) copy-start(bf16[768,3,256]{2,0,1:T(8,128)(2,1)} %get-tuple-element.53) | copy-start | bytes 3538948
  16.6 11.6 %copy-start.4 = (bf16[768,3,256]{2,0,1:T(8,128)(2,1)S(1)}, bf16[768,3,256]{2,0,1:T(8,128)(2,1)}, u32[]{:S(2)}) copy-start(bf16[768,3,256]{2,0,1:T(8,128)(2,1)} %get-tuple-element.64) | copy-start | bytes 3538948
  16.6 216.1 %all-gather.12.cloned.1.call-start = ((), (), s32[]{:S(2)}) async-start(), calls=%async_computation.4 | async-start | bytes 5898240 | tf_op jit(solution)/shard_map/all_gather | solution.py:31
  114.6 178.2 %all-gather.14.cloned.1.call-start = ((), (), s32[]{:S(2)}) async-start(), calls=%async_computation.5 | async-start | bytes 2949120 | tf_op jit(solution)/shard_map/all_gather | solution.py:31
  154.1 78.6 %collective-permute-start = (bf16[3,768,3,256]{1,3,2,0:T(8,128)(2,1)S(1)}, bf16[3,768,3,256]{1,3,2,0:T(8,128)(2,1)}, u32[]{:S(2)}, u32[]{:S(2)}) collective-permute-start(bf16[3,768,3,256]{1,3,2,0:T(8,128)(2,1)S(1)} %pad_maximum_fusion.1), channel_id=1, source_target_pairs={{0,16},{16,0},{1,17},{17,1},{2,18},{18,2},{3,19},{19,3},{4,20},{20... | collective-permute-start | bytes 10616840 | tf_op jit(solution)/shard_map/ppermute | solution.py:40
  167.9 8.6 %copy-start = (bf16[3,256,6144]{2,1,0:T(8,128)(2,1)S(1)}, bf16[3,256,6144]{2,1,0:T(8,128)(2,1)}, u32[]{:S(2)}) copy-start(bf16[3,256,6144]{2,1,0:T(8,128)(2,1)} %fusion.3) | copy-start | bytes 28311556
  172.2 7.0 %slice-start = ((s8[4718592]{0:T(1024)(128)(4,1)}), s8[4194304]{0:T(1024)(128)(4,1)S(1)}, s32[]{:S(2)}) async-start(s8[4718592]{0:T(1024)(128)(4,1)} %bitcast.210), calls=%async_computation.6 | async-start | bytes 8388608
  179.2 7.8 %copy-start.17 = (bf16[768,1,768]{2,0,1:T(8,128)(2,1)}, bf16[768,1,768]{2,0,1:T(8,128)(2,1)S(1)}, u32[]{:S(2)}) copy-start(bf16[768,1,768]{2,0,1:T(8,128)(2,1)S(1)} %get-tuple-element.32) | copy-start | bytes 3538948
  179.2 7.8 %copy-start.19 = (bf16[768,1,768]{2,0,1:T(8,128)(2,1)}, bf16[768,1,768]{2,0,1:T(8,128)(2,1)S(1)}, u32[]{:S(2)}) copy-start(bf16[768,1,768]{2,0,1:T(8,128)(2,1)S(1)} %get-tuple-element.33) | copy-start | bytes 3538948
  242.8 164.4 %all-gather.8.cloned.1.call-start = ((), (), s32[]{:S(2)}) async-start(), calls=%async_computation.1 | async-start | bytes 5898240 | tf_op jit(solution)/shard_map/all_gather | solution.py:75
  260.5 3.9 copy-start.25
  260.7 3.7 copy-start.8
  260.8 3.8 copy-start.14
  260.8 4.6 copy-start.24
  263.0 77.9 %collective-permute-start.1 = (bf16[3,768,3,256]{1,3,2,0:T(8,128)(2,1)}, bf16[3,768,3,256]{1,3,2,0:T(8,128)(2,1)}, u32[]{:S(2)}, u32[]{:S(2)}) collective-permute-start(bf16[3,768,3,256]{1,3,2,0:T(8,128)(2,1)} %pad_maximum_fusion.3), channel_id=1, source_target_pairs={{0,16},{16,0},{1,17},{17,1},{2,18},{18,2},{3,19},{19,3},{4,20},{20... | collective-permute-start | bytes 10616840 | tf_op jit(solution)/shard_map/ppermute | solution.py:40
  279.3 18.2 %copy-start.18 = (bf16[768,1,768]{2,0,1:T(8,128)(2,1)S(1)}, bf16[768,1,768]{2,0,1:T(8,128)(2,1)}, u32[]{:S(2)}) copy-start(bf16[768,1,768]{2,0,1:T(8,128)(2,1)} %copy-done.17) | copy-start | bytes 3538948
  297.4 166.9 %reduce-scatter.2.cloned.1.call-start = ((), (), s32[]{:S(2)}) async-start(), calls=%async_computation.2 | async-start | bytes 1474560 | tf_op jit(solution)/shard_map/reduce_scatter | solution.py:126
  297.5 43.4 %copy-start.9 = (bf16[768,1,768]{2,0,1:T(8,128)(2,1)S(1)}, bf16[768,1,768]{2,0,1:T(8,128)(2,1)}, u32[]{:S(2)}) copy-start(bf16[768,1,768]{2,0,1:T(8,128)(2,1)} %get-tuple-element.29) | copy-start | bytes 3538948
  297.5 43.3 %copy-start.12 = (bf16[768,1,768]{2,0,1:T(8,128)(2,1)S(1)}, bf16[768,1,768]{2,0,1:T(8,128)(2,1)}, u32[]{:S(2)}) copy-start(bf16[768,1,768]{2,0,1:T(8,128)(2,1)} %get-tuple-element.30) | copy-start | bytes 3538948
  297.5 43.3 %copy-start.15 = (bf16[768,1,768]{2,0,1:T(8,128)(2,1)S(1)}, bf16[768,1,768]{2,0,1:T(8,128)(2,1)}, u32[]{:S(2)}) copy-start(bf16[768,1,768]{2,0,1:T(8,128)(2,1)} %get-tuple-element.31) | copy-start | bytes 3538948
  297.5 43.3 %copy-start.23 = (f32[768,768]{1,0:T(8,128)S(1)}, f32[768,768]{1,0:T(8,128)}, u32[]{:S(2)}) copy-start(f32[768,768]{1,0:T(8,128)} %fusion.30) | copy-start | bytes 7077892
  358.7 39.1 %collective-permute-start.2 = (bf16[3,768,3,128]{1,3,2,0:T(8,128)(2,1)}, bf16[3,768,3,128]{1,3,2,0:T(8,128)(2,1)}, u32[]{:S(2)}, u32[]{:S(2)}) collective-permute-start(bf16[3,768,3,128]{1,3,2,0:T(8,128)(2,1)} %pad_maximum_fusion.4), channel_id=1, source_target_pairs={{0,16},{16,0},{1,17},{17,1},{2,18},{18,2},{3,19},{19,3},{4,20},{20... | collective-permute-start | bytes 5308424 | tf_op jit(solution)/shard_map/ppermute | solution.py:40
  368.0 4.5 copy-start.6
  372.6 25.2 %copy-start.10 = (bf16[768,1,768]{2,0,1:T(8,128)(2,1)S(1)}, bf16[768,1,768]{2,0,1:T(8,128)(2,1)}, u32[]{:S(2)}) copy-start(bf16[768,1,768]{2,0,1:T(8,128)(2,1)} %get-tuple-element.29) | copy-start | bytes 3538948
  372.6 25.2 %copy-start.13 = (bf16[768,1,768]{2,0,1:T(8,128)(2,1)S(1)}, bf16[768,1,768]{2,0,1:T(8,128)(2,1)}, u32[]{:S(2)}) copy-start(bf16[768,1,768]{2,0,1:T(8,128)(2,1)} %get-tuple-element.30) | copy-start | bytes 3538948
  372.6 25.2 %copy-start.16 = (bf16[768,1,768]{2,0,1:T(8,128)(2,1)S(1)}, bf16[768,1,768]{2,0,1:T(8,128)(2,1)}, u32[]{:S(2)}) copy-start(bf16[768,1,768]{2,0,1:T(8,128)(2,1)} %get-tuple-element.31) | copy-start | bytes 3538948
  464.4 24.5 %collective-permute-start.3 = (bf16[48,3,1024]{2,0,1:T(8,128)(2,1)}, bf16[48,3,1024]{2,0,1:T(8,128)(2,1)S(1)}, u32[]{:S(2)}, u32[]{:S(2)}) collective-permute-start(bf16[48,3,1024]{2,0,1:T(8,128)(2,1)} %reduce-scatter.2.cloned.1.call-done), channel_id=1, source_target_pairs={{0,0},{1,4},{2,8},{3,12},{4,1},{5,5},{6,9},{7,13},{8,2},{9,6},{10,... | collective-permute-start | bytes 884744 | tf_op jit(solution)/shard_map/ppermute | solution.py:136
  468.1 27.5 %collective-permute-start.4 = (bf16[48,3,1024]{2,0,1:T(8,128)(2,1)}, bf16[48,3,1024]{2,0,1:T(8,128)(2,1)S(1)}, u32[]{:S(2)}, u32[]{:S(2)}) collective-permute-start(bf16[48,3,1024]{2,0,1:T(8,128)(2,1)} %reduce-scatter.2.cloned.1.call-done), channel_id=1, source_target_pairs={{0,4},{1,8},{2,12},{3,0},{4,5},{5,9},{6,13},{7,1},{8,6},{9,10},{10... | collective-permute-start | bytes 884744 | tf_op jit(solution)/shard_map/ppermute | solution.py:136
  469.3 27.3 %collective-permute-start.5 = (bf16[48,3,1024]{2,0,1:T(8,128)(2,1)}, bf16[48,3,1024]{2,0,1:T(8,128)(2,1)S(1)}, u32[]{:S(2)}, u32[]{:S(2)}) collective-permute-start(bf16[48,3,1024]{2,0,1:T(8,128)(2,1)} %reduce-scatter.2.cloned.1.call-done), channel_id=1, source_target_pairs={{0,8},{1,12},{2,0},{3,4},{4,9},{5,13},{6,1},{7,5},{8,10},{9,14},{1... | collective-permute-start | bytes 884744 | tf_op jit(solution)/shard_map/ppermute | solution.py:136
  470.2 28.0 %collective-permute-start.6 = (bf16[48,3,1024]{2,0,1:T(8,128)(2,1)}, bf16[48,3,1024]{2,0,1:T(8,128)(2,1)S(1)}, u32[]{:S(2)}, u32[]{:S(2)}) collective-permute-start(bf16[48,3,1024]{2,0,1:T(8,128)(2,1)} %reduce-scatter.2.cloned.1.call-done), channel_id=1, source_target_pairs={{0,12},{1,0},{2,4},{3,8},{4,13},{5,1},{6,5},{7,9},{8,14},{9,2},{10... | collective-permute-start | bytes 884744 | tf_op jit(solution)/shard_map/ppermute | solution.py:136
  (8 other events, 19.1 us)
Sparse Core Ops, SparseCore 0:
  16.8 88.0 all-gather.9
  114.8 87.8 all-gather.11
  243.0 49.8 all-gather.13
  297.6 87.2 all-gather.7
  438.5 25.7 reduce-scatter.1

commit v10 on v7

--- a/solution.py
+++ b/solution.py
@@ -28,10 +28,10 @@
     if after is not None:
         mine, after = lax.optimization_barrier((mine, after))
     other = lax.dynamic_slice_in_dim(chunk, (1 - g) * half, half, axis=0)
-    gathered = lax.all_gather(mine, "video", axis=0, tiled=False)
-    onward = jnp.stack(
-        [lax.dynamic_index_in_dim(gathered, (v + 1 + i) % n_video, axis=0, keepdims=False)
-         for i in range(n_video - 1)]
+    gathered = lax.all_gather(mine, "video", axis=0, tiled=True)
+    onward = jnp.concatenate(
+        [lax.dynamic_slice_in_dim(gathered, ((v + 1 + i) % n_video) * half, half, axis=0)
+         for i in range(n_video - 1)], axis=0
     )
     return [other, gathered, onward], after
 
@@ -89,9 +89,11 @@
     def columns(shard, which):
         return lax.dynamic_slice_in_dim(normed, shard * local_rows + which * half, half, axis=1)
 
-    own_half = jnp.stack([columns(u, g) for u in range(n_video)], axis=1)
+    own_half = jnp.concatenate([columns(u, g) for u in range(n_video)], axis=1)
     own_piece = columns(v, 1 - g)
-    rolled = jnp.stack([columns((v + 1 + i) % n_video, 1 - g) for i in range(n_video - 1)], axis=1)
+    rolled = jnp.concatenate(
+        [columns((v + 1 + i) % n_video, 1 - g) for i in range(n_video - 1)], axis=1
+    )
     video_all = lax.all_gather(frame_video, "video", axis=0, tiled=True)
     pooled_parts = []
     for index, size in enumerate(sizes):
@@ -108,12 +110,11 @@
         else:
             received = forward(onward)
         proj = jnp.dot(own_piece, other.reshape(half, width), preferred_element_type=jnp.float32)
-        proj = proj + jnp.einsum(
-            "nvd,vdc->nc", own_half, gathered.reshape(n_video, half, width),
-            preferred_element_type=jnp.float32,
+        proj = proj + jnp.dot(
+            own_half, gathered.reshape(n_video * half, width), preferred_element_type=jnp.float32
         )
-        proj = proj + jnp.einsum(
-            "nvd,vdc->nc", rolled, received.reshape(n_video - 1, half, width),
+        proj = proj + jnp.dot(
+            rolled, received.reshape((n_video - 1) * half, width),
             preferred_element_type=jnp.float32,
         )
         pooled_parts.append(attend(proj, nframes, size, scale, blocks, inner))

time: 505 us -> 485 us (0.960)
  local copies, waits for them, and re-layouts: 104 us -> 37.3 us
  waiting for transfers between devices: 239 us -> 286 us
    dynamic_slice x3 -> x4, local copies, waits for them, and re-layouts: 34.4 us -> 5.13 us  [the longest x1 4.18 us: columns(): lax.dynamic_slice_in_dim(normed, shard * local_rows + which * half, half,...]
    all_gather x3, waiting for transfers between devices: 108 us -> 135 us  [moved_weights(): gathered = lax.all_gather(mine, 'video', axis=0, tiled=True)]
    all_gather x3 -> x0, local copies, waits for them, and re-layouts: 24.2 us -> none  [moved_weights(): gathered = lax.all_gather(mine, 'video', axis=0, tiled=False)]
    ppermute x3, waiting for transfers between devices: 79.5 us -> 99.9 us  [forward(): return lax.ppermute(onward, 'groups', [(0, 1), (1, 0)])]
    unnamed x83 -> x78, local copies, waits for them, and re-layouts: 16.5 us -> 6.16 us
    another operation x3 -> x0, other arithmetic: 5.7 us -> none  [moved_weights(): jnp.stack([lax.dynamic_index_in_dim(gathered, (v + 1 + i) % n_video, axis...]
    concatenate x0 -> x3, other arithmetic: none -> 5.41 us  [moved_weights(): jnp.concatenate([lax.dynamic_slice_in_dim(gathered, (v + 1 + i) % n_video...]
  transfers between devices with their start and end apart: 12 -> 12, of which waited for: 9 -> 11; matrix products, arithmetic and copies ran while one was open for 36% -> 24% of each run, Pallas kernels for 0% -> 0%
where the time goes in v10:
time: 485 us; the launch traced here: 480 us
  waiting for transfers between devices  286 us (59%)
  matrix products  68.4 us (14%)
  local copies, waits for them, and re-layouts  37.3 us (8%)
  other arithmetic  37.2 us (8%)
  blocking collectives  23.7 us (5%)
  between operations  15 us (3%)
  starting transfers between devices  11.8 us (2%)
    all_gather x3, waiting for transfers between devices, moved_weights(): gathered = lax.all_gather(mine, 'video', axis=0, tiled=True)  135 us
    ppermute x3, waiting for transfers between devices, forward(): return lax.ppermute(onward, 'groups', [(0, 1), (1, 0)])  99.9 us
    ppermute x4, waiting for transfers between devices, per_device(): got = lax.ppermute(clip_rows, ('video', 'tensor'), pairs)  26.4 us
    reduce_scatter x1, waiting for transfers between devices, per_device(): lax.psum_scatter(partial_proj.astype(jnp.bfloat16), 'tensor', scatter_dim...  24.8 us
    dot_general x3, matrix products, per_device(): jnp.dot(own_half, gathered.reshape(n_video * half, width), preferred_elem...  16.7 us
    dot_general x3, matrix products, per_device(): jnp.dot(rolled, received.reshape((n_video - 1) * half, width), preferred_...  16.3 us
    all_gather x1, blocking collectives, per_device(): pooled_all = lax.all_gather(pooled, 'video', axis=0, tiled=True)  15 us
    convert_element_type x1, other arithmetic, per_device(): normed = normed.astype(jnp.bfloat16).reshape(patch_rows, frames.shape[2])  12.4 us
  transfers between devices with their start and end apart: 12, of which 11 were waited for; matrix products, arithmetic and copies ran while one was open for 24% of the time, Pallas kernels for 0%

profile of v10, /device:TPU:10, one launch (start us, length us, event | category | flops | bytes accessed | tf_op | source)
XLA Modules:
  0.0 479.9 jit_solution(8366585630378617813)
XLA Ops:
  6.5 2.8 fusion.66
  11.4 2.7 fusion.67
  17.9 43.6 %all-gather.5.cloned.1.call-done = bf16[3072,3,128]{0,2,1:T(8,128)(2,1)} async-done(((bf16[768,3,128]{0,2,1:T(8,128)(2,1)}), bf16[3072,3,128]{0,2,1:T(8,128)(2,1)}) %all-gather.5.cloned.1.call-update) | async-done | bytes 2359312 | tf_op jit(solution)/shard_map/all_gather | solution.py:31
  63.2 5.0 %convert_reduce_fusion = f32[3,256]{1,0:T(4,128)S(1)} fusion(bf16[3,256,6144]{2,1,0:T(8,128)(2,1)} %param.4), kind=kLoop, calls=%fused_computation.2 | loop fusion | flops 9436416 | bytes 9440256 | tf_op jit(solution)/shard_map/reduce_sum | solution.py:83
  68.2 6.8 %fusion.2 = f32[3,256]{1,0:T(4,128)S(1)} fusion(bf16[3,256,6144]{2,1,0:T(8,128)(2,1)} %param.4, f32[3,256]{1,0:T(4,128)S(1)} %broadcast_multiply_fusion), kind=kLoop, calls=%fused_computation.5 | loop fusion | flops 18873600 | bytes 9443328 | tf_op jit(solution)/shard_map/reduce_sum | solution.py:84
  75.1 75.4 %all-gather.7.cloned.1.call-done = bf16[3072,3,256]{0,2,1:T(8,128)(2,1)} async-done(((bf16[768,3,256]{0,2,1:T(8,128)(2,1)}), bf16[3072,3,256]{0,2,1:T(8,128)(2,1)}) %all-gather.7.cloned.1.call-update) | async-done | bytes 4718608 | tf_op jit(solution)/shard_map/all_gather | solution.py:31
  153.8 12.4 %fusion.3 = bf16[3,256,6144]{2,1,0:T(8,128)(2,1)} fusion(bf16[3,256,6144]{2,1,0:T(8,128)(2,1)} %param.4, f32[3,256]{1,0:T(4,128)S(1)} %add_rsqrt_fusion.10, f32[3,256]{1,0:T(4,128)S(1)} %broadcast_multiply_fusion), kind=kLoop, calls=%fused_computation.6 | loop fusion | flops 18874368 | bytes 18880512 | tf_op jit(solution)/shard_map/convert_element_type | solution.py:85
  169.2 4.0 fusion.21
  173.1 8.7 %all-reduce = s32[12]{0:T(128)S(1)} all-reduce(s32[12]{0:T(128)S(1)} %dynamic-update-slice), channel_id=1, replica_groups=mesh['groups'=2,'video'=4,'tensor'=4] {'video'}, use_global_device_ids=true, to_apply=%add | all-reduce | flops 12 | bytes 96 | tf_op jit(solution)/shard_map/optimization_barrier | solution.py:109
  184.3 3.8 fusion.19
  188.2 4.2 constant_dynamic-slice_fusion.14
  192.4 2.6 fusion.64
  195.1 3.7 convolution_add_fusion
  198.8 9.6 %collective-permute-done = bf16[2304,3,128]{0,2,1:T(8,128)(2,1)} collective-permute-done((bf16[2304,3,128]{0,2,1:T(8,128)(2,1)}, bf16[2304,3,128]{0,2,1:T(8,128)(2,1)}, u32[]{:S(2)}, u32[]{:S(2)}) %collective-permute-start) | collective-permute-done | bytes 1769504 | tf_op jit(solution)/shard_map/ppermute | solution.py:40
  212.1 3.5 convolution_add_fusion.1
  217.0 3.3 multiply_reduce_fusion.8
  223.7 16.3 %all-gather.9.cloned.1.call-done = bf16[3072,3,256]{0,2,1:T(8,128)(2,1)} async-done(((bf16[768,3,256]{0,2,1:T(8,128)(2,1)}), bf16[3072,3,256]{0,2,1:T(8,128)(2,1)}) %all-gather.9.cloned.1.call-update) | async-done | bytes 4718608 | tf_op jit(solution)/shard_map/all_gather | solution.py:31
  240.1 7.0 %fusion.63 = f32[768,768]{1,0:T(8,128)S(1)} fusion(bf16[3072,768]{0,1:T(8,128)(2,1)} %bitcast.181, bf16[768,768]{1,0:T(8,128)(2,1)S(1)} %copy-done.15, bf16[768,768]{1,0:T(8,128)(2,1)S(1)} %copy-done.18, bf16[768,768]{1,0:T(8,128)(2,1)} %copy-done.20, bf16[768,768]{1,0:T(8,128)(2,1)} %copy-done.21), kind=kOutput, calls=%fused_computation.162 | convolution fusion | flops 3642753024 | bytes 11796480 | tf_op jit(solution)/shard_map/dot_general | solution.py:113
  251.3 39.2 %collective-permute-done.1 = bf16[2304,3,256]{0,2,1:T(8,128)(2,1)} collective-permute-done((bf16[2304,3,256]{0,2,1:T(8,128)(2,1)}, bf16[2304,3,256]{0,2,1:T(8,128)(2,1)}, u32[]{:S(2)}, u32[]{:S(2)}) %collective-permute-start.1) | collective-permute-done | bytes 3538976 | tf_op jit(solution)/shard_map/ppermute | solution.py:40
  290.5 6.4 %add_add_fusion.1 = f32[768,768]{1,0:T(8,128)} fusion(f32[768,768]{1,0:T(8,128)S(1)} %copy-done.24, f32[768,768]{1,0:T(8,128)S(1)} %fusion.63, bf16[2304,768]{0,1:T(8,128)(2,1)} %bitcast.18, bf16[768,768]{1,0:T(8,128)(2,1)S(1)} %copy-done.9, bf16[768,768]{1,0:T(8,128)(2,1)S(1)} %copy-done.12, bf16[768,768]{1,0:T(8,128)(2,1)S(1)} %copy-done.6), kind=kOutput, calls=%fused_computation.15 | convolution fusion | flops 2729705472 | bytes 14155776 | tf_op jit(solution)/shard_map/dot_general | solution.py:116
  296.9 2.9 reshape.418
  306.0 7.0 %fusion.62 = f32[768,768]{1,0:T(8,128)S(1)} fusion(bf16[3072,768]{0,1:T(8,128)(2,1)} %bitcast.178, bf16[768,768]{1,0:T(8,128)(2,1)S(1)} %copy-done.16, bf16[768,768]{1,0:T(8,128)(2,1)S(1)} %copy-done.19, bf16[768,768]{1,0:T(8,128)(2,1)} %copy-done.20, bf16[768,768]{1,0:T(8,128)(2,1)} %copy-done.21), kind=kOutput, calls=%fused_computation.161 | convolution fusion | flops 3642753024 | bytes 11796480 | tf_op jit(solution)/shard_map/dot_general | solution.py:113
  313.0 51.2 %collective-permute-done.2 = bf16[2304,3,256]{0,2,1:T(8,128)(2,1)} collective-permute-done((bf16[2304,3,256]{0,2,1:T(8,128)(2,1)}, bf16[2304,3,256]{0,2,1:T(8,128)(2,1)}, u32[]{:S(2)}, u32[]{:S(2)}) %collective-permute-start.2) | collective-permute-done | bytes 3538976 | tf_op jit(solution)/shard_map/ppermute | solution.py:40
  364.2 6.4 %add_add_fusion = f32[768,768]{1,0:T(8,128)} fusion(f32[768,768]{1,0:T(8,128)S(1)} %copy-done.25, f32[768,768]{1,0:T(8,128)S(1)} %fusion.62, bf16[2304,768]{0,1:T(8,128)(2,1)} %bitcast.26, bf16[768,768]{1,0:T(8,128)(2,1)S(1)} %copy-done.10, bf16[768,768]{1,0:T(8,128)(2,1)S(1)} %copy-done.13, bf16[768,768]{1,0:T(8,128)(2,1)S(1)} %copy-done.7), kind=kOutput, calls=%fused_computation.14 | convolution fusion | flops 2729705472 | bytes 14155776 | tf_op jit(solution)/shard_map/dot_general | solution.py:116
  370.6 2.9 reshape.423
  377.7 10.9 %fusion.7 = f32[3,256,3,1,128]{1,4,2,0,3:T(8,128)S(1)} fusion(bf16[6144,3,128]{0,2,1:T(8,128)(2,1)} %all-gather.11.cloned.1.call-done, bf16[3,256,6144]{2,1,0:T(8,128)(2,1)} %fusion.3), kind=kOutput, calls=%fused_computation.22 | convolution fusion | flops 3623878656 | bytes 15335424 | tf_op jit(solution)/shard_map/dot_general | solution.py:103
  389.7 15.0 %all_gather.23 = bf16[192,768]{1,0:T(8,128)(2,1)S(1)} all-gather(bf16[48,768]{1,0:T(8,128)(2,1)S(1)} %pad_maximum_fusion.6), channel_id=1, replica_groups=mesh['groups'=2,'video'=4,'tensor'=4] {'video'}, dimensions={0}, use_global_device_ids=true | all-gather | bytes 368640 | tf_op jit(solution)/shard_map/all_gather | solution.py:122
  404.6 4.5 convolution_convert_fusion
  410.3 24.8 %reduce-scatter.2.cloned.1.call-done = bf16[48,3,1024]{2,0,1:T(8,128)(2,1)} async-done(((bf16[192,3,1024]{2,0,1:T(8,128)(2,1)}), bf16[48,3,1024]{2,0,1:T(8,128)(2,1)}) %reduce-scatter.2.cloned.1.call-update) | async-done | bytes 294928 | tf_op jit(solution)/shard_map/reduce_scatter | solution.py:127
  435.1 3.7 collective-permute-start.3
  442.5 17.1 %collective-permute-done.3 = bf16[48,3,1024]{2,0,1:T(8,128)(2,1)S(1)} collective-permute-done((bf16[48,3,1024]{2,0,1:T(8,128)(2,1)}, bf16[48,3,1024]{2,0,1:T(8,128)(2,1)S(1)}, u32[]{:S(2)}, u32[]{:S(2)}) %collective-permute-start.3) | collective-permute-done | bytes 294944 | tf_op jit(solution)/shard_map/ppermute | solution.py:137
  459.5 6.8 %collective-permute-done.4 = bf16[48,3,1024]{2,0,1:T(8,128)(2,1)S(1)} collective-permute-done((bf16[48,3,1024]{2,0,1:T(8,128)(2,1)}, bf16[48,3,1024]{2,0,1:T(8,128)(2,1)S(1)}, u32[]{:S(2)}, u32[]{:S(2)}) %collective-permute-start.4) | collective-permute-done | bytes 294944 | tf_op jit(solution)/shard_map/ppermute | solution.py:137
  (186 shorter events, 50.7 us)
Async XLA Ops:
  6.5 55.0 %all-gather.5.cloned.1.call-start = ((), (), s32[]{:S(2)}) async-start(), calls=%async_computation.1 | async-start | bytes 2949120 | tf_op jit(solution)/shard_map/all_gather | solution.py:31
  11.3 139.1 %all-gather.7.cloned.1.call-start = ((), (), s32[]{:S(2)}) async-start(), calls=%async_computation.2 | async-start | bytes 5898240 | tf_op jit(solution)/shard_map/all_gather | solution.py:31
  61.5 178.4 %all-gather.9.cloned.1.call-start = ((), (), s32[]{:S(2)}) async-start(), calls=%async_computation.3 | async-start | bytes 5898240 | tf_op jit(solution)/shard_map/all_gather | solution.py:31
  75.0 77.3 %copy-start.23 = (u32[32]{0:T(128)S(1)}, u32[32]{0:T(128)}, u32[]{:S(2)}) copy-start(u32[32]{0:T(128)} %constant.172) | copy-start | bytes 388
  75.1 78.5 %copy-start.22 = (s32[3]{0:T(128)S(1)}, s32[3]{0:T(128)}, u32[]{:S(2)}) copy-start(s32[3]{0:T(128)} %param.5) | copy-start | bytes 40
  150.4 227.2 %all-gather.11.cloned.1.call-start = ((), (), s32[]{:S(2)}) async-start(), calls=%async_computation.4 | async-start | bytes 5898240 | tf_op jit(solution)/shard_map/all_gather | solution.py:75
  153.8 12.4 %copy-start.2 = (bf16[3072,3,128]{0,2,1:T(8,128)(2,1)S(1)}, bf16[3072,3,128]{0,2,1:T(8,128)(2,1)}, u32[]{:S(2)}) copy-start(bf16[3072,3,128]{0,2,1:T(8,128)(2,1)} %all-gather.5.cloned.1.call-done) | copy-start | bytes 7077892
  167.7 40.7 %collective-permute-start = (bf16[2304,3,128]{0,2,1:T(8,128)(2,1)}, bf16[2304,3,128]{0,2,1:T(8,128)(2,1)}, u32[]{:S(2)}, u32[]{:S(2)}) collective-permute-start(bf16[2304,3,128]{0,2,1:T(8,128)(2,1)} %pad_maximum_fusion.4), channel_id=1, source_target_pairs={{0,16},{16,0},{1,17},{17,1},{2,18},{18,2},{3,19},{19,3},{4,20},{20... | collective-permute-start | bytes 5308424 | tf_op jit(solution)/shard_map/ppermute | solution.py:40
  169.1 12.7 %copy-start.1 = (bf16[768,3,128]{2,0,1:T(8,128)(2,1)S(1)}, bf16[768,3,128]{2,0,1:T(8,128)(2,1)}, u32[]{:S(2)}) copy-start(bf16[768,3,128]{2,0,1:T(8,128)(2,1)} %get-tuple-element.59) | copy-start | bytes 1769476
  169.1 13.0 %copy-start = (bf16[1536,3,128]{2,0,1:T(8,128)(2,1)S(1)}, bf16[1536,3,128]{2,0,1:T(8,128)(2,1)}, u32[]{:S(2)}) copy-start(bf16[1536,3,128]{2,0,1:T(8,128)(2,1)} %get-tuple-element.37) | copy-start | bytes 3538948
  192.4 19.8 %copy-start.5 = (bf16[768,768]{1,0:T(8,128)(2,1)}, bf16[768,768]{1,0:T(8,128)(2,1)S(1)}, u32[]{:S(2)}) copy-start(bf16[768,768]{1,0:T(8,128)(2,1)S(1)} %get-tuple-element.29) | copy-start | bytes 3538948
  192.4 19.8 %copy-start.8 = (bf16[768,768]{1,0:T(8,128)(2,1)}, bf16[768,768]{1,0:T(8,128)(2,1)S(1)}, u32[]{:S(2)}) copy-start(bf16[768,768]{1,0:T(8,128)(2,1)S(1)} %get-tuple-element.30) | copy-start | bytes 3538948
  192.4 19.7 %copy-start.11 = (bf16[768,768]{1,0:T(8,128)(2,1)}, bf16[768,768]{1,0:T(8,128)(2,1)S(1)}, u32[]{:S(2)}) copy-start(bf16[768,768]{1,0:T(8,128)(2,1)S(1)} %get-tuple-element.31) | copy-start | bytes 3538948
  192.4 15.9 %slice-start.2 = ((s8[4718592]{0:T(1024)(128)(4,1)}), s8[4194304]{0:T(1024)(128)(4,1)S(1)}, s32[]{:S(2)}) async-start(s8[4718592]{0:T(1024)(128)(4,1)} %bitcast.182), calls=%async_computation.8 | async-start | bytes 8388608
  192.4 15.9 %slice-start.3 = ((s8[4718592]{0:T(1024)(128)(4,1)}), s8[524288]{0:T(1024)(128)(4,1)S(1)}, s32[]{:S(2)}) async-start(s8[4718592]{0:T(1024)(128)(4,1)} %bitcast.182), calls=%async_computation.9 | async-start | bytes 1048576
  210.7 79.8 %collective-permute-start.1 = (bf16[2304,3,256]{0,2,1:T(8,128)(2,1)}, bf16[2304,3,256]{0,2,1:T(8,128)(2,1)}, u32[]{:S(2)}, u32[]{:S(2)}) collective-permute-start(bf16[2304,3,256]{0,2,1:T(8,128)(2,1)} %pad_maximum_fusion.2), channel_id=1, source_target_pairs={{0,16},{16,0},{1,17},{17,1},{2,18},{18,2},{3,19},{19,3},{4,20},{20... | collective-permute-start | bytes 10616840 | tf_op jit(solution)/shard_map/ppermute | solution.py:40
  221.6 18.5 %copy-start.15 = (bf16[768,768]{1,0:T(8,128)(2,1)S(1)}, bf16[768,768]{1,0:T(8,128)(2,1)}, u32[]{:S(2)}) copy-start(bf16[768,768]{1,0:T(8,128)(2,1)} %copy-done.14) | copy-start | bytes 3538948
  221.6 18.5 %copy-start.18 = (bf16[768,768]{1,0:T(8,128)(2,1)S(1)}, bf16[768,768]{1,0:T(8,128)(2,1)}, u32[]{:S(2)}) copy-start(bf16[768,768]{1,0:T(8,128)(2,1)} %copy-done.17) | copy-start | bytes 3538948
  240.0 195.1 %reduce-scatter.2.cloned.1.call-start = ((), (), s32[]{:S(2)}) async-start(), calls=%async_computation.5 | async-start | bytes 1474560 | tf_op jit(solution)/shard_map/reduce_scatter | solution.py:127
  247.6 42.9 %copy-start.6 = (bf16[768,768]{1,0:T(8,128)(2,1)S(1)}, bf16[768,768]{1,0:T(8,128)(2,1)}, u32[]{:S(2)}) copy-start(bf16[768,768]{1,0:T(8,128)(2,1)} %copy-done.5) | copy-start | bytes 3538948
  247.6 42.9 %copy-start.9 = (bf16[768,768]{1,0:T(8,128)(2,1)S(1)}, bf16[768,768]{1,0:T(8,128)(2,1)}, u32[]{:S(2)}) copy-start(bf16[768,768]{1,0:T(8,128)(2,1)} %copy-done.8) | copy-start | bytes 3538948
  247.6 42.9 %copy-start.12 = (bf16[768,768]{1,0:T(8,128)(2,1)S(1)}, bf16[768,768]{1,0:T(8,128)(2,1)}, u32[]{:S(2)}) copy-start(bf16[768,768]{1,0:T(8,128)(2,1)} %copy-done.11) | copy-start | bytes 3538948
  247.6 42.9 %copy-start.24 = (f32[768,768]{1,0:T(8,128)S(1)}, f32[768,768]{1,0:T(8,128)}, u32[]{:S(2)}) copy-start(f32[768,768]{1,0:T(8,128)} %fusion.21) | copy-start | bytes 7077892
  249.8 114.4 %collective-permute-start.2 = (bf16[2304,3,256]{0,2,1:T(8,128)(2,1)}, bf16[2304,3,256]{0,2,1:T(8,128)(2,1)}, u32[]{:S(2)}, u32[]{:S(2)}) collective-permute-start(bf16[2304,3,256]{0,2,1:T(8,128)(2,1)} %pad_maximum_fusion.3), channel_id=1, source_target_pairs={{0,16},{16,0},{1,17},{17,1},{2,18},{18,2},{3,19},{19,3},{4,20},{20... | collective-permute-start | bytes 10616840 | tf_op jit(solution)/shard_map/ppermute | solution.py:40
  306.0 58.2 %copy-start.7 = (bf16[768,768]{1,0:T(8,128)(2,1)S(1)}, bf16[768,768]{1,0:T(8,128)(2,1)}, u32[]{:S(2)}) copy-start(bf16[768,768]{1,0:T(8,128)(2,1)} %copy-done.5) | copy-start | bytes 3538948
  306.0 58.2 %copy-start.10 = (bf16[768,768]{1,0:T(8,128)(2,1)S(1)}, bf16[768,768]{1,0:T(8,128)(2,1)}, u32[]{:S(2)}) copy-start(bf16[768,768]{1,0:T(8,128)(2,1)} %copy-done.8) | copy-start | bytes 3538948
  306.0 58.2 %copy-start.13 = (bf16[768,768]{1,0:T(8,128)(2,1)S(1)}, bf16[768,768]{1,0:T(8,128)(2,1)}, u32[]{:S(2)}) copy-start(bf16[768,768]{1,0:T(8,128)(2,1)} %copy-done.11) | copy-start | bytes 3538948
  306.0 58.2 %copy-start.25 = (f32[768,768]{1,0:T(8,128)S(1)}, f32[768,768]{1,0:T(8,128)}, u32[]{:S(2)}) copy-start(f32[768,768]{1,0:T(8,128)} %fusion.19) | copy-start | bytes 7077892
  435.1 24.4 %collective-permute-start.3 = (bf16[48,3,1024]{2,0,1:T(8,128)(2,1)}, bf16[48,3,1024]{2,0,1:T(8,128)(2,1)S(1)}, u32[]{:S(2)}, u32[]{:S(2)}) collective-permute-start(bf16[48,3,1024]{2,0,1:T(8,128)(2,1)} %reduce-scatter.2.cloned.1.call-done), channel_id=1, source_target_pairs={{0,0},{1,4},{2,8},{3,12},{4,1},{5,5},{6,9},{7,13},{8,2},{9,6},{10,... | collective-permute-start | bytes 884744 | tf_op jit(solution)/shard_map/ppermute | solution.py:137
  438.9 27.5 %collective-permute-start.4 = (bf16[48,3,1024]{2,0,1:T(8,128)(2,1)}, bf16[48,3,1024]{2,0,1:T(8,128)(2,1)S(1)}, u32[]{:S(2)}, u32[]{:S(2)}) collective-permute-start(bf16[48,3,1024]{2,0,1:T(8,128)(2,1)} %reduce-scatter.2.cloned.1.call-done), channel_id=1, source_target_pairs={{0,4},{1,8},{2,12},{3,0},{4,5},{5,9},{6,13},{7,1},{8,6},{9,10},{10... | collective-permute-start | bytes 884744 | tf_op jit(solution)/shard_map/ppermute | solution.py:137
  440.1 27.3 %collective-permute-start.5 = (bf16[48,3,1024]{2,0,1:T(8,128)(2,1)}, bf16[48,3,1024]{2,0,1:T(8,128)(2,1)S(1)}, u32[]{:S(2)}, u32[]{:S(2)}) collective-permute-start(bf16[48,3,1024]{2,0,1:T(8,128)(2,1)} %reduce-scatter.2.cloned.1.call-done), channel_id=1, source_target_pairs={{0,8},{1,12},{2,0},{3,4},{4,9},{5,13},{6,1},{7,5},{8,10},{9,14},{1... | collective-permute-start | bytes 884744 | tf_op jit(solution)/shard_map/ppermute | solution.py:137
  440.9 27.9 %collective-permute-start.6 = (bf16[48,3,1024]{2,0,1:T(8,128)(2,1)}, bf16[48,3,1024]{2,0,1:T(8,128)(2,1)S(1)}, u32[]{:S(2)}, u32[]{:S(2)}) collective-permute-start(bf16[48,3,1024]{2,0,1:T(8,128)(2,1)} %reduce-scatter.2.cloned.1.call-done), channel_id=1, source_target_pairs={{0,12},{1,0},{2,4},{3,8},{4,13},{5,1},{6,5},{7,9},{8,14},{9,2},{10... | collective-permute-start | bytes 884744 | tf_op jit(solution)/shard_map/ppermute | solution.py:137
  (10 other events, 35.9 us)
Sparse Core Ops, SparseCore 0:
  11.5 50.0 all-gather.4
  63.1 87.2 all-gather.6
  152.0 87.9 all-gather.8
  241.4 87.8 all-gather.10
  409.3 25.7 reduce-scatter.1

commit v11 on v10

--- a/solution.py
+++ b/solution.py
@@ -78,6 +78,7 @@
         else:
             step, _ = moved_weights(chunk, n_video)
             step.append(forward(step[2]))
+            step[3], frames = lax.optimization_barrier((step[3], frames))
         moved.append(step)
     wide = frames.astype(jnp.float32)
     center = wide - jnp.mean(wide, axis=-1, keepdims=True)

time: 485 us -> 464 us (0.957)
  waiting for transfers between devices: 286 us -> 263 us
  local copies, waits for them, and re-layouts: 37.3 us -> 44.2 us
    all_gather x3, waiting for transfers between devices: 135 us -> 120 us  [moved_weights(): gathered = lax.all_gather(mine, 'video', axis=0, tiled=True)]
    ppermute x3, waiting for transfers between devices: 99.9 us -> 91.7 us  [forward(): return lax.ppermute(onward, 'groups', [(0, 1), (1, 0)])]
  transfers between devices with their start and end apart: 12 -> 12, of which waited for: 11 -> 11; matrix products, arithmetic and copies ran while one was open for 24% -> 26% of each run, Pallas kernels for 0% -> 0%
where the time goes in v11:
time: 464 us; the launch traced here: 459 us
  waiting for transfers between devices  263 us (57%)
  matrix products  66.1 us (14%)
  local copies, waits for them, and re-layouts  44.2 us (10%)
  other arithmetic  36.9 us (8%)
  blocking collectives  22 us (5%)
  between operations  15 us (3%)
  starting transfers between devices  11.9 us (3%)
    all_gather x3, waiting for transfers between devices, moved_weights(): gathered = lax.all_gather(mine, 'video', axis=0, tiled=True)  120 us
    ppermute x3, waiting for transfers between devices, forward(): return lax.ppermute(onward, 'groups', [(0, 1), (1, 0)])  91.7 us
    ppermute x4, waiting for transfers between devices, per_device(): got = lax.ppermute(clip_rows, ('video', 'tensor'), pairs)  26.4 us
    reduce_scatter x1, waiting for transfers between devices, per_device(): lax.psum_scatter(partial_proj.astype(jnp.bfloat16), 'tensor', scatter_dim...  25.1 us
    dot_general x3, matrix products, per_device(): jnp.dot(rolled, received.reshape((n_video - 1) * half, width), preferred_...  17.7 us
    dot_general x3, matrix products, per_device(): jnp.dot(own_half, gathered.reshape(n_video * half, width), preferred_elem...  16.7 us
    all_gather x1, blocking collectives, per_device(): pooled_all = lax.all_gather(pooled, 'video', axis=0, tiled=True)  14.4 us
    convert_element_type x1, other arithmetic, per_device(): normed = normed.astype(jnp.bfloat16).reshape(patch_rows, frames.shape[2])  12.6 us
  transfers between devices with their start and end apart: 12, of which 11 were waited for; matrix products, arithmetic and copies ran while one was open for 26% of the time, Pallas kernels for 0%

profile of v11, /device:TPU:10, one launch (start us, length us, event | category | flops | bytes accessed | tf_op | source)
XLA Modules:
  0.0 459.4 jit_solution(10586164418597185783)
XLA Ops:
  6.5 2.8 fusion.68
  11.4 2.7 fusion.69
  15.5 2.4 copy.147
  17.9 43.7 %all-gather.5.cloned.1.call-done = bf16[3072,3,128]{0,2,1:T(8,128)(2,1)} async-done(((bf16[768,3,128]{0,2,1:T(8,128)(2,1)}), bf16[3072,3,128]{0,2,1:T(8,128)(2,1)}) %all-gather.5.cloned.1.call-update) | async-done | bytes 2359312 | tf_op jit(solution)/shard_map/all_gather | solution.py:31
  67.6 7.6 %all-reduce = s32[12]{0:T(128)S(1)} all-reduce(s32[12]{0:T(128)S(1)} %dynamic-update-slice), channel_id=1, replica_groups=mesh['groups'=2,'video'=4,'tensor'=4] {'video'}, use_global_device_ids=true, to_apply=%add | all-reduce | flops 12 | bytes 96 | tf_op jit(solution)/shard_map/optimization_barrier | solution.py:110
  83.5 21.5 %collective-permute-done = bf16[2304,3,128]{0,2,1:T(8,128)(2,1)} collective-permute-done((bf16[2304,3,128]{0,2,1:T(8,128)(2,1)}, bf16[2304,3,128]{0,2,1:T(8,128)(2,1)}, u32[]{:S(2)}, u32[]{:S(2)}) %collective-permute-start) | collective-permute-done | bytes 1769504 | tf_op jit(solution)/shard_map/ppermute | solution.py:40
  105.0 5.1 %convert_reduce_fusion = f32[3,256]{1,0:T(4,128)S(1)} fusion(bf16[3,256,6144]{2,1,0:T(8,128)(2,1)} %param.4), kind=kLoop, calls=%fused_computation.2 | loop fusion | flops 9436416 | bytes 9440256 | tf_op jit(solution)/shard_map/reduce_sum | solution.py:84
  110.1 40.4 %all-gather.7.cloned.1.call-done = bf16[3072,3,256]{0,2,1:T(8,128)(2,1)} async-done(((bf16[768,3,256]{0,2,1:T(8,128)(2,1)}), bf16[3072,3,256]{0,2,1:T(8,128)(2,1)}) %all-gather.7.cloned.1.call-update) | async-done | bytes 4718608 | tf_op jit(solution)/shard_map/all_gather | solution.py:31
  150.9 6.3 %fusion.2 = f32[3,256]{1,0:T(4,128)S(1)} fusion(bf16[3,256,6144]{2,1,0:T(8,128)(2,1)} %param.4, f32[3,256]{1,0:T(4,128)S(1)} %broadcast_multiply_fusion), kind=kLoop, calls=%fused_computation.5 | loop fusion | flops 18873600 | bytes 9443328 | tf_op jit(solution)/shard_map/reduce_sum | solution.py:85
  157.2 12.6 %fusion.3 = bf16[3,256,6144]{2,1,0:T(8,128)(2,1)} fusion(bf16[3,256,6144]{2,1,0:T(8,128)(2,1)} %param.4, f32[3,256]{1,0:T(4,128)S(1)} %add_rsqrt_fusion.10, f32[3,256]{1,0:T(4,128)S(1)} %broadcast_multiply_fusion), kind=kLoop, calls=%fused_computation.6 | loop fusion | flops 18874368 | bytes 18880512 | tf_op jit(solution)/shard_map/convert_element_type | solution.py:86
  169.8 4.0 constant_dynamic-slice_fusion.11
  173.9 5.0 %fusion.63 = f32[768,384]{1,0:T(8,128)S(1)} fusion(bf16[2304,384]{0,1:T(8,128)(2,1)} %bitcast.8, bf16[768,768]{1,0:T(8,128)(2,1)S(1)} %get-tuple-element.34, bf16[768,768]{1,0:T(8,128)(2,1)S(1)} %get-tuple-element.35, bf16[768,768]{1,0:T(8,128)(2,1)S(1)} %get-tuple-element.33), kind=kOutput, calls=%fused_computation.161 | convolution fusion | flops 1369571328 | bytes 6488064 | tf_op jit(solution)/shard_map/dot_general | solution.py:117
  179.0 2.6 fusion.66
  191.2 3.3 multiply_reduce_fusion.8
  196.2 3.9 fusion.22
  200.1 3.9 fusion.20
  204.1 35.9 %all-gather.9.cloned.1.call-done = bf16[3072,3,256]{0,2,1:T(8,128)(2,1)} async-done(((bf16[768,3,256]{0,2,1:T(8,128)(2,1)}), bf16[3072,3,256]{0,2,1:T(8,128)(2,1)}) %all-gather.9.cloned.1.call-update) | async-done | bytes 4718608 | tf_op jit(solution)/shard_map/all_gather | solution.py:31
  240.1 7.0 %fusion.65 = f32[768,768]{1,0:T(8,128)S(1)} fusion(bf16[3072,768]{0,1:T(8,128)(2,1)} %bitcast.178, bf16[768,768]{1,0:T(8,128)(2,1)S(1)} %copy-done.15, bf16[768,768]{1,0:T(8,128)(2,1)S(1)} %copy-done.18, bf16[768,768]{1,0:T(8,128)(2,1)} %copy-done.20, bf16[768,768]{1,0:T(8,128)(2,1)} %copy-done.21), kind=kOutput, calls=%fused_computation.163 | convolution fusion | flops 3642753024 | bytes 11796480 | tf_op jit(solution)/shard_map/dot_general | solution.py:114
  251.2 18.2 %collective-permute-done.1 = bf16[2304,3,256]{0,2,1:T(8,128)(2,1)} collective-permute-done((bf16[2304,3,256]{0,2,1:T(8,128)(2,1)}, bf16[2304,3,256]{0,2,1:T(8,128)(2,1)}, u32[]{:S(2)}, u32[]{:S(2)}) %collective-permute-start.1) | collective-permute-done | bytes 3538976 | tf_op jit(solution)/shard_map/ppermute | solution.py:40
  269.5 6.4 %add_add_fusion.1 = f32[768,768]{1,0:T(8,128)} fusion(f32[768,768]{1,0:T(8,128)S(1)} %copy-done.25, f32[768,768]{1,0:T(8,128)S(1)} %fusion.65, bf16[2304,768]{0,1:T(8,128)(2,1)} %bitcast.18, bf16[768,768]{1,0:T(8,128)(2,1)S(1)} %copy-done.9, bf16[768,768]{1,0:T(8,128)(2,1)S(1)} %copy-done.12, bf16[768,768]{1,0:T(8,128)(2,1)S(1)} %copy-done.6), kind=kOutput, calls=%fused_computation.15 | convolution fusion | flops 2729705472 | bytes 14155776 | tf_op jit(solution)/shard_map/dot_general | solution.py:117
  275.9 2.9 reshape.418
  285.0 7.1 %fusion.64 = f32[768,768]{1,0:T(8,128)S(1)} fusion(bf16[3072,768]{0,1:T(8,128)(2,1)} %bitcast.179, bf16[768,768]{1,0:T(8,128)(2,1)S(1)} %copy-done.16, bf16[768,768]{1,0:T(8,128)(2,1)S(1)} %copy-done.19, bf16[768,768]{1,0:T(8,128)(2,1)} %copy-done.20, bf16[768,768]{1,0:T(8,128)(2,1)} %copy-done.21), kind=kOutput, calls=%fused_computation.162 | convolution fusion | flops 3642753024 | bytes 11796480 | tf_op jit(solution)/shard_map/dot_general | solution.py:114
  292.1 51.9 %collective-permute-done.2 = bf16[2304,3,256]{0,2,1:T(8,128)(2,1)} collective-permute-done((bf16[2304,3,256]{0,2,1:T(8,128)(2,1)}, bf16[2304,3,256]{0,2,1:T(8,128)(2,1)}, u32[]{:S(2)}, u32[]{:S(2)}) %collective-permute-start.2) | collective-permute-done | bytes 3538976 | tf_op jit(solution)/shard_map/ppermute | solution.py:40
  344.0 6.4 %add_add_fusion = f32[768,768]{1,0:T(8,128)} fusion(f32[768,768]{1,0:T(8,128)S(1)} %copy-done.24, f32[768,768]{1,0:T(8,128)S(1)} %fusion.64, bf16[2304,768]{0,1:T(8,128)(2,1)} %bitcast.26, bf16[768,768]{1,0:T(8,128)(2,1)S(1)} %copy-done.10, bf16[768,768]{1,0:T(8,128)(2,1)S(1)} %copy-done.13, bf16[768,768]{1,0:T(8,128)(2,1)S(1)} %copy-done.7), kind=kOutput, calls=%fused_computation.14 | convolution fusion | flops 2729705472 | bytes 14155776 | tf_op jit(solution)/shard_map/dot_general | solution.py:117
  350.4 2.9 reshape.423
  357.5 10.9 %fusion.7 = f32[3,256,3,1,128]{1,4,2,0,3:T(8,128)S(1)} fusion(bf16[6144,3,128]{0,2,1:T(8,128)(2,1)} %all-gather.11.cloned.1.call-done, bf16[3,256,6144]{2,1,0:T(8,128)(2,1)} %fusion.3), kind=kOutput, calls=%fused_computation.22 | convolution fusion | flops 3623878656 | bytes 15335424 | tf_op jit(solution)/shard_map/dot_general | solution.py:104
  369.5 14.4 %all_gather.23 = bf16[192,768]{1,0:T(8,128)(2,1)S(1)} all-gather(bf16[48,768]{1,0:T(8,128)(2,1)S(1)} %pad_maximum_fusion.6), channel_id=1, replica_groups=mesh['groups'=2,'video'=4,'tensor'=4] {'video'}, dimensions={0}, use_global_device_ids=true | all-gather | bytes 368640 | tf_op jit(solution)/shard_map/all_gather | solution.py:123
  383.8 4.5 convolution_convert_fusion
  389.5 25.1 %reduce-scatter.2.cloned.1.call-done = bf16[48,3,1024]{2,0,1:T(8,128)(2,1)} async-done(((bf16[192,3,1024]{2,0,1:T(8,128)(2,1)}), bf16[48,3,1024]{2,0,1:T(8,128)(2,1)}) %reduce-scatter.2.cloned.1.call-update) | async-done | bytes 294928 | tf_op jit(solution)/shard_map/reduce_scatter | solution.py:128
  414.6 3.7 collective-permute-start.3
  421.9 17.2 %collective-permute-done.3 = bf16[48,3,1024]{2,0,1:T(8,128)(2,1)S(1)} collective-permute-done((bf16[48,3,1024]{2,0,1:T(8,128)(2,1)}, bf16[48,3,1024]{2,0,1:T(8,128)(2,1)S(1)}, u32[]{:S(2)}, u32[]{:S(2)}) %collective-permute-start.3) | collective-permute-done | bytes 294944 | tf_op jit(solution)/shard_map/ppermute | solution.py:138
  439.1 6.7 %collective-permute-done.4 = bf16[48,3,1024]{2,0,1:T(8,128)(2,1)S(1)} collective-permute-done((bf16[48,3,1024]{2,0,1:T(8,128)(2,1)}, bf16[48,3,1024]{2,0,1:T(8,128)(2,1)S(1)}, u32[]{:S(2)}, u32[]{:S(2)}) %collective-permute-start.4) | collective-permute-done | bytes 294944 | tf_op jit(solution)/shard_map/ppermute | solution.py:138
  (181 shorter events, 55.3 us)
Async XLA Ops:
  6.5 55.0 %all-gather.5.cloned.1.call-start = ((), (), s32[]{:S(2)}) async-start(), calls=%async_computation.1 | async-start | bytes 2949120 | tf_op jit(solution)/shard_map/all_gather | solution.py:31
  11.4 139.2 %all-gather.7.cloned.1.call-start = ((), (), s32[]{:S(2)}) async-start(), calls=%async_computation.2 | async-start | bytes 5898240 | tf_op jit(solution)/shard_map/all_gather | solution.py:31
  61.6 178.4 %all-gather.9.cloned.1.call-start = ((), (), s32[]{:S(2)}) async-start(), calls=%async_computation.3 | async-start | bytes 5898240 | tf_op jit(solution)/shard_map/all_gather | solution.py:31
  64.6 40.4 %collective-permute-start = (bf16[2304,3,128]{0,2,1:T(8,128)(2,1)}, bf16[2304,3,128]{0,2,1:T(8,128)(2,1)}, u32[]{:S(2)}, u32[]{:S(2)}) collective-permute-start(bf16[2304,3,128]{0,2,1:T(8,128)(2,1)} %pad_maximum_fusion.4), channel_id=1, source_target_pairs={{0,16},{16,0},{1,17},{17,1},{2,18},{18,2},{3,19},{19,3},{4,20},{20... | collective-permute-start | bytes 5308424 | tf_op jit(solution)/shard_map/ppermute | solution.py:40
  150.6 206.9 %all-gather.11.cloned.1.call-start = ((), (), s32[]{:S(2)}) async-start(), calls=%async_computation.4 | async-start | bytes 5898240 | tf_op jit(solution)/shard_map/all_gather | solution.py:75
  173.8 5.1 %copy-start.5 = (bf16[768,768]{1,0:T(8,128)(2,1)}, bf16[768,768]{1,0:T(8,128)(2,1)S(1)}, u32[]{:S(2)}) copy-start(bf16[768,768]{1,0:T(8,128)(2,1)S(1)} %get-tuple-element.33) | copy-start | bytes 3538948
  173.8 5.1 %copy-start.8 = (bf16[768,768]{1,0:T(8,128)(2,1)}, bf16[768,768]{1,0:T(8,128)(2,1)S(1)}, u32[]{:S(2)}) copy-start(bf16[768,768]{1,0:T(8,128)(2,1)S(1)} %get-tuple-element.34) | copy-start | bytes 3538948
  173.8 5.1 %copy-start.11 = (bf16[768,768]{1,0:T(8,128)(2,1)}, bf16[768,768]{1,0:T(8,128)(2,1)S(1)}, u32[]{:S(2)}) copy-start(bf16[768,768]{1,0:T(8,128)(2,1)S(1)} %get-tuple-element.35) | copy-start | bytes 3538948
  173.8 5.1 %copy-start.14 = (bf16[768,768]{1,0:T(8,128)(2,1)}, bf16[768,768]{1,0:T(8,128)(2,1)S(1)}, u32[]{:S(2)}) copy-start(bf16[768,768]{1,0:T(8,128)(2,1)S(1)} %get-tuple-element.36) | copy-start | bytes 3538948
  173.8 5.1 %copy-start.17 = (bf16[768,768]{1,0:T(8,128)(2,1)}, bf16[768,768]{1,0:T(8,128)(2,1)S(1)}, u32[]{:S(2)}) copy-start(bf16[768,768]{1,0:T(8,128)(2,1)S(1)} %get-tuple-element.37) | copy-start | bytes 3538948
  173.9 5.1 %copy-start.20 = (bf16[768,768]{1,0:T(8,128)(2,1)}, bf16[768,768]{1,0:T(8,128)(2,1)S(1)}, u32[]{:S(2)}) copy-start(bf16[768,768]{1,0:T(8,128)(2,1)S(1)} %get-tuple-element.38) | copy-start | bytes 3538948
  173.9 5.1 %copy-start.21 = (bf16[768,768]{1,0:T(8,128)(2,1)}, bf16[768,768]{1,0:T(8,128)(2,1)S(1)}, u32[]{:S(2)}) copy-start(bf16[768,768]{1,0:T(8,128)(2,1)S(1)} %get-tuple-element.39) | copy-start | bytes 3538948
  173.9 5.1 %copy-start.2 = (bf16[3072,3,128]{0,2,1:T(8,128)(2,1)S(1)}, bf16[3072,3,128]{0,2,1:T(8,128)(2,1)}, u32[]{:S(2)}) copy-start(bf16[3072,3,128]{0,2,1:T(8,128)(2,1)} %all-gather.5.cloned.1.call-done) | copy-start | bytes 7077892
  189.7 79.7 %collective-permute-start.1 = (bf16[2304,3,256]{0,2,1:T(8,128)(2,1)}, bf16[2304,3,256]{0,2,1:T(8,128)(2,1)}, u32[]{:S(2)}, u32[]{:S(2)}) collective-permute-start(bf16[2304,3,256]{0,2,1:T(8,128)(2,1)} %pad_maximum_fusion.2), channel_id=1, source_target_pairs={{0,16},{16,0},{1,17},{17,1},{2,18},{18,2},{3,19},{19,3},{4,20},{20... | collective-permute-start | bytes 10616840 | tf_op jit(solution)/shard_map/ppermute | solution.py:40
  200.1 39.9 %copy-start.15 = (bf16[768,768]{1,0:T(8,128)(2,1)S(1)}, bf16[768,768]{1,0:T(8,128)(2,1)}, u32[]{:S(2)}) copy-start(bf16[768,768]{1,0:T(8,128)(2,1)} %copy-done.14) | copy-start | bytes 3538948
  200.1 39.9 %copy-start.18 = (bf16[768,768]{1,0:T(8,128)(2,1)S(1)}, bf16[768,768]{1,0:T(8,128)(2,1)}, u32[]{:S(2)}) copy-start(bf16[768,768]{1,0:T(8,128)(2,1)} %copy-done.17) | copy-start | bytes 3538948
  240.0 7.1 %slice-start = ((s8[4718592]{0:T(1024)(128)(4,1)}), s8[524288]{0:T(1024)(128)(4,1)S(1)}, s32[]{:S(2)}) async-start(s8[4718592]{0:T(1024)(128)(4,1)} %bitcast.180), calls=%async_computation.6 | async-start | bytes 1048576
  240.0 174.6 %reduce-scatter.2.cloned.1.call-start = ((), (), s32[]{:S(2)}) async-start(), calls=%async_computation.5 | async-start | bytes 1474560 | tf_op jit(solution)/shard_map/reduce_scatter | solution.py:128
  240.1 7.1 %slice-start.1 = ((s8[4718592]{0:T(1024)(128)(4,1)}), s8[4194304]{0:T(1024)(128)(4,1)S(1)}, s32[]{:S(2)}) async-start(s8[4718592]{0:T(1024)(128)(4,1)} %bitcast.180), calls=%async_computation.7 | async-start | bytes 8388608
  247.5 21.9 %copy-start.6 = (bf16[768,768]{1,0:T(8,128)(2,1)S(1)}, bf16[768,768]{1,0:T(8,128)(2,1)}, u32[]{:S(2)}) copy-start(bf16[768,768]{1,0:T(8,128)(2,1)} %copy-done.5) | copy-start | bytes 3538948
  247.6 21.9 %copy-start.9 = (bf16[768,768]{1,0:T(8,128)(2,1)S(1)}, bf16[768,768]{1,0:T(8,128)(2,1)}, u32[]{:S(2)}) copy-start(bf16[768,768]{1,0:T(8,128)(2,1)} %copy-done.8) | copy-start | bytes 3538948
  247.6 21.9 %copy-start.12 = (bf16[768,768]{1,0:T(8,128)(2,1)S(1)}, bf16[768,768]{1,0:T(8,128)(2,1)}, u32[]{:S(2)}) copy-start(bf16[768,768]{1,0:T(8,128)(2,1)} %copy-done.11) | copy-start | bytes 3538948
  247.6 21.9 %copy-start.25 = (f32[768,768]{1,0:T(8,128)S(1)}, f32[768,768]{1,0:T(8,128)}, u32[]{:S(2)}) copy-start(f32[768,768]{1,0:T(8,128)} %fusion.22) | copy-start | bytes 7077892
  249.8 94.3 %collective-permute-start.2 = (bf16[2304,3,256]{0,2,1:T(8,128)(2,1)}, bf16[2304,3,256]{0,2,1:T(8,128)(2,1)}, u32[]{:S(2)}, u32[]{:S(2)}) collective-permute-start(bf16[2304,3,256]{0,2,1:T(8,128)(2,1)} %pad_maximum_fusion.3), channel_id=1, source_target_pairs={{0,16},{16,0},{1,17},{17,1},{2,18},{18,2},{3,19},{19,3},{4,20},{20... | collective-permute-start | bytes 10616840 | tf_op jit(solution)/shard_map/ppermute | solution.py:40
  285.0 59.1 %copy-start.7 = (bf16[768,768]{1,0:T(8,128)(2,1)S(1)}, bf16[768,768]{1,0:T(8,128)(2,1)}, u32[]{:S(2)}) copy-start(bf16[768,768]{1,0:T(8,128)(2,1)} %copy-done.5) | copy-start | bytes 3538948
  285.0 59.1 %copy-start.10 = (bf16[768,768]{1,0:T(8,128)(2,1)S(1)}, bf16[768,768]{1,0:T(8,128)(2,1)}, u32[]{:S(2)}) copy-start(bf16[768,768]{1,0:T(8,128)(2,1)} %copy-done.8) | copy-start | bytes 3538948
  285.0 59.0 %copy-start.13 = (bf16[768,768]{1,0:T(8,128)(2,1)S(1)}, bf16[768,768]{1,0:T(8,128)(2,1)}, u32[]{:S(2)}) copy-start(bf16[768,768]{1,0:T(8,128)(2,1)} %copy-done.11) | copy-start | bytes 3538948
  285.0 59.0 %copy-start.24 = (f32[768,768]{1,0:T(8,128)S(1)}, f32[768,768]{1,0:T(8,128)}, u32[]{:S(2)}) copy-start(f32[768,768]{1,0:T(8,128)} %fusion.20) | copy-start | bytes 7077892
  414.6 24.5 %collective-permute-start.3 = (bf16[48,3,1024]{2,0,1:T(8,128)(2,1)}, bf16[48,3,1024]{2,0,1:T(8,128)(2,1)S(1)}, u32[]{:S(2)}, u32[]{:S(2)}) collective-permute-start(bf16[48,3,1024]{2,0,1:T(8,128)(2,1)} %reduce-scatter.2.cloned.1.call-done), channel_id=1, source_target_pairs={{0,0},{1,4},{2,8},{3,12},{4,1},{5,5},{6,9},{7,13},{8,2},{9,6},{10,... | collective-permute-start | bytes 884744 | tf_op jit(solution)/shard_map/ppermute | solution.py:138
  418.3 27.5 %collective-permute-start.4 = (bf16[48,3,1024]{2,0,1:T(8,128)(2,1)}, bf16[48,3,1024]{2,0,1:T(8,128)(2,1)S(1)}, u32[]{:S(2)}, u32[]{:S(2)}) collective-permute-start(bf16[48,3,1024]{2,0,1:T(8,128)(2,1)} %reduce-scatter.2.cloned.1.call-done), channel_id=1, source_target_pairs={{0,4},{1,8},{2,12},{3,0},{4,5},{5,9},{6,13},{7,1},{8,6},{9,10},{10... | collective-permute-start | bytes 884744 | tf_op jit(solution)/shard_map/ppermute | solution.py:138
  419.5 27.3 %collective-permute-start.5 = (bf16[48,3,1024]{2,0,1:T(8,128)(2,1)}, bf16[48,3,1024]{2,0,1:T(8,128)(2,1)S(1)}, u32[]{:S(2)}, u32[]{:S(2)}) collective-permute-start(bf16[48,3,1024]{2,0,1:T(8,128)(2,1)} %reduce-scatter.2.cloned.1.call-done), channel_id=1, source_target_pairs={{0,8},{1,12},{2,0},{3,4},{4,9},{5,13},{6,1},{7,5},{8,10},{9,14},{1... | collective-permute-start | bytes 884744 | tf_op jit(solution)/shard_map/ppermute | solution.py:138
  420.4 28.0 %collective-permute-start.6 = (bf16[48,3,1024]{2,0,1:T(8,128)(2,1)}, bf16[48,3,1024]{2,0,1:T(8,128)(2,1)S(1)}, u32[]{:S(2)}, u32[]{:S(2)}) collective-permute-start(bf16[48,3,1024]{2,0,1:T(8,128)(2,1)} %reduce-scatter.2.cloned.1.call-done), channel_id=1, source_target_pairs={{0,12},{1,0},{2,4},{3,8},{4,13},{5,1},{6,5},{7,9},{8,14},{9,2},{10... | collective-permute-start | bytes 884744 | tf_op jit(solution)/shard_map/ppermute | solution.py:138
  (8 other events, 20.0 us)
Sparse Core Ops, SparseCore 0:
  11.5 50.0 all-gather.4
  63.1 87.3 all-gather.6
  152.1 87.7 all-gather.8
  241.4 87.8 all-gather.10
  388.5 26.0 reduce-scatter.1

commit v12 on v11

--- a/solution.py
+++ b/solution.py
@@ -75,6 +75,7 @@
             step = [lax.all_gather(whole_rows, "video", axis=0, tiled=True), None, None]
         elif moved:
             step, moved[-1][1] = moved_weights(chunk, n_video, after=moved[-1][1])
+            step.append(forward(step[2]))
         else:
             step, _ = moved_weights(chunk, n_video)
             step.append(forward(step[2]))
@@ -95,6 +96,8 @@
     rolled = jnp.concatenate(
         [columns((v + 1 + i) % n_video, 1 - g) for i in range(n_video - 1)], axis=1
     )
+    if len(moved) > 2 and moved[1][3] is not None:
+        moved[1][3], own_half = lax.optimization_barrier((moved[1][3], own_half))
     video_all = lax.all_gather(frame_video, "video", axis=0, tiled=True)
     pooled_parts = []
     for index, size in enumerate(sizes):
@@ -104,12 +107,9 @@
             proj = jnp.dot(normed, full, preferred_element_type=jnp.float32)
             pooled_parts.append(attend(proj, nframes, size, scale, blocks, inner))
             continue
-        other, gathered, onward = moved[index][:3]
+        other, gathered, onward, received = moved[index]
         if index == 0:
-            received = moved[index][3]
             video_all, received = lax.optimization_barrier((video_all, received))
-        else:
-            received = forward(onward)
         proj = jnp.dot(own_piece, other.reshape(half, width), preferred_element_type=jnp.float32)
         proj = proj + jnp.dot(
             own_half, gathered.reshape(n_video * half, width), preferred_element_type=jnp.float32

time: 464 us -> 458 us (0.987)
  local copies, waits for them, and re-layouts: 44.2 us -> 57.6 us
  waiting for transfers between devices: 263 us -> 250 us
    all_gather x3, waiting for transfers between devices: 120 us -> 77.7 us  [moved_weights(): gathered = lax.all_gather(mine, 'video', axis=0, tiled=True)]
    ppermute x3, waiting for transfers between devices: 91.7 us -> 121 us  [forward(): return lax.ppermute(onward, 'groups', [(0, 1), (1, 0)])]
    reshape x3, local copies, waits for them, and re-layouts: 6.8 us -> 19 us  [attend(): proj = proj.reshape(nframes, PATCH, 3, heads, HD)]
    unnamed x74 -> x56, local copies, waits for them, and re-layouts: 9.57 us -> 11.9 us
  transfers between devices with their start and end apart: 12 -> 12, of which waited for: 11 -> 10; matrix products, arithmetic and copies ran while one was open for 26% -> 28% of each run, Pallas kernels for 0% -> 0%
where the time goes in v12:
time: 458 us
  waiting for transfers between devices  250 us (55%)
  matrix products  64.5 us (14%)
  local copies, waits for them, and re-layouts  57.6 us (13%)
  other arithmetic  35.8 us (8%)
  blocking collectives  22.6 us (5%)
  between operations  14.9 us (3%)
  starting transfers between devices  11.8 us (3%)
    ppermute x3, waiting for transfers between devices, forward(): return lax.ppermute(onward, 'groups', [(0, 1), (1, 0)])  121 us
    all_gather x3, waiting for transfers between devices, moved_weights(): gathered = lax.all_gather(mine, 'video', axis=0, tiled=True)  77.7 us
    ppermute x4, waiting for transfers between devices, per_device(): got = lax.ppermute(clip_rows, ('video', 'tensor'), pairs)  26.4 us
    reduce_scatter x1, waiting for transfers between devices, per_device(): lax.psum_scatter(partial_proj.astype(jnp.bfloat16), 'tensor', scatter_dim...  24.8 us
    reshape x3, local copies, waits for them, and re-layouts, attend(): proj = proj.reshape(nframes, PATCH, 3, heads, HD)  19 us
    dot_general x3, matrix products, per_device(): jnp.dot(own_half, gathered.reshape(n_video * half, width), preferred_elem...  17.1 us
    dot_general x3, matrix products, per_device(): jnp.dot(rolled, received.reshape((n_video - 1) * half, width), preferred_...  16.6 us
    all_gather x1, blocking collectives, per_device(): pooled_all = lax.all_gather(pooled, 'video', axis=0, tiled=True)  15 us
  transfers between devices with their start and end apart: 12, of which 10 were waited for; matrix products, arithmetic and copies ran while one was open for 28% of the time, Pallas kernels for 0%

profile of v12, /device:TPU:10, one launch (start us, length us, event | category | flops | bytes accessed | tf_op | source)
XLA Modules:
  0.0 457.6 jit_solution(10416039511466223369)
XLA Ops:
  6.5 2.8 fusion.66
  11.4 2.7 fusion.67
  15.5 2.4 copy.147
  17.9 43.7 %all-gather.5.cloned.1.call-done = bf16[3072,3,128]{0,2,1:T(8,128)(2,1)} async-done(((bf16[768,3,128]{0,2,1:T(8,128)(2,1)}), bf16[3072,3,128]{0,2,1:T(8,128)(2,1)}) %all-gather.5.cloned.1.call-update) | async-done | bytes 2359312 | tf_op jit(solution)/shard_map/all_gather | solution.py:31
  67.6 7.6 %all-reduce = s32[12]{0:T(128)S(1)} all-reduce(s32[12]{0:T(128)S(1)} %dynamic-update-slice), channel_id=1, replica_groups=mesh['groups'=2,'video'=4,'tensor'=4] {'video'}, use_global_device_ids=true, to_apply=%add | all-reduce | flops 12 | bytes 96 | tf_op jit(solution)/shard_map/optimization_barrier | solution.py:112
  83.4 21.6 %collective-permute-done = bf16[2304,3,128]{0,2,1:T(8,128)(2,1)} collective-permute-done((bf16[2304,3,128]{0,2,1:T(8,128)(2,1)}, bf16[2304,3,128]{0,2,1:T(8,128)(2,1)}, u32[]{:S(2)}, u32[]{:S(2)}) %collective-permute-start) | collective-permute-done | bytes 1769504 | tf_op jit(solution)/shard_map/ppermute | solution.py:40
  105.0 5.1 %convert_reduce_fusion = f32[3,256]{1,0:T(4,128)S(1)} fusion(bf16[3,256,6144]{2,1,0:T(8,128)(2,1)} %param.4), kind=kLoop, calls=%fused_computation.2 | loop fusion | flops 9436416 | bytes 9440256 | tf_op jit(solution)/shard_map/reduce_sum | solution.py:85
  110.2 6.3 %fusion.2 = f32[3,256]{1,0:T(4,128)S(1)} fusion(bf16[3,256,6144]{2,1,0:T(8,128)(2,1)} %param.4, f32[3,256]{1,0:T(4,128)S(1)} %broadcast_multiply_fusion), kind=kLoop, calls=%fused_computation.5 | loop fusion | flops 18873600 | bytes 9443328 | tf_op jit(solution)/shard_map/reduce_sum | solution.py:86
  116.5 34.0 %all-gather.7.cloned.1.call-done = bf16[3072,3,256]{0,2,1:T(8,128)(2,1)} async-done(((bf16[768,3,256]{0,2,1:T(8,128)(2,1)}), bf16[3072,3,256]{0,2,1:T(8,128)(2,1)}) %all-gather.7.cloned.1.call-update) | async-done | bytes 4718608 | tf_op jit(solution)/shard_map/all_gather | solution.py:31
  155.1 12.2 %fusion.3 = bf16[3,256,6144]{2,1,0:T(8,128)(2,1)} fusion(bf16[3,256,6144]{2,1,0:T(8,128)(2,1)} %param.4, f32[3,256]{1,0:T(4,128)S(1)} %add_rsqrt_fusion.10, f32[3,256]{1,0:T(4,128)S(1)} %broadcast_multiply_fusion), kind=kLoop, calls=%fused_computation.6 | loop fusion | flops 18874368 | bytes 18880512 | tf_op jit(solution)/shard_map/convert_element_type | solution.py:87
  169.7 4.0 fusion.22
  173.7 3.8 fusion.20
  177.5 2.5 constant_dynamic-slice_fusion.8
  183.2 3.7 fusion.64
  186.9 45.0 %collective-permute-done.1 = bf16[2304,3,256]{0,2,1:T(8,128)(2,1)} collective-permute-done((bf16[2304,3,256]{0,2,1:T(8,128)(2,1)S(1)}, bf16[2304,3,256]{0,2,1:T(8,128)(2,1)}, u32[]{:S(2)}, u32[]{:S(2)}) %collective-permute-start.1) | collective-permute-done | bytes 3538976 | tf_op jit(solution)/shard_map/ppermute | solution.py:40
  231.9 2.7 fusion.12
  234.6 13.2 %reshape.413 = f32[3,256,3,1,128]{4,2,1,0,3:T(4,128)S(1)} reshape(f32[768,384]{1,0:T(8,128)S(1)} %fusion.12) | data formatting | bytes 2359296 | tf_op jit(solution)/shard_map/reshape | solution.py:44
  248.6 3.3 multiply_reduce_fusion.8
  252.8 7.2 %fusion.71 = f32[768,768]{1,0:T(8,128)S(1)} fusion(bf16[768,3072]{1,0:T(8,128)(2,1)} %copy-done.1, bf16[3072,768]{0,1:T(8,128)(2,1)} %bitcast.181), kind=kOutput, calls=%fused_computation.169 | convolution fusion | flops 3623878656 | bytes 11796480 | tf_op jit(solution)/shard_map/dot_general | solution.py:114
  266.3 6.6 %add_add_fusion.1 = f32[768,768]{1,0:T(8,128)} fusion(f32[768,768]{1,0:T(8,128)S(1)} %copy-done.18, f32[768,768]{1,0:T(8,128)S(1)} %fusion.71, bf16[2304,768]{0,1:T(8,128)(2,1)} %bitcast.18, bf16[768,768]{1,0:T(8,128)(2,1)S(1)} %copy-done.10, bf16[768,768]{1,0:T(8,128)(2,1)S(1)} %copy-done.13, bf16[768,768]{1,0:T(8,128)(2,1)S(1)} %copy-done.7), kind=kOutput, calls=%fused_computation.15 | convolution fusion | flops 2729705472 | bytes 14155776 | tf_op jit(solution)/shard_map/dot_general | solution.py:117
  272.9 2.9 reshape.418
  279.9 7.3 %fusion.72 = f32[768,768]{1,0:T(8,128)S(1)} fusion(bf16[768,3072]{1,0:T(8,128)(2,1)} %copy-done.1, bf16[3072,768]{0,1:T(8,128)(2,1)} %bitcast.182), kind=kOutput, calls=%fused_computation.170 | convolution fusion | flops 3623878656 | bytes 11796480 | tf_op jit(solution)/shard_map/dot_general | solution.py:114
  287.2 54.8 %collective-permute-done.2 = bf16[2304,3,256]{0,2,1:T(8,128)(2,1)} collective-permute-done((bf16[2304,3,256]{0,2,1:T(8,128)(2,1)}, bf16[2304,3,256]{0,2,1:T(8,128)(2,1)}, u32[]{:S(2)}, u32[]{:S(2)}) %collective-permute-start.2) | collective-permute-done | bytes 3538976 | tf_op jit(solution)/shard_map/ppermute | solution.py:40
  342.0 6.4 %add_add_fusion = f32[768,768]{1,0:T(8,128)} fusion(f32[768,768]{1,0:T(8,128)S(1)} %copy-done.17, f32[768,768]{1,0:T(8,128)S(1)} %fusion.72, bf16[2304,768]{0,1:T(8,128)(2,1)} %bitcast.26, bf16[768,768]{1,0:T(8,128)(2,1)S(1)} %copy-done.11, bf16[768,768]{1,0:T(8,128)(2,1)S(1)} %copy-done.14, bf16[768,768]{1,0:T(8,128)(2,1)S(1)} %copy-done.8), kind=kOutput, calls=%fused_computation.14 | convolution fusion | flops 2729705472 | bytes 14155776 | tf_op jit(solution)/shard_map/dot_general | solution.py:117
  348.4 2.9 reshape.423
  355.2 11.1 %fusion.7 = f32[3,256,3,1,128]{1,4,2,0,3:T(8,128)S(1)} fusion(bf16[6144,3,128]{0,2,1:T(8,128)(2,1)} %all-gather.11.cloned.1.call-done, bf16[3,256,6144]{2,1,0:T(8,128)(2,1)} %fusion.3), kind=kOutput, calls=%fused_computation.22 | convolution fusion | flops 3623878656 | bytes 15335424 | tf_op jit(solution)/shard_map/dot_general | solution.py:107
  367.4 15.0 %all_gather.23 = bf16[192,768]{1,0:T(8,128)(2,1)S(1)} all-gather(bf16[48,768]{1,0:T(8,128)(2,1)S(1)} %pad_maximum_fusion.6), channel_id=1, replica_groups=mesh['groups'=2,'video'=4,'tensor'=4] {'video'}, dimensions={0}, use_global_device_ids=true | all-gather | bytes 368640 | tf_op jit(solution)/shard_map/all_gather | solution.py:123
  382.4 4.5 convolution_convert_fusion
  388.1 24.8 %reduce-scatter.2.cloned.1.call-done = bf16[48,3,1024]{2,0,1:T(8,128)(2,1)} async-done(((bf16[192,3,1024]{2,0,1:T(8,128)(2,1)}), bf16[48,3,1024]{2,0,1:T(8,128)(2,1)}) %reduce-scatter.2.cloned.1.call-update) | async-done | bytes 294928 | tf_op jit(solution)/shard_map/reduce_scatter | solution.py:128
  412.8 3.7 collective-permute-start.3
  420.2 17.2 %collective-permute-done.3 = bf16[48,3,1024]{2,0,1:T(8,128)(2,1)S(1)} collective-permute-done((bf16[48,3,1024]{2,0,1:T(8,128)(2,1)}, bf16[48,3,1024]{2,0,1:T(8,128)(2,1)S(1)}, u32[]{:S(2)}, u32[]{:S(2)}) %collective-permute-start.3) | collective-permute-done | bytes 294944 | tf_op jit(solution)/shard_map/ppermute | solution.py:138
  437.3 6.8 %collective-permute-done.4 = bf16[48,3,1024]{2,0,1:T(8,128)(2,1)S(1)} collective-permute-done((bf16[48,3,1024]{2,0,1:T(8,128)(2,1)}, bf16[48,3,1024]{2,0,1:T(8,128)(2,1)S(1)}, u32[]{:S(2)}, u32[]{:S(2)}) %collective-permute-start.4) | collective-permute-done | bytes 294944 | tf_op jit(solution)/shard_map/ppermute | solution.py:138
  (163 shorter events, 55.2 us)
Async XLA Ops:
  6.5 55.0 %all-gather.5.cloned.1.call-start = ((), (), s32[]{:S(2)}) async-start(), calls=%async_computation.1 | async-start | bytes 2949120 | tf_op jit(solution)/shard_map/all_gather | solution.py:31
  11.4 139.1 %all-gather.7.cloned.1.call-start = ((), (), s32[]{:S(2)}) async-start(), calls=%async_computation.2 | async-start | bytes 5898240 | tf_op jit(solution)/shard_map/all_gather | solution.py:31
  61.6 198.4 %all-gather.9.cloned.1.call-start = ((), (), s32[]{:S(2)}) async-start(), calls=%async_computation.3 | async-start | bytes 5898240 | tf_op jit(solution)/shard_map/all_gather | solution.py:31
  63.2 2.8 copy-start.16
  63.2 4.1 copy-start.15
  64.6 40.4 %collective-permute-start = (bf16[2304,3,128]{0,2,1:T(8,128)(2,1)}, bf16[2304,3,128]{0,2,1:T(8,128)(2,1)}, u32[]{:S(2)}, u32[]{:S(2)}) collective-permute-start(bf16[2304,3,128]{0,2,1:T(8,128)(2,1)} %pad_maximum_fusion.4), channel_id=1, source_target_pairs={{0,16},{16,0},{1,17},{17,1},{2,18},{18,2},{3,19},{19,3},{4,20},{20... | collective-permute-start | bytes 5308424 | tf_op jit(solution)/shard_map/ppermute | solution.py:40
  78.9 1.5 copy-start.2
  150.5 204.7 %all-gather.11.cloned.1.call-start = ((), (), s32[]{:S(2)}) async-start(), calls=%async_computation.4 | async-start | bytes 5898240 | tf_op jit(solution)/shard_map/all_gather | solution.py:75
  153.5 78.4 %collective-permute-start.1 = (bf16[2304,3,256]{0,2,1:T(8,128)(2,1)S(1)}, bf16[2304,3,256]{0,2,1:T(8,128)(2,1)}, u32[]{:S(2)}, u32[]{:S(2)}) collective-permute-start(bf16[2304,3,256]{0,2,1:T(8,128)(2,1)S(1)} %pad_maximum_fusion.1), channel_id=1, source_target_pairs={{0,16},{16,0},{1,17},{17,1},{2,18},{18,2},{3,19},{19,3},{4,20},{20... | collective-permute-start | bytes 10616840 | tf_op jit(solution)/shard_map/ppermute | solution.py:40
  167.3 2.4 copy-start.4
  167.3 6.4 %copy-start.5 = (bf16[768,3,256]{0,2,1:T(8,128)(2,1)S(1)}, bf16[768,3,256]{0,2,1:T(8,128)(2,1)}, u32[]{:S(2)}) copy-start(bf16[768,3,256]{0,2,1:T(8,128)(2,1)} %copy.153) | copy-start | bytes 3538948
  169.7 7.8 %copy-start = (bf16[3,256,6144]{2,1,0:T(8,128)(2,1)S(1)}, bf16[3,256,6144]{2,1,0:T(8,128)(2,1)}, u32[]{:S(2)}) copy-start(bf16[3,256,6144]{2,1,0:T(8,128)(2,1)} %fusion.3) | copy-start | bytes 28311556
  179.9 1.0 copy-start.6
  179.9 2.0 copy-start.9
  179.9 3.3 copy-start.12
  180.6 51.4 %copy-start.1 = (bf16[768,3072]{1,0:T(8,128)(2,1)}, bf16[768,3072]{1,0:T(8,128)(2,1)S(1)}, u32[]{:S(2)}) copy-start(bf16[768,3072]{1,0:T(8,128)(2,1)S(1)} %pad_maximum_fusion) | copy-start | bytes 14155780
  183.2 48.7 %copy-start.3 = (bf16[3072,3,128]{0,2,1:T(8,128)(2,1)S(1)}, bf16[3072,3,128]{0,2,1:T(8,128)(2,1)}, u32[]{:S(2)}) copy-start(bf16[3072,3,128]{0,2,1:T(8,128)(2,1)} %all-gather.5.cloned.1.call-done) | copy-start | bytes 7077892
  260.0 152.8 %reduce-scatter.2.cloned.1.call-start = ((), (), s32[]{:S(2)}) async-start(), calls=%async_computation.5 | async-start | bytes 1474560 | tf_op jit(solution)/shard_map/reduce_scatter | solution.py:128
  262.3 3.5 copy-start.7
  262.3 3.5 copy-start.10
  262.3 3.5 copy-start.13
  262.3 4.0 copy-start.18
  264.3 77.7 %collective-permute-start.2 = (bf16[2304,3,256]{0,2,1:T(8,128)(2,1)}, bf16[2304,3,256]{0,2,1:T(8,128)(2,1)}, u32[]{:S(2)}, u32[]{:S(2)}) collective-permute-start(bf16[2304,3,256]{0,2,1:T(8,128)(2,1)} %pad_maximum_fusion.3), channel_id=1, source_target_pairs={{0,16},{16,0},{1,17},{17,1},{2,18},{18,2},{3,19},{19,3},{4,20},{20... | collective-permute-start | bytes 10616840 | tf_op jit(solution)/shard_map/ppermute | solution.py:40
  279.9 62.1 %copy-start.8 = (bf16[768,768]{1,0:T(8,128)(2,1)S(1)}, bf16[768,768]{1,0:T(8,128)(2,1)}, u32[]{:S(2)}) copy-start(bf16[768,768]{1,0:T(8,128)(2,1)} %copy-done.6) | copy-start | bytes 3538948
  279.9 62.1 %copy-start.11 = (bf16[768,768]{1,0:T(8,128)(2,1)S(1)}, bf16[768,768]{1,0:T(8,128)(2,1)}, u32[]{:S(2)}) copy-start(bf16[768,768]{1,0:T(8,128)(2,1)} %get-tuple-element.38) | copy-start | bytes 3538948
  279.9 62.1 %copy-start.14 = (bf16[768,768]{1,0:T(8,128)(2,1)S(1)}, bf16[768,768]{1,0:T(8,128)(2,1)}, u32[]{:S(2)}) copy-start(bf16[768,768]{1,0:T(8,128)(2,1)} %get-tuple-element.39) | copy-start | bytes 3538948
  279.9 62.1 %copy-start.17 = (f32[768,768]{1,0:T(8,128)S(1)}, f32[768,768]{1,0:T(8,128)}, u32[]{:S(2)}) copy-start(f32[768,768]{1,0:T(8,128)} %fusion.20) | copy-start | bytes 7077892
  412.8 24.5 %collective-permute-start.3 = (bf16[48,3,1024]{2,0,1:T(8,128)(2,1)}, bf16[48,3,1024]{2,0,1:T(8,128)(2,1)S(1)}, u32[]{:S(2)}, u32[]{:S(2)}) collective-permute-start(bf16[48,3,1024]{2,0,1:T(8,128)(2,1)} %reduce-scatter.2.cloned.1.call-done), channel_id=1, source_target_pairs={{0,0},{1,4},{2,8},{3,12},{4,1},{5,5},{6,9},{7,13},{8,2},{9,6},{10,... | collective-permute-start | bytes 884744 | tf_op jit(solution)/shard_map/ppermute | solution.py:138
  416.6 27.5 %collective-permute-start.4 = (bf16[48,3,1024]{2,0,1:T(8,128)(2,1)}, bf16[48,3,1024]{2,0,1:T(8,128)(2,1)S(1)}, u32[]{:S(2)}, u32[]{:S(2)}) collective-permute-start(bf16[48,3,1024]{2,0,1:T(8,128)(2,1)} %reduce-scatter.2.cloned.1.call-done), channel_id=1, source_target_pairs={{0,4},{1,8},{2,12},{3,0},{4,5},{5,9},{6,13},{7,1},{8,6},{9,10},{10... | collective-permute-start | bytes 884744 | tf_op jit(solution)/shard_map/ppermute | solution.py:138
  417.8 27.3 %collective-permute-start.5 = (bf16[48,3,1024]{2,0,1:T(8,128)(2,1)}, bf16[48,3,1024]{2,0,1:T(8,128)(2,1)S(1)}, u32[]{:S(2)}, u32[]{:S(2)}) collective-permute-start(bf16[48,3,1024]{2,0,1:T(8,128)(2,1)} %reduce-scatter.2.cloned.1.call-done), channel_id=1, source_target_pairs={{0,8},{1,12},{2,0},{3,4},{4,9},{5,13},{6,1},{7,5},{8,10},{9,14},{1... | collective-permute-start | bytes 884744 | tf_op jit(solution)/shard_map/ppermute | solution.py:138
  418.6 28.0 %collective-permute-start.6 = (bf16[48,3,1024]{2,0,1:T(8,128)(2,1)}, bf16[48,3,1024]{2,0,1:T(8,128)(2,1)S(1)}, u32[]{:S(2)}, u32[]{:S(2)}) collective-permute-start(bf16[48,3,1024]{2,0,1:T(8,128)(2,1)} %reduce-scatter.2.cloned.1.call-done), channel_id=1, source_target_pairs={{0,12},{1,0},{2,4},{3,8},{4,13},{5,1},{6,5},{7,9},{8,14},{9,2},{10... | collective-permute-start | bytes 884744 | tf_op jit(solution)/shard_map/ppermute | solution.py:138
Sparse Core Ops, SparseCore 0:
  11.5 50.0 all-gather.4
  63.1 87.3 all-gather.6
  152.1 87.7 all-gather.8
  260.1 88.0 all-gather.10
  387.0 25.7 reduce-scatter.1

commit v13 on v12

--- a/solution.py
+++ b/solution.py
@@ -98,6 +98,7 @@
     )
     if len(moved) > 2 and moved[1][3] is not None:
         moved[1][3], own_half = lax.optimization_barrier((moved[1][3], own_half))
+        moved[2][1], own_half = lax.optimization_barrier((moved[2][1], own_half))
     video_all = lax.all_gather(frame_video, "video", axis=0, tiled=True)
     pooled_parts = []
     for index, size in enumerate(sizes):

time: 458 us -> 486 us (1.061); the launches traced: 458 us -> 479 us
  waiting for transfers between devices: 250 us -> 275 us
  local copies, waits for them, and re-layouts: 57.6 us -> 44 us
  matrix products: 64.5 us -> 73.5 us
    all_gather x3, waiting for transfers between devices: 77.7 us -> 127 us  [moved_weights(): gathered = lax.all_gather(mine, 'video', axis=0, tiled=True)]
    ppermute x3, waiting for transfers between devices: 121 us -> 97 us  [forward(): return lax.ppermute(onward, 'groups', [(0, 1), (1, 0)])]
    reshape x3, local copies, waits for them, and re-layouts: 19 us -> 6.8 us  [attend(): proj = proj.reshape(nframes, PATCH, 3, heads, HD)]
    unnamed x56 -> x58, local copies, waits for them, and re-layouts: 11.9 us -> 9.81 us
  transfers between devices with their start and end apart: 12 -> 12, of which waited for: 10 -> 9; matrix products, arithmetic and copies ran while one was open for 28% -> 22% of each run, Pallas kernels for 0% -> 0%
where the time goes in v13:
time: 486 us; the launch traced here: 479 us
  waiting for transfers between devices  275 us (57%)
  matrix products  73.5 us (15%)
  local copies, waits for them, and re-layouts  44 us (9%)
  other arithmetic  38 us (8%)
  blocking collectives  21.8 us (4%)
  between operations  14.8 us (3%)
  starting transfers between devices  11.6 us (2%)
    all_gather x3, waiting for transfers between devices, moved_weights(): gathered = lax.all_gather(mine, 'video', axis=0, tiled=True)  127 us
    ppermute x3, waiting for transfers between devices, forward(): return lax.ppermute(onward, 'groups', [(0, 1), (1, 0)])  97 us
    ppermute x4, waiting for transfers between devices, per_device(): got = lax.ppermute(clip_rows, ('video', 'tensor'), pairs)  26.4 us
    reduce_scatter x1, waiting for transfers between devices, per_device(): lax.psum_scatter(partial_proj.astype(jnp.bfloat16), 'tensor', scatter_dim...  24.8 us
    dot_general x3, matrix products, per_device(): jnp.dot(own_half, gathered.reshape(n_video * half, width), preferred_elem...  21.6 us
    dot_general x3, matrix products, per_device(): jnp.dot(rolled, received.reshape((n_video - 1) * half, width), preferred_...  17.5 us
    all_gather x1, blocking collectives, per_device(): pooled_all = lax.all_gather(pooled, 'video', axis=0, tiled=True)  13.6 us
    convert_element_type x1, other arithmetic, per_device(): normed = normed.astype(jnp.bfloat16).reshape(patch_rows, frames.shape[2])  12.3 us
  transfers between devices with their start and end apart: 12, of which 9 were waited for; matrix products, arithmetic and copies ran while one was open for 22% of the time, Pallas kernels for 0%

profile of v13, /device:TPU:10, one launch (start us, length us, event | category | flops | bytes accessed | tf_op | source)
XLA Modules:
  0.0 478.6 jit_solution(16788691349955099003)
XLA Ops:
  6.5 2.8 fusion.65
  11.4 2.7 fusion.66
  15.5 2.4 copy.150
  17.9 43.7 %all-gather.5.cloned.1.call-done = bf16[3072,3,128]{0,2,1:T(8,128)(2,1)} async-done(((bf16[768,3,128]{0,2,1:T(8,128)(2,1)}), bf16[3072,3,128]{0,2,1:T(8,128)(2,1)}) %all-gather.5.cloned.1.call-update) | async-done | bytes 2359312 | tf_op jit(solution)/shard_map/all_gather | solution.py:31
  67.6 82.9 %all-gather.7.cloned.1.call-done = bf16[3072,3,256]{0,2,1:T(8,128)(2,1)} async-done(((bf16[768,3,256]{0,2,1:T(8,128)(2,1)}), bf16[3072,3,256]{0,2,1:T(8,128)(2,1)}) %all-gather.7.cloned.1.call-update) | async-done | bytes 4718608 | tf_op jit(solution)/shard_map/all_gather | solution.py:31
  152.1 8.2 %all-reduce = s32[12]{0:T(128)S(1)} all-reduce(s32[12]{0:T(128)S(1)} %dynamic-update-slice), channel_id=1, replica_groups=mesh['groups'=2,'video'=4,'tensor'=4] {'video'}, use_global_device_ids=true, to_apply=%add | all-reduce | flops 12 | bytes 96 | tf_op jit(solution)/shard_map/optimization_barrier | solution.py:113
  160.3 2.6 copy.146
  167.0 5.2 %convert_reduce_fusion = f32[3,256]{1,0:T(4,128)S(1)} fusion(bf16[3,256,6144]{2,1,0:T(8,128)(2,1)} %param.4), kind=kLoop, calls=%fused_computation.2 | loop fusion | flops 9436416 | bytes 9440256 | tf_op jit(solution)/shard_map/reduce_sum | solution.py:85
  172.2 6.3 %fusion.2 = f32[3,256]{1,0:T(4,128)S(1)} fusion(bf16[3,256,6144]{2,1,0:T(8,128)(2,1)} %param.4, f32[3,256]{1,0:T(4,128)S(1)} %broadcast_multiply_fusion), kind=kLoop, calls=%fused_computation.5 | loop fusion | flops 18873600 | bytes 9443328 | tf_op jit(solution)/shard_map/reduce_sum | solution.py:86
  181.1 12.3 %fusion.3 = bf16[3,256,6144]{2,1,0:T(8,128)(2,1)} fusion(bf16[3,256,6144]{2,1,0:T(8,128)(2,1)} %param.4, f32[3,256]{1,0:T(4,128)S(1)} %add_rsqrt_fusion.10, f32[3,256]{1,0:T(4,128)S(1)} %broadcast_multiply_fusion), kind=kLoop, calls=%fused_computation.6 | loop fusion | flops 18874368 | bytes 18880512 | tf_op jit(solution)/shard_map/convert_element_type | solution.py:87
  193.4 4.3 fusion.22
  197.7 4.2 fusion.20
  203.9 2.5 pad_maximum_fusion
  206.8 4.5 fusion.63
  211.3 44.8 %collective-permute-done.1 = bf16[2304,3,256]{0,2,1:T(8,128)(2,1)} collective-permute-done((bf16[2304,3,256]{0,2,1:T(8,128)(2,1)S(1)}, bf16[2304,3,256]{0,2,1:T(8,128)(2,1)}, u32[]{:S(2)}, u32[]{:S(2)}) %collective-permute-start.1) | collective-permute-done | bytes 3538976 | tf_op jit(solution)/shard_map/ppermute | solution.py:40
  256.1 5.3 %fusion.70 = f32[768,384]{1,0:T(8,128)S(1)} fusion(bf16[768,3072]{1,0:T(8,128)(2,1)} %pad_maximum_fusion, bf16[3072,384]{0,1:T(8,128)(2,1)} %bitcast.191), kind=kOutput, calls=%fused_computation.168 | convolution fusion | flops 1811939328 | bytes 8257536 | tf_op jit(solution)/shard_map/dot_general | solution.py:115
  264.7 3.3 multiply_reduce_fusion.8
  269.4 9.0 %fusion.71 = f32[768,768]{1,0:T(8,128)} fusion(bf16[768,3072]{1,0:T(8,128)(2,1)} %pad_maximum_fusion, bf16[3072,768]{0,1:T(8,128)(2,1)} %bitcast.181), kind=kOutput, calls=%fused_computation.169 | convolution fusion | flops 3623878656 | bytes 11796480 | tf_op jit(solution)/shard_map/dot_general | solution.py:115
  282.0 2.5 convolution_bitcast_fusion.3
  290.9 6.6 %add_add_fusion.1 = f32[768,768]{1,0:T(8,128)} fusion(f32[768,768]{1,0:T(8,128)S(1)} %copy-done.17, f32[768,768]{1,0:T(8,128)} %fusion.71, bf16[2304,768]{0,1:T(8,128)(2,1)} %bitcast.18, bf16[768,768]{1,0:T(8,128)(2,1)S(1)} %copy-done.9, bf16[768,768]{1,0:T(8,128)(2,1)S(1)} %copy-done.12, bf16[768,768]{1,0:T(8,128)(2,1)S(1)} %copy-done.6), kind=kOutput, calls=%fused_computation.15 | convolution fusion | flops 2729705472 | bytes 14155776 | tf_op jit(solution)/shard_map/dot_general | solution.py:118
  297.5 2.9 reshape.418
  304.9 7.3 %fusion.72 = f32[768,768]{1,0:T(8,128)S(1)} fusion(bf16[768,3072]{1,0:T(8,128)(2,1)} %pad_maximum_fusion, bf16[3072,768]{0,1:T(8,128)(2,1)} %bitcast.184), kind=kOutput, calls=%fused_computation.170 | convolution fusion | flops 3623878656 | bytes 11796480 | tf_op jit(solution)/shard_map/dot_general | solution.py:115
  312.2 52.2 %collective-permute-done.2 = bf16[2304,3,256]{0,2,1:T(8,128)(2,1)} collective-permute-done((bf16[2304,3,256]{0,2,1:T(8,128)(2,1)}, bf16[2304,3,256]{0,2,1:T(8,128)(2,1)}, u32[]{:S(2)}, u32[]{:S(2)}) %collective-permute-start.2) | collective-permute-done | bytes 3538976 | tf_op jit(solution)/shard_map/ppermute | solution.py:40
  364.3 6.4 %add_add_fusion = f32[768,768]{1,0:T(8,128)} fusion(f32[768,768]{1,0:T(8,128)S(1)} %copy-done.16, f32[768,768]{1,0:T(8,128)S(1)} %fusion.72, bf16[2304,768]{0,1:T(8,128)(2,1)} %bitcast.26, bf16[768,768]{1,0:T(8,128)(2,1)S(1)} %copy-done.10, bf16[768,768]{1,0:T(8,128)(2,1)S(1)} %copy-done.13, bf16[768,768]{1,0:T(8,128)(2,1)S(1)} %copy-done.7), kind=kOutput, calls=%fused_computation.14 | convolution fusion | flops 2729705472 | bytes 14155776 | tf_op jit(solution)/shard_map/dot_general | solution.py:118
  370.7 2.9 reshape.423
  377.6 11.2 %fusion.7 = f32[3,256,3,1,128]{1,4,2,0,3:T(8,128)S(1)} fusion(bf16[6144,3,128]{0,2,1:T(8,128)(2,1)} %all-gather.11.cloned.1.call-done, bf16[3,256,6144]{2,1,0:T(8,128)(2,1)} %fusion.3), kind=kOutput, calls=%fused_computation.22 | convolution fusion | flops 3623878656 | bytes 15335424 | tf_op jit(solution)/shard_map/dot_general | solution.py:108
  389.8 13.6 %all_gather.23 = bf16[192,768]{1,0:T(8,128)(2,1)S(1)} all-gather(bf16[48,768]{1,0:T(8,128)(2,1)S(1)} %pad_maximum_fusion.6), channel_id=1, replica_groups=mesh['groups'=2,'video'=4,'tensor'=4] {'video'}, dimensions={0}, use_global_device_ids=true | all-gather | bytes 368640 | tf_op jit(solution)/shard_map/all_gather | solution.py:124
  403.4 4.5 convolution_convert_fusion
  409.0 24.8 %reduce-scatter.2.cloned.1.call-done = bf16[48,3,1024]{2,0,1:T(8,128)(2,1)} async-done(((bf16[192,3,1024]{2,0,1:T(8,128)(2,1)}), bf16[48,3,1024]{2,0,1:T(8,128)(2,1)}) %reduce-scatter.2.cloned.1.call-update) | async-done | bytes 294928 | tf_op jit(solution)/shard_map/reduce_scatter | solution.py:129
  433.9 3.7 collective-permute-start.3
  441.2 17.2 %collective-permute-done.3 = bf16[48,3,1024]{2,0,1:T(8,128)(2,1)S(1)} collective-permute-done((bf16[48,3,1024]{2,0,1:T(8,128)(2,1)}, bf16[48,3,1024]{2,0,1:T(8,128)(2,1)S(1)}, u32[]{:S(2)}, u32[]{:S(2)}) %collective-permute-start.3) | collective-permute-done | bytes 294944 | tf_op jit(solution)/shard_map/ppermute | solution.py:139
  458.4 6.7 %collective-permute-done.4 = bf16[48,3,1024]{2,0,1:T(8,128)(2,1)S(1)} collective-permute-done((bf16[48,3,1024]{2,0,1:T(8,128)(2,1)}, bf16[48,3,1024]{2,0,1:T(8,128)(2,1)S(1)}, u32[]{:S(2)}, u32[]{:S(2)}) %collective-permute-start.4) | collective-permute-done | bytes 294944 | tf_op jit(solution)/shard_map/ppermute | solution.py:139
  (166 shorter events, 54.4 us)
Async XLA Ops:
  6.5 55.0 %all-gather.5.cloned.1.call-start = ((), (), s32[]{:S(2)}) async-start(), calls=%async_computation.1 | async-start | bytes 2949120 | tf_op jit(solution)/shard_map/all_gather | solution.py:31
  11.4 139.1 %all-gather.7.cloned.1.call-start = ((), (), s32[]{:S(2)}) async-start(), calls=%async_computation.2 | async-start | bytes 5898240 | tf_op jit(solution)/shard_map/all_gather | solution.py:31
  61.6 194.5 %all-gather.9.cloned.1.call-start = ((), (), s32[]{:S(2)}) async-start(), calls=%async_computation.3 | async-start | bytes 5898240 | tf_op jit(solution)/shard_map/all_gather | solution.py:31
  64.6 86.0 %copy-start.15 = (u32[32]{0:T(128)S(1)}, u32[32]{0:T(128)}, u32[]{:S(2)}) copy-start(u32[32]{0:T(128)} %constant.172) | copy-start | bytes 388
  64.6 87.2 %copy-start.14 = (s32[3]{0:T(128)S(1)}, s32[3]{0:T(128)}, u32[]{:S(2)}) copy-start(s32[3]{0:T(128)} %param.5) | copy-start | bytes 40
  64.6 102.4 %collective-permute-start = (bf16[2304,3,128]{0,2,1:T(8,128)(2,1)}, bf16[2304,3,128]{0,2,1:T(8,128)(2,1)}, u32[]{:S(2)}, u32[]{:S(2)}) collective-permute-start(bf16[2304,3,128]{0,2,1:T(8,128)(2,1)} %pad_maximum_fusion.4), channel_id=1, source_target_pairs={{0,16},{16,0},{1,17},{17,1},{2,18},{18,2},{3,19},{19,3},{4,20},{20... | collective-permute-start | bytes 5308424 | tf_op jit(solution)/shard_map/ppermute | solution.py:40
  67.6 95.2 %copy-start.1 = (bf16[768,3,128]{2,0,1:T(8,128)(2,1)S(1)}, bf16[768,3,128]{2,0,1:T(8,128)(2,1)}, u32[]{:S(2)}) copy-start(bf16[768,3,128]{2,0,1:T(8,128)(2,1)} %get-tuple-element.71) | copy-start | bytes 1769476
  150.5 227.1 %all-gather.11.cloned.1.call-start = ((), (), s32[]{:S(2)}) async-start(), calls=%async_computation.4 | async-start | bytes 5898240 | tf_op jit(solution)/shard_map/all_gather | solution.py:75
  167.0 11.6 %slice-start = ((s8[4718592]{0:T(1024)(128)(4,1)}), s8[4194304]{0:T(1024)(128)(4,1)S(1)}, s32[]{:S(2)}) async-start(s8[4718592]{0:T(1024)(128)(4,1)} %bitcast.182), calls=%async_computation.6 | async-start | bytes 8388608
  172.2 6.4 %slice-start.1 = ((s8[4718592]{0:T(1024)(128)(4,1)}), s8[524288]{0:T(1024)(128)(4,1)S(1)}, s32[]{:S(2)}) async-start(s8[4718592]{0:T(1024)(128)(4,1)} %bitcast.182), calls=%async_computation.7 | async-start | bytes 1048576
  179.6 76.6 %collective-permute-start.1 = (bf16[2304,3,256]{0,2,1:T(8,128)(2,1)S(1)}, bf16[2304,3,256]{0,2,1:T(8,128)(2,1)}, u32[]{:S(2)}, u32[]{:S(2)}) collective-permute-start(bf16[2304,3,256]{0,2,1:T(8,128)(2,1)S(1)} %pad_maximum_fusion.1), channel_id=1, source_target_pairs={{0,16},{16,0},{1,17},{17,1},{2,18},{18,2},{3,19},{19,3},{4,20},{20... | collective-permute-start | bytes 10616840 | tf_op jit(solution)/shard_map/ppermute | solution.py:40
  193.4 8.5 %copy-start = (bf16[3,256,6144]{2,1,0:T(8,128)(2,1)S(1)}, bf16[3,256,6144]{2,1,0:T(8,128)(2,1)}, u32[]{:S(2)}) copy-start(bf16[3,256,6144]{2,1,0:T(8,128)(2,1)} %fusion.3) | copy-start | bytes 28311556
  203.9 2.5 copy-start.5
  203.9 2.9 copy-start.8
  203.9 2.9 copy-start.11
  256.1 5.3 %copy-start.2 = (bf16[768,3,128]{0,2,1:T(8,128)(2,1)S(1)}, bf16[768,3,128]{0,2,1:T(8,128)(2,1)}, u32[]{:S(2)}) copy-start(bf16[768,3,128]{0,2,1:T(8,128)(2,1)} %copy.145) | copy-start | bytes 1769476
  256.1 5.4 %copy-start.4 = (f32[768,384]{1,0:T(8,128)S(1)}, f32[768,384]{1,0:T(8,128)}, u32[]{:S(2)}) copy-start(f32[768,384]{1,0:T(8,128)} %fusion.63) | copy-start | bytes 3538948
  278.4 155.5 %reduce-scatter.2.cloned.1.call-start = ((), (), s32[]{:S(2)}) async-start(), calls=%async_computation.5 | async-start | bytes 1474560 | tf_op jit(solution)/shard_map/reduce_scatter | solution.py:129
  286.4 3.7 copy-start.6
  286.4 3.7 copy-start.9
  286.4 3.7 copy-start.12
  286.4 4.5 copy-start.17
  288.6 75.8 %collective-permute-start.2 = (bf16[2304,3,256]{0,2,1:T(8,128)(2,1)}, bf16[2304,3,256]{0,2,1:T(8,128)(2,1)}, u32[]{:S(2)}, u32[]{:S(2)}) collective-permute-start(bf16[2304,3,256]{0,2,1:T(8,128)(2,1)} %pad_maximum_fusion.3), channel_id=1, source_target_pairs={{0,16},{16,0},{1,17},{17,1},{2,18},{18,2},{3,19},{19,3},{4,20},{20... | collective-permute-start | bytes 10616840 | tf_op jit(solution)/shard_map/ppermute | solution.py:40
  303.4 1.0 copy-start.3
  304.8 59.5 %copy-start.7 = (bf16[768,768]{1,0:T(8,128)(2,1)S(1)}, bf16[768,768]{1,0:T(8,128)(2,1)}, u32[]{:S(2)}) copy-start(bf16[768,768]{1,0:T(8,128)(2,1)} %copy-done.5) | copy-start | bytes 3538948
  304.8 59.5 %copy-start.10 = (bf16[768,768]{1,0:T(8,128)(2,1)S(1)}, bf16[768,768]{1,0:T(8,128)(2,1)}, u32[]{:S(2)}) copy-start(bf16[768,768]{1,0:T(8,128)(2,1)} %copy-done.8) | copy-start | bytes 3538948
  304.8 59.5 %copy-start.13 = (bf16[768,768]{1,0:T(8,128)(2,1)S(1)}, bf16[768,768]{1,0:T(8,128)(2,1)}, u32[]{:S(2)}) copy-start(bf16[768,768]{1,0:T(8,128)(2,1)} %get-tuple-element.43) | copy-start | bytes 3538948
  304.9 59.5 %copy-start.16 = (f32[768,768]{1,0:T(8,128)S(1)}, f32[768,768]{1,0:T(8,128)}, u32[]{:S(2)}) copy-start(f32[768,768]{1,0:T(8,128)} %fusion.20) | copy-start | bytes 7077892
  433.9 24.5 %collective-permute-start.3 = (bf16[48,3,1024]{2,0,1:T(8,128)(2,1)}, bf16[48,3,1024]{2,0,1:T(8,128)(2,1)S(1)}, u32[]{:S(2)}, u32[]{:S(2)}) collective-permute-start(bf16[48,3,1024]{2,0,1:T(8,128)(2,1)} %reduce-scatter.2.cloned.1.call-done), channel_id=1, source_target_pairs={{0,0},{1,4},{2,8},{3,12},{4,1},{5,5},{6,9},{7,13},{8,2},{9,6},{10,... | collective-permute-start | bytes 884744 | tf_op jit(solution)/shard_map/ppermute | solution.py:139
  437.6 27.5 %collective-permute-start.4 = (bf16[48,3,1024]{2,0,1:T(8,128)(2,1)}, bf16[48,3,1024]{2,0,1:T(8,128)(2,1)S(1)}, u32[]{:S(2)}, u32[]{:S(2)}) collective-permute-start(bf16[48,3,1024]{2,0,1:T(8,128)(2,1)} %reduce-scatter.2.cloned.1.call-done), channel_id=1, source_target_pairs={{0,4},{1,8},{2,12},{3,0},{4,5},{5,9},{6,13},{7,1},{8,6},{9,10},{10... | collective-permute-start | bytes 884744 | tf_op jit(solution)/shard_map/ppermute | solution.py:139
  438.8 27.3 %collective-permute-start.5 = (bf16[48,3,1024]{2,0,1:T(8,128)(2,1)}, bf16[48,3,1024]{2,0,1:T(8,128)(2,1)S(1)}, u32[]{:S(2)}, u32[]{:S(2)}) collective-permute-start(bf16[48,3,1024]{2,0,1:T(8,128)(2,1)} %reduce-scatter.2.cloned.1.call-done), channel_id=1, source_target_pairs={{0,8},{1,12},{2,0},{3,4},{4,9},{5,13},{6,1},{7,5},{8,10},{9,14},{1... | collective-permute-start | bytes 884744 | tf_op jit(solution)/shard_map/ppermute | solution.py:139
  439.7 28.0 %collective-permute-start.6 = (bf16[48,3,1024]{2,0,1:T(8,128)(2,1)}, bf16[48,3,1024]{2,0,1:T(8,128)(2,1)S(1)}, u32[]{:S(2)}, u32[]{:S(2)}) collective-permute-start(bf16[48,3,1024]{2,0,1:T(8,128)(2,1)} %reduce-scatter.2.cloned.1.call-done), channel_id=1, source_target_pairs={{0,12},{1,0},{2,4},{3,8},{4,13},{5,1},{6,5},{7,9},{8,14},{9,2},{10... | collective-permute-start | bytes 884744 | tf_op jit(solution)/shard_map/ppermute | solution.py:139
Sparse Core Ops, SparseCore 0:
  11.5 50.0 all-gather.4
  63.1 87.2 all-gather.6
  152.0 87.8 all-gather.8
  278.5 87.5 all-gather.10
  408.0 25.7 reduce-scatter.1

commit v14 on v12

--- a/solution.py
+++ b/solution.py
@@ -71,7 +71,7 @@
         chunk = qkv_weight[:, :, first * HD:(first + size) * HD]
         first += size
         if len(moved) == len(sizes) - 1 and len(sizes) > 2:
-            whole_rows, moved[-1][1] = lax.optimization_barrier((chunk, moved[-1][1]))
+            whole_rows, moved[-2][1] = lax.optimization_barrier((chunk, moved[-2][1]))
             step = [lax.all_gather(whole_rows, "video", axis=0, tiled=True), None, None]
         elif moved:
             step, moved[-1][1] = moved_weights(chunk, n_video, after=moved[-1][1])

time: 458 us -> 476 us (1.039); the launches traced: 458 us -> 469 us
  waiting for transfers between devices: 250 us -> 266 us
  local copies, waits for them, and re-layouts: 57.6 us -> 44.8 us
  matrix products: 64.5 us -> 69.5 us
    ppermute x3, waiting for transfers between devices: 121 us -> 50.2 us  [forward(): return lax.ppermute(onward, 'groups', [(0, 1), (1, 0)])]
    all_gather x3, waiting for transfers between devices: 77.7 us -> 127 us  [moved_weights(): gathered = lax.all_gather(mine, 'video', axis=0, tiled=True)]
    all_gather x1, waiting for transfers between devices: 0.02 us -> 37.8 us  [per_device(): step = [lax.all_gather(whole_rows, 'video', axis=0, tiled=True), None, None]]
    reshape x3, local copies, waits for them, and re-layouts: 19 us -> 6.69 us  [attend(): proj = proj.reshape(nframes, PATCH, 3, heads, HD)]
    unnamed x56 -> x70, local copies, waits for them, and re-layouts: 11.9 us -> 11.5 us
  transfers between devices with their start and end apart: 12 -> 12, of which waited for: 10 -> 10; matrix products, arithmetic and copies ran while one was open for 28% -> 27% of each run, Pallas kernels for 0% -> 0%
where the time goes in v14:
time: 476 us; the launch traced here: 469 us
  waiting for transfers between devices  266 us (56%)
  matrix products  69.5 us (15%)
  local copies, waits for them, and re-layouts  44.8 us (9%)
  other arithmetic  40 us (8%)
  blocking collectives  21.8 us (5%)
  between operations  14.9 us (3%)
  starting transfers between devices  11.7 us (2%)
    all_gather x3, waiting for transfers between devices, moved_weights(): gathered = lax.all_gather(mine, 'video', axis=0, tiled=True)  127 us
    ppermute x3, waiting for transfers between devices, forward(): return lax.ppermute(onward, 'groups', [(0, 1), (1, 0)])  50.2 us
    all_gather x1, waiting for transfers between devices, per_device(): step = [lax.all_gather(whole_rows, 'video', axis=0, tiled=True), None, None]  37.8 us
    ppermute x4, waiting for transfers between devices, per_device(): got = lax.ppermute(clip_rows, ('video', 'tensor'), pairs)  26.4 us
    reduce_scatter x1, waiting for transfers between devices, per_device(): lax.psum_scatter(partial_proj.astype(jnp.bfloat16), 'tensor', scatter_dim...  24.8 us
    dot_general x3, matrix products, per_device(): jnp.dot(own_half, gathered.reshape(n_video * half, width), preferred_elem...  17.3 us
    dot_general x3, matrix products, per_device(): jnp.dot(rolled, received.reshape((n_video - 1) * half, width), preferred_...  16.8 us
    all_gather x1, blocking collectives, per_device(): pooled_all = lax.all_gather(pooled, 'video', axis=0, tiled=True)  13.6 us
  transfers between devices with their start and end apart: 12, of which 10 were waited for; matrix products, arithmetic and copies ran while one was open for 27% of the time, Pallas kernels for 0%

profile of v14, /device:TPU:10, one launch (start us, length us, event | category | flops | bytes accessed | tf_op | source)
XLA Modules:
  0.0 468.5 jit_solution(15248560179879355961)
XLA Ops:
  6.5 2.8 fusion.66
  11.4 2.7 fusion.67
  17.9 43.6 %all-gather.5.cloned.1.call-done = bf16[3072,3,128]{0,2,1:T(8,128)(2,1)} async-done(((bf16[768,3,128]{0,2,1:T(8,128)(2,1)}), bf16[3072,3,128]{0,2,1:T(8,128)(2,1)}) %all-gather.5.cloned.1.call-update) | async-done | bytes 2359312 | tf_op jit(solution)/shard_map/all_gather | solution.py:31
  67.6 82.9 %all-gather.7.cloned.1.call-done = bf16[3072,3,256]{0,2,1:T(8,128)(2,1)} async-done(((bf16[768,3,256]{0,2,1:T(8,128)(2,1)}), bf16[3072,3,256]{0,2,1:T(8,128)(2,1)}) %all-gather.7.cloned.1.call-update) | async-done | bytes 4718608 | tf_op jit(solution)/shard_map/all_gather | solution.py:31
  152.0 8.2 %all-reduce = s32[12]{0:T(128)S(1)} all-reduce(s32[12]{0:T(128)S(1)} %dynamic-update-slice), channel_id=1, replica_groups=mesh['groups'=2,'video'=4,'tensor'=4] {'video'}, use_global_device_ids=true, to_apply=%add | all-reduce | flops 12 | bytes 96 | tf_op jit(solution)/shard_map/optimization_barrier | solution.py:112
  167.0 5.2 %convert_reduce_fusion = f32[3,256]{1,0:T(4,128)S(1)} fusion(bf16[3,256,6144]{2,1,0:T(8,128)(2,1)} %param.4), kind=kLoop, calls=%fused_computation.2 | loop fusion | flops 9436416 | bytes 9440256 | tf_op jit(solution)/shard_map/reduce_sum | solution.py:85
  172.2 6.3 %fusion.2 = f32[3,256]{1,0:T(4,128)S(1)} fusion(bf16[3,256,6144]{2,1,0:T(8,128)(2,1)} %param.4, f32[3,256]{1,0:T(4,128)S(1)} %broadcast_multiply_fusion), kind=kLoop, calls=%fused_computation.5 | loop fusion | flops 18873600 | bytes 9443328 | tf_op jit(solution)/shard_map/reduce_sum | solution.py:86
  181.0 12.3 %fusion.3 = bf16[3,256,6144]{2,1,0:T(8,128)(2,1)} fusion(bf16[3,256,6144]{2,1,0:T(8,128)(2,1)} %param.4, f32[3,256]{1,0:T(4,128)S(1)} %add_rsqrt_fusion.10, f32[3,256]{1,0:T(4,128)S(1)} %broadcast_multiply_fusion), kind=kLoop, calls=%fused_computation.6 | loop fusion | flops 18874368 | bytes 18880512 | tf_op jit(solution)/shard_map/convert_element_type | solution.py:87
  193.3 4.3 fusion.22
  197.6 4.2 fusion.20
  201.8 2.4 constant_dynamic-slice_fusion.8
  204.2 2.4 pad_maximum_fusion
  209.2 4.0 fusion.64
  213.2 42.9 %collective-permute-done.1 = bf16[2304,3,256]{0,2,1:T(8,128)(2,1)} collective-permute-done((bf16[2304,3,256]{0,2,1:T(8,128)(2,1)S(1)}, bf16[2304,3,256]{0,2,1:T(8,128)(2,1)}, u32[]{:S(2)}, u32[]{:S(2)}) %collective-permute-start.1) | collective-permute-done | bytes 3538976 | tf_op jit(solution)/shard_map/ppermute | solution.py:40
  256.0 2.6 fusion.12
  260.4 3.3 multiply_reduce_fusion.8
  264.7 7.4 %fusion.71 = f32[768,768]{1,0:T(8,128)S(1)} fusion(bf16[768,3072]{1,0:T(8,128)(2,1)} %pad_maximum_fusion, bf16[3072,768]{0,1:T(8,128)(2,1)} %bitcast.183), kind=kOutput, calls=%fused_computation.169 | convolution fusion | flops 3623878656 | bytes 11796480 | tf_op jit(solution)/shard_map/dot_general | solution.py:114
  272.1 6.4 %add_add_fusion.1 = f32[768,768]{1,0:T(8,128)} fusion(f32[768,768]{1,0:T(8,128)S(1)} %copy-done.21, f32[768,768]{1,0:T(8,128)S(1)} %fusion.71, bf16[2304,768]{0,1:T(8,128)(2,1)} %bitcast.18, bf16[768,768]{1,0:T(8,128)(2,1)S(1)} %copy-done.9, bf16[768,768]{1,0:T(8,128)(2,1)S(1)} %copy-done.11, bf16[768,768]{1,0:T(8,128)(2,1)S(1)} %copy-done.6), kind=kOutput, calls=%fused_computation.15 | convolution fusion | flops 2729705472 | bytes 14155776 | tf_op jit(solution)/shard_map/dot_general | solution.py:117
  278.5 2.9 reshape.418
  291.4 37.8 %all-gather.11.cloned.1.call-done = bf16[6144,3,128]{0,2,1:T(8,128)(2,1)} async-done(((bf16[1536,3,128]{0,2,1:T(8,128)(2,1)}), bf16[6144,3,128]{0,2,1:T(8,128)(2,1)}) %all-gather.11.cloned.1.call-update) | async-done | bytes 4718608 | tf_op jit(solution)/shard_map/all_gather | solution.py:75
  329.2 11.1 %fusion.7 = f32[3,256,3,1,128]{1,4,2,0,3:T(8,128)S(1)} fusion(bf16[6144,3,128]{0,2,1:T(8,128)(2,1)} %all-gather.11.cloned.1.call-done, bf16[3,256,6144]{2,1,0:T(8,128)(2,1)} %fusion.3), kind=kOutput, calls=%fused_computation.22 | convolution fusion | flops 3623878656 | bytes 15335424 | tf_op jit(solution)/shard_map/dot_general | solution.py:107
  342.5 2.6 convolution_bitcast_fusion.2
  350.0 7.3 %fusion.72 = f32[768,768]{1,0:T(8,128)S(1)} fusion(bf16[768,3072]{1,0:T(8,128)(2,1)} %pad_maximum_fusion, bf16[3072,768]{0,1:T(8,128)(2,1)} %bitcast.186), kind=kOutput, calls=%fused_computation.170 | convolution fusion | flops 3623878656 | bytes 11796480 | tf_op jit(solution)/shard_map/dot_general | solution.py:114
  357.3 7.4 %collective-permute-done.2 = bf16[2304,3,256]{0,2,1:T(8,128)(2,1)} collective-permute-done((bf16[2304,3,256]{0,2,1:T(8,128)(2,1)S(1)}, bf16[2304,3,256]{0,2,1:T(8,128)(2,1)}, u32[]{:S(2)}, u32[]{:S(2)}) %collective-permute-start.2) | collective-permute-done | bytes 3538976 | tf_op jit(solution)/shard_map/ppermute | solution.py:40
  364.7 6.4 %add_add_fusion = f32[768,768]{1,0:T(8,128)} fusion(f32[768,768]{1,0:T(8,128)S(1)} %copy-done.20, f32[768,768]{1,0:T(8,128)S(1)} %fusion.72, bf16[2304,768]{0,1:T(8,128)(2,1)} %bitcast.26, bf16[768,768]{1,0:T(8,128)(2,1)S(1)} %copy-done.10, bf16[768,768]{1,0:T(8,128)(2,1)S(1)} %copy-done.12, bf16[768,768]{1,0:T(8,128)(2,1)S(1)} %copy-done.7), kind=kOutput, calls=%fused_computation.14 | convolution fusion | flops 2729705472 | bytes 14155776 | tf_op jit(solution)/shard_map/dot_general | solution.py:117
  371.1 2.9 reshape.423
  379.8 13.6 %all_gather.23 = bf16[192,768]{1,0:T(8,128)(2,1)S(1)} all-gather(bf16[48,768]{1,0:T(8,128)(2,1)S(1)} %pad_maximum_fusion.6), channel_id=1, replica_groups=mesh['groups'=2,'video'=4,'tensor'=4] {'video'}, dimensions={0}, use_global_device_ids=true | all-gather | bytes 368640 | tf_op jit(solution)/shard_map/all_gather | solution.py:123
  393.4 4.5 convolution_convert_fusion
  399.0 24.8 %reduce-scatter.2.cloned.1.call-done = bf16[48,3,1024]{2,0,1:T(8,128)(2,1)} async-done(((bf16[192,3,1024]{2,0,1:T(8,128)(2,1)}), bf16[48,3,1024]{2,0,1:T(8,128)(2,1)}) %reduce-scatter.2.cloned.1.call-update) | async-done | bytes 294928 | tf_op jit(solution)/shard_map/reduce_scatter | solution.py:128
  423.8 3.7 collective-permute-start.3
  431.2 17.1 %collective-permute-done.3 = bf16[48,3,1024]{2,0,1:T(8,128)(2,1)S(1)} collective-permute-done((bf16[48,3,1024]{2,0,1:T(8,128)(2,1)}, bf16[48,3,1024]{2,0,1:T(8,128)(2,1)S(1)}, u32[]{:S(2)}, u32[]{:S(2)}) %collective-permute-start.3) | collective-permute-done | bytes 294944 | tf_op jit(solution)/shard_map/ppermute | solution.py:138
  448.3 6.8 %collective-permute-done.4 = bf16[48,3,1024]{2,0,1:T(8,128)(2,1)S(1)} collective-permute-done((bf16[48,3,1024]{2,0,1:T(8,128)(2,1)}, bf16[48,3,1024]{2,0,1:T(8,128)(2,1)S(1)}, u32[]{:S(2)}, u32[]{:S(2)}) %collective-permute-start.4) | collective-permute-done | bytes 294944 | tf_op jit(solution)/shard_map/ppermute | solution.py:138
  (179 shorter events, 61.0 us)
Async XLA Ops:
  6.5 55.0 %all-gather.5.cloned.1.call-start = ((), (), s32[]{:S(2)}) async-start(), calls=%async_computation.1 | async-start | bytes 2949120 | tf_op jit(solution)/shard_map/all_gather | solution.py:31
  11.4 139.1 %all-gather.7.cloned.1.call-start = ((), (), s32[]{:S(2)}) async-start(), calls=%async_computation.2 | async-start | bytes 5898240 | tf_op jit(solution)/shard_map/all_gather | solution.py:31
  61.6 225.0 %all-gather.9.cloned.1.call-start = ((), (), s32[]{:S(2)}) async-start(), calls=%async_computation.3 | async-start | bytes 5898240 | tf_op jit(solution)/shard_map/all_gather | solution.py:31
  64.6 85.9 %copy-start.19 = (u32[32]{0:T(128)S(1)}, u32[32]{0:T(128)}, u32[]{:S(2)}) copy-start(u32[32]{0:T(128)} %constant.172) | copy-start | bytes 388
  64.6 87.2 %copy-start.18 = (s32[3]{0:T(128)S(1)}, s32[3]{0:T(128)}, u32[]{:S(2)}) copy-start(s32[3]{0:T(128)} %param.5) | copy-start | bytes 40
  64.6 102.4 %collective-permute-start = (bf16[2304,3,128]{0,2,1:T(8,128)(2,1)}, bf16[2304,3,128]{0,2,1:T(8,128)(2,1)}, u32[]{:S(2)}, u32[]{:S(2)}) collective-permute-start(bf16[2304,3,128]{0,2,1:T(8,128)(2,1)} %pad_maximum_fusion.4), channel_id=1, source_target_pairs={{0,16},{16,0},{1,17},{17,1},{2,18},{18,2},{3,19},{19,3},{4,20},{20... | collective-permute-start | bytes 5308424 | tf_op jit(solution)/shard_map/ppermute | solution.py:40
  67.6 94.9 %copy-start.2 = (bf16[1536,3,128]{2,0,1:T(8,128)(2,1)S(1)}, bf16[1536,3,128]{2,0,1:T(8,128)(2,1)}, u32[]{:S(2)}) copy-start(bf16[1536,3,128]{2,0,1:T(8,128)(2,1)} %get-tuple-element.45) | copy-start | bytes 3538948
  150.5 178.7 %all-gather.11.cloned.1.call-start = ((), (), s32[]{:S(2)}) async-start(), calls=%async_computation.4 | async-start | bytes 5898240 | tf_op jit(solution)/shard_map/all_gather | solution.py:75
  167.0 11.6 %slice-start.2 = ((s8[4718592]{0:T(1024)(128)(4,1)}), s8[4194304]{0:T(1024)(128)(4,1)S(1)}, s32[]{:S(2)}) async-start(s8[4718592]{0:T(1024)(128)(4,1)} %bitcast.184), calls=%async_computation.8 | async-start | bytes 8388608
  172.2 6.4 %slice-start.3 = ((s8[4718592]{0:T(1024)(128)(4,1)}), s8[524288]{0:T(1024)(128)(4,1)S(1)}, s32[]{:S(2)}) async-start(s8[4718592]{0:T(1024)(128)(4,1)} %bitcast.184), calls=%async_computation.9 | async-start | bytes 1048576
  179.4 76.6 %collective-permute-start.1 = (bf16[2304,3,256]{0,2,1:T(8,128)(2,1)S(1)}, bf16[2304,3,256]{0,2,1:T(8,128)(2,1)}, u32[]{:S(2)}, u32[]{:S(2)}) collective-permute-start(bf16[2304,3,256]{0,2,1:T(8,128)(2,1)S(1)} %pad_maximum_fusion.1), channel_id=1, source_target_pairs={{0,16},{16,0},{1,17},{17,1},{2,18},{18,2},{3,19},{19,3},{4,20},{20... | collective-permute-start | bytes 10616840 | tf_op jit(solution)/shard_map/ppermute | solution.py:40
  193.3 8.5 %copy-start = (bf16[3,256,6144]{2,1,0:T(8,128)(2,1)S(1)}, bf16[3,256,6144]{2,1,0:T(8,128)(2,1)}, u32[]{:S(2)}) copy-start(bf16[3,256,6144]{2,1,0:T(8,128)(2,1)} %fusion.3) | copy-start | bytes 28311556
  206.7 217.2 %reduce-scatter.2.cloned.1.call-start = ((), (), s32[]{:S(2)}) async-start(), calls=%async_computation.5 | async-start | bytes 1474560 | tf_op jit(solution)/shard_map/reduce_scatter | solution.py:128
  206.7 2.4 copy-start.5
  206.7 2.4 copy-start.8
  206.7 49.3 %slice-start = ((s8[4718592]{0:T(1024)(128)(4,1)}), s8[4194304]{0:T(1024)(128)(4,1)S(1)}, s32[]{:S(2)}) async-start(s8[4718592]{0:T(1024)(128)(4,1)} %bitcast.179), calls=%async_computation.6 | async-start | bytes 8388608
  209.1 46.9 %slice-start.1 = ((s8[4718592]{0:T(1024)(128)(4,1)}), s8[524288]{0:T(1024)(128)(4,1)S(1)}, s32[]{:S(2)}) async-start(s8[4718592]{0:T(1024)(128)(4,1)} %bitcast.179), calls=%async_computation.7 | async-start | bytes 1048576
  209.1 46.9 %copy-start.4 = (bf16[3072,3,128]{0,2,1:T(8,128)(2,1)S(1)}, bf16[3072,3,128]{0,2,1:T(8,128)(2,1)}, u32[]{:S(2)}) copy-start(bf16[3072,3,128]{0,2,1:T(8,128)(2,1)} %all-gather.5.cloned.1.call-done) | copy-start | bytes 7077892
  264.6 7.4 %copy-start.6 = (bf16[768,768]{1,0:T(8,128)(2,1)S(1)}, bf16[768,768]{1,0:T(8,128)(2,1)}, u32[]{:S(2)}) copy-start(bf16[768,768]{1,0:T(8,128)(2,1)} %get-tuple-element.37) | copy-start | bytes 3538948
  264.6 7.4 %copy-start.9 = (bf16[768,768]{1,0:T(8,128)(2,1)S(1)}, bf16[768,768]{1,0:T(8,128)(2,1)}, u32[]{:S(2)}) copy-start(bf16[768,768]{1,0:T(8,128)(2,1)} %get-tuple-element.38) | copy-start | bytes 3538948
  264.6 7.4 %copy-start.11 = (bf16[768,768]{1,0:T(8,128)(2,1)S(1)}, bf16[768,768]{1,0:T(8,128)(2,1)}, u32[]{:S(2)}) copy-start(bf16[768,768]{1,0:T(8,128)(2,1)} %get-tuple-element.39) | copy-start | bytes 3538948
  264.6 7.4 %copy-start.21 = (f32[768,768]{1,0:T(8,128)S(1)}, f32[768,768]{1,0:T(8,128)}, u32[]{:S(2)}) copy-start(f32[768,768]{1,0:T(8,128)} %fusion.22) | copy-start | bytes 7077892
  288.8 1.9 copy-start.16
  289.1 75.6 %collective-permute-start.2 = (bf16[2304,3,256]{0,2,1:T(8,128)(2,1)S(1)}, bf16[2304,3,256]{0,2,1:T(8,128)(2,1)}, u32[]{:S(2)}, u32[]{:S(2)}) collective-permute-start(bf16[2304,3,256]{0,2,1:T(8,128)(2,1)S(1)} %pad_maximum_fusion.3), channel_id=1, source_target_pairs={{0,16},{16,0},{1,17},{17,1},{2,18},{18,2},{3,19},{19,3},{4,20},{20... | collective-permute-start | bytes 10616840 | tf_op jit(solution)/shard_map/ppermute | solution.py:40
  350.0 14.7 %copy-start.7 = (bf16[768,768]{1,0:T(8,128)(2,1)S(1)}, bf16[768,768]{1,0:T(8,128)(2,1)}, u32[]{:S(2)}) copy-start(bf16[768,768]{1,0:T(8,128)(2,1)} %get-tuple-element.37) | copy-start | bytes 3538948
  350.0 14.7 %copy-start.10 = (bf16[768,768]{1,0:T(8,128)(2,1)S(1)}, bf16[768,768]{1,0:T(8,128)(2,1)}, u32[]{:S(2)}) copy-start(bf16[768,768]{1,0:T(8,128)(2,1)} %get-tuple-element.38) | copy-start | bytes 3538948
  350.0 14.7 %copy-start.12 = (bf16[768,768]{1,0:T(8,128)(2,1)S(1)}, bf16[768,768]{1,0:T(8,128)(2,1)}, u32[]{:S(2)}) copy-start(bf16[768,768]{1,0:T(8,128)(2,1)} %get-tuple-element.39) | copy-start | bytes 3538948
  350.0 14.7 %copy-start.20 = (f32[768,768]{1,0:T(8,128)S(1)}, f32[768,768]{1,0:T(8,128)}, u32[]{:S(2)}) copy-start(f32[768,768]{1,0:T(8,128)} %fusion.20) | copy-start | bytes 7077892
  423.8 24.5 %collective-permute-start.3 = (bf16[48,3,1024]{2,0,1:T(8,128)(2,1)}, bf16[48,3,1024]{2,0,1:T(8,128)(2,1)S(1)}, u32[]{:S(2)}, u32[]{:S(2)}) collective-permute-start(bf16[48,3,1024]{2,0,1:T(8,128)(2,1)} %reduce-scatter.2.cloned.1.call-done), channel_id=1, source_target_pairs={{0,0},{1,4},{2,8},{3,12},{4,1},{5,5},{6,9},{7,13},{8,2},{9,6},{10,... | collective-permute-start | bytes 884744 | tf_op jit(solution)/shard_map/ppermute | solution.py:138
  427.5 27.5 %collective-permute-start.4 = (bf16[48,3,1024]{2,0,1:T(8,128)(2,1)}, bf16[48,3,1024]{2,0,1:T(8,128)(2,1)S(1)}, u32[]{:S(2)}, u32[]{:S(2)}) collective-permute-start(bf16[48,3,1024]{2,0,1:T(8,128)(2,1)} %reduce-scatter.2.cloned.1.call-done), channel_id=1, source_target_pairs={{0,4},{1,8},{2,12},{3,0},{4,5},{5,9},{6,13},{7,1},{8,6},{9,10},{10... | collective-permute-start | bytes 884744 | tf_op jit(solution)/shard_map/ppermute | solution.py:138
  428.8 27.3 %collective-permute-start.5 = (bf16[48,3,1024]{2,0,1:T(8,128)(2,1)}, bf16[48,3,1024]{2,0,1:T(8,128)(2,1)S(1)}, u32[]{:S(2)}, u32[]{:S(2)}) collective-permute-start(bf16[48,3,1024]{2,0,1:T(8,128)(2,1)} %reduce-scatter.2.cloned.1.call-done), channel_id=1, source_target_pairs={{0,8},{1,12},{2,0},{3,4},{4,9},{5,13},{6,1},{7,5},{8,10},{9,14},{1... | collective-permute-start | bytes 884744 | tf_op jit(solution)/shard_map/ppermute | solution.py:138
  429.6 27.9 %collective-permute-start.6 = (bf16[48,3,1024]{2,0,1:T(8,128)(2,1)}, bf16[48,3,1024]{2,0,1:T(8,128)(2,1)S(1)}, u32[]{:S(2)}, u32[]{:S(2)}) collective-permute-start(bf16[48,3,1024]{2,0,1:T(8,128)(2,1)} %reduce-scatter.2.cloned.1.call-done), channel_id=1, source_target_pairs={{0,12},{1,0},{2,4},{3,8},{4,13},{5,1},{6,5},{7,9},{8,14},{9,2},{10... | collective-permute-start | bytes 884744 | tf_op jit(solution)/shard_map/ppermute | solution.py:138
  (6 other events, 7.1 us)
Sparse Core Ops, SparseCore 0:
  11.5 50.0 all-gather.4
  63.1 87.2 all-gather.6
  152.0 87.8 all-gather.8
  241.3 87.8 all-gather.10
  398.0 25.7 reduce-scatter.1

commit v15 on v12

--- a/solution.py
+++ b/solution.py
@@ -120,7 +120,12 @@
         )
         pooled_parts.append(attend(proj, nframes, size, scale, blocks, inner))
     pooled = jnp.concatenate(pooled_parts, axis=1)
-    pooled_all = lax.all_gather(pooled, "video", axis=0, tiled=True)
+    shifted = [pooled] + [
+        lax.ppermute(pooled, "video", [(a, (a + k) % n_video) for a in range(n_video)])
+        for k in range(1, n_video)
+    ]
+    came_from = jnp.argsort(jnp.stack([(v - k) % n_video for k in range(n_video)]))
+    pooled_all = jnp.take(jnp.stack(shifted), came_from, axis=0).reshape(-1, pooled.shape[1])
     rows = pooled_all.shape[0]
     partial_proj = jnp.einsum(
         "rc,ckt->rkt", pooled_all, conn_weight, preferred_element_type=jnp.float32

time: 458 us -> 454 us (level)
  blocking collectives: 22.6 us -> 7.65 us
  starting transfers between devices: 11.8 us -> 17.5 us
    all_gather x1 -> x0, blocking collectives: 15 us -> none  [per_device(): pooled_all = lax.all_gather(pooled, 'video', axis=0, tiled=True)]
    ppermute x0 -> x3, starting transfers between devices: none -> 5.69 us  [per_device(): lax.ppermute(pooled, 'video', [(a, (a + k) % n_video) for a in range(n_vi...]
    unnamed x56 -> x58, local copies, waits for them, and re-layouts: 11.9 us -> 11.9 us
  transfers between devices with their start and end apart: 12 -> 15, of which waited for: 10 -> 13; matrix products, arithmetic and copies ran while one was open for 28% -> 29% of each run, Pallas kernels for 0% -> 0%
where the time goes in v15:
time: 454 us; the launch traced here: 453 us
  waiting for transfers between devices  254 us (56%)
  matrix products  64.5 us (14%)
  local copies, waits for them, and re-layouts  58.3 us (13%)
  other arithmetic  36.4 us (8%)
  starting transfers between devices  17.5 us (4%)
  between operations  14.8 us (3%)
  blocking collectives  7.65 us (2%)
    ppermute x3, waiting for transfers between devices, forward(): return lax.ppermute(onward, 'groups', [(0, 1), (1, 0)])  120 us
    all_gather x3, waiting for transfers between devices, moved_weights(): gathered = lax.all_gather(mine, 'video', axis=0, tiled=True)  77.6 us
    ppermute x4, waiting for transfers between devices, per_device(): got = lax.ppermute(clip_rows, ('video', 'tensor'), pairs)  26.4 us
    reduce_scatter x1, waiting for transfers between devices, per_device(): lax.psum_scatter(partial_proj.astype(jnp.bfloat16), 'tensor', scatter_dim...  25.2 us
    reshape x3, local copies, waits for them, and re-layouts, attend(): proj = proj.reshape(nframes, PATCH, 3, heads, HD)  19 us
    dot_general x3, matrix products, per_device(): jnp.dot(own_half, gathered.reshape(n_video * half, width), preferred_elem...  17.1 us
    dot_general x3, matrix products, per_device(): jnp.dot(rolled, received.reshape((n_video - 1) * half, width), preferred_...  16.6 us
    convert_element_type x1, other arithmetic, per_device(): normed = normed.astype(jnp.bfloat16).reshape(patch_rows, frames.shape[2])  12.2 us
  transfers between devices with their start and end apart: 15, of which 13 were waited for; matrix products, arithmetic and copies ran while one was open for 29% of the time, Pallas kernels for 0%

profile of v15, /device:TPU:10, one launch (start us, length us, event | category | flops | bytes accessed | tf_op | source)
XLA Modules:
  0.0 452.8 jit_solution(4902223139229890149)
XLA Ops:
  6.5 2.8 fusion.67
  11.4 2.7 fusion.68
  18.0 43.6 %all-gather.5.cloned.1.call-done = bf16[3072,3,128]{0,2,1:T(8,128)(2,1)} async-done(((bf16[768,3,128]{0,2,1:T(8,128)(2,1)}), bf16[3072,3,128]{0,2,1:T(8,128)(2,1)}) %all-gather.5.cloned.1.call-update) | async-done | bytes 2359312 | tf_op jit(solution)/shard_map/all_gather | solution.py:31
  67.6 7.6 %all-reduce = s32[12]{0:T(128)S(1)} all-reduce(s32[12]{0:T(128)S(1)} %dynamic-update-slice), channel_id=1, replica_groups=mesh['groups'=2,'video'=4,'tensor'=4] {'video'}, use_global_device_ids=true, to_apply=%add | all-reduce | flops 12 | bytes 96 | tf_op jit(solution)/shard_map/optimization_barrier | solution.py:112
  84.9 20.1 %collective-permute-done = bf16[2304,3,128]{0,2,1:T(8,128)(2,1)} collective-permute-done((bf16[2304,3,128]{0,2,1:T(8,128)(2,1)}, bf16[2304,3,128]{0,2,1:T(8,128)(2,1)}, u32[]{:S(2)}, u32[]{:S(2)}) %collective-permute-start) | collective-permute-done | bytes 1769504 | tf_op jit(solution)/shard_map/ppermute | solution.py:40
  105.0 5.1 %convert_reduce_fusion = f32[3,256]{1,0:T(4,128)S(1)} fusion(bf16[3,256,6144]{2,1,0:T(8,128)(2,1)} %param.4), kind=kLoop, calls=%fused_computation.3 | loop fusion | flops 9436416 | bytes 9440256 | tf_op jit(solution)/shard_map/reduce_sum | solution.py:85
  110.2 6.3 %fusion.2 = f32[3,256]{1,0:T(4,128)S(1)} fusion(bf16[3,256,6144]{2,1,0:T(8,128)(2,1)} %param.4, f32[3,256]{1,0:T(4,128)S(1)} %broadcast_multiply_fusion), kind=kLoop, calls=%fused_computation.6 | loop fusion | flops 18873600 | bytes 9443328 | tf_op jit(solution)/shard_map/reduce_sum | solution.py:86
  116.5 34.0 %all-gather.7.cloned.1.call-done = bf16[3072,3,256]{0,2,1:T(8,128)(2,1)} async-done(((bf16[768,3,256]{0,2,1:T(8,128)(2,1)}), bf16[3072,3,256]{0,2,1:T(8,128)(2,1)}) %all-gather.7.cloned.1.call-update) | async-done | bytes 4718608 | tf_op jit(solution)/shard_map/all_gather | solution.py:31
  155.1 12.2 %fusion.3 = bf16[3,256,6144]{2,1,0:T(8,128)(2,1)} fusion(bf16[3,256,6144]{2,1,0:T(8,128)(2,1)} %param.4, f32[3,256]{1,0:T(4,128)S(1)} %add_rsqrt_fusion.10, f32[3,256]{1,0:T(4,128)S(1)} %broadcast_multiply_fusion), kind=kLoop, calls=%fused_computation.7 | loop fusion | flops 18874368 | bytes 18880512 | tf_op jit(solution)/shard_map/convert_element_type | solution.py:87
  169.7 4.0 fusion.22
  173.7 3.8 fusion.20
  177.5 2.5 constant_dynamic-slice_fusion.8
  183.2 3.7 fusion.65
  186.9 45.0 %collective-permute-done.1 = bf16[2304,3,256]{0,2,1:T(8,128)(2,1)} collective-permute-done((bf16[2304,3,256]{0,2,1:T(8,128)(2,1)S(1)}, bf16[2304,3,256]{0,2,1:T(8,128)(2,1)}, u32[]{:S(2)}, u32[]{:S(2)}) %collective-permute-start.1) | collective-permute-done | bytes 3538976 | tf_op jit(solution)/shard_map/ppermute | solution.py:40
  231.9 2.7 fusion.12
  234.6 13.2 %reshape.416 = f32[3,256,3,1,128]{4,2,1,0,3:T(4,128)S(1)} reshape(f32[768,384]{1,0:T(8,128)S(1)} %fusion.12) | data formatting | bytes 2359296 | tf_op jit(solution)/shard_map/reshape | solution.py:44
  248.6 3.3 multiply_reduce_fusion.8
  252.8 7.1 %fusion.72 = f32[768,768]{1,0:T(8,128)S(1)} fusion(bf16[768,3072]{1,0:T(8,128)(2,1)} %copy-done.1, bf16[3072,768]{0,1:T(8,128)(2,1)} %bitcast.188), kind=kOutput, calls=%fused_computation.173 | convolution fusion | flops 3623878656 | bytes 11796480 | tf_op jit(solution)/shard_map/dot_general | solution.py:114
  266.3 6.6 %add_add_fusion.1 = f32[768,768]{1,0:T(8,128)} fusion(f32[768,768]{1,0:T(8,128)S(1)} %copy-done.19, f32[768,768]{1,0:T(8,128)S(1)} %fusion.72, bf16[2304,768]{0,1:T(8,128)(2,1)} %bitcast.18, bf16[768,768]{1,0:T(8,128)(2,1)S(1)} %copy-done.10, bf16[768,768]{1,0:T(8,128)(2,1)S(1)} %copy-done.13, bf16[768,768]{1,0:T(8,128)(2,1)S(1)} %copy-done.7), kind=kOutput, calls=%fused_computation.16 | convolution fusion | flops 2729705472 | bytes 14155776 | tf_op jit(solution)/shard_map/dot_general | solution.py:117
  272.9 2.9 reshape.421
  279.9 7.3 %fusion.73 = f32[768,768]{1,0:T(8,128)S(1)} fusion(bf16[768,3072]{1,0:T(8,128)(2,1)} %copy-done.1, bf16[3072,768]{0,1:T(8,128)(2,1)} %bitcast.189), kind=kOutput, calls=%fused_computation.174 | convolution fusion | flops 3623878656 | bytes 11796480 | tf_op jit(solution)/shard_map/dot_general | solution.py:114
  287.2 54.8 %collective-permute-done.2 = bf16[2304,3,256]{0,2,1:T(8,128)(2,1)} collective-permute-done((bf16[2304,3,256]{0,2,1:T(8,128)(2,1)}, bf16[2304,3,256]{0,2,1:T(8,128)(2,1)}, u32[]{:S(2)}, u32[]{:S(2)}) %collective-permute-start.2) | collective-permute-done | bytes 3538976 | tf_op jit(solution)/shard_map/ppermute | solution.py:40
  342.0 6.4 %add_add_fusion = f32[768,768]{1,0:T(8,128)} fusion(f32[768,768]{1,0:T(8,128)S(1)} %copy-done.18, f32[768,768]{1,0:T(8,128)S(1)} %fusion.73, bf16[2304,768]{0,1:T(8,128)(2,1)} %bitcast.26, bf16[768,768]{1,0:T(8,128)(2,1)S(1)} %copy-done.11, bf16[768,768]{1,0:T(8,128)(2,1)S(1)} %copy-done.14, bf16[768,768]{1,0:T(8,128)(2,1)S(1)} %copy-done.8), kind=kOutput, calls=%fused_computation.15 | convolution fusion | flops 2729705472 | bytes 14155776 | tf_op jit(solution)/shard_map/dot_general | solution.py:117
  348.4 2.9 reshape.426
  355.2 11.1 %fusion.7 = f32[3,256,3,1,128]{1,4,2,0,3:T(8,128)S(1)} fusion(bf16[6144,3,128]{0,2,1:T(8,128)(2,1)} %all-gather.11.cloned.1.call-done, bf16[3,256,6144]{2,1,0:T(8,128)(2,1)} %fusion.3), kind=kOutput, calls=%fused_computation.23 | convolution fusion | flops 3623878656 | bytes 15335424 | tf_op jit(solution)/shard_map/dot_general | solution.py:107
  369.9 3.2 collective-permute-start.4
  373.2 3.1 collective-permute-done.4
  378.2 4.5 convolution_convert_fusion
  382.8 25.2 %reduce-scatter.2.cloned.1.call-done = bf16[48,3,1024]{2,0,1:T(8,128)(2,1)} async-done(((bf16[192,3,1024]{2,0,1:T(8,128)(2,1)}), bf16[48,3,1024]{2,0,1:T(8,128)(2,1)}) %reduce-scatter.2.cloned.1.call-update) | async-done | bytes 294928 | tf_op jit(solution)/shard_map/reduce_scatter | solution.py:133
  408.0 3.7 collective-permute-start.6
  415.4 17.1 %collective-permute-done.6 = bf16[48,3,1024]{2,0,1:T(8,128)(2,1)S(1)} collective-permute-done((bf16[48,3,1024]{2,0,1:T(8,128)(2,1)}, bf16[48,3,1024]{2,0,1:T(8,128)(2,1)S(1)}, u32[]{:S(2)}, u32[]{:S(2)}) %collective-permute-start.6) | collective-permute-done | bytes 294944 | tf_op jit(solution)/shard_map/ppermute | solution.py:143
  432.5 6.8 %collective-permute-done.7 = bf16[48,3,1024]{2,0,1:T(8,128)(2,1)S(1)} collective-permute-done((bf16[48,3,1024]{2,0,1:T(8,128)(2,1)}, bf16[48,3,1024]{2,0,1:T(8,128)(2,1)S(1)}, u32[]{:S(2)}, u32[]{:S(2)}) %collective-permute-start.7) | collective-permute-done | bytes 294944 | tf_op jit(solution)/shard_map/ppermute | solution.py:143
  (173 shorter events, 62.6 us)
Async XLA Ops:
  6.5 55.0 %all-gather.5.cloned.1.call-start = ((), (), s32[]{:S(2)}) async-start(), calls=%async_computation.1 | async-start | bytes 2949120 | tf_op jit(solution)/shard_map/all_gather | solution.py:31
  11.4 139.1 %all-gather.7.cloned.1.call-start = ((), (), s32[]{:S(2)}) async-start(), calls=%async_computation.2 | async-start | bytes 5898240 | tf_op jit(solution)/shard_map/all_gather | solution.py:31
  61.6 198.4 %all-gather.9.cloned.1.call-start = ((), (), s32[]{:S(2)}) async-start(), calls=%async_computation.3 | async-start | bytes 5898240 | tf_op jit(solution)/shard_map/all_gather | solution.py:31
  63.2 2.8 copy-start.17
  63.3 4.1 copy-start.16
  64.6 40.4 %collective-permute-start = (bf16[2304,3,128]{0,2,1:T(8,128)(2,1)}, bf16[2304,3,128]{0,2,1:T(8,128)(2,1)}, u32[]{:S(2)}, u32[]{:S(2)}) collective-permute-start(bf16[2304,3,128]{0,2,1:T(8,128)(2,1)} %pad_maximum_fusion.4), channel_id=1, source_target_pairs={{0,16},{16,0},{1,17},{17,1},{2,18},{18,2},{3,19},{19,3},{4,20},{20... | collective-permute-start | bytes 5308424 | tf_op jit(solution)/shard_map/ppermute | solution.py:40
  150.5 204.7 %all-gather.11.cloned.1.call-start = ((), (), s32[]{:S(2)}) async-start(), calls=%async_computation.4 | async-start | bytes 5898240 | tf_op jit(solution)/shard_map/all_gather | solution.py:75
  153.5 78.4 %collective-permute-start.1 = (bf16[2304,3,256]{0,2,1:T(8,128)(2,1)S(1)}, bf16[2304,3,256]{0,2,1:T(8,128)(2,1)}, u32[]{:S(2)}, u32[]{:S(2)}) collective-permute-start(bf16[2304,3,256]{0,2,1:T(8,128)(2,1)S(1)} %pad_maximum_fusion.1), channel_id=1, source_target_pairs={{0,16},{16,0},{1,17},{17,1},{2,18},{18,2},{3,19},{19,3},{4,20},{20... | collective-permute-start | bytes 10616840 | tf_op jit(solution)/shard_map/ppermute | solution.py:40
  167.3 2.4 copy-start.4
  167.3 6.4 %copy-start.5 = (bf16[768,3,256]{0,2,1:T(8,128)(2,1)S(1)}, bf16[768,3,256]{0,2,1:T(8,128)(2,1)}, u32[]{:S(2)}) copy-start(bf16[768,3,256]{0,2,1:T(8,128)(2,1)} %copy.179) | copy-start | bytes 3538948
  169.7 7.8 %copy-start = (bf16[3,256,6144]{2,1,0:T(8,128)(2,1)S(1)}, bf16[3,256,6144]{2,1,0:T(8,128)(2,1)}, u32[]{:S(2)}) copy-start(bf16[3,256,6144]{2,1,0:T(8,128)(2,1)} %fusion.3) | copy-start | bytes 28311556
  179.9 3.3 copy-start.12
  180.6 51.4 %copy-start.1 = (bf16[768,3072]{1,0:T(8,128)(2,1)}, bf16[768,3072]{1,0:T(8,128)(2,1)S(1)}, u32[]{:S(2)}) copy-start(bf16[768,3072]{1,0:T(8,128)(2,1)S(1)} %pad_maximum_fusion) | copy-start | bytes 14155780
  183.2 48.7 %copy-start.3 = (bf16[3072,3,128]{0,2,1:T(8,128)(2,1)S(1)}, bf16[3072,3,128]{0,2,1:T(8,128)(2,1)}, u32[]{:S(2)}) copy-start(bf16[3072,3,128]{0,2,1:T(8,128)(2,1)} %all-gather.5.cloned.1.call-done) | copy-start | bytes 7077892
  260.0 148.0 %reduce-scatter.2.cloned.1.call-start = ((), (), s32[]{:S(2)}) async-start(), calls=%async_computation.5 | async-start | bytes 1474560 | tf_op jit(solution)/shard_map/reduce_scatter | solution.py:133
  262.3 3.5 copy-start.7
  262.3 3.5 copy-start.10
  262.3 3.5 copy-start.13
  262.3 4.0 copy-start.19
  264.3 77.7 %collective-permute-start.2 = (bf16[2304,3,256]{0,2,1:T(8,128)(2,1)}, bf16[2304,3,256]{0,2,1:T(8,128)(2,1)}, u32[]{:S(2)}, u32[]{:S(2)}) collective-permute-start(bf16[2304,3,256]{0,2,1:T(8,128)(2,1)} %pad_maximum_fusion.3), channel_id=1, source_target_pairs={{0,16},{16,0},{1,17},{17,1},{2,18},{18,2},{3,19},{19,3},{4,20},{20... | collective-permute-start | bytes 10616840 | tf_op jit(solution)/shard_map/ppermute | solution.py:40
  279.9 62.1 %copy-start.8 = (bf16[768,768]{1,0:T(8,128)(2,1)S(1)}, bf16[768,768]{1,0:T(8,128)(2,1)}, u32[]{:S(2)}) copy-start(bf16[768,768]{1,0:T(8,128)(2,1)} %copy-done.6) | copy-start | bytes 3538948
  279.9 62.1 %copy-start.11 = (bf16[768,768]{1,0:T(8,128)(2,1)S(1)}, bf16[768,768]{1,0:T(8,128)(2,1)}, u32[]{:S(2)}) copy-start(bf16[768,768]{1,0:T(8,128)(2,1)} %get-tuple-element.38) | copy-start | bytes 3538948
  279.9 62.1 %copy-start.14 = (bf16[768,768]{1,0:T(8,128)(2,1)S(1)}, bf16[768,768]{1,0:T(8,128)(2,1)}, u32[]{:S(2)}) copy-start(bf16[768,768]{1,0:T(8,128)(2,1)} %get-tuple-element.39) | copy-start | bytes 3538948
  279.9 62.1 %copy-start.18 = (f32[768,768]{1,0:T(8,128)S(1)}, f32[768,768]{1,0:T(8,128)}, u32[]{:S(2)}) copy-start(f32[768,768]{1,0:T(8,128)} %fusion.20) | copy-start | bytes 7077892
  366.8 6.3 %copy-start.15 = (s32[4]{0:T(128)S(1)}, s32[4]{0:T(128)}, u32[]{:S(2)}) copy-start(s32[4]{0:T(128)} %compare_select_fusion) | copy-start | bytes 52
  367.4 5.8 %collective-permute-start.3 = (bf16[48,768]{1,0:T(8,128)(2,1)S(1)}, bf16[48,768]{1,0:T(8,128)(2,1)S(1)}, u32[]{:S(2)}, u32[]{:S(2)}) collective-permute-start(bf16[48,768]{1,0:T(8,128)(2,1)S(1)} %get-tuple-element.70), channel_id=1, source_target_pairs={{0,4},{4,8},{8,12},{12,0},{1,5},{5,9},{9,13},{13,1},{2,6},{6,10},{... | collective-permute-start | bytes 221192 | tf_op jit(solution)/shard_map/ppermute | solution.py:124
  369.9 6.5 %collective-permute-start.4 = (bf16[48,768]{1,0:T(8,128)(2,1)S(1)}, bf16[48,768]{1,0:T(8,128)(2,1)S(1)}, u32[]{:S(2)}, u32[]{:S(2)}) collective-permute-start(bf16[48,768]{1,0:T(8,128)(2,1)S(1)} %get-tuple-element.70), channel_id=1, source_target_pairs={{0,8},{4,12},{8,0},{12,4},{1,9},{5,13},{9,1},{13,5},{2,10},{6,14},... | collective-permute-start | bytes 221192 | tf_op jit(solution)/shard_map/ppermute | solution.py:124
  373.1 4.4 collective-permute-start.5
  408.0 24.5 %collective-permute-start.6 = (bf16[48,3,1024]{2,0,1:T(8,128)(2,1)}, bf16[48,3,1024]{2,0,1:T(8,128)(2,1)S(1)}, u32[]{:S(2)}, u32[]{:S(2)}) collective-permute-start(bf16[48,3,1024]{2,0,1:T(8,128)(2,1)} %reduce-scatter.2.cloned.1.call-done), channel_id=1, source_target_pairs={{0,0},{1,4},{2,8},{3,12},{4,1},{5,5},{6,9},{7,13},{8,2},{9,6},{10,... | collective-permute-start | bytes 884744 | tf_op jit(solution)/shard_map/ppermute | solution.py:143
  411.7 27.5 %collective-permute-start.7 = (bf16[48,3,1024]{2,0,1:T(8,128)(2,1)}, bf16[48,3,1024]{2,0,1:T(8,128)(2,1)S(1)}, u32[]{:S(2)}, u32[]{:S(2)}) collective-permute-start(bf16[48,3,1024]{2,0,1:T(8,128)(2,1)} %reduce-scatter.2.cloned.1.call-done), channel_id=1, source_target_pairs={{0,4},{1,8},{2,12},{3,0},{4,5},{5,9},{6,13},{7,1},{8,6},{9,10},{10... | collective-permute-start | bytes 884744 | tf_op jit(solution)/shard_map/ppermute | solution.py:143
  412.9 27.3 %collective-permute-start.8 = (bf16[48,3,1024]{2,0,1:T(8,128)(2,1)}, bf16[48,3,1024]{2,0,1:T(8,128)(2,1)S(1)}, u32[]{:S(2)}, u32[]{:S(2)}) collective-permute-start(bf16[48,3,1024]{2,0,1:T(8,128)(2,1)} %reduce-scatter.2.cloned.1.call-done), channel_id=1, source_target_pairs={{0,8},{1,12},{2,0},{3,4},{4,9},{5,13},{6,1},{7,5},{8,10},{9,14},{1... | collective-permute-start | bytes 884744 | tf_op jit(solution)/shard_map/ppermute | solution.py:143
  413.8 28.0 %collective-permute-start.9 = (bf16[48,3,1024]{2,0,1:T(8,128)(2,1)}, bf16[48,3,1024]{2,0,1:T(8,128)(2,1)S(1)}, u32[]{:S(2)}, u32[]{:S(2)}) collective-permute-start(bf16[48,3,1024]{2,0,1:T(8,128)(2,1)} %reduce-scatter.2.cloned.1.call-done), channel_id=1, source_target_pairs={{0,12},{1,0},{2,4},{3,8},{4,13},{5,1},{6,5},{7,9},{8,14},{9,2},{10... | collective-permute-start | bytes 884744 | tf_op jit(solution)/shard_map/ppermute | solution.py:143
  (3 other events, 4.6 us)
Sparse Core Ops, SparseCore 0:
  11.5 50.0 all-gather.4
  63.1 87.3 all-gather.6
  152.1 87.7 all-gather.8
  260.1 88.0 all-gather.10
  382.9 25.0 reduce-scatter.1

commit v16 on v15

--- a/solution.py
+++ b/solution.py
@@ -130,12 +130,17 @@
     partial_proj = jnp.einsum(
         "rc,ckt->rkt", pooled_all, conn_weight, preferred_element_type=jnp.float32
     )
-    clip_rows = lax.psum_scatter(
-        partial_proj.astype(jnp.bfloat16), "tensor", scatter_dimension=0, tiled=True
-    )
     n_tensor = lax.axis_size("tensor")
+    t = lax.axis_index("tensor")
+    sent = partial_proj.astype(jnp.bfloat16)
+    block = rows // n_tensor
+    total = lax.dynamic_slice_in_dim(sent, t * block, block, axis=0).astype(jnp.float32)
+    for k in range(1, n_tensor):
+        piece = lax.dynamic_slice_in_dim(sent, ((t + k) % n_tensor) * block, block, axis=0)
+        got = lax.ppermute(piece, "tensor", [(a, (a + k) % n_tensor) for a in range(n_tensor)])
+        total = total + got.astype(jnp.float32)
+    clip_rows = total.astype(jnp.bfloat16)
     if n_video == n_tensor:
-        t = lax.axis_index("tensor")
         pieces = [None] * n_tensor
         for k in range(n_tensor):
             pairs = [(a * n_tensor + b, ((b + k) % n_tensor) * n_tensor + a)

time: 454 us -> 433 us (0.954); the launches traced: 453 us -> 426 us
  waiting for transfers between devices: 254 us -> 238 us
  local copies, waits for them, and re-layouts: 58.3 us -> 45.9 us
    reduce_scatter x1 -> x0, waiting for transfers between devices: 25.2 us -> none  [per_device(): lax.psum_scatter(partial_proj.astype(jnp.bfloat16), 'tensor', scatter_dim...]
    reshape x3, local copies, waits for them, and re-layouts: 19 us -> 6.48 us  [attend(): proj = proj.reshape(nframes, PATCH, 3, heads, HD)]
    ppermute x0 -> x3, waiting for transfers between devices: none -> 11.7 us  [per_device(): lax.ppermute(piece, 'tensor', [(a, (a + k) % n_tensor) for a in range(n_t...]
  transfers between devices with their start and end apart: 15 -> 17, of which waited for: 13 -> 13; matrix products, arithmetic and copies ran while one was open for 29% -> 28% of each run, Pallas kernels for 0% -> 0%
where the time goes in v16:
time: 433 us; the launch traced here: 426 us
  waiting for transfers between devices  238 us (55%)
  matrix products  63.8 us (15%)
  local copies, waits for them, and re-layouts  45.9 us (11%)
  other arithmetic  36.4 us (8%)
  starting transfers between devices  19.9 us (5%)
  between operations  14.8 us (3%)
  blocking collectives  7.65 us (2%)
    ppermute x3, waiting for transfers between devices, forward(): return lax.ppermute(onward, 'groups', [(0, 1), (1, 0)])  119 us
    all_gather x3, waiting for transfers between devices, moved_weights(): gathered = lax.all_gather(mine, 'video', axis=0, tiled=True)  77.6 us
    ppermute x4, waiting for transfers between devices, per_device(): got = lax.ppermute(clip_rows, ('video', 'tensor'), pairs)  24.5 us
    dot_general x3, matrix products, per_device(): jnp.dot(own_half, gathered.reshape(n_video * half, width), preferred_elem...  17.6 us
    dot_general x3, matrix products, per_device(): jnp.dot(rolled, received.reshape((n_video - 1) * half, width), preferred_...  16.6 us
    convert_element_type x1, other arithmetic, per_device(): normed = normed.astype(jnp.bfloat16).reshape(patch_rows, frames.shape[2])  12.2 us
    unnamed x58, local copies, waits for them, and re-layouts  11.9 us
    ppermute x3, waiting for transfers between devices, per_device(): lax.ppermute(piece, 'tensor', [(a, (a + k) % n_tensor) for a in range(n_t...  11.7 us
  transfers between devices with their start and end apart: 17, of which 13 were waited for; matrix products, arithmetic and copies ran while one was open for 28% of the time, Pallas kernels for 0%

profile of v16, /device:TPU:10, one launch (start us, length us, event | category | flops | bytes accessed | tf_op | source)
XLA Modules:
  0.0 426.1 jit_solution(2278427198608820344)
XLA Ops:
  6.5 2.8 fusion.67
  11.4 2.7 fusion.68
  18.0 43.6 %all-gather.5.cloned.1.call-done = bf16[3072,3,128]{0,2,1:T(8,128)(2,1)} async-done(((bf16[768,3,128]{0,2,1:T(8,128)(2,1)}), bf16[3072,3,128]{0,2,1:T(8,128)(2,1)}) %all-gather.5.cloned.1.call-update) | async-done | bytes 2359312 | tf_op jit(solution)/shard_map/all_gather | solution.py:31
  67.6 7.6 %all-reduce = s32[12]{0:T(128)S(1)} all-reduce(s32[12]{0:T(128)S(1)} %dynamic-update-slice), channel_id=1, replica_groups=mesh['groups'=2,'video'=4,'tensor'=4] {'video'}, use_global_device_ids=true, to_apply=%add | all-reduce | flops 12 | bytes 96 | tf_op jit(solution)/shard_map/optimization_barrier | solution.py:112
  84.9 20.1 %collective-permute-done = bf16[2304,3,128]{0,2,1:T(8,128)(2,1)} collective-permute-done((bf16[2304,3,128]{0,2,1:T(8,128)(2,1)}, bf16[2304,3,128]{0,2,1:T(8,128)(2,1)}, u32[]{:S(2)}, u32[]{:S(2)}) %collective-permute-start) | collective-permute-done | bytes 1769504 | tf_op jit(solution)/shard_map/ppermute | solution.py:40
  105.0 5.1 %convert_reduce_fusion = f32[3,256]{1,0:T(4,128)S(1)} fusion(bf16[3,256,6144]{2,1,0:T(8,128)(2,1)} %param.4), kind=kLoop, calls=%fused_computation.3 | loop fusion | flops 9436416 | bytes 9440256 | tf_op jit(solution)/shard_map/reduce_sum | solution.py:85
  110.2 6.3 %fusion.2 = f32[3,256]{1,0:T(4,128)S(1)} fusion(bf16[3,256,6144]{2,1,0:T(8,128)(2,1)} %param.4, f32[3,256]{1,0:T(4,128)S(1)} %broadcast_multiply_fusion), kind=kLoop, calls=%fused_computation.6 | loop fusion | flops 18873600 | bytes 9443328 | tf_op jit(solution)/shard_map/reduce_sum | solution.py:86
  116.5 34.0 %all-gather.7.cloned.1.call-done = bf16[3072,3,256]{0,2,1:T(8,128)(2,1)} async-done(((bf16[768,3,256]{0,2,1:T(8,128)(2,1)}), bf16[3072,3,256]{0,2,1:T(8,128)(2,1)}) %all-gather.7.cloned.1.call-update) | async-done | bytes 4718608 | tf_op jit(solution)/shard_map/all_gather | solution.py:31
  154.9 12.2 %fusion.3 = bf16[3,256,6144]{2,1,0:T(8,128)(2,1)} fusion(bf16[3,256,6144]{2,1,0:T(8,128)(2,1)} %param.4, f32[3,256]{1,0:T(4,128)S(1)} %add_rsqrt_fusion.10, f32[3,256]{1,0:T(4,128)S(1)} %broadcast_multiply_fusion), kind=kLoop, calls=%fused_computation.7 | loop fusion | flops 18874368 | bytes 18880512 | tf_op jit(solution)/shard_map/convert_element_type | solution.py:87
  169.5 4.0 fusion.22
  173.5 3.8 fusion.20
  183.0 3.7 fusion.65
  186.7 45.0 %collective-permute-done.1 = bf16[2304,3,256]{0,2,1:T(8,128)(2,1)} collective-permute-done((bf16[2304,3,256]{0,2,1:T(8,128)(2,1)S(1)}, bf16[2304,3,256]{0,2,1:T(8,128)(2,1)}, u32[]{:S(2)}, u32[]{:S(2)}) %collective-permute-start.1) | collective-permute-done | bytes 3538976 | tf_op jit(solution)/shard_map/ppermute | solution.py:40
  231.7 2.7 fusion.12
  235.9 3.3 multiply_reduce_fusion.8
  240.1 7.2 %fusion.72 = f32[768,768]{1,0:T(8,128)S(1)} fusion(bf16[768,3072]{1,0:T(8,128)(2,1)} %copy-done.1, bf16[3072,768]{0,1:T(8,128)(2,1)} %bitcast.188), kind=kOutput, calls=%fused_computation.177 | convolution fusion | flops 3623878656 | bytes 11796480 | tf_op jit(solution)/shard_map/dot_general | solution.py:114
  253.6 6.6 %add_add_fusion.1 = f32[768,768]{1,0:T(8,128)} fusion(f32[768,768]{1,0:T(8,128)S(1)} %copy-done.19, f32[768,768]{1,0:T(8,128)S(1)} %fusion.72, bf16[2304,768]{0,1:T(8,128)(2,1)} %bitcast.18, bf16[768,768]{1,0:T(8,128)(2,1)S(1)} %copy-done.10, bf16[768,768]{1,0:T(8,128)(2,1)S(1)} %copy-done.13, bf16[768,768]{1,0:T(8,128)(2,1)S(1)} %copy-done.7), kind=kOutput, calls=%fused_computation.16 | convolution fusion | flops 2729705472 | bytes 14155776 | tf_op jit(solution)/shard_map/dot_general | solution.py:117
  260.2 2.9 reshape.421
  267.2 7.8 %fusion.73 = f32[768,768]{1,0:T(8,128)S(1)} fusion(bf16[768,3072]{1,0:T(8,128)(2,1)} %copy-done.1, bf16[3072,768]{0,1:T(8,128)(2,1)} %bitcast.189), kind=kOutput, calls=%fused_computation.178 | convolution fusion | flops 3623878656 | bytes 11796480 | tf_op jit(solution)/shard_map/dot_general | solution.py:114
  275.0 54.3 %collective-permute-done.2 = bf16[2304,3,256]{0,2,1:T(8,128)(2,1)} collective-permute-done((bf16[2304,3,256]{0,2,1:T(8,128)(2,1)}, bf16[2304,3,256]{0,2,1:T(8,128)(2,1)}, u32[]{:S(2)}, u32[]{:S(2)}) %collective-permute-start.2) | collective-permute-done | bytes 3538976 | tf_op jit(solution)/shard_map/ppermute | solution.py:40
  329.3 6.4 %add_add_fusion = f32[768,768]{1,0:T(8,128)} fusion(f32[768,768]{1,0:T(8,128)S(1)} %copy-done.18, f32[768,768]{1,0:T(8,128)S(1)} %fusion.73, bf16[2304,768]{0,1:T(8,128)(2,1)} %bitcast.26, bf16[768,768]{1,0:T(8,128)(2,1)S(1)} %copy-done.11, bf16[768,768]{1,0:T(8,128)(2,1)S(1)} %copy-done.14, bf16[768,768]{1,0:T(8,128)(2,1)S(1)} %copy-done.8), kind=kOutput, calls=%fused_computation.15 | convolution fusion | flops 2729705472 | bytes 14155776 | tf_op jit(solution)/shard_map/dot_general | solution.py:117
  335.6 2.9 reshape.426
  342.5 11.0 %fusion.7 = f32[3,256,3,1,128]{1,4,2,0,3:T(8,128)S(1)} fusion(bf16[6144,3,128]{0,2,1:T(8,128)(2,1)} %all-gather.11.cloned.1.call-done, bf16[3,256,6144]{2,1,0:T(8,128)(2,1)} %fusion.3), kind=kOutput, calls=%fused_computation.23 | convolution fusion | flops 3623878656 | bytes 15335424 | tf_op jit(solution)/shard_map/dot_general | solution.py:107
  357.0 3.2 collective-permute-start.4
  360.3 3.2 collective-permute-done.4
  365.3 3.5 convolution_convert_fusion
  371.0 6.7 %collective-permute-done.6 = bf16[48,3,1024]{2,0,1:T(8,128)(2,1)S(1)} collective-permute-done((bf16[48,3,1024]{2,0,1:T(8,128)(2,1)S(1)}, bf16[48,3,1024]{2,0,1:T(8,128)(2,1)S(1)}, u32[]{:S(2)}, u32[]{:S(2)}) %collective-permute-start.6) | collective-permute-done | bytes 294944 | tf_op jit(solution)/shard_map/ppermute | solution.py:140
  378.9 3.8 collective-permute-done.8
  382.9 3.4 collective-permute-start.9
  386.3 3.5 collective-permute-start.10
  390.6 14.1 %collective-permute-done.9 = bf16[48,3,1024]{2,0,1:T(8,128)(2,1)S(1)} collective-permute-done((bf16[48,3,1024]{2,0,1:T(8,128)(2,1)S(1)}, bf16[48,3,1024]{2,0,1:T(8,128)(2,1)S(1)}, u32[]{:S(2)}, u32[]{:S(2)}) %collective-permute-start.9) | collective-permute-done | bytes 294944 | tf_op jit(solution)/shard_map/ppermute | solution.py:148
  404.7 9.2 %collective-permute-done.10 = bf16[48,3,1024]{2,0,1:T(8,128)(2,1)S(1)} collective-permute-done((bf16[48,3,1024]{2,0,1:T(8,128)(2,1)S(1)}, bf16[48,3,1024]{2,0,1:T(8,128)(2,1)S(1)}, u32[]{:S(2)}, u32[]{:S(2)}) %collective-permute-start.10) | collective-permute-done | bytes 294944 | tf_op jit(solution)/shard_map/ppermute | solution.py:148
  (178 shorter events, 65.0 us)
Async XLA Ops:
  6.5 55.0 %all-gather.5.cloned.1.call-start = ((), (), s32[]{:S(2)}) async-start(), calls=%async_computation | async-start | bytes 2949120 | tf_op jit(solution)/shard_map/all_gather | solution.py:31
  11.4 139.1 %all-gather.7.cloned.1.call-start = ((), (), s32[]{:S(2)}) async-start(), calls=%async_computation.1 | async-start | bytes 5898240 | tf_op jit(solution)/shard_map/all_gather | solution.py:31
  61.6 185.7 %all-gather.9.cloned.1.call-start = ((), (), s32[]{:S(2)}) async-start(), calls=%async_computation.2 | async-start | bytes 5898240 | tf_op jit(solution)/shard_map/all_gather | solution.py:31
  63.3 4.1 copy-start.16
  64.6 40.4 %collective-permute-start = (bf16[2304,3,128]{0,2,1:T(8,128)(2,1)}, bf16[2304,3,128]{0,2,1:T(8,128)(2,1)}, u32[]{:S(2)}, u32[]{:S(2)}) collective-permute-start(bf16[2304,3,128]{0,2,1:T(8,128)(2,1)} %pad_maximum_fusion.4), channel_id=1, source_target_pairs={{0,16},{16,0},{1,17},{17,1},{2,18},{18,2},{3,19},{19,3},{4,20},{20... | collective-permute-start | bytes 5308424 | tf_op jit(solution)/shard_map/ppermute | solution.py:40
  150.5 192.0 %all-gather.11.cloned.1.call-start = ((), (), s32[]{:S(2)}) async-start(), calls=%async_computation.3 | async-start | bytes 5898240 | tf_op jit(solution)/shard_map/all_gather | solution.py:75
  153.3 78.4 %collective-permute-start.1 = (bf16[2304,3,256]{0,2,1:T(8,128)(2,1)S(1)}, bf16[2304,3,256]{0,2,1:T(8,128)(2,1)}, u32[]{:S(2)}, u32[]{:S(2)}) collective-permute-start(bf16[2304,3,256]{0,2,1:T(8,128)(2,1)S(1)} %pad_maximum_fusion.1), channel_id=1, source_target_pairs={{0,16},{16,0},{1,17},{17,1},{2,18},{18,2},{3,19},{19,3},{4,20},{20... | collective-permute-start | bytes 10616840 | tf_op jit(solution)/shard_map/ppermute | solution.py:40
  167.1 6.4 %copy-start.5 = (bf16[768,3,256]{0,2,1:T(8,128)(2,1)S(1)}, bf16[768,3,256]{0,2,1:T(8,128)(2,1)}, u32[]{:S(2)}) copy-start(bf16[768,3,256]{0,2,1:T(8,128)(2,1)} %copy.179) | copy-start | bytes 3538948
  169.5 7.8 %copy-start = (bf16[3,256,6144]{2,1,0:T(8,128)(2,1)S(1)}, bf16[3,256,6144]{2,1,0:T(8,128)(2,1)}, u32[]{:S(2)}) copy-start(bf16[3,256,6144]{2,1,0:T(8,128)(2,1)} %fusion.3) | copy-start | bytes 28311556
  179.7 3.3 copy-start.12
  180.4 51.3 %copy-start.1 = (bf16[768,3072]{1,0:T(8,128)(2,1)}, bf16[768,3072]{1,0:T(8,128)(2,1)S(1)}, u32[]{:S(2)}) copy-start(bf16[768,3072]{1,0:T(8,128)(2,1)S(1)} %pad_maximum_fusion) | copy-start | bytes 14155780
  183.0 48.7 %copy-start.3 = (bf16[3072,3,128]{0,2,1:T(8,128)(2,1)S(1)}, bf16[3072,3,128]{0,2,1:T(8,128)(2,1)}, u32[]{:S(2)}) copy-start(bf16[3072,3,128]{0,2,1:T(8,128)(2,1)} %all-gather.5.cloned.1.call-done) | copy-start | bytes 7077892
  249.6 3.5 copy-start.7
  249.6 3.5 copy-start.10
  249.6 3.5 copy-start.13
  249.6 4.0 copy-start.19
  251.6 77.7 %collective-permute-start.2 = (bf16[2304,3,256]{0,2,1:T(8,128)(2,1)}, bf16[2304,3,256]{0,2,1:T(8,128)(2,1)}, u32[]{:S(2)}, u32[]{:S(2)}) collective-permute-start(bf16[2304,3,256]{0,2,1:T(8,128)(2,1)} %pad_maximum_fusion.3), channel_id=1, source_target_pairs={{0,16},{16,0},{1,17},{17,1},{2,18},{18,2},{3,19},{19,3},{4,20},{20... | collective-permute-start | bytes 10616840 | tf_op jit(solution)/shard_map/ppermute | solution.py:40
  267.1 62.1 %copy-start.8 = (bf16[768,768]{1,0:T(8,128)(2,1)S(1)}, bf16[768,768]{1,0:T(8,128)(2,1)}, u32[]{:S(2)}) copy-start(bf16[768,768]{1,0:T(8,128)(2,1)} %copy-done.6) | copy-start | bytes 3538948
  267.2 62.1 %copy-start.11 = (bf16[768,768]{1,0:T(8,128)(2,1)S(1)}, bf16[768,768]{1,0:T(8,128)(2,1)}, u32[]{:S(2)}) copy-start(bf16[768,768]{1,0:T(8,128)(2,1)} %get-tuple-element.38) | copy-start | bytes 3538948
  267.2 62.1 %copy-start.14 = (bf16[768,768]{1,0:T(8,128)(2,1)S(1)}, bf16[768,768]{1,0:T(8,128)(2,1)}, u32[]{:S(2)}) copy-start(bf16[768,768]{1,0:T(8,128)(2,1)} %get-tuple-element.39) | copy-start | bytes 3538948
  267.2 62.1 %copy-start.18 = (f32[768,768]{1,0:T(8,128)S(1)}, f32[768,768]{1,0:T(8,128)}, u32[]{:S(2)}) copy-start(f32[768,768]{1,0:T(8,128)} %fusion.20) | copy-start | bytes 7077892
  353.9 6.3 %copy-start.15 = (s32[4]{0:T(128)S(1)}, s32[4]{0:T(128)}, u32[]{:S(2)}) copy-start(s32[4]{0:T(128)} %compare_select_fusion) | copy-start | bytes 52
  354.5 5.8 %collective-permute-start.3 = (bf16[48,768]{1,0:T(8,128)(2,1)S(1)}, bf16[48,768]{1,0:T(8,128)(2,1)S(1)}, u32[]{:S(2)}, u32[]{:S(2)}) collective-permute-start(bf16[48,768]{1,0:T(8,128)(2,1)S(1)} %get-tuple-element.73), channel_id=1, source_target_pairs={{0,4},{4,8},{8,12},{12,0},{1,5},{5,9},{9,13},{13,1},{2,6},{6,10},{... | collective-permute-start | bytes 221192 | tf_op jit(solution)/shard_map/ppermute | solution.py:124
  357.0 6.5 %collective-permute-start.4 = (bf16[48,768]{1,0:T(8,128)(2,1)S(1)}, bf16[48,768]{1,0:T(8,128)(2,1)S(1)}, u32[]{:S(2)}, u32[]{:S(2)}) collective-permute-start(bf16[48,768]{1,0:T(8,128)(2,1)S(1)} %get-tuple-element.73), channel_id=1, source_target_pairs={{0,8},{4,12},{8,0},{12,4},{1,9},{5,13},{9,1},{13,5},{2,10},{6,14},... | collective-permute-start | bytes 221192 | tf_op jit(solution)/shard_map/ppermute | solution.py:124
  360.2 4.4 %collective-permute-start.5 = (bf16[48,768]{1,0:T(8,128)(2,1)S(1)}, bf16[48,768]{1,0:T(8,128)(2,1)S(1)}, u32[]{:S(2)}, u32[]{:S(2)}) collective-permute-start(bf16[48,768]{1,0:T(8,128)(2,1)S(1)} %get-tuple-element.73), channel_id=1, source_target_pairs={{0,12},{4,0},{8,4},{12,8},{1,13},{5,1},{9,5},{13,9},{2,14},{6,2},{... | collective-permute-start | bytes 221192 | tf_op jit(solution)/shard_map/ppermute | solution.py:124
  368.9 8.8 %collective-permute-start.6 = (bf16[48,3,1024]{2,0,1:T(8,128)(2,1)S(1)}, bf16[48,3,1024]{2,0,1:T(8,128)(2,1)S(1)}, u32[]{:S(2)}, u32[]{:S(2)}) collective-permute-start(bf16[48,3,1024]{2,0,1:T(8,128)(2,1)S(1)} %get-tuple-element.67), channel_id=1, source_target_pairs={{0,1},{1,2},{2,3},{3,0},{4,5},{5,6},{6,7},{7,4},{8,9},{9,10},{10,1... | collective-permute-start | bytes 884744 | tf_op jit(solution)/shard_map/ppermute | solution.py:140
  369.0 9.9 %collective-permute-start.7 = (bf16[48,3,1024]{2,0,1:T(8,128)(2,1)S(1)}, bf16[48,3,1024]{2,0,1:T(8,128)(2,1)S(1)}, u32[]{:S(2)}, u32[]{:S(2)}) collective-permute-start(bf16[48,3,1024]{2,0,1:T(8,128)(2,1)S(1)} %get-tuple-element.69), channel_id=1, source_target_pairs={{0,2},{1,3},{2,0},{3,1},{4,6},{5,7},{6,4},{7,5},{8,10},{9,11},{10,... | collective-permute-start | bytes 884744 | tf_op jit(solution)/shard_map/ppermute | solution.py:140
  369.6 13.1 %collective-permute-start.8 = (bf16[48,3,1024]{2,0,1:T(8,128)(2,1)S(1)}, bf16[48,3,1024]{2,0,1:T(8,128)(2,1)S(1)}, u32[]{:S(2)}, u32[]{:S(2)}) collective-permute-start(bf16[48,3,1024]{2,0,1:T(8,128)(2,1)S(1)} %get-tuple-element.68), channel_id=1, source_target_pairs={{0,3},{1,0},{2,1},{3,2},{4,7},{5,4},{6,5},{7,6},{8,11},{9,8},{10,9... | collective-permute-start | bytes 884744 | tf_op jit(solution)/shard_map/ppermute | solution.py:140
  382.9 21.9 %collective-permute-start.9 = (bf16[48,3,1024]{2,0,1:T(8,128)(2,1)S(1)}, bf16[48,3,1024]{2,0,1:T(8,128)(2,1)S(1)}, u32[]{:S(2)}, u32[]{:S(2)}) collective-permute-start(bf16[48,3,1024]{2,0,1:T(8,128)(2,1)S(1)} %add_convert_fusion), channel_id=1, source_target_pairs={{0,0},{1,4},{2,8},{3,12},{4,1},{5,5},{6,9},{7,13},{8,2},{9,6},{10,... | collective-permute-start | bytes 884744 | tf_op jit(solution)/shard_map/ppermute | solution.py:148
  386.3 27.6 %collective-permute-start.10 = (bf16[48,3,1024]{2,0,1:T(8,128)(2,1)S(1)}, bf16[48,3,1024]{2,0,1:T(8,128)(2,1)S(1)}, u32[]{:S(2)}, u32[]{:S(2)}) collective-permute-start(bf16[48,3,1024]{2,0,1:T(8,128)(2,1)S(1)} %add_convert_fusion), channel_id=1, source_target_pairs={{0,4},{1,8},{2,12},{3,0},{4,5},{5,9},{6,13},{7,1},{8,6},{9,10},{10... | collective-permute-start | bytes 884744 | tf_op jit(solution)/shard_map/ppermute | solution.py:148
  389.7 24.2 %collective-permute-start.11 = (bf16[48,3,1024]{2,0,1:T(8,128)(2,1)S(1)}, bf16[48,3,1024]{2,0,1:T(8,128)(2,1)S(1)}, u32[]{:S(2)}, u32[]{:S(2)}) collective-permute-start(bf16[48,3,1024]{2,0,1:T(8,128)(2,1)S(1)} %add_convert_fusion), channel_id=1, source_target_pairs={{0,8},{1,12},{2,0},{3,4},{4,9},{5,13},{6,1},{7,5},{8,10},{9,14},{1... | collective-permute-start | bytes 884744 | tf_op jit(solution)/shard_map/ppermute | solution.py:148
  389.7 25.4 %collective-permute-start.12 = (bf16[48,3,1024]{2,0,1:T(8,128)(2,1)S(1)}, bf16[48,3,1024]{2,0,1:T(8,128)(2,1)S(1)}, u32[]{:S(2)}, u32[]{:S(2)}) collective-permute-start(bf16[48,3,1024]{2,0,1:T(8,128)(2,1)S(1)} %add_convert_fusion), channel_id=1, source_target_pairs={{0,12},{1,0},{2,4},{3,8},{4,13},{5,1},{6,5},{7,9},{8,14},{9,2},{10... | collective-permute-start | bytes 884744 | tf_op jit(solution)/shard_map/ppermute | solution.py:148
  (5 other events, 9.8 us)
Sparse Core Ops, SparseCore 0:
  11.5 50.0 all-gather.4
  63.1 87.3 all-gather.6
  152.1 87.8 all-gather.8
  247.5 88.0 all-gather.10

commit v17 on v16

--- a/solution.py
+++ b/solution.py
@@ -98,7 +98,12 @@
     )
     if len(moved) > 2 and moved[1][3] is not None:
         moved[1][3], own_half = lax.optimization_barrier((moved[1][3], own_half))
-    video_all = lax.all_gather(frame_video, "video", axis=0, tiled=True)
+    ids = [frame_video] + [
+        lax.ppermute(frame_video, "video", [(a, (a + k) % n_video) for a in range(n_video)])
+        for k in range(1, n_video)
+    ]
+    ids_from = jnp.argsort(jnp.stack([(v - k) % n_video for k in range(n_video)]))
+    video_all = jnp.take(jnp.stack(ids), ids_from, axis=0).reshape(-1)
     pooled_parts = []
     for index, size in enumerate(sizes):
         width = 3 * size * HD

time: 433 us -> 431 us (level)
  blocking collectives: 7.65 us -> 0 us
  starting transfers between devices: 19.9 us -> 24.4 us
    optimization_barrier x1 -> x0, blocking collectives: 7.65 us -> none  [per_device(): video_all, received = lax.optimization_barrier((video_all, received))]
    ppermute x0 -> x3, starting transfers between devices: none -> 5.61 us  [per_device(): lax.ppermute(frame_video, 'video', [(a, (a + k) % n_video) for a in range...]
    unnamed x58 -> x55, local copies, waits for them, and re-layouts: 11.9 us -> 11.3 us
  transfers between devices with their start and end apart: 17 -> 20, of which waited for: 13 -> 13; matrix products, arithmetic and copies ran while one was open for 28% -> 28% of each run, Pallas kernels for 0% -> 0%
where the time goes in v17:
time: 431 us; the launch traced here: 423 us
  waiting for transfers between devices  239 us (55%)
  matrix products  63.8 us (15%)
  local copies, waits for them, and re-layouts  45.9 us (11%)
  other arithmetic  36.6 us (8%)
  starting transfers between devices  24.4 us (6%)
  between operations  14.2 us (3%)
    ppermute x3, waiting for transfers between devices, forward(): return lax.ppermute(onward, 'groups', [(0, 1), (1, 0)])  122 us
    all_gather x3, waiting for transfers between devices, moved_weights(): gathered = lax.all_gather(mine, 'video', axis=0, tiled=True)  77.6 us
    ppermute x4, waiting for transfers between devices, per_device(): got = lax.ppermute(clip_rows, ('video', 'tensor'), pairs)  24.5 us
    dot_general x3, matrix products, per_device(): jnp.dot(own_half, gathered.reshape(n_video * half, width), preferred_elem...  17.6 us
    dot_general x3, matrix products, per_device(): jnp.dot(rolled, received.reshape((n_video - 1) * half, width), preferred_...  16.6 us
    convert_element_type x1, other arithmetic, per_device(): normed = normed.astype(jnp.bfloat16).reshape(patch_rows, frames.shape[2])  12.2 us
    unnamed x55, local copies, waits for them, and re-layouts  11.3 us
    dot_general x1, matrix products, per_device(): proj = jnp.dot(normed, full, preferred_element_type=jnp.float32)  11 us
  transfers between devices with their start and end apart: 20, of which 13 were waited for; matrix products, arithmetic and copies ran while one was open for 28% of the time, Pallas kernels for 0%

profile of v17, /device:TPU:10, one launch (start us, length us, event | category | flops | bytes accessed | tf_op | source)
XLA Modules:
  0.0 423.4 jit_solution(11651524342442306222)
XLA Ops:
  6.5 2.8 fusion.67
  11.4 2.7 fusion.68
  18.0 43.6 %all-gather.5.cloned.1.call-done = bf16[3072,3,128]{0,2,1:T(8,128)(2,1)} async-done(((bf16[768,3,128]{0,2,1:T(8,128)(2,1)}), bf16[3072,3,128]{0,2,1:T(8,128)(2,1)}) %all-gather.5.cloned.1.call-update) | async-done | bytes 2359312 | tf_op jit(solution)/shard_map/all_gather | solution.py:31
  68.2 3.5 collective-permute-start.3
  82.2 22.9 %collective-permute-done = bf16[2304,3,128]{0,2,1:T(8,128)(2,1)} collective-permute-done((bf16[2304,3,128]{0,2,1:T(8,128)(2,1)}, bf16[2304,3,128]{0,2,1:T(8,128)(2,1)}, u32[]{:S(2)}, u32[]{:S(2)}) %collective-permute-start) | collective-permute-done | bytes 1769504 | tf_op jit(solution)/shard_map/ppermute | solution.py:40
  105.0 5.1 %convert_reduce_fusion = f32[3,256]{1,0:T(4,128)S(1)} fusion(bf16[3,256,6144]{2,1,0:T(8,128)(2,1)} %param.4), kind=kLoop, calls=%fused_computation.4 | loop fusion | flops 9436416 | bytes 9440256 | tf_op jit(solution)/shard_map/reduce_sum | solution.py:85
  110.2 6.3 %fusion.2 = f32[3,256]{1,0:T(4,128)S(1)} fusion(bf16[3,256,6144]{2,1,0:T(8,128)(2,1)} %param.4, f32[3,256]{1,0:T(4,128)S(1)} %broadcast_multiply_fusion), kind=kLoop, calls=%fused_computation.7 | loop fusion | flops 18873600 | bytes 9443328 | tf_op jit(solution)/shard_map/reduce_sum | solution.py:86
  116.5 34.0 %all-gather.7.cloned.1.call-done = bf16[3072,3,256]{0,2,1:T(8,128)(2,1)} async-done(((bf16[768,3,256]{0,2,1:T(8,128)(2,1)}), bf16[3072,3,256]{0,2,1:T(8,128)(2,1)}) %all-gather.7.cloned.1.call-update) | async-done | bytes 4718608 | tf_op jit(solution)/shard_map/all_gather | solution.py:31
  154.8 12.2 %fusion.3 = bf16[3,256,6144]{2,1,0:T(8,128)(2,1)} fusion(bf16[3,256,6144]{2,1,0:T(8,128)(2,1)} %param.4, f32[3,256]{1,0:T(4,128)S(1)} %add_rsqrt_fusion.10, f32[3,256]{1,0:T(4,128)S(1)} %broadcast_multiply_fusion), kind=kLoop, calls=%fused_computation.8 | loop fusion | flops 18874368 | bytes 18880512 | tf_op jit(solution)/shard_map/convert_element_type | solution.py:87
  169.4 4.0 fusion.22
  173.4 3.8 fusion.20
  177.2 2.5 constant_dynamic-slice_fusion.11
  182.9 3.6 fusion.65
  186.6 45.1 %collective-permute-done.1 = bf16[2304,3,256]{0,2,1:T(8,128)(2,1)} collective-permute-done((bf16[2304,3,256]{0,2,1:T(8,128)(2,1)S(1)}, bf16[2304,3,256]{0,2,1:T(8,128)(2,1)}, u32[]{:S(2)}, u32[]{:S(2)}) %collective-permute-start.1) | collective-permute-done | bytes 3538976 | tf_op jit(solution)/shard_map/ppermute | solution.py:40
  231.7 2.7 fusion.12
  235.9 3.3 multiply_reduce_fusion.8
  240.1 7.1 %fusion.72 = f32[768,768]{1,0:T(8,128)S(1)} fusion(bf16[768,3072]{1,0:T(8,128)(2,1)} %copy-done.1, bf16[3072,768]{0,1:T(8,128)(2,1)} %bitcast.191), kind=kOutput, calls=%fused_computation.180 | convolution fusion | flops 3623878656 | bytes 11796480 | tf_op jit(solution)/shard_map/dot_general | solution.py:119
  253.6 6.6 %add_add_fusion.1 = f32[768,768]{1,0:T(8,128)} fusion(f32[768,768]{1,0:T(8,128)S(1)} %copy-done.19, f32[768,768]{1,0:T(8,128)S(1)} %fusion.72, bf16[2304,768]{0,1:T(8,128)(2,1)} %bitcast.21, bf16[768,768]{1,0:T(8,128)(2,1)S(1)} %copy-done.10, bf16[768,768]{1,0:T(8,128)(2,1)S(1)} %copy-done.13, bf16[768,768]{1,0:T(8,128)(2,1)S(1)} %copy-done.7), kind=kOutput, calls=%fused_computation.17 | convolution fusion | flops 2729705472 | bytes 14155776 | tf_op jit(solution)/shard_map/dot_general | solution.py:122
  260.1 2.9 reshape.426
  267.2 7.8 %fusion.73 = f32[768,768]{1,0:T(8,128)S(1)} fusion(bf16[768,3072]{1,0:T(8,128)(2,1)} %copy-done.1, bf16[3072,768]{0,1:T(8,128)(2,1)} %bitcast.192), kind=kOutput, calls=%fused_computation.181 | convolution fusion | flops 3623878656 | bytes 11796480 | tf_op jit(solution)/shard_map/dot_general | solution.py:119
  274.9 54.3 %collective-permute-done.5 = bf16[2304,3,256]{0,2,1:T(8,128)(2,1)} collective-permute-done((bf16[2304,3,256]{0,2,1:T(8,128)(2,1)}, bf16[2304,3,256]{0,2,1:T(8,128)(2,1)}, u32[]{:S(2)}, u32[]{:S(2)}) %collective-permute-start.5) | collective-permute-done | bytes 3538976 | tf_op jit(solution)/shard_map/ppermute | solution.py:40
  329.2 6.4 %add_add_fusion = f32[768,768]{1,0:T(8,128)} fusion(f32[768,768]{1,0:T(8,128)S(1)} %copy-done.18, f32[768,768]{1,0:T(8,128)S(1)} %fusion.73, bf16[2304,768]{0,1:T(8,128)(2,1)} %bitcast.29, bf16[768,768]{1,0:T(8,128)(2,1)S(1)} %copy-done.11, bf16[768,768]{1,0:T(8,128)(2,1)S(1)} %copy-done.14, bf16[768,768]{1,0:T(8,128)(2,1)S(1)} %copy-done.8), kind=kOutput, calls=%fused_computation.16 | convolution fusion | flops 2729705472 | bytes 14155776 | tf_op jit(solution)/shard_map/dot_general | solution.py:122
  335.6 2.9 reshape.431
  342.5 11.0 %fusion.7 = f32[3,256,3,1,128]{1,4,2,0,3:T(8,128)S(1)} fusion(bf16[6144,3,128]{0,2,1:T(8,128)(2,1)} %all-gather.11.cloned.1.call-done, bf16[3,256,6144]{2,1,0:T(8,128)(2,1)} %fusion.3), kind=kOutput, calls=%fused_computation.24 | convolution fusion | flops 3623878656 | bytes 15335424 | tf_op jit(solution)/shard_map/dot_general | solution.py:112
  354.5 2.5 collective-permute-start.6
  357.0 3.2 collective-permute-start.7
  365.2 3.5 convolution_convert_fusion
  369.9 8.8 %collective-permute-done.10 = bf16[48,3,1024]{2,0,1:T(8,128)(2,1)S(1)} collective-permute-done((bf16[48,3,1024]{2,0,1:T(8,128)(2,1)S(1)}, bf16[48,3,1024]{2,0,1:T(8,128)(2,1)S(1)}, u32[]{:S(2)}, u32[]{:S(2)}) %collective-permute-start.10) | collective-permute-done | bytes 294944 | tf_op jit(solution)/shard_map/ppermute | solution.py:145
  380.2 3.4 collective-permute-start.12
  383.6 3.4 collective-permute-start.13
  388.0 14.2 %collective-permute-done.12 = bf16[48,3,1024]{2,0,1:T(8,128)(2,1)S(1)} collective-permute-done((bf16[48,3,1024]{2,0,1:T(8,128)(2,1)S(1)}, bf16[48,3,1024]{2,0,1:T(8,128)(2,1)S(1)}, u32[]{:S(2)}, u32[]{:S(2)}) %collective-permute-start.12) | collective-permute-done | bytes 294944 | tf_op jit(solution)/shard_map/ppermute | solution.py:153
  402.2 9.1 %collective-permute-done.13 = bf16[48,3,1024]{2,0,1:T(8,128)(2,1)S(1)} collective-permute-done((bf16[48,3,1024]{2,0,1:T(8,128)(2,1)S(1)}, bf16[48,3,1024]{2,0,1:T(8,128)(2,1)S(1)}, u32[]{:S(2)}, u32[]{:S(2)}) %collective-permute-start.13) | collective-permute-done | bytes 294944 | tf_op jit(solution)/shard_map/ppermute | solution.py:153
  (184 shorter events, 64.2 us)
Async XLA Ops:
  6.5 55.0 %all-gather.5.cloned.1.call-start = ((), (), s32[]{:S(2)}) async-start(), calls=%async_computation | async-start | bytes 2949120 | tf_op jit(solution)/shard_map/all_gather | solution.py:31
  11.4 139.1 %all-gather.7.cloned.1.call-start = ((), (), s32[]{:S(2)}) async-start(), calls=%async_computation.1 | async-start | bytes 5898240 | tf_op jit(solution)/shard_map/all_gather | solution.py:31
  61.6 185.7 %all-gather.9.cloned.1.call-start = ((), (), s32[]{:S(2)}) async-start(), calls=%async_computation.2 | async-start | bytes 5898240 | tf_op jit(solution)/shard_map/all_gather | solution.py:31
  64.6 40.4 %collective-permute-start = (bf16[2304,3,128]{0,2,1:T(8,128)(2,1)}, bf16[2304,3,128]{0,2,1:T(8,128)(2,1)}, u32[]{:S(2)}, u32[]{:S(2)}) collective-permute-start(bf16[2304,3,128]{0,2,1:T(8,128)(2,1)} %pad_maximum_fusion.4), channel_id=1, source_target_pairs={{0,16},{16,0},{1,17},{17,1},{2,18},{18,2},{3,19},{19,3},{4,20},{20... | collective-permute-start | bytes 5308424 | tf_op jit(solution)/shard_map/ppermute | solution.py:40
  66.1 14.8 %collective-permute-start.4 = (s32[3]{0:T(128)S(1)}, s32[3]{0:T(128)S(1)}, u32[]{:S(2)}, u32[]{:S(2)}) collective-permute-start(s32[3]{0:T(128)S(1)} %copy-done.17), channel_id=1, source_target_pairs={{0,12},{4,0},{8,4},{12,8},{1,13},{5,1},{9,5},{13,9},{2,14},{6,2},{... | collective-permute-start | bytes 44 | tf_op jit(solution)/shard_map/ppermute | solution.py:102
  68.2 12.7 %collective-permute-start.2 = (s32[3]{0:T(128)S(1)}, s32[3]{0:T(128)S(1)}, u32[]{:S(2)}, u32[]{:S(2)}) collective-permute-start(s32[3]{0:T(128)S(1)} %copy-done.17), channel_id=1, source_target_pairs={{0,4},{4,8},{8,12},{12,0},{1,5},{5,9},{9,13},{13,1},{2,6},{6,10},{... | collective-permute-start | bytes 44 | tf_op jit(solution)/shard_map/ppermute | solution.py:102
  68.2 12.7 %collective-permute-start.3 = (s32[3]{0:T(128)S(1)}, s32[3]{0:T(128)}, u32[]{:S(2)}, u32[]{:S(2)}) collective-permute-start(s32[3]{0:T(128)S(1)} %copy-done.17), channel_id=1, source_target_pairs={{0,8},{4,12},{8,0},{12,4},{1,9},{5,13},{9,1},{13,5},{2,10},{6,14},... | collective-permute-start | bytes 44 | tf_op jit(solution)/shard_map/ppermute | solution.py:102
  80.8 29.3 %copy-start.15 = (pred[4]{0:T(512)(128)(4,1)}, pred[4]{0:T(512)(128)(4,1)S(1)}, u32[]{:S(2)}) copy-start(pred[4]{0:T(512)(128)(4,1)S(1)} %compare_and_fusion.1) | copy-start | bytes 16
  150.5 192.0 %all-gather.11.cloned.1.call-start = ((), (), s32[]{:S(2)}) async-start(), calls=%async_computation.3 | async-start | bytes 5898240 | tf_op jit(solution)/shard_map/all_gather | solution.py:75
  153.2 78.4 %collective-permute-start.1 = (bf16[2304,3,256]{0,2,1:T(8,128)(2,1)S(1)}, bf16[2304,3,256]{0,2,1:T(8,128)(2,1)}, u32[]{:S(2)}, u32[]{:S(2)}) collective-permute-start(bf16[2304,3,256]{0,2,1:T(8,128)(2,1)S(1)} %pad_maximum_fusion.1), channel_id=1, source_target_pairs={{0,16},{16,0},{1,17},{17,1},{2,18},{18,2},{3,19},{19,3},{4,20},{20... | collective-permute-start | bytes 10616840 | tf_op jit(solution)/shard_map/ppermute | solution.py:40
  167.0 6.4 %copy-start.5 = (bf16[768,3,256]{0,2,1:T(8,128)(2,1)S(1)}, bf16[768,3,256]{0,2,1:T(8,128)(2,1)}, u32[]{:S(2)}) copy-start(bf16[768,3,256]{0,2,1:T(8,128)(2,1)} %copy.179) | copy-start | bytes 3538948
  169.4 7.8 %copy-start = (bf16[3,256,6144]{2,1,0:T(8,128)(2,1)S(1)}, bf16[3,256,6144]{2,1,0:T(8,128)(2,1)}, u32[]{:S(2)}) copy-start(bf16[3,256,6144]{2,1,0:T(8,128)(2,1)} %fusion.3) | copy-start | bytes 28311556
  180.3 51.4 %copy-start.1 = (bf16[768,3072]{1,0:T(8,128)(2,1)}, bf16[768,3072]{1,0:T(8,128)(2,1)S(1)}, u32[]{:S(2)}) copy-start(bf16[768,3072]{1,0:T(8,128)(2,1)S(1)} %pad_maximum_fusion) | copy-start | bytes 14155780
  182.9 48.8 %copy-start.3 = (bf16[3072,3,128]{0,2,1:T(8,128)(2,1)S(1)}, bf16[3072,3,128]{0,2,1:T(8,128)(2,1)}, u32[]{:S(2)}) copy-start(bf16[3072,3,128]{0,2,1:T(8,128)(2,1)} %all-gather.5.cloned.1.call-done) | copy-start | bytes 7077892
  249.5 3.5 copy-start.7
  249.6 4.0 copy-start.19
  251.5 77.7 %collective-permute-start.5 = (bf16[2304,3,256]{0,2,1:T(8,128)(2,1)}, bf16[2304,3,256]{0,2,1:T(8,128)(2,1)}, u32[]{:S(2)}, u32[]{:S(2)}) collective-permute-start(bf16[2304,3,256]{0,2,1:T(8,128)(2,1)} %pad_maximum_fusion.3), channel_id=1, source_target_pairs={{0,16},{16,0},{1,17},{17,1},{2,18},{18,2},{3,19},{19,3},{4,20},{20... | collective-permute-start | bytes 10616840 | tf_op jit(solution)/shard_map/ppermute | solution.py:40
  267.1 62.1 %copy-start.8 = (bf16[768,768]{1,0:T(8,128)(2,1)S(1)}, bf16[768,768]{1,0:T(8,128)(2,1)}, u32[]{:S(2)}) copy-start(bf16[768,768]{1,0:T(8,128)(2,1)} %copy-done.6) | copy-start | bytes 3538948
  267.1 62.1 %copy-start.11 = (bf16[768,768]{1,0:T(8,128)(2,1)S(1)}, bf16[768,768]{1,0:T(8,128)(2,1)}, u32[]{:S(2)}) copy-start(bf16[768,768]{1,0:T(8,128)(2,1)} %get-tuple-element.38) | copy-start | bytes 3538948
  267.1 62.1 %copy-start.14 = (bf16[768,768]{1,0:T(8,128)(2,1)S(1)}, bf16[768,768]{1,0:T(8,128)(2,1)}, u32[]{:S(2)}) copy-start(bf16[768,768]{1,0:T(8,128)(2,1)} %get-tuple-element.39) | copy-start | bytes 3538948
  267.1 62.1 %copy-start.18 = (f32[768,768]{1,0:T(8,128)S(1)}, f32[768,768]{1,0:T(8,128)}, u32[]{:S(2)}) copy-start(f32[768,768]{1,0:T(8,128)} %fusion.20) | copy-start | bytes 7077892
  353.9 6.3 %copy-start.16 = (pred[4]{0:T(512)(128)(4,1)S(1)}, pred[4]{0:T(512)(128)(4,1)}, u32[]{:S(2)}) copy-start(pred[4]{0:T(512)(128)(4,1)} %copy-done.15) | copy-start | bytes 16
  354.5 6.5 %collective-permute-start.6 = (bf16[48,768]{1,0:T(8,128)(2,1)S(1)}, bf16[48,768]{1,0:T(8,128)(2,1)S(1)}, u32[]{:S(2)}, u32[]{:S(2)}) collective-permute-start(bf16[48,768]{1,0:T(8,128)(2,1)S(1)} %get-tuple-element.73), channel_id=1, source_target_pairs={{0,4},{4,8},{8,12},{12,0},{1,5},{5,9},{9,13},{13,1},{2,6},{6,10},{... | collective-permute-start | bytes 221192 | tf_op jit(solution)/shard_map/ppermute | solution.py:129
  357.0 6.4 %collective-permute-start.7 = (bf16[48,768]{1,0:T(8,128)(2,1)S(1)}, bf16[48,768]{1,0:T(8,128)(2,1)S(1)}, u32[]{:S(2)}, u32[]{:S(2)}) collective-permute-start(bf16[48,768]{1,0:T(8,128)(2,1)S(1)} %get-tuple-element.73), channel_id=1, source_target_pairs={{0,8},{4,12},{8,0},{12,4},{1,9},{5,13},{9,1},{13,5},{2,10},{6,14},... | collective-permute-start | bytes 221192 | tf_op jit(solution)/shard_map/ppermute | solution.py:129
  360.2 4.4 %collective-permute-start.8 = (bf16[48,768]{1,0:T(8,128)(2,1)S(1)}, bf16[48,768]{1,0:T(8,128)(2,1)S(1)}, u32[]{:S(2)}, u32[]{:S(2)}) collective-permute-start(bf16[48,768]{1,0:T(8,128)(2,1)S(1)} %get-tuple-element.73), channel_id=1, source_target_pairs={{0,12},{4,0},{8,4},{12,8},{1,13},{5,1},{9,5},{13,9},{2,14},{6,2},{... | collective-permute-start | bytes 221192 | tf_op jit(solution)/shard_map/ppermute | solution.py:129
  368.8 9.9 %collective-permute-start.10 = (bf16[48,3,1024]{2,0,1:T(8,128)(2,1)S(1)}, bf16[48,3,1024]{2,0,1:T(8,128)(2,1)S(1)}, u32[]{:S(2)}, u32[]{:S(2)}) collective-permute-start(bf16[48,3,1024]{2,0,1:T(8,128)(2,1)S(1)} %get-tuple-element.69), channel_id=1, source_target_pairs={{0,2},{1,3},{2,0},{3,1},{4,6},{5,7},{6,4},{7,5},{8,10},{9,11},{10,... | collective-permute-start | bytes 884744 | tf_op jit(solution)/shard_map/ppermute | solution.py:145
  369.4 10.6 %collective-permute-start.11 = (bf16[48,3,1024]{2,0,1:T(8,128)(2,1)S(1)}, bf16[48,3,1024]{2,0,1:T(8,128)(2,1)S(1)}, u32[]{:S(2)}, u32[]{:S(2)}) collective-permute-start(bf16[48,3,1024]{2,0,1:T(8,128)(2,1)S(1)} %get-tuple-element.68), channel_id=1, source_target_pairs={{0,3},{1,0},{2,1},{3,2},{4,7},{5,4},{6,5},{7,6},{8,11},{9,8},{10,9... | collective-permute-start | bytes 884744 | tf_op jit(solution)/shard_map/ppermute | solution.py:145
  369.4 10.6 %collective-permute-start.9 = (bf16[48,3,1024]{2,0,1:T(8,128)(2,1)S(1)}, bf16[48,3,1024]{2,0,1:T(8,128)(2,1)S(1)}, u32[]{:S(2)}, u32[]{:S(2)}) collective-permute-start(bf16[48,3,1024]{2,0,1:T(8,128)(2,1)S(1)} %get-tuple-element.67), channel_id=1, source_target_pairs={{0,1},{1,2},{2,3},{3,0},{4,5},{5,6},{6,7},{7,4},{8,9},{9,10},{10,1... | collective-permute-start | bytes 884744 | tf_op jit(solution)/shard_map/ppermute | solution.py:145
  380.2 22.0 %collective-permute-start.12 = (bf16[48,3,1024]{2,0,1:T(8,128)(2,1)S(1)}, bf16[48,3,1024]{2,0,1:T(8,128)(2,1)S(1)}, u32[]{:S(2)}, u32[]{:S(2)}) collective-permute-start(bf16[48,3,1024]{2,0,1:T(8,128)(2,1)S(1)} %add_convert_fusion), channel_id=1, source_target_pairs={{0,0},{1,4},{2,8},{3,12},{4,1},{5,5},{6,9},{7,13},{8,2},{9,6},{10,... | collective-permute-start | bytes 884744 | tf_op jit(solution)/shard_map/ppermute | solution.py:153
  383.6 27.6 %collective-permute-start.13 = (bf16[48,3,1024]{2,0,1:T(8,128)(2,1)S(1)}, bf16[48,3,1024]{2,0,1:T(8,128)(2,1)S(1)}, u32[]{:S(2)}, u32[]{:S(2)}) collective-permute-start(bf16[48,3,1024]{2,0,1:T(8,128)(2,1)S(1)} %add_convert_fusion), channel_id=1, source_target_pairs={{0,4},{1,8},{2,12},{3,0},{4,5},{5,9},{6,13},{7,1},{8,6},{9,10},{10... | collective-permute-start | bytes 884744 | tf_op jit(solution)/shard_map/ppermute | solution.py:153
  387.1 24.2 %collective-permute-start.14 = (bf16[48,3,1024]{2,0,1:T(8,128)(2,1)S(1)}, bf16[48,3,1024]{2,0,1:T(8,128)(2,1)S(1)}, u32[]{:S(2)}, u32[]{:S(2)}) collective-permute-start(bf16[48,3,1024]{2,0,1:T(8,128)(2,1)S(1)} %add_convert_fusion), channel_id=1, source_target_pairs={{0,8},{1,12},{2,0},{3,4},{4,9},{5,13},{6,1},{7,5},{8,10},{9,14},{1... | collective-permute-start | bytes 884744 | tf_op jit(solution)/shard_map/ppermute | solution.py:153
  387.2 25.2 %collective-permute-start.15 = (bf16[48,3,1024]{2,0,1:T(8,128)(2,1)S(1)}, bf16[48,3,1024]{2,0,1:T(8,128)(2,1)S(1)}, u32[]{:S(2)}, u32[]{:S(2)}) collective-permute-start(bf16[48,3,1024]{2,0,1:T(8,128)(2,1)S(1)} %add_convert_fusion), channel_id=1, source_target_pairs={{0,12},{1,0},{2,4},{3,8},{4,13},{5,1},{6,5},{7,9},{8,14},{9,2},{10... | collective-permute-start | bytes 884744 | tf_op jit(solution)/shard_map/ppermute | solution.py:153
  (8 other events, 20.0 us)
Sparse Core Ops, SparseCore 0:
  11.5 50.0 all-gather.4
  63.1 87.2 all-gather.6
  152.0 87.8 all-gather.8
  247.4 87.9 all-gather.10
